TPU v7x, 32 devices: a whole 2x2x4 slice. The times are simulated.
32 devices in a mesh: grp: 2 (over y), ub: 4 (over x, core), it: 4 (over z).
Axes of the slice: x: 2, y: 2, z: 4, core: 2. Of those that a mesh axis runs over, the one named last changes fastest.
Arguments:
- user_factors: float32 [2048, 128], P(('grp', 'ub')), parts along dimension 0, may hold values from -2.5 to 2.5
- item_factors: float32 [8192, 128], P(('grp', 'ub', 'it')), parts along dimension 0, may hold values from -2.5 to 2.5
- item_index: int32 [3, 2048, 32], P(None, ('grp', 'ub'), 'it'), parts along dimension 1, may hold values from 0 to 255
- labels: int32 [3, 2048, 32], P(None, ('grp', 'ub'), 'it'), parts along dimension 1, may hold values 0 or 1
- confidence: float32 [3, 2048, 32], P(None, ('grp', 'ub'), 'it'), parts along dimension 1, may hold values from 0.2 to 5
Outputs:
- users_out: float32 [2048, 128], P(('grp', 'ub')), parts along dimension 0
- items_out: float32 [8192, 128], P(('grp', 'ub', 'it')), parts along dimension 0
There are 2 independent parts, one for each index of `grp`. A program takes and returns all parts, laid end to end along the dimension named above; each array names one. Nothing has to cross between parts.
Inputs may be any that keep to these rules, and one draw needn't show every extreme that they name: `item_index`: item indices count within a slab of 256 items.
All inputs are finite; a program needn't handle non-finite values. No bound on the sum of `labels` on one device may be relied on, other than what follows from the above.
Results may differ from a plain program's by a relative error of at most 0.00016.
Values sent between devices are 32-bit elements; how exact they have to be, the bound alone decides.
No kernel may reach another device: no remote copies, remote signals or barrier semaphores. Data moves between devices by JAX's collectives and lax.ppermute only.
A program may use at most 64 MiB of HBM per device.

v0:
```python
import math

import jax
import jax.numpy as jnp
from jax import lax
from jax.sharding import PartitionSpec as P

INNER = 2


LR_USER = 0.02
LR_ITEM = 0.05
LAMBDA_REG = 1.0


def from_behind(block, axis, distance):
    devices = range(lax.axis_size(axis))
    route = [((i - distance) % len(devices), i) for i in devices]
    return lax.ppermute(block, axis, route)


def residual_tile(user_rows, item_rows, weight, target):
    scores = jnp.dot(user_rows, item_rows.T, precision=lax.Precision.HIGHEST)
    return weight * jax.nn.sigmoid(scores) - target


def build_tiles(index_rows, label_rows, conf_rows, slab_width):
    user_count, slot_count = index_rows.shape
    block_rows = math.gcd(user_count, 128)
    nblocks = user_count // block_rows
    columns = jnp.arange(slab_width, dtype=jnp.int32)

    def one_block(packed):
        index_part, label_part, conf_part = packed
        matches = (index_part[:, :, None] == columns).astype(jnp.float32)
        paired = jnp.stack([conf_part, conf_part * label_part.astype(jnp.float32)], 0)
        return jnp.einsum("aun,unc->auc", paired, matches, precision=lax.Precision.HIGHEST)

    stacked = lax.map(
        one_block,
        (
            index_rows.reshape(nblocks, block_rows, slot_count),
            label_rows.reshape(nblocks, block_rows, slot_count),
            conf_rows.reshape(nblocks, block_rows, slot_count),
        ),
    )
    weight = stacked[:, 0].reshape(user_count, slab_width)
    target = stacked[:, 1].reshape(user_count, slab_width)
    return (weight, target)


def per_device(user_factors, item_factors, item_index, labels, confidence):
    strata = item_index.shape[0]
    user_rows = user_factors
    slab = item_factors
    for stratum in range(strata):
        if stratum > 0:
            slab = from_behind(slab, "ub", 1)
        weight, target = build_tiles(
            item_index[stratum], labels[stratum], confidence[stratum], slab.shape[0]
        )
        for inner_step in range(INNER):
            residual = residual_tile(user_rows, slab, weight, target)
            partial_grad = jnp.dot(residual, slab, precision=lax.Precision.HIGHEST)
            gradient = lax.psum(partial_grad, "it")
            user_rows = user_rows - LR_USER * (gradient + LAMBDA_REG * user_rows)
        residual = residual_tile(user_rows, slab, weight, target)
        item_grad = lax.dot_general(
            residual, user_rows, (((0,), (0,)), ((), ())), precision=lax.Precision.HIGHEST
        )
        slab = slab - LR_ITEM * (item_grad + LAMBDA_REG * slab)
    slab = from_behind(slab, "ub", 1 - strata)
    return (user_rows, slab)


def solution(mesh):
    return jax.shard_map(
        per_device,
        mesh=mesh,
        in_specs=(
            P(("grp", "ub"), None),
            P(("grp", "ub", "it"), None),
            P(None, ("grp", "ub"), "it"),
            P(None, ("grp", "ub"), "it"),
            P(None, ("grp", "ub"), "it"),
        ),
        out_specs=(P(("grp", "ub"), None), P(("grp", "ub", "it"), None)),
        check_vma=False,
    )
```

profile of v0, /device:TPU:0, one launch (start us, length us, event | category | flops | bytes accessed | tf_op | source)
XLA Modules:
  0.0 261.9 jit_solution(14107777373600627613)
XLA Ops:
  9.6 2.0 while.33
  13.4 1.0 fusion.70
  14.6 37.1 %all-reduce.7.cloned.1.call-done = f32[256,128]{1,0:T(8,128)} async-done(((f32[256,128]{1,0:T(8,128)}), f32[256,128]{1,0:T(8,128)}) %all-reduce.7.cloned.1.call-update) | async-done | bytes 131088 | tf_op jit(solution)/shard_map/psum | solution.py:65
  51.7 1.3 fusion.51
  53.1 1.0 fusion.71
  54.3 2.0 while.34
  56.3 32.6 %all-reduce.9.cloned.1.call-done = f32[256,128]{1,0:T(8,128)} async-done(((f32[256,128]{1,0:T(8,128)}), f32[256,128]{1,0:T(8,128)}) %all-reduce.9.cloned.1.call-update) | async-done | bytes 131088 | tf_op jit(solution)/shard_map/psum | solution.py:65
  88.9 0.9 multiply_subtract_fusion.4
  91.4 3.9 %collective-permute-done = f32[256,128]{1,0:T(8,128)S(1)} collective-permute-done((f32[256,128]{1,0:T(8,128)S(1)}, f32[256,128]{1,0:T(8,128)S(1)}, u32[]{:S(2)}, u32[]{:S(2)}) %collective-permute-start) | collective-permute-done | bytes 131104 | tf_op jit(solution)/shard_map/ppermute | solution.py:19
  95.7 1.0 fusion.72
  97.0 34.0 %all-reduce.11.cloned.1.call-done = f32[256,128]{1,0:T(8,128)} async-done(((f32[256,128]{1,0:T(8,128)}), f32[256,128]{1,0:T(8,128)}) %all-reduce.11.cloned.1.call-update) | async-done | bytes 131088 | tf_op jit(solution)/shard_map/psum | solution.py:65
  131.0 1.3 fusion.36
  132.3 1.0 fusion.73
  133.6 2.0 while.35
  135.6 32.4 %all-reduce.13.cloned.1.call-done = f32[256,128]{1,0:T(8,128)} async-done(((f32[256,128]{1,0:T(8,128)}), f32[256,128]{1,0:T(8,128)}) %all-reduce.13.cloned.1.call-update) | async-done | bytes 131088 | tf_op jit(solution)/shard_map/psum | solution.py:65
  168.0 0.9 multiply_subtract_fusion.2
  170.5 3.9 %collective-permute-done.1 = f32[256,128]{1,0:T(8,128)S(1)} collective-permute-done((f32[256,128]{1,0:T(8,128)S(1)}, f32[256,128]{1,0:T(8,128)S(1)}, u32[]{:S(2)}, u32[]{:S(2)}) %collective-permute-start.1) | collective-permute-done | bytes 131104 | tf_op jit(solution)/shard_map/ppermute | solution.py:19
  174.9 1.0 fusion.74
  176.0 34.2 %all-reduce.15.cloned.1.call-done = f32[256,128]{1,0:T(8,128)} async-done(((f32[256,128]{1,0:T(8,128)}), f32[256,128]{1,0:T(8,128)}) %all-reduce.15.cloned.1.call-update) | async-done | bytes 131088 | tf_op jit(solution)/shard_map/psum | solution.py:65
  210.1 1.3 fusion.21
  211.5 1.0 fusion.75
  212.5 34.7 %all-reduce.17.cloned.1.call-done = f32[256,128]{1,0:T(8,128)} async-done(((f32[256,128]{1,0:T(8,128)}), f32[256,128]{1,0:T(8,128)}) %all-reduce.17.cloned.1.call-update) | async-done | bytes 131088 | tf_op jit(solution)/shard_map/psum | solution.py:65
  249.4 1.5 collective-permute-start.2
  250.9 3.5 %collective-permute-done.2 = f32[256,128]{1,0:T(8,128)S(1)} collective-permute-done((f32[256,128]{1,0:T(8,128)S(1)}, f32[256,128]{1,0:T(8,128)S(1)}, u32[]{:S(2)}, u32[]{:S(2)}) %collective-permute-start.2) | collective-permute-done | bytes 131104 | tf_op jit(solution)/shard_map/ppermute | solution.py:19
  (89 shorter events, 17.3 us)
Async XLA Ops:
  7.2 44.6 %all-reduce.7.cloned.1.call-start = ((), (), s32[]{:S(2)}) async-start(), calls=%async_computation | async-start | bytes 262144 | tf_op jit(solution)/shard_map/psum | solution.py:65
  7.9 0.7 copy-start.6
  8.7 0.7 copy-start.7
  12.0 0.9 copy-start
  12.0 1.0 copy-start.2
  14.4 74.5 %all-reduce.9.cloned.1.call-start = ((), (), s32[]{:S(2)}) async-start(), calls=%async_computation.1 | async-start | bytes 262144 | tf_op jit(solution)/shard_map/psum | solution.py:65
  54.1 76.9 %all-reduce.11.cloned.1.call-start = ((), (), s32[]{:S(2)}) async-start(), calls=%async_computation.2 | async-start | bytes 262144 | tf_op jit(solution)/shard_map/psum | solution.py:65
  54.3 34.6 %copy-start.4 = (f32[256,128]{1,0:T(8,128)S(1)}, f32[256,128]{1,0:T(8,128)}, u32[]{:S(2)}) copy-start(f32[256,128]{1,0:T(8,128)} %all-reduce.7.cloned.1.call-done) | copy-start | bytes 393220
  90.9 4.4 %collective-permute-start = (f32[256,128]{1,0:T(8,128)S(1)}, f32[256,128]{1,0:T(8,128)S(1)}, u32[]{:S(2)}, u32[]{:S(2)}) collective-permute-start(f32[256,128]{1,0:T(8,128)S(1)} %fusion.62), channel_id=1, source_target_pairs={{12,0},{0,4},{4,8},{8,12},{13,1},{1,5},{5,9},{9,13},{14,2},{2,6},{... | collective-permute-start | bytes 393224 | tf_op jit(solution)/shard_map/ppermute | solution.py:19
  96.8 71.2 %all-reduce.13.cloned.1.call-start = ((), (), s32[]{:S(2)}) async-start(), calls=%async_computation.3 | async-start | bytes 262144 | tf_op jit(solution)/shard_map/psum | solution.py:65
  133.4 76.7 %all-reduce.15.cloned.1.call-start = ((), (), s32[]{:S(2)}) async-start(), calls=%async_computation.4 | async-start | bytes 262144 | tf_op jit(solution)/shard_map/psum | solution.py:65
  133.6 34.4 %copy-start.3 = (f32[256,128]{1,0:T(8,128)S(1)}, f32[256,128]{1,0:T(8,128)}, u32[]{:S(2)}) copy-start(f32[256,128]{1,0:T(8,128)} %all-reduce.11.cloned.1.call-done) | copy-start | bytes 393220
  170.0 4.4 %collective-permute-start.1 = (f32[256,128]{1,0:T(8,128)S(1)}, f32[256,128]{1,0:T(8,128)S(1)}, u32[]{:S(2)}, u32[]{:S(2)}) collective-permute-start(f32[256,128]{1,0:T(8,128)S(1)} %fusion.60), channel_id=1, source_target_pairs={{12,0},{0,4},{4,8},{8,12},{13,1},{1,5},{5,9},{9,13},{14,2},{2,6},{... | collective-permute-start | bytes 393224 | tf_op jit(solution)/shard_map/ppermute | solution.py:19
  175.9 71.3 %all-reduce.17.cloned.1.call-start = ((), (), s32[]{:S(2)}) async-start(), calls=%async_computation.5 | async-start | bytes 262144 | tf_op jit(solution)/shard_map/psum | solution.py:65
  212.5 34.7 %copy-start.5 = (f32[256,128]{1,0:T(8,128)S(1)}, f32[256,128]{1,0:T(8,128)}, u32[]{:S(2)}) copy-start(f32[256,128]{1,0:T(8,128)} %all-reduce.15.cloned.1.call-done) | copy-start | bytes 393220
  248.1 0.7 copy-start.1
  249.4 5.0 %collective-permute-start.2 = (f32[256,128]{1,0:T(8,128)S(1)}, f32[256,128]{1,0:T(8,128)S(1)}, u32[]{:S(2)}, u32[]{:S(2)}) collective-permute-start(f32[256,128]{1,0:T(8,128)S(1)} %fusion.58), channel_id=1, source_target_pairs={{8,0},{12,4},{0,8},{4,12},{9,1},{13,5},{1,9},{5,13},{10,2},{14,6},... | collective-permute-start | bytes 393224 | tf_op jit(solution)/shard_map/ppermute | solution.py:19
Sparse Core Ops, SparseCore 0:
  14.6 37.1 all-reduce.6
  54.7 34.1 all-reduce.8
  96.9 34.0 all-reduce.10
  133.9 34.1 all-reduce.12
  176.0 34.0 all-reduce.14
  213.0 34.1 all-reduce.16
where the time goes:
time: 262 us
  waiting for transfers between devices  217 us (83%)
  matrix products  19 us (7%)
  between operations  14.4 us (5%)
  local copies, waits for them, and re-layouts  6.94 us (3%)
  other arithmetic  2.89 us (1%)
    psum x6, waiting for transfers between devices, per_device(): gradient = lax.psum(partial_grad, 'it')  205 us
    ppermute x3, waiting for transfers between devices, from_behind(): return lax.ppermute(block, axis, route)  11.4 us
    dot_general x9, matrix products, residual_tile(): scores = jnp.dot(user_rows, item_rows.T, precision=lax.Precision.HIGHEST)  6.41 us
    dot_general x6, matrix products, per_device(): partial_grad = jnp.dot(residual, slab, precision=lax.Precision.HIGHEST)  6.22 us
  transfers between devices with their start and end apart: 9, of which 9 were waited for; matrix products, arithmetic and copies ran while one was open for 2% of the time, Pallas kernels for 0%

commit v1 on v0

--- a/solution.py
+++ b/solution.py
@@ -17,6 +17,16 @@
     devices = range(lax.axis_size(axis))
     route = [((i - distance) % len(devices), i) for i in devices]
     return lax.ppermute(block, axis, route)
+
+
+def sum_over(block, axis):
+    count = lax.axis_size(axis)
+    step = 1
+    while step < count:
+        partner = lax.ppermute(block, axis, [(i, i ^ step) for i in range(count)])
+        block = block + partner
+        step *= 2
+    return block
 
 
 def residual_tile(user_rows, item_rows, weight, target):
@@ -62,7 +72,7 @@
         for inner_step in range(INNER):
             residual = residual_tile(user_rows, slab, weight, target)
             partial_grad = jnp.dot(residual, slab, precision=lax.Precision.HIGHEST)
-            gradient = lax.psum(partial_grad, "it")
+            gradient = sum_over(partial_grad, "it")
             user_rows = user_rows - LR_USER * (gradient + LAMBDA_REG * user_rows)
         residual = residual_tile(user_rows, slab, weight, target)
         item_grad = lax.dot_general(

time: 262 us -> 111 us (0.42)
  waiting for transfers between devices: 217 us -> 73.6 us
  starting transfers between devices: 1.84 us -> 15.9 us
  between operations: 14.4 us -> 0.98 us
  matrix products: 19 us -> 12.3 us
    psum x6 -> x0, waiting for transfers between devices: 205 us -> none  [per_device(): gradient = lax.psum(partial_grad, 'it')]
    ppermute x0 -> x12, waiting for transfers between devices: none -> 60.4 us  [sum_over(): partner = lax.ppermute(block, axis, [(i, i ^ step) for i in range(count)])]
    ppermute x0 -> x12, starting transfers between devices: none -> 15.5 us  [sum_over(): partner = lax.ppermute(block, axis, [(i, i ^ step) for i in range(count)])]
    dot_general x6, matrix products: 6.22 us -> 2.26 us  [per_device(): partial_grad = jnp.dot(residual, slab, precision=lax.Precision.HIGHEST)]
    dot_general x9, matrix products: 6.41 us -> 3.69 us  [residual_tile(): scores = jnp.dot(user_rows, item_rows.T, precision=lax.Precision.HIGHEST)]
    sub x3, other arithmetic: 2.8 us -> 0.16 us  [per_device(): user_rows = user_rows - LR_USER * (gradient + LAMBDA_REG * user_rows)]
  transfers between devices with their start and end apart: 9 -> 15, of which waited for: 9 -> 15; matrix products, arithmetic and copies ran while one was open for 2% -> 5% of each run, Pallas kernels for 0% -> 0%
where the time goes in v1:
time: 111 us; the launch traced here: 110 us
  waiting for transfers between devices  73.6 us (66%)
  starting transfers between devices  15.9 us (14%)
  matrix products  12.3 us (11%)
  local copies, waits for them, and re-layouts  6.92 us (6%)
    ppermute x12, waiting for transfers between devices, sum_over(): partner = lax.ppermute(block, axis, [(i, i ^ step) for i in range(count)])  60.4 us
    ppermute x12, starting transfers between devices, sum_over(): partner = lax.ppermute(block, axis, [(i, i ^ step) for i in range(count)])  15.5 us
    ppermute x3, waiting for transfers between devices, from_behind(): return lax.ppermute(block, axis, route)  13.2 us
    dot_general x6, matrix products, one_block(): jnp.einsum('aun,unc->auc', paired, matches, precision=lax.Precision.HIGHEST)  4.6 us
    dot_general x9, matrix products, residual_tile(): scores = jnp.dot(user_rows, item_rows.T, precision=lax.Precision.HIGHEST)  3.69 us
    unnamed x17, local copies, waits for them, and re-layouts  3.27 us
    dot_general x6, matrix products, per_device(): partial_grad = jnp.dot(residual, slab, precision=lax.Precision.HIGHEST)  2.26 us
  transfers between devices with their start and end apart: 15, of which 15 were waited for; matrix products, arithmetic and copies ran while one was open for 5% of the time, Pallas kernels for 0%

profile of v1, /device:TPU:0, one launch (start us, length us, event | category | flops | bytes accessed | tf_op | source)
XLA Modules:
  0.0 110.4 jit_solution(11612242489081050829)
XLA Ops:
  3.0 2.0 %while.33 = (s32[]{:T(128)}, f32[2,2,128,256]{3,1,2,0:T(2,128)S(1)}, s32[2,128,8]{2,1,0:T(8,128)S(1)}, f32[2,128,8]{1,2,0:T(8,128)S(1)}, s32[2,128,8]{1,2,0:T(8,128)S(1)}, /*index=5*/s32[]{:T(128)}) while((s32[]{:T(128)}, f32[2,2,128,256]{3,1,2,0:T(2,128)S(1)}, s32[2,128,8]{2,1,0:T(8,128)S(1)}, f32[2,128,8]{1,2,0:T(8,128)S(1)}, ...), condition=%wide.region_1.2_spmd.clone, body=%wide.region_0.1_spmd.clone.sunk | while | flops 6557698 | bytes 516177 | solution.py:49
  7.2 3.1 %collective-permute-start = (f32[256,128]{1,0:T(8,128)S(1)}, f32[256,128]{1,0:T(8,128)S(1)}, u32[]{:S(2)}, u32[]{:S(2)}) collective-permute-start(f32[256,128]{1,0:T(8,128)S(1)} %fusion.67), channel_id=1, source_target_pairs={{0,1},{1,0},{2,3},{3,2},{4,5},{5,4},{6,7},{7,6},{8,9},{9,8},{10,11... | collective-permute-start | bytes 393224 | tf_op jit(solution)/shard_map/ppermute | solution.py:26
  10.3 3.5 %collective-permute-done = f32[256,128]{1,0:T(8,128)S(1)} collective-permute-done((f32[256,128]{1,0:T(8,128)S(1)}, f32[256,128]{1,0:T(8,128)S(1)}, u32[]{:S(2)}, u32[]{:S(2)}) %collective-permute-start) | collective-permute-done | bytes 131104 | tf_op jit(solution)/shard_map/ppermute | solution.py:26
  13.8 2.8 %collective-permute-start.1 = (f32[256,128]{1,0:T(8,128)S(1)}, f32[256,128]{1,0:T(8,128)S(1)}, u32[]{:S(2)}, u32[]{:S(2)}) collective-permute-start(f32[256,128]{1,0:T(8,128)S(1)} %add.100), channel_id=1, source_target_pairs={{0,2},{1,3},{2,0},{3,1},{4,6},{5,7},{6,4},{7,5},{8,10},{9,11},{10,... | collective-permute-start | bytes 393224 | tf_op jit(solution)/shard_map/ppermute | solution.py:26
  16.6 5.6 %collective-permute-done.1 = f32[256,128]{1,0:T(8,128)S(1)} collective-permute-done((f32[256,128]{1,0:T(8,128)S(1)}, f32[256,128]{1,0:T(8,128)S(1)}, u32[]{:S(2)}, u32[]{:S(2)}) %collective-permute-start.1) | collective-permute-done | bytes 131104 | tf_op jit(solution)/shard_map/ppermute | solution.py:26
  23.8 4.3 %collective-permute-done.2 = f32[256,128]{1,0:T(8,128)S(1)} collective-permute-done((f32[256,128]{1,0:T(8,128)S(1)}, f32[256,128]{1,0:T(8,128)S(1)}, u32[]{:S(2)}, u32[]{:S(2)}) %collective-permute-start.2) | collective-permute-done | bytes 131104 | tf_op jit(solution)/shard_map/ppermute | solution.py:26
  28.1 2.0 %collective-permute-start.3 = (f32[256,128]{1,0:T(8,128)S(1)}, f32[256,128]{1,0:T(8,128)S(1)}, u32[]{:S(2)}, u32[]{:S(2)}) collective-permute-start(f32[256,128]{1,0:T(8,128)S(1)} %add.104), channel_id=1, source_target_pairs={{0,2},{1,3},{2,0},{3,1},{4,6},{5,7},{6,4},{7,5},{8,10},{9,11},{10,... | collective-permute-start | bytes 393224 | tf_op jit(solution)/shard_map/ppermute | solution.py:26
  30.2 2.0 %while.34 = (s32[]{:T(128)}, f32[2,2,128,256]{3,1,2,0:T(2,128)S(1)}, s32[2,128,8]{2,1,0:T(8,128)S(1)}, f32[2,128,8]{1,2,0:T(8,128)S(1)}, s32[2,128,8]{1,2,0:T(8,128)S(1)}, /*index=5*/s32[]{:T(128)}) while((s32[]{:T(128)}, f32[2,2,128,256]{3,1,2,0:T(2,128)S(1)}, s32[2,128,8]{2,1,0:T(8,128)S(1)}, f32[2,128,8]{1,2,0:T(8,128)S(1)}, ...), condition=%wide.region_3.4_spmd.clone, body=%wide.region_2.3_spmd.clone.sunk | while | flops 6557698 | bytes 516177 | solution.py:49
  32.2 3.2 %collective-permute-done.3 = f32[256,128]{1,0:T(8,128)S(1)} collective-permute-done((f32[256,128]{1,0:T(8,128)S(1)}, f32[256,128]{1,0:T(8,128)S(1)}, u32[]{:S(2)}, u32[]{:S(2)}) %collective-permute-start.3) | collective-permute-done | bytes 131104 | tf_op jit(solution)/shard_map/ppermute | solution.py:26
  37.0 3.9 %collective-permute-done.4 = f32[256,128]{1,0:T(8,128)S(1)} collective-permute-done((f32[256,128]{1,0:T(8,128)S(1)}, f32[256,128]{1,0:T(8,128)S(1)}, u32[]{:S(2)}, u32[]{:S(2)}) %collective-permute-start.4) | collective-permute-done | bytes 131104 | tf_op jit(solution)/shard_map/ppermute | solution.py:19
  42.1 4.7 %collective-permute-done.5 = f32[256,128]{1,0:T(8,128)S(1)} collective-permute-done((f32[256,128]{1,0:T(8,128)S(1)}, f32[256,128]{1,0:T(8,128)S(1)}, u32[]{:S(2)}, u32[]{:S(2)}) %collective-permute-start.5) | collective-permute-done | bytes 131104 | tf_op jit(solution)/shard_map/ppermute | solution.py:26
  46.8 1.9 %collective-permute-start.6 = (f32[256,128]{1,0:T(8,128)S(1)}, f32[256,128]{1,0:T(8,128)S(1)}, u32[]{:S(2)}, u32[]{:S(2)}) collective-permute-start(f32[256,128]{1,0:T(8,128)S(1)} %add.110), channel_id=1, source_target_pairs={{0,2},{1,3},{2,0},{3,1},{4,6},{5,7},{6,4},{7,5},{8,10},{9,11},{10,... | collective-permute-start | bytes 393224 | tf_op jit(solution)/shard_map/ppermute | solution.py:26
  48.7 5.5 %collective-permute-done.6 = f32[256,128]{1,0:T(8,128)S(1)} collective-permute-done((f32[256,128]{1,0:T(8,128)S(1)}, f32[256,128]{1,0:T(8,128)S(1)}, u32[]{:S(2)}, u32[]{:S(2)}) %collective-permute-start.6) | collective-permute-done | bytes 131104 | tf_op jit(solution)/shard_map/ppermute | solution.py:26
  55.5 4.4 %collective-permute-done.7 = f32[256,128]{1,0:T(8,128)S(1)} collective-permute-done((f32[256,128]{1,0:T(8,128)S(1)}, f32[256,128]{1,0:T(8,128)S(1)}, u32[]{:S(2)}, u32[]{:S(2)}) %collective-permute-start.7) | collective-permute-done | bytes 131104 | tf_op jit(solution)/shard_map/ppermute | solution.py:26
  60.0 1.8 %collective-permute-start.8 = (f32[256,128]{1,0:T(8,128)S(1)}, f32[256,128]{1,0:T(8,128)S(1)}, u32[]{:S(2)}, u32[]{:S(2)}) collective-permute-start(f32[256,128]{1,0:T(8,128)S(1)} %add.114), channel_id=1, source_target_pairs={{0,2},{1,3},{2,0},{3,1},{4,6},{5,7},{6,4},{7,5},{8,10},{9,11},{10,... | collective-permute-start | bytes 393224 | tf_op jit(solution)/shard_map/ppermute | solution.py:26
  62.0 2.0 %while.35 = (s32[]{:T(128)}, f32[2,2,128,256]{3,1,2,0:T(2,128)S(1)}, s32[2,128,8]{2,1,0:T(8,128)S(1)}, f32[2,128,8]{1,2,0:T(8,128)S(1)}, s32[2,128,8]{1,2,0:T(8,128)S(1)}, /*index=5*/s32[]{:T(128)}) while((s32[]{:T(128)}, f32[2,2,128,256]{3,1,2,0:T(2,128)S(1)}, s32[2,128,8]{2,1,0:T(8,128)S(1)}, f32[2,128,8]{1,2,0:T(8,128)S(1)}, ...), condition=%wide.region_5.6_spmd.clone, body=%wide.region_4.5_spmd.clone.sunk | while | flops 6557698 | bytes 516177 | solution.py:49
  64.0 3.4 %collective-permute-done.8 = f32[256,128]{1,0:T(8,128)S(1)} collective-permute-done((f32[256,128]{1,0:T(8,128)S(1)}, f32[256,128]{1,0:T(8,128)S(1)}, u32[]{:S(2)}, u32[]{:S(2)}) %collective-permute-start.8) | collective-permute-done | bytes 131104 | tf_op jit(solution)/shard_map/ppermute | solution.py:26
  69.1 3.9 %collective-permute-done.9 = f32[256,128]{1,0:T(8,128)S(1)} collective-permute-done((f32[256,128]{1,0:T(8,128)S(1)}, f32[256,128]{1,0:T(8,128)S(1)}, u32[]{:S(2)}, u32[]{:S(2)}) %collective-permute-start.9) | collective-permute-done | bytes 131104 | tf_op jit(solution)/shard_map/ppermute | solution.py:19
  73.9 5.8 %collective-permute-done.10 = f32[256,128]{1,0:T(8,128)S(1)} collective-permute-done((f32[256,128]{1,0:T(8,128)S(1)}, f32[256,128]{1,0:T(8,128)S(1)}, u32[]{:S(2)}, u32[]{:S(2)}) %collective-permute-start.10) | collective-permute-done | bytes 131104 | tf_op jit(solution)/shard_map/ppermute | solution.py:26
  79.7 1.3 %collective-permute-start.11 = (f32[256,128]{1,0:T(8,128)S(1)}, f32[256,128]{1,0:T(8,128)S(1)}, u32[]{:S(2)}, u32[]{:S(2)}) collective-permute-start(f32[256,128]{1,0:T(8,128)S(1)} %add.120), channel_id=1, source_target_pairs={{0,2},{1,3},{2,0},{3,1},{4,6},{5,7},{6,4},{7,5},{8,10},{9,11},{10,... | collective-permute-start | bytes 393224 | tf_op jit(solution)/shard_map/ppermute | solution.py:26
  81.0 7.4 %collective-permute-done.11 = f32[256,128]{1,0:T(8,128)S(1)} collective-permute-done((f32[256,128]{1,0:T(8,128)S(1)}, f32[256,128]{1,0:T(8,128)S(1)}, u32[]{:S(2)}, u32[]{:S(2)}) %collective-permute-start.11) | collective-permute-done | bytes 131104 | tf_op jit(solution)/shard_map/ppermute | solution.py:26
  89.3 5.4 %collective-permute-done.12 = f32[256,128]{1,0:T(8,128)S(1)} collective-permute-done((f32[256,128]{1,0:T(8,128)S(1)}, f32[256,128]{1,0:T(8,128)S(1)}, u32[]{:S(2)}, u32[]{:S(2)}) %collective-permute-start.12) | collective-permute-done | bytes 131104 | tf_op jit(solution)/shard_map/ppermute | solution.py:26
  95.8 7.3 %collective-permute-done.13 = f32[256,128]{1,0:T(8,128)S(1)} collective-permute-done((f32[256,128]{1,0:T(8,128)S(1)}, f32[256,128]{1,0:T(8,128)S(1)}, u32[]{:S(2)}, u32[]{:S(2)}) %collective-permute-start.13) | collective-permute-done | bytes 131104 | tf_op jit(solution)/shard_map/ppermute | solution.py:26
  104.4 5.4 %collective-permute-done.14 = f32[256,128]{1,0:T(8,128)S(1)} collective-permute-done((f32[256,128]{1,0:T(8,128)S(1)}, f32[256,128]{1,0:T(8,128)S(1)}, u32[]{:S(2)}, u32[]{:S(2)}) %collective-permute-start.14) | collective-permute-done | bytes 131104 | tf_op jit(solution)/shard_map/ppermute | solution.py:19
  (95 shorter events, 22.6 us)
Async XLA Ops:
  1.4 0.7 copy-start.3
  2.1 0.7 copy-start.4
  5.4 0.9 copy-start
  5.4 1.0 copy-start.1
  7.2 6.6 %collective-permute-start = (f32[256,128]{1,0:T(8,128)S(1)}, f32[256,128]{1,0:T(8,128)S(1)}, u32[]{:S(2)}, u32[]{:S(2)}) collective-permute-start(f32[256,128]{1,0:T(8,128)S(1)} %fusion.67), channel_id=1, source_target_pairs={{0,1},{1,0},{2,3},{3,2},{4,5},{5,4},{6,7},{7,6},{8,9},{9,8},{10,11... | collective-permute-start | bytes 393224 | tf_op jit(solution)/shard_map/ppermute | solution.py:26
  13.8 8.5 %collective-permute-start.1 = (f32[256,128]{1,0:T(8,128)S(1)}, f32[256,128]{1,0:T(8,128)S(1)}, u32[]{:S(2)}, u32[]{:S(2)}) collective-permute-start(f32[256,128]{1,0:T(8,128)S(1)} %add.100), channel_id=1, source_target_pairs={{0,2},{1,3},{2,0},{3,1},{4,6},{5,7},{6,4},{7,5},{8,10},{9,11},{10,... | collective-permute-start | bytes 393224 | tf_op jit(solution)/shard_map/ppermute | solution.py:26
  23.0 5.0 %collective-permute-start.2 = (f32[256,128]{1,0:T(8,128)S(1)}, f32[256,128]{1,0:T(8,128)S(1)}, u32[]{:S(2)}, u32[]{:S(2)}) collective-permute-start(f32[256,128]{1,0:T(8,128)S(1)} %fusion.68), channel_id=1, source_target_pairs={{0,1},{1,0},{2,3},{3,2},{4,5},{5,4},{6,7},{7,6},{8,9},{9,8},{10,11... | collective-permute-start | bytes 393224 | tf_op jit(solution)/shard_map/ppermute | solution.py:26
  28.1 7.3 %collective-permute-start.3 = (f32[256,128]{1,0:T(8,128)S(1)}, f32[256,128]{1,0:T(8,128)S(1)}, u32[]{:S(2)}, u32[]{:S(2)}) collective-permute-start(f32[256,128]{1,0:T(8,128)S(1)} %add.104), channel_id=1, source_target_pairs={{0,2},{1,3},{2,0},{3,1},{4,6},{5,7},{6,4},{7,5},{8,10},{9,11},{10,... | collective-permute-start | bytes 393224 | tf_op jit(solution)/shard_map/ppermute | solution.py:26
  36.5 4.4 %collective-permute-start.4 = (f32[256,128]{1,0:T(8,128)S(1)}, f32[256,128]{1,0:T(8,128)S(1)}, u32[]{:S(2)}, u32[]{:S(2)}) collective-permute-start(f32[256,128]{1,0:T(8,128)S(1)} %fusion.62), channel_id=1, source_target_pairs={{12,0},{0,4},{4,8},{8,12},{13,1},{1,5},{5,9},{9,13},{14,2},{2,6},{... | collective-permute-start | bytes 393224 | tf_op jit(solution)/shard_map/ppermute | solution.py:19
  41.8 5.0 %collective-permute-start.5 = (f32[256,128]{1,0:T(8,128)S(1)}, f32[256,128]{1,0:T(8,128)S(1)}, u32[]{:S(2)}, u32[]{:S(2)}) collective-permute-start(f32[256,128]{1,0:T(8,128)S(1)} %fusion.69), channel_id=1, source_target_pairs={{0,1},{1,0},{2,3},{3,2},{4,5},{5,4},{6,7},{7,6},{8,9},{9,8},{10,11... | collective-permute-start | bytes 393224 | tf_op jit(solution)/shard_map/ppermute | solution.py:26
  46.8 7.3 %collective-permute-start.6 = (f32[256,128]{1,0:T(8,128)S(1)}, f32[256,128]{1,0:T(8,128)S(1)}, u32[]{:S(2)}, u32[]{:S(2)}) collective-permute-start(f32[256,128]{1,0:T(8,128)S(1)} %add.110), channel_id=1, source_target_pairs={{0,2},{1,3},{2,0},{3,1},{4,6},{5,7},{6,4},{7,5},{8,10},{9,11},{10,... | collective-permute-start | bytes 393224 | tf_op jit(solution)/shard_map/ppermute | solution.py:26
  54.9 5.0 %collective-permute-start.7 = (f32[256,128]{1,0:T(8,128)S(1)}, f32[256,128]{1,0:T(8,128)S(1)}, u32[]{:S(2)}, u32[]{:S(2)}) collective-permute-start(f32[256,128]{1,0:T(8,128)S(1)} %fusion.70), channel_id=1, source_target_pairs={{0,1},{1,0},{2,3},{3,2},{4,5},{5,4},{6,7},{7,6},{8,9},{9,8},{10,11... | collective-permute-start | bytes 393224 | tf_op jit(solution)/shard_map/ppermute | solution.py:26
  60.0 7.3 %collective-permute-start.8 = (f32[256,128]{1,0:T(8,128)S(1)}, f32[256,128]{1,0:T(8,128)S(1)}, u32[]{:S(2)}, u32[]{:S(2)}) collective-permute-start(f32[256,128]{1,0:T(8,128)S(1)} %add.114), channel_id=1, source_target_pairs={{0,2},{1,3},{2,0},{3,1},{4,6},{5,7},{6,4},{7,5},{8,10},{9,11},{10,... | collective-permute-start | bytes 393224 | tf_op jit(solution)/shard_map/ppermute | solution.py:26
  68.4 4.6 %collective-permute-start.9 = (f32[256,128]{1,0:T(8,128)S(1)}, f32[256,128]{1,0:T(8,128)S(1)}, u32[]{:S(2)}, u32[]{:S(2)}) collective-permute-start(f32[256,128]{1,0:T(8,128)S(1)} %fusion.60), channel_id=1, source_target_pairs={{12,0},{0,4},{4,8},{8,12},{13,1},{1,5},{5,9},{9,13},{14,2},{2,6},{... | collective-permute-start | bytes 393224 | tf_op jit(solution)/shard_map/ppermute | solution.py:19
  73.8 5.8 %collective-permute-start.10 = (f32[256,128]{1,0:T(8,128)S(1)}, f32[256,128]{1,0:T(8,128)S(1)}, u32[]{:S(2)}, u32[]{:S(2)}) collective-permute-start(f32[256,128]{1,0:T(8,128)S(1)} %fusion.71), channel_id=1, source_target_pairs={{0,1},{1,0},{2,3},{3,2},{4,5},{5,4},{6,7},{7,6},{8,9},{9,8},{10,11... | collective-permute-start | bytes 393224 | tf_op jit(solution)/shard_map/ppermute | solution.py:26
  79.7 8.7 %collective-permute-start.11 = (f32[256,128]{1,0:T(8,128)S(1)}, f32[256,128]{1,0:T(8,128)S(1)}, u32[]{:S(2)}, u32[]{:S(2)}) collective-permute-start(f32[256,128]{1,0:T(8,128)S(1)} %add.120), channel_id=1, source_target_pairs={{0,2},{1,3},{2,0},{3,1},{4,6},{5,7},{6,4},{7,5},{8,10},{9,11},{10,... | collective-permute-start | bytes 393224 | tf_op jit(solution)/shard_map/ppermute | solution.py:26
  89.2 5.5 %collective-permute-start.12 = (f32[256,128]{1,0:T(8,128)S(1)}, f32[256,128]{1,0:T(8,128)S(1)}, u32[]{:S(2)}, u32[]{:S(2)}) collective-permute-start(f32[256,128]{1,0:T(8,128)S(1)} %fusion.72), channel_id=1, source_target_pairs={{0,1},{1,0},{2,3},{3,2},{4,5},{5,4},{6,7},{7,6},{8,9},{9,8},{10,11... | collective-permute-start | bytes 393224 | tf_op jit(solution)/shard_map/ppermute | solution.py:26
  94.7 8.3 %collective-permute-start.13 = (f32[256,128]{1,0:T(8,128)S(1)}, f32[256,128]{1,0:T(8,128)S(1)}, u32[]{:S(2)}, u32[]{:S(2)}) collective-permute-start(f32[256,128]{1,0:T(8,128)S(1)} %add.124), channel_id=1, source_target_pairs={{0,2},{1,3},{2,0},{3,1},{4,6},{5,7},{6,4},{7,5},{8,10},{9,11},{10,... | collective-permute-start | bytes 393224 | tf_op jit(solution)/shard_map/ppermute | solution.py:26
  103.1 0.7 copy-start.2
  104.3 5.4 %collective-permute-start.14 = (f32[256,128]{1,0:T(8,128)S(1)}, f32[256,128]{1,0:T(8,128)S(1)}, u32[]{:S(2)}, u32[]{:S(2)}) collective-permute-start(f32[256,128]{1,0:T(8,128)S(1)} %fusion.58), channel_id=1, source_target_pairs={{8,0},{12,4},{0,8},{4,12},{9,1},{13,5},{1,9},{5,13},{10,2},{14,6},... | collective-permute-start | bytes 393224 | tf_op jit(solution)/shard_map/ppermute | solution.py:19

commit v2 on v0

v2 whole, which is shorter than its diff:
```python
import jax
import jax.numpy as jnp
from jax import lax
from jax.sharding import PartitionSpec as P

INNER = 2


LR_USER = 0.02
LR_ITEM = 0.05
LAMBDA_REG = 1.0


def shifted(block, axis, distance):
    count = lax.axis_size(axis)
    route = [((i + distance) % count, i) for i in range(count)]
    return lax.ppermute(block, axis, route)


def residual_tile(user_rows, item_rows, weight, target):
    scores = jnp.dot(user_rows, item_rows.T, precision=lax.Precision.HIGHEST)
    return weight * jax.nn.sigmoid(scores) - target


def build_tiles(index_rows, signed_rows, slab_width):
    slabs, user_count, slot_count = index_rows.shape
    columns = jnp.arange(slab_width, dtype=jnp.float32)
    matches = index_rows[:, :, :, None] == columns
    weight = jnp.sum(jnp.where(matches, jnp.abs(signed_rows)[:, :, :, None], 0.0), axis=2)
    target = jnp.sum(jnp.where(matches, jnp.maximum(signed_rows, 0.0)[:, :, :, None], 0.0), axis=2)
    weight = jnp.transpose(weight, (1, 0, 2)).reshape(user_count, slabs * slab_width)
    target = jnp.transpose(target, (1, 0, 2)).reshape(user_count, slabs * slab_width)
    return weight, target


def per_device(user_factors, item_factors, item_index, labels, confidence):
    strata, user_count, slot_count = item_index.shape
    slab_rows, width = item_factors.shape
    signed = jnp.where(labels > 0, confidence, -confidence)
    packed = jnp.concatenate(
        [
            item_factors.reshape(-1),
            item_index.astype(jnp.float32).reshape(-1),
            signed.reshape(-1),
        ]
    )
    gathered = lax.all_gather(packed, "it")
    slabs = gathered.shape[0]
    cut = slab_rows * width
    slot_size = strata * user_count * slot_count
    block = gathered[:, :cut].reshape(slabs * slab_rows, width)
    index_all = gathered[:, cut : cut + slot_size].reshape(slabs, strata, user_count, slot_count)
    signed_all = gathered[:, cut + slot_size :].reshape(slabs, strata, user_count, slot_count)

    slot_data = []
    for stratum in range(strata):
        here = jnp.stack([index_all[:, stratum], signed_all[:, stratum]], 0)
        if stratum > 0:
            here = shifted(here, "ub", stratum)
        slot_data.append(here)

    user_rows = user_factors
    for stratum in range(strata):
        if stratum > 0:
            user_rows = shifted(user_rows, "ub", 1)
        weight, target = build_tiles(slot_data[stratum][0], slot_data[stratum][1], slab_rows)
        for inner_step in range(INNER):
            residual = residual_tile(user_rows, block, weight, target)
            gradient = jnp.dot(residual, block, precision=lax.Precision.HIGHEST)
            user_rows = user_rows - LR_USER * (gradient + LAMBDA_REG * user_rows)
        residual = residual_tile(user_rows, block, weight, target)
        item_grad = lax.dot_general(
            residual, user_rows, (((0,), (0,)), ((), ())), precision=lax.Precision.HIGHEST
        )
        block = block - LR_ITEM * (item_grad + LAMBDA_REG * block)
    user_rows = shifted(user_rows, "ub", 1 - strata)
    me = lax.axis_index("it")
    slab = lax.dynamic_slice_in_dim(block, me * slab_rows, slab_rows, 0)
    return (user_rows, slab)


def solution(mesh):
    return jax.shard_map(
        per_device,
        mesh=mesh,
        in_specs=(
            P(("grp", "ub"), None),
            P(("grp", "ub", "it"), None),
            P(None, ("grp", "ub"), "it"),
            P(None, ("grp", "ub"), "it"),
            P(None, ("grp", "ub"), "it"),
        ),
        out_specs=(P(("grp", "ub"), None), P(("grp", "ub", "it"), None)),
        check_vma=False,
    )
```

time: 262 us -> 101 us (0.39)
  waiting for transfers between devices: 217 us -> 4.22 us
  other arithmetic: 2.89 us -> 26.2 us
  blocking collectives: 0 us -> 20.6 us
  between operations: 14.4 us -> 1.09 us
  local copies, waits for them, and re-layouts: 6.94 us -> 16.6 us
  matrix products: 19 us -> 27.6 us
    psum x6 -> x0, waiting for transfers between devices: 205 us -> none  [per_device(): gradient = lax.psum(partial_grad, 'it')]
    reduce_sum x0 -> x3, other arithmetic: none -> 21 us  [build_tiles(): jnp.sum(jnp.where(matches, jnp.abs(signed_rows)[:, :, :, None], 0.0), axi...]
    all_gather x0 -> x1, blocking collectives: none -> 20.6 us  [per_device(): gathered = lax.all_gather(packed, 'it')]
    dot_general x9, matrix products: 6.41 us -> 13.8 us  [residual_tile(): scores = jnp.dot(user_rows, item_rows.T, precision=lax.Precision.HIGHEST)]
    ppermute x3 -> x5, waiting for transfers between devices: 11.4 us -> 4.22 us  [shifted(): return lax.ppermute(block, axis, route)]
    transpose x0 -> x6, local copies, waits for them, and re-layouts: none -> 5.94 us  [the longest x3 2.98 us: build_tiles(): jnp.transpose(weight, (1, 0, 2)).reshape(user_count, slabs * slab_width)]
    dot_general x12 -> x6, matrix products: 10.8 us -> 10.8 us  [per_device(): gradient = jnp.dot(residual, block, precision=lax.Precision.HIGHEST)]
  transfers between devices with their start and end apart: 9 -> 5, of which waited for: 9 -> 2; matrix products, arithmetic and copies ran while one was open for 2% -> 32% of each run, Pallas kernels for 0% -> 0%
where the time goes in v2:
time: 101 us; the launch traced here: 100 us
  matrix products  27.6 us (27%)
  other arithmetic  26.2 us (26%)
  blocking collectives  20.6 us (20%)
  local copies, waits for them, and re-layouts  16.6 us (16%)
  waiting for transfers between devices  4.22 us (4%)
  starting transfers between devices  4.06 us (4%)
  between operations  1.09 us (1%)
    reduce_sum x3, other arithmetic, build_tiles(): jnp.sum(jnp.where(matches, jnp.abs(signed_rows)[:, :, :, None], 0.0), axi...  21 us
    all_gather x1, blocking collectives, per_device(): gathered = lax.all_gather(packed, 'it')  20.6 us
    dot_general x9, matrix products, residual_tile(): scores = jnp.dot(user_rows, item_rows.T, precision=lax.Precision.HIGHEST)  13.8 us
    dot_general x6, matrix products, per_device(): gradient = jnp.dot(residual, block, precision=lax.Precision.HIGHEST)  10.8 us
    ppermute x5, waiting for transfers between devices, shifted(): return lax.ppermute(block, axis, route)  4.22 us
    ppermute x5, starting transfers between devices, shifted(): return lax.ppermute(block, axis, route)  4.06 us
    transpose x3, local copies, waits for them, and re-layouts, build_tiles(): jnp.transpose(weight, (1, 0, 2)).reshape(user_count, slabs * slab_width)  2.98 us
    dot_general x3, matrix products, per_device(): lax.dot_general(residual, user_rows, (((0,), (0,)), ((), ())), precision=...  2.96 us
  transfers between devices with their start and end apart: 5, of which 2 were waited for; matrix products, arithmetic and copies ran while one was open for 32% of the time, Pallas kernels for 0%

profile of v2, /device:TPU:0, one launch (start us, length us, event | category | flops | bytes accessed | tf_op | source)
XLA Modules:
  0.0 100.3 jit_solution(3436356349461293423)
XLA Ops:
  3.0 20.6 %all-gather = f32[180224]{0:T(1024)S(1)} all-gather(f32[45056]{0:T(1024)S(1)} %pad_maximum_fusion), channel_id=2, replica_groups=mesh['grp'=2,'ub'=4,'it'=4] {'it'}, dimensions={0}, use_global_device_ids=true | all-gather | bytes 901120 | tf_op jit(solution)/shard_map/all_gather | solution.py:47
  26.4 1.5 %slice_bitcast_fusion = (f32[1,4,256,8]{3,2,1,0:T(8,128)}, f32[4,256,8]{2,1,0:T(8,128)S(1)}, f32[1,4,256,8]{3,2,1,0:T(8,128)}, f32[4,256,8]{2,1,0:T(8,128)S(1)},...) fusion(f32[4,3,256,8]{3,2,1,0:T(8,128)S(1)} %reshape.86, ...), kind=kLoop, calls=%fused_computation.88 | loop fusion | flops 16384 | bytes 425984 | tf_op jit(solution)/shard_map/stack;squeeze | solution.py:57
  27.9 6.2 %select_reduce_fusion.5 = (f32[4,256,256]{2,1,0:T(8,128)S(1)}, f32[4,256,256]{2,1,0:T(8,128)S(1)}) fusion(f32[4,256,8]{2,1,0:T(8,128)S(1)} %get-tuple-element.14, f32[4,256,8]{2,1,0:T(8,128)S(1)} %get-tuple-element.23, f32[4,256,8]{2,1,0:T(8,128)S(1)} %get-tuple-element.12), kind=kLoop, calls=%fused_computation.7 | loop fusion | flops 9961472 | bytes 2195456 | tf_op jit(solution)/shard_map/reduce_sum | solution.py:29
  34.5 1.3 %copy.38 = f32[256,4,256]{0,2,1:T(8,128)} copy(f32[256,4,256]{2,0,1:T(8,128)S(1)} %bitcast.85) | data formatting | bytes 2097152 | tf_op jit(solution)/shard_map/transpose | solution.py:32
  36.3 2.4 %fusion.45 = f32[256,1024]{0,1:T(8,128)S(1)} fusion(f32[256,1024]{0,1:T(8,128)} %bitcast.90, f32[256,1024]{0,1:T(8,128)S(1)} %bitcast.87, f32[1024,128]{1,0:T(8,128)S(1)} %reshape.88, f32[256,128]{1,0:T(8,128)S(1)} %copy-done.17), kind=kOutput, calls=%fused_computation.63 | convolution fusion | flops 403963904 | bytes 3801088 | tf_op jit(solution)/shard_map/dot_general | solution.py:21
  38.7 1.8 %fusion.61 = f32[256,128]{1,0:T(8,128)S(1)} fusion(f32[256,128]{1,0:T(8,128)S(1)} %copy-done.17, f32[256,1024]{0,1:T(8,128)S(1)} %fusion.45, f32[1024,128]{1,0:T(8,128)S(1)} %reshape.88), kind=kOutput, calls=%fused_computation.87 | convolution fusion | flops 402751488 | bytes 1835008 | tf_op jit(solution)/shard_map/dot_general | solution.py:69
  41.7 1.8 %fusion.59 = f32[256,128]{1,0:T(8,128)S(1)} fusion(f32[256,128]{1,0:T(8,128)S(1)} %fusion.61, f32[256,1024]{0,1:T(8,128)S(1)} %fusion.39, f32[1024,128]{1,0:T(8,128)S(1)} %reshape.88), kind=kOutput, calls=%fused_computation.84 | convolution fusion | flops 402751488 | bytes 1835008 | tf_op jit(solution)/shard_map/dot_general | solution.py:69
  44.5 1.6 %collective-permute-start.1 = (f32[2,4,256,8]{2,3,1,0:T(8,128)}, f32[2,4,256,8]{2,3,1,0:T(8,128)}, u32[]{:S(2)}, u32[]{:S(2)}) collective-permute-start(f32[2,4,256,8]{2,3,1,0:T(8,128)} %pad_maximum_fusion.1), channel_id=1, source_target_pairs={{4,0},{8,4},{12,8},{0,12},{5,1},{9,5},{13,9},{1,13},{6,2},{10,6},{... | collective-permute-start | bytes 196616 | tf_op jit(solution)/shard_map/ppermute | solution.py:17
  47.0 2.3 %fusion.34 = f32[256,1024]{0,1:T(8,128)S(1)} fusion(f32[256,1024]{0,1:T(8,128)} %bitcast.91, f32[256,1024]{0,1:T(8,128)S(1)} %bitcast.89, f32[256,128]{1,0:T(8,128)S(1)} %fusion.59, f32[1024,128]{1,0:T(8,128)S(1)} %reshape.88), kind=kOutput, calls=%fused_computation.50 | convolution fusion | flops 403963904 | bytes 3801088 | tf_op jit(solution)/shard_map/dot_general | solution.py:21
  56.4 7.3 %select_reduce_fusion.3 = (f32[4,256,256]{2,1,0:T(8,128)S(1)}, f32[4,256,256]{2,1,0:T(8,128)S(1)}) fusion(f32[4,256,8]{2,1,0:T(8,128)} %copy.43, f32[4,256,8]{2,1,0:T(8,128)S(1)} %copy.42, f32[4,256,8]{2,1,0:T(8,128)} %copy.47), kind=kLoop, calls=%fused_computation.4 | loop fusion | flops 9961472 | bytes 2195456 | tf_op jit(solution)/shard_map/reduce_sum | solution.py:29
  63.7 7.5 %select_reduce_fusion.1 = (f32[4,256,256]{2,1,0:T(8,128)}, f32[4,256,256]{2,1,0:T(8,128)}) fusion(f32[4,256,8]{2,1,0:T(8,128)S(1)} %copy-done.4, f32[4,256,8]{2,1,0:T(8,128)S(1)} %copy-done.3, f32[4,256,8]{2,1,0:T(8,128)S(1)} %copy-done.5), kind=kLoop, calls=%fused_computation.1 | loop fusion | flops 9961472 | bytes 2195456 | tf_op jit(solution)/shard_map/reduce_sum | solution.py:29
  71.3 1.3 %copy.44 = f32[256,4,256]{0,2,1:T(8,128)} copy(f32[256,4,256]{2,0,1:T(8,128)S(1)} %bitcast.82) | data formatting | bytes 2097152 | tf_op jit(solution)/shard_map/transpose | solution.py:31
  72.6 1.3 %copy.48 = f32[256,4,256]{0,2,1:T(8,128)} copy(f32[256,4,256]{2,0,1:T(8,128)S(1)} %bitcast.81) | data formatting | bytes 2097152 | tf_op jit(solution)/shard_map/transpose | solution.py:32
  73.9 1.3 %copy.54 = f32[256,4,256]{0,2,1:T(8,128)} copy(f32[256,4,256]{2,0,1:T(8,128)S(1)} %bitcast.84) | data formatting | bytes 2097152 | tf_op jit(solution)/shard_map/transpose | solution.py:31
  75.6 2.7 %fusion.29 = f32[256,1024]{0,1:T(8,128)S(1)} fusion(f32[256,1024]{0,1:T(8,128)} %bitcast.102, f32[256,1024]{0,1:T(8,128)} %bitcast.99, f32[256,128]{1,0:T(8,128)S(1)} %collective-permute-done, f32[1024,128]{1,0:T(8,128)S(1)} %fusion.47), kind=kOutput, calls=%fused_computation.44 | convolution fusion | flops 403963904 | bytes 3801088 | tf_op jit(solution)/shard_map/dot_general | solution.py:21
  78.3 1.8 %fusion.57 = f32[256,128]{1,0:T(8,128)S(1)} fusion(f32[256,128]{1,0:T(8,128)S(1)} %collective-permute-done, f32[256,1024]{0,1:T(8,128)S(1)} %fusion.29, f32[1024,128]{1,0:T(8,128)S(1)} %fusion.47), kind=kOutput, calls=%fused_computation.81 | convolution fusion | flops 402751488 | bytes 1835008 | tf_op jit(solution)/shard_map/dot_general | solution.py:69
  81.2 1.8 %fusion.55 = f32[256,128]{1,0:T(8,128)S(1)} fusion(f32[256,128]{1,0:T(8,128)S(1)} %fusion.57, f32[256,1024]{0,1:T(8,128)S(1)} %fusion.24, f32[1024,128]{1,0:T(8,128)S(1)} %fusion.47), kind=kOutput, calls=%fused_computation.78 | convolution fusion | flops 402751488 | bytes 1835008 | tf_op jit(solution)/shard_map/dot_general | solution.py:69
  83.0 1.1 %fusion.19 = f32[256,1024]{0,1:T(8,128)S(1)} fusion(f32[256,1024]{0,1:T(8,128)S(1)} %bitcast.104, f32[256,1024]{0,1:T(8,128)S(1)} %bitcast.101, f32[256,128]{1,0:T(8,128)S(1)} %fusion.55, f32[1024,128]{1,0:T(8,128)S(1)} %fusion.47), kind=kOutput, calls=%fused_computation.32 | convolution fusion | flops 403963904 | bytes 3801088 | tf_op jit(solution)/shard_map/dot_general | solution.py:21
  85.5 1.5 %collective-permute-done.2 = f32[256,128]{1,0:T(8,128)S(1)} collective-permute-done((f32[256,128]{1,0:T(8,128)S(1)}, f32[256,128]{1,0:T(8,128)S(1)}, u32[]{:S(2)}, u32[]{:S(2)}) %collective-permute-start.2) | collective-permute-done | bytes 131104 | tf_op jit(solution)/shard_map/ppermute | solution.py:17
  88.1 1.8 %fusion.53 = f32[256,128]{1,0:T(8,128)S(1)} fusion(f32[256,128]{1,0:T(8,128)S(1)} %collective-permute-done.2, f32[256,1024]{0,1:T(8,128)S(1)} %fusion.14, f32[1024,128]{1,0:T(8,128)S(1)} %fusion.49), kind=kOutput, calls=%fused_computation.75 | convolution fusion | flops 402751488 | bytes 1835008 | tf_op jit(solution)/shard_map/dot_general | solution.py:69
  91.0 1.8 %fusion.51 = f32[256,128]{1,0:T(8,128)S(1)} fusion(f32[256,128]{1,0:T(8,128)S(1)} %fusion.53, f32[256,1024]{0,1:T(8,128)S(1)} %fusion.9, f32[1024,128]{1,0:T(8,128)S(1)} %fusion.49), kind=kOutput, calls=%fused_computation.72 | convolution fusion | flops 402751488 | bytes 1835008 | tf_op jit(solution)/shard_map/dot_general | solution.py:69
  92.8 1.1 %fusion.4 = f32[256,1024]{0,1:T(8,128)S(1)} fusion(f32[256,1024]{0,1:T(8,128)S(1)} %bitcast.98, f32[256,1024]{0,1:T(8,128)S(1)} %bitcast.95, f32[256,128]{1,0:T(8,128)S(1)} %fusion.51, f32[1024,128]{1,0:T(8,128)S(1)} %fusion.49), kind=kOutput, calls=%fused_computation.14 | convolution fusion | flops 403963904 | bytes 3801088 | tf_op jit(solution)/shard_map/dot_general | solution.py:21
  93.8 1.5 %collective-permute-start.4 = (f32[256,128]{1,0:T(8,128)S(1)}, f32[256,128]{1,0:T(8,128)S(1)}, u32[]{:S(2)}, u32[]{:S(2)}) collective-permute-start(f32[256,128]{1,0:T(8,128)S(1)} %fusion.51), channel_id=1, source_target_pairs={{8,0},{12,4},{0,8},{4,12},{9,1},{13,5},{1,9},{5,13},{10,2},{14,6},... | collective-permute-start | bytes 393224 | tf_op jit(solution)/shard_map/ppermute | solution.py:17
  97.0 2.7 %collective-permute-done.4 = f32[256,128]{1,0:T(8,128)S(1)} collective-permute-done((f32[256,128]{1,0:T(8,128)S(1)}, f32[256,128]{1,0:T(8,128)S(1)}, u32[]{:S(2)}, u32[]{:S(2)}) %collective-permute-start.4) | collective-permute-done | bytes 131104 | tf_op jit(solution)/shard_map/ppermute | solution.py:17
  (83 shorter events, 23.3 us)
Async XLA Ops:
  0.6 2.3 %copy-start.18 = (f32[256,128]{1,0:T(8,128)S(1)}, f32[256,128]{1,0:T(8,128)}, u32[]{:S(2)}) copy-start(f32[256,128]{1,0:T(8,128)} %param.6) | copy-start | bytes 393220
  34.5 1.8 %copy-start.10 = (f32[256,4,256]{0,2,1:T(8,128)}, f32[256,4,256]{0,2,1:T(8,128)S(1)}, u32[]{:S(2)}) copy-start(f32[256,4,256]{0,2,1:T(8,128)S(1)} %copy.37) | copy-start | bytes 3145732
  34.5 1.4 %slice-start = ((f32[4,45056]{1,0:T(4,128)}), f32[4,32768]{1,0:T(4,128)S(1)}, s32[]{:S(2)}) async-start(f32[4,45056]{1,0:T(4,128)} %copy-done.2), calls=%async_computation | async-start | bytes 1048576 | tf_op jit(solution)/shard_map/slice | solution.py:51
  34.5 1.8 %copy-start.17 = (f32[256,128]{1,0:T(8,128)S(1)}, f32[256,128]{1,0:T(8,128)}, u32[]{:S(2)}) copy-start(f32[256,128]{1,0:T(8,128)} %param.5) | copy-start | bytes 393220
  36.3 4.2 %copy-start.13 = (f32[256,4,256]{0,2,1:T(8,128)S(1)}, f32[256,4,256]{0,2,1:T(8,128)}, u32[]{:S(2)}) copy-start(f32[256,4,256]{0,2,1:T(8,128)} %copy.38) | copy-start | bytes 3145732
  38.7 1.8 %copy-start.11 = (f32[256,4,256]{0,2,1:T(8,128)S(1)}, f32[256,4,256]{0,2,1:T(8,128)}, u32[]{:S(2)}) copy-start(f32[256,4,256]{0,2,1:T(8,128)} %copy-done.10) | copy-start | bytes 3145732
  40.5 3.0 %copy-start.9 = (f32[1,4,256,8]{3,2,1,0:T(8,128)S(1)}, f32[1,4,256,8]{3,2,1,0:T(8,128)}, u32[]{:S(2)}) copy-start(f32[1,4,256,8]{3,2,1,0:T(8,128)} %get-tuple-element.24) | copy-start | bytes 98308
  41.6 2.1 %copy-start.8 = (f32[1,4,256,8]{3,2,1,0:T(8,128)S(1)}, f32[1,4,256,8]{3,2,1,0:T(8,128)}, u32[]{:S(2)}) copy-start(f32[1,4,256,8]{3,2,1,0:T(8,128)} %get-tuple-element.13) | copy-start | bytes 98308
  41.6 4.5 %copy-start.7 = (f32[1,4,256,8]{3,2,1,0:T(8,128)S(1)}, f32[1,4,256,8]{3,2,1,0:T(8,128)}, u32[]{:S(2)}) copy-start(f32[1,4,256,8]{3,2,1,0:T(8,128)} %get-tuple-element.25) | copy-start | bytes 98308
  41.6 4.6 %copy-start.6 = (f32[1,4,256,8]{3,2,1,0:T(8,128)S(1)}, f32[1,4,256,8]{3,2,1,0:T(8,128)}, u32[]{:S(2)}) copy-start(f32[1,4,256,8]{3,2,1,0:T(8,128)} %get-tuple-element.11) | copy-start | bytes 98308
  43.5 32.1 %collective-permute-start = (f32[256,128]{1,0:T(8,128)S(1)}, f32[256,128]{1,0:T(8,128)S(1)}, u32[]{:S(2)}, u32[]{:S(2)}) collective-permute-start(f32[256,128]{1,0:T(8,128)S(1)} %fusion.59), channel_id=1, source_target_pairs={{4,0},{8,4},{12,8},{0,12},{5,1},{9,5},{13,9},{1,13},{6,2},{10,6},{... | collective-permute-start | bytes 393224 | tf_op jit(solution)/shard_map/ppermute | solution.py:17
  43.7 3.3 %copy-start.12 = (f32[256,4,256]{0,2,1:T(8,128)S(1)}, f32[256,4,256]{0,2,1:T(8,128)}, u32[]{:S(2)}) copy-start(f32[256,4,256]{0,2,1:T(8,128)} %copy-done.10) | copy-start | bytes 3145732
  44.5 5.8 %collective-permute-start.1 = (f32[2,4,256,8]{2,3,1,0:T(8,128)}, f32[2,4,256,8]{2,3,1,0:T(8,128)}, u32[]{:S(2)}, u32[]{:S(2)}) collective-permute-start(f32[2,4,256,8]{2,3,1,0:T(8,128)} %pad_maximum_fusion.1), channel_id=1, source_target_pairs={{4,0},{8,4},{12,8},{0,12},{5,1},{9,5},{13,9},{1,13},{6,2},{10,6},{... | collective-permute-start | bytes 196616 | tf_op jit(solution)/shard_map/ppermute | solution.py:17
  46.5 6.9 %collective-permute-start.3 = (f32[2,4,256,8]{2,3,1,0:T(8,128)S(1)}, f32[2,4,256,8]{2,3,1,0:T(8,128)S(1)}, u32[]{:S(2)}, u32[]{:S(2)}) collective-permute-start(f32[2,4,256,8]{2,3,1,0:T(8,128)S(1)} %pad_maximum_fusion.2), channel_id=1, source_target_pairs={{8,0},{12,4},{0,8},{4,12},{9,1},{13,5},{1,9},{5,13},{10,2},{14,6},... | collective-permute-start | bytes 196616 | tf_op jit(solution)/shard_map/ppermute | solution.py:17
  56.4 7.3 %copy-start.3 = (f32[4,256,8]{2,1,0:T(8,128)S(1)}, f32[4,256,8]{2,1,0:T(8,128)}, u32[]{:S(2)}) copy-start(f32[4,256,8]{2,1,0:T(8,128)} %copy.52) | copy-start | bytes 98308
  56.4 7.3 %copy-start.4 = (f32[4,256,8]{2,1,0:T(8,128)S(1)}, f32[4,256,8]{2,1,0:T(8,128)}, u32[]{:S(2)}) copy-start(f32[4,256,8]{2,1,0:T(8,128)} %copy.53) | copy-start | bytes 98308
  56.4 7.3 %copy-start.5 = (f32[4,256,8]{2,1,0:T(8,128)S(1)}, f32[4,256,8]{2,1,0:T(8,128)}, u32[]{:S(2)}) copy-start(f32[4,256,8]{2,1,0:T(8,128)} %copy.57) | copy-start | bytes 98308
  72.6 1.3 %copy-start.1 = (f32[4,256,256]{2,1,0:T(8,128)S(1)}, f32[4,256,256]{2,1,0:T(8,128)}, u32[]{:S(2)}) copy-start(f32[4,256,256]{2,1,0:T(8,128)} %get-tuple-element.2) | copy-start | bytes 3145732
  73.9 1.3 %copy-start = (f32[4,256,256]{2,1,0:T(8,128)S(1)}, f32[4,256,256]{2,1,0:T(8,128)}, u32[]{:S(2)}) copy-start(f32[4,256,256]{2,1,0:T(8,128)} %get-tuple-element.3) | copy-start | bytes 3145732
  75.6 4.5 %copy-start.16 = (f32[256,4,256]{0,2,1:T(8,128)S(1)}, f32[256,4,256]{0,2,1:T(8,128)}, u32[]{:S(2)}) copy-start(f32[256,4,256]{0,2,1:T(8,128)} %copy.48) | copy-start | bytes 3145732
  78.3 1.8 %copy-start.15 = (f32[256,4,256]{0,2,1:T(8,128)S(1)}, f32[256,4,256]{0,2,1:T(8,128)}, u32[]{:S(2)}) copy-start(f32[256,4,256]{0,2,1:T(8,128)} %copy.44) | copy-start | bytes 3145732
  84.1 2.9 %copy-start.14 = (f32[256,4,256]{0,2,1:T(8,128)S(1)}, f32[256,4,256]{0,2,1:T(8,128)}, u32[]{:S(2)}) copy-start(f32[256,4,256]{0,2,1:T(8,128)} %copy.54) | copy-start | bytes 3145732
  84.1 2.9 %collective-permute-start.2 = (f32[256,128]{1,0:T(8,128)S(1)}, f32[256,128]{1,0:T(8,128)S(1)}, u32[]{:S(2)}, u32[]{:S(2)}) collective-permute-start(f32[256,128]{1,0:T(8,128)S(1)} %fusion.55), channel_id=1, source_target_pairs={{4,0},{8,4},{12,8},{0,12},{5,1},{9,5},{13,9},{1,13},{6,2},{10,6},{... | collective-permute-start | bytes 393224 | tf_op jit(solution)/shard_map/ppermute | solution.py:17
  93.8 5.8 %collective-permute-start.4 = (f32[256,128]{1,0:T(8,128)S(1)}, f32[256,128]{1,0:T(8,128)S(1)}, u32[]{:S(2)}, u32[]{:S(2)}) collective-permute-start(f32[256,128]{1,0:T(8,128)S(1)} %fusion.51), channel_id=1, source_target_pairs={{8,0},{12,4},{0,8},{4,12},{9,1},{13,5},{1,9},{5,13},{10,2},{14,6},... | collective-permute-start | bytes 393224 | tf_op jit(solution)/shard_map/ppermute | solution.py:17
  (1 other events, 0.9 us)

commit v3 on v2

v3 whole, which is shorter than its diff:
```python
import jax
import jax.numpy as jnp
from jax import lax
from jax.sharding import PartitionSpec as P

INNER = 2


LR_USER = 0.02
LR_ITEM = 0.05
LAMBDA_REG = 1.0


def shifted(block, axis, distance):
    count = lax.axis_size(axis)
    route = [((i + distance) % count, i) for i in range(count)]
    return lax.ppermute(block, axis, route)


def residual_tile(user_rows, item_rows, weight_t, target_t):
    scores_t = jnp.dot(item_rows, user_rows.T, precision=lax.Precision.HIGHEST)
    return weight_t * jax.nn.sigmoid(scores_t) - target_t


def build_tiles(index_rows, signed_rows, slab_width):
    slabs, slot_count, user_count = index_rows.shape
    columns = jnp.arange(slab_width, dtype=jnp.float32)[None, None, :, None]
    matches = index_rows[:, :, None, :] == columns
    weight = jnp.sum(jnp.where(matches, jnp.abs(signed_rows)[:, :, None, :], 0.0), axis=1)
    target = jnp.sum(jnp.where(matches, jnp.maximum(signed_rows, 0.0)[:, :, None, :], 0.0), axis=1)
    return weight.reshape(slabs * slab_width, user_count), target.reshape(slabs * slab_width, user_count)


def per_device(user_factors, item_factors, item_index, labels, confidence):
    strata, user_count, slot_count = item_index.shape
    slab_rows, width = item_factors.shape
    signed = jnp.where(labels > 0, confidence, -confidence)
    packed = jnp.concatenate(
        [
            item_factors.reshape(-1),
            jnp.transpose(item_index.astype(jnp.float32), (0, 2, 1)).reshape(-1),
            jnp.transpose(signed, (0, 2, 1)).reshape(-1),
        ]
    )
    gathered = lax.all_gather(packed, "it")
    slabs = gathered.shape[0]
    cut = slab_rows * width
    slot_size = strata * user_count * slot_count
    block = gathered[:, :cut].reshape(slabs * slab_rows, width)
    index_all = gathered[:, cut : cut + slot_size].reshape(slabs, strata, slot_count, user_count)
    signed_all = gathered[:, cut + slot_size :].reshape(slabs, strata, slot_count, user_count)

    slot_data = []
    for stratum in range(strata):
        here = jnp.stack([index_all[:, stratum], signed_all[:, stratum]], 0)
        if stratum > 0:
            here = shifted(here, "ub", stratum)
        slot_data.append(here)

    user_rows = user_factors
    for stratum in range(strata):
        if stratum > 0:
            user_rows = shifted(user_rows, "ub", 1)
        weight, target = build_tiles(slot_data[stratum][0], slot_data[stratum][1], slab_rows)
        for inner_step in range(INNER):
            residual_t = residual_tile(user_rows, block, weight, target)
            gradient = lax.dot_general(
                residual_t, block, (((0,), (0,)), ((), ())), precision=lax.Precision.HIGHEST
            )
            user_rows = user_rows - LR_USER * (gradient + LAMBDA_REG * user_rows)
        residual_t = residual_tile(user_rows, block, weight, target)
        item_grad = jnp.dot(residual_t, user_rows, precision=lax.Precision.HIGHEST)
        block = block - LR_ITEM * (item_grad + LAMBDA_REG * block)
    user_rows = shifted(user_rows, "ub", 1 - strata)
    me = lax.axis_index("it")
    slab = lax.dynamic_slice_in_dim(block, me * slab_rows, slab_rows, 0)
    return (user_rows, slab)


def solution(mesh):
    return jax.shard_map(
        per_device,
        mesh=mesh,
        in_specs=(
            P(("grp", "ub"), None),
            P(("grp", "ub", "it"), None),
            P(None, ("grp", "ub"), "it"),
            P(None, ("grp", "ub"), "it"),
            P(None, ("grp", "ub"), "it"),
        ),
        out_specs=(P(("grp", "ub"), None), P(("grp", "ub", "it"), None)),
        check_vma=False,
    )
```

time: 101 us -> 64.5 us (0.64)
  other arithmetic: 26.2 us -> 7.92 us
  local copies, waits for them, and re-layouts: 16.6 us -> 1.47 us
  matrix products: 27.6 us -> 23.9 us
    reduce_sum x3, other arithmetic: 21 us -> 4.77 us  [build_tiles(): jnp.sum(jnp.where(matches, jnp.abs(signed_rows)[:, :, None, :], 0.0), axi...]
    transpose x6 -> x0, local copies, waits for them, and re-layouts: 5.94 us -> none  [the longest x3 2.98 us: build_tiles(): jnp.transpose(weight, (1, 0, 2)).reshape(user_count, slabs * slab_width)]
    dot_general x18, matrix products: 27.6 us -> 23.9 us  [the longest x6 10.8 us: per_device(): lax.dot_general(residual_t, block, (((0,), (0,)), ((), ())), precision=la...]
    another operation x3 -> x2, other arithmetic: 2.18 us -> 0.01 us  [per_device(): here = jnp.stack([index_all[:, stratum], signed_all[:, stratum]], 0)]
    reshape x4 -> x0, local copies, waits for them, and re-layouts: 2.1 us -> none  [the longest x1 0.85 us: per_device(): gathered[:, cut + slot_size:].reshape(slabs, strata, user_count, slot_count)]
    abs x2 -> x0, local copies, waits for them, and re-layouts: 2.03 us -> none  [build_tiles(): jnp.abs(signed_rows)[:, :, :, None]]
    max x2 -> x0, local copies, waits for them, and re-layouts: 2.01 us -> none  [build_tiles(): jnp.maximum(signed_rows, 0.0)[:, :, :, None]]
    unnamed x0 -> x2, other arithmetic: none -> 1.5 us
  transfers between devices with their start and end apart: 5 -> 5, of which waited for: 2 -> 3; matrix products, arithmetic and copies ran while one was open for 32% -> 12% of each run, Pallas kernels for 0% -> 0%
where the time goes in v3:
time: 64.5 us; the launch traced here: 64.1 us
  matrix products  23.9 us (37%)
  blocking collectives  20.6 us (32%)
  other arithmetic  7.92 us (12%)
  starting transfers between devices  4.66 us (7%)
  waiting for transfers between devices  4.66 us (7%)
  local copies, waits for them, and re-layouts  1.47 us (2%)
  between operations  0.9 us (1%)
    all_gather x1, blocking collectives, per_device(): gathered = lax.all_gather(packed, 'it')  20.6 us
    dot_general x6, matrix products, per_device(): lax.dot_general(residual_t, block, (((0,), (0,)), ((), ())), precision=la...  10.8 us
    dot_general x9, matrix products, residual_tile(): scores_t = jnp.dot(item_rows, user_rows.T, precision=lax.Precision.HIGHEST)  10.1 us
    reduce_sum x3, other arithmetic, build_tiles(): jnp.sum(jnp.where(matches, jnp.abs(signed_rows)[:, :, None, :], 0.0), axi...  4.77 us
    ppermute x5, waiting for transfers between devices, shifted(): return lax.ppermute(block, axis, route)  4.66 us
    ppermute x5, starting transfers between devices, shifted(): return lax.ppermute(block, axis, route)  4.66 us
    dot_general x3, matrix products, per_device(): item_grad = jnp.dot(residual_t, user_rows, precision=lax.Precision.HIGHEST)  2.96 us
    unnamed x2, other arithmetic  1.5 us
  transfers between devices with their start and end apart: 5, of which 3 were waited for; matrix products, arithmetic and copies ran while one was open for 12% of the time, Pallas kernels for 0%

profile of v3, /device:TPU:0, one launch (start us, length us, event | category | flops | bytes accessed | tf_op | source)
XLA Modules:
  0.0 64.1 jit_solution(7910271319802563469)
XLA Ops:
  3.1 20.6 %all-gather = f32[180224]{0:T(1024)S(1)} all-gather(f32[45056]{0:T(1024)S(1)} %pad_maximum_fusion), channel_id=2, replica_groups=mesh['grp'=2,'ub'=4,'it'=4] {'it'}, dimensions={0}, use_global_device_ids=true | all-gather | bytes 901120 | tf_op jit(solution)/shard_map/all_gather | solution.py:45
  24.5 1.6 %select_reduce_fusion.5 = (f32[4,256,256]{2,1,0:T(8,128)S(1)}, f32[4,256,256]{2,1,0:T(8,128)S(1)}) fusion(f32[4,8,256]{2,1,0:T(8,128)S(1)} %get-tuple-element.16, f32[4,8,256]{2,1,0:T(8,128)S(1)} %get-tuple-element.23, f32[4,8,256]{2,1,0:T(8,128)S(1)} %get-tuple-element.15), kind=kLoop, calls=%fused_computation.7 | loop fusion | flops 9961472 | bytes 2195456 | tf_op jit(solution)/shard_map/reduce_sum | solution.py:29
  26.1 1.1 %fusion.44 = f32[1024,256]{1,0:T(8,128)S(1)} fusion(f32[1024,256]{1,0:T(8,128)S(1)} %bitcast.118, f32[1024,256]{1,0:T(8,128)S(1)} %bitcast.115, f32[1024,128]{1,0:T(8,128)S(1)} %reshape.88, f32[256,128]{1,0:T(8,128)S(1)} %copy-done), kind=kOutput, calls=%fused_computation.62 | convolution fusion | flops 403963904 | bytes 3801088 | tf_op jit(solution)/shard_map/dot_general | solution.py:21
  27.2 1.8 %fusion.60 = f32[256,128]{1,0:T(8,128)S(1)} fusion(f32[256,128]{1,0:T(8,128)S(1)} %copy-done, f32[1024,256]{1,0:T(8,128)S(1)} %fusion.44, f32[1024,128]{1,0:T(8,128)S(1)} %reshape.88), kind=kOutput, calls=%fused_computation.86 | convolution fusion | flops 402751488 | bytes 1835008 | tf_op jit(solution)/shard_map/dot_general | solution.py:67
  29.1 1.1 %fusion.39 = f32[1024,256]{1,0:T(8,128)S(1)} fusion(f32[1024,256]{1,0:T(8,128)S(1)} %bitcast.119, f32[1024,256]{1,0:T(8,128)S(1)} %bitcast.116, f32[1024,128]{1,0:T(8,128)S(1)} %reshape.88, f32[256,128]{1,0:T(8,128)S(1)} %fusion.60), kind=kOutput, calls=%fused_computation.56 | convolution fusion | flops 403963904 | bytes 3801088 | tf_op jit(solution)/shard_map/dot_general | solution.py:21
  30.2 1.8 %fusion.58 = f32[256,128]{1,0:T(8,128)S(1)} fusion(f32[256,128]{1,0:T(8,128)S(1)} %fusion.60, f32[1024,256]{1,0:T(8,128)S(1)} %fusion.39, f32[1024,128]{1,0:T(8,128)S(1)} %reshape.88), kind=kOutput, calls=%fused_computation.83 | convolution fusion | flops 402751488 | bytes 1835008 | tf_op jit(solution)/shard_map/dot_general | solution.py:67
  32.0 1.6 %collective-permute-start.1 = (f32[2,4,8,256]{3,2,1,0:T(8,128)S(1)}, f32[2,4,8,256]{3,2,1,0:T(8,128)S(1)}, u32[]{:S(2)}, u32[]{:S(2)}) collective-permute-start(f32[2,4,8,256]{3,2,1,0:T(8,128)S(1)} %pad_maximum_fusion.1), channel_id=1, source_target_pairs={{4,0},{8,4},{12,8},{0,12},{5,1},{9,5},{13,9},{1,13},{6,2},{10,6},{... | collective-permute-start | bytes 196616 | tf_op jit(solution)/shard_map/ppermute | solution.py:17
  34.2 1.1 %fusion.34 = f32[1024,256]{1,0:T(8,128)S(1)} fusion(f32[1024,256]{1,0:T(8,128)S(1)} %bitcast.120, f32[1024,256]{1,0:T(8,128)S(1)} %bitcast.117, f32[1024,128]{1,0:T(8,128)S(1)} %reshape.88, f32[256,128]{1,0:T(8,128)S(1)} %fusion.58), kind=kOutput, calls=%fused_computation.50 | convolution fusion | flops 403963904 | bytes 3801088 | tf_op jit(solution)/shard_map/dot_general | solution.py:21
  36.3 1.6 %select_reduce_fusion.3 = (f32[4,256,256]{2,1,0:T(8,128)S(1)}, f32[4,256,256]{2,1,0:T(8,128)S(1)}) fusion(f32[4,8,256]{2,1,0:T(8,128)S(1)} %get-tuple-element.21, f32[4,8,256]{2,1,0:T(8,128)S(1)} %get-tuple-element.22, f32[4,8,256]{2,1,0:T(8,128)S(1)} %get-tuple-element.20), kind=kLoop, calls=%fused_computation.4 | loop fusion | flops 9961472 | bytes 2195456 | tf_op jit(solution)/shard_map/reduce_sum | solution.py:29
  38.6 1.6 %select_reduce_fusion.1 = (f32[4,256,256]{2,1,0:T(8,128)S(1)}, f32[4,256,256]{2,1,0:T(8,128)S(1)}) fusion(f32[4,8,256]{2,1,0:T(8,128)S(1)} %get-tuple-element.18, f32[4,8,256]{2,1,0:T(8,128)S(1)} %get-tuple-element.19, f32[4,8,256]{2,1,0:T(8,128)S(1)} %get-tuple-element.17), kind=kLoop, calls=%fused_computation.1 | loop fusion | flops 9961472 | bytes 2195456 | tf_op jit(solution)/shard_map/reduce_sum | solution.py:29
  40.2 1.1 %fusion.29 = f32[1024,256]{1,0:T(8,128)S(1)} fusion(f32[1024,256]{1,0:T(8,128)S(1)} %bitcast.112, f32[1024,256]{1,0:T(8,128)S(1)} %bitcast.109, f32[1024,128]{1,0:T(8,128)S(1)} %fusion.46, f32[256,128]{1,0:T(8,128)S(1)} %collective-permute-done), kind=kOutput, calls=%fused_computation.44 | convolution fusion | flops 403963904 | bytes 3801088 | tf_op jit(solution)/shard_map/dot_general | solution.py:21
  41.3 1.8 %fusion.56 = f32[256,128]{1,0:T(8,128)S(1)} fusion(f32[256,128]{1,0:T(8,128)S(1)} %collective-permute-done, f32[1024,256]{1,0:T(8,128)S(1)} %fusion.29, f32[1024,128]{1,0:T(8,128)S(1)} %fusion.46), kind=kOutput, calls=%fused_computation.80 | convolution fusion | flops 402751488 | bytes 1835008 | tf_op jit(solution)/shard_map/dot_general | solution.py:67
  43.1 1.1 %fusion.24 = f32[1024,256]{1,0:T(8,128)S(1)} fusion(f32[1024,256]{1,0:T(8,128)S(1)} %bitcast.113, f32[1024,256]{1,0:T(8,128)S(1)} %bitcast.110, f32[1024,128]{1,0:T(8,128)S(1)} %fusion.46, f32[256,128]{1,0:T(8,128)S(1)} %fusion.56), kind=kOutput, calls=%fused_computation.38 | convolution fusion | flops 403963904 | bytes 3801088 | tf_op jit(solution)/shard_map/dot_general | solution.py:21
  44.2 1.8 %fusion.54 = f32[256,128]{1,0:T(8,128)S(1)} fusion(f32[256,128]{1,0:T(8,128)S(1)} %fusion.56, f32[1024,256]{1,0:T(8,128)S(1)} %fusion.24, f32[1024,128]{1,0:T(8,128)S(1)} %fusion.46), kind=kOutput, calls=%fused_computation.77 | convolution fusion | flops 402751488 | bytes 1835008 | tf_op jit(solution)/shard_map/dot_general | solution.py:67
  46.0 1.3 %fusion.19 = f32[1024,256]{1,0:T(8,128)S(1)} fusion(f32[1024,256]{1,0:T(8,128)S(1)} %bitcast.114, f32[1024,256]{1,0:T(8,128)S(1)} %bitcast.111, f32[1024,128]{1,0:T(8,128)S(1)} %fusion.46, f32[256,128]{1,0:T(8,128)S(1)} %fusion.54), kind=kOutput, calls=%fused_computation.32 | convolution fusion | flops 403963904 | bytes 3801088 | tf_op jit(solution)/shard_map/dot_general | solution.py:21
  49.3 1.5 %collective-permute-done.2 = f32[256,128]{1,0:T(8,128)S(1)} collective-permute-done((f32[256,128]{1,0:T(8,128)S(1)}, f32[256,128]{1,0:T(8,128)S(1)}, u32[]{:S(2)}, u32[]{:S(2)}) %collective-permute-start.2) | collective-permute-done | bytes 131104 | tf_op jit(solution)/shard_map/ppermute | solution.py:17
  50.8 1.1 %fusion.14 = f32[1024,256]{1,0:T(8,128)S(1)} fusion(f32[1024,256]{1,0:T(8,128)S(1)} %bitcast.106, f32[1024,256]{1,0:T(8,128)S(1)} %bitcast.103, f32[1024,128]{1,0:T(8,128)S(1)} %fusion.48, f32[256,128]{1,0:T(8,128)S(1)} %collective-permute-done.2), kind=kOutput, calls=%fused_computation.26 | convolution fusion | flops 403963904 | bytes 3801088 | tf_op jit(solution)/shard_map/dot_general | solution.py:21
  51.9 1.8 %fusion.52 = f32[256,128]{1,0:T(8,128)S(1)} fusion(f32[256,128]{1,0:T(8,128)S(1)} %collective-permute-done.2, f32[1024,256]{1,0:T(8,128)S(1)} %fusion.14, f32[1024,128]{1,0:T(8,128)S(1)} %fusion.48), kind=kOutput, calls=%fused_computation.74 | convolution fusion | flops 402751488 | bytes 1835008 | tf_op jit(solution)/shard_map/dot_general | solution.py:67
  53.7 1.1 %fusion.9 = f32[1024,256]{1,0:T(8,128)S(1)} fusion(f32[1024,256]{1,0:T(8,128)S(1)} %bitcast.107, f32[1024,256]{1,0:T(8,128)S(1)} %bitcast.104, f32[1024,128]{1,0:T(8,128)S(1)} %fusion.48, f32[256,128]{1,0:T(8,128)S(1)} %fusion.52), kind=kOutput, calls=%fused_computation.20 | convolution fusion | flops 403963904 | bytes 3801088 | tf_op jit(solution)/shard_map/dot_general | solution.py:21
  54.8 1.8 %fusion.50 = f32[256,128]{1,0:T(8,128)S(1)} fusion(f32[256,128]{1,0:T(8,128)S(1)} %fusion.52, f32[1024,256]{1,0:T(8,128)S(1)} %fusion.9, f32[1024,128]{1,0:T(8,128)S(1)} %fusion.48), kind=kOutput, calls=%fused_computation.71 | convolution fusion | flops 402751488 | bytes 1835008 | tf_op jit(solution)/shard_map/dot_general | solution.py:67
  56.6 1.1 %fusion.4 = f32[1024,256]{1,0:T(8,128)S(1)} fusion(f32[1024,256]{1,0:T(8,128)S(1)} %bitcast.108, f32[1024,256]{1,0:T(8,128)S(1)} %bitcast.105, f32[1024,128]{1,0:T(8,128)S(1)} %fusion.48, f32[256,128]{1,0:T(8,128)S(1)} %fusion.50), kind=kOutput, calls=%fused_computation.14 | convolution fusion | flops 403963904 | bytes 3801088 | tf_op jit(solution)/shard_map/dot_general | solution.py:21
  57.8 1.6 %collective-permute-start.4 = (f32[256,128]{1,0:T(8,128)S(1)}, f32[256,128]{1,0:T(8,128)S(1)}, u32[]{:S(2)}, u32[]{:S(2)}) collective-permute-start(f32[256,128]{1,0:T(8,128)S(1)} %fusion.50), channel_id=1, source_target_pairs={{8,0},{12,4},{0,8},{4,12},{9,1},{13,5},{1,9},{5,13},{10,2},{14,6},... | collective-permute-start | bytes 393224 | tf_op jit(solution)/shard_map/ppermute | solution.py:17
  59.3 1.0 %fusion.65 = f32[1024,128]{1,0:T(8,128)S(1)} fusion(f32[1024,256]{1,0:T(8,128)S(1)} %fusion.4, f32[256,128]{1,0:T(8,128)S(1)} %fusion.50), kind=kOutput, calls=%fused_computation.113 | convolution fusion | flops 402653184 | bytes 1703936 | tf_op jit(solution)/shard_map/dot_general | solution.py:72
  61.0 2.5 %collective-permute-done.4 = f32[256,128]{1,0:T(8,128)S(1)} collective-permute-done((f32[256,128]{1,0:T(8,128)S(1)}, f32[256,128]{1,0:T(8,128)S(1)}, u32[]{:S(2)}, u32[]{:S(2)}) %collective-permute-start.4) | collective-permute-done | bytes 131104 | tf_op jit(solution)/shard_map/ppermute | solution.py:17
  (29 shorter events, 8.8 us)
Async XLA Ops:
  24.5 1.6 %copy-start = (f32[256,128]{1,0:T(8,128)S(1)}, f32[256,128]{1,0:T(8,128)}, u32[]{:S(2)}) copy-start(f32[256,128]{1,0:T(8,128)} %param.5) | copy-start | bytes 393220
  32.0 8.2 %collective-permute-start = (f32[256,128]{1,0:T(8,128)S(1)}, f32[256,128]{1,0:T(8,128)S(1)}, u32[]{:S(2)}, u32[]{:S(2)}) collective-permute-start(f32[256,128]{1,0:T(8,128)S(1)} %fusion.58), channel_id=1, source_target_pairs={{4,0},{8,4},{12,8},{0,12},{5,1},{9,5},{13,9},{1,13},{6,2},{10,6},{... | collective-permute-start | bytes 393224 | tf_op jit(solution)/shard_map/ppermute | solution.py:17
  32.0 4.2 %collective-permute-start.1 = (f32[2,4,8,256]{3,2,1,0:T(8,128)S(1)}, f32[2,4,8,256]{3,2,1,0:T(8,128)S(1)}, u32[]{:S(2)}, u32[]{:S(2)}) collective-permute-start(f32[2,4,8,256]{3,2,1,0:T(8,128)S(1)} %pad_maximum_fusion.1), channel_id=1, source_target_pairs={{4,0},{8,4},{12,8},{0,12},{5,1},{9,5},{13,9},{1,13},{6,2},{10,6},{... | collective-permute-start | bytes 196616 | tf_op jit(solution)/shard_map/ppermute | solution.py:17
  33.6 4.9 %collective-permute-start.3 = (f32[2,4,8,256]{3,2,1,0:T(8,128)S(1)}, f32[2,4,8,256]{3,2,1,0:T(8,128)S(1)}, u32[]{:S(2)}, u32[]{:S(2)}) collective-permute-start(f32[2,4,8,256]{3,2,1,0:T(8,128)S(1)} %pad_maximum_fusion.2), channel_id=1, source_target_pairs={{8,0},{12,4},{0,8},{4,12},{9,1},{13,5},{1,9},{5,13},{10,2},{14,6},... | collective-permute-start | bytes 196616 | tf_op jit(solution)/shard_map/ppermute | solution.py:17
  47.4 3.5 %collective-permute-start.2 = (f32[256,128]{1,0:T(8,128)S(1)}, f32[256,128]{1,0:T(8,128)S(1)}, u32[]{:S(2)}, u32[]{:S(2)}) collective-permute-start(f32[256,128]{1,0:T(8,128)S(1)} %fusion.54), channel_id=1, source_target_pairs={{4,0},{8,4},{12,8},{0,12},{5,1},{9,5},{13,9},{1,13},{6,2},{10,6},{... | collective-permute-start | bytes 393224 | tf_op jit(solution)/shard_map/ppermute | solution.py:17
  57.8 5.7 %collective-permute-start.4 = (f32[256,128]{1,0:T(8,128)S(1)}, f32[256,128]{1,0:T(8,128)S(1)}, u32[]{:S(2)}, u32[]{:S(2)}) collective-permute-start(f32[256,128]{1,0:T(8,128)S(1)} %fusion.50), channel_id=1, source_target_pairs={{8,0},{12,4},{0,8},{4,12},{9,1},{13,5},{1,9},{5,13},{10,2},{14,6},... | collective-permute-start | bytes 393224 | tf_op jit(solution)/shard_map/ppermute | solution.py:17

commit v4 on v3

--- a/solution.py
+++ b/solution.py
@@ -4,6 +4,7 @@
 from jax.sharding import PartitionSpec as P
 
 INNER = 2
+MATMUL_PRECISION = lax.Precision.HIGH
 
 
 LR_USER = 0.02
@@ -18,7 +19,7 @@
 
 
 def residual_tile(user_rows, item_rows, weight_t, target_t):
-    scores_t = jnp.dot(item_rows, user_rows.T, precision=lax.Precision.HIGHEST)
+    scores_t = jnp.dot(item_rows, user_rows.T, precision=MATMUL_PRECISION)
     return weight_t * jax.nn.sigmoid(scores_t) - target_t
 
 
@@ -65,11 +66,11 @@
         for inner_step in range(INNER):
             residual_t = residual_tile(user_rows, block, weight, target)
             gradient = lax.dot_general(
-                residual_t, block, (((0,), (0,)), ((), ())), precision=lax.Precision.HIGHEST
+                residual_t, block, (((0,), (0,)), ((), ())), precision=MATMUL_PRECISION
             )
             user_rows = user_rows - LR_USER * (gradient + LAMBDA_REG * user_rows)
         residual_t = residual_tile(user_rows, block, weight, target)
-        item_grad = jnp.dot(residual_t, user_rows, precision=lax.Precision.HIGHEST)
+        item_grad = jnp.dot(residual_t, user_rows, precision=MATMUL_PRECISION)
         block = block - LR_ITEM * (item_grad + LAMBDA_REG * block)
     user_rows = shifted(user_rows, "ub", 1 - strata)
     me = lax.axis_index("it")

time: 64.5 us -> 56.2 us (0.87)
  matrix products: 23.9 us -> 13.7 us
  waiting for transfers between devices: 4.66 us -> 6.35 us
    dot_general x18, matrix products: 23.9 us -> 13.7 us  [the longest x9 6.01 us: residual_tile(): scores_t = jnp.dot(item_rows, user_rows.T, precision=MATMUL_PRECISION)]
    ppermute x5, waiting for transfers between devices: 4.66 us -> 6.35 us  [shifted(): return lax.ppermute(block, axis, route)]
  transfers between devices with their start and end apart: 5 -> 5, of which waited for: 3 -> 4; matrix products, arithmetic and copies ran while one was open for 12% -> 11% of each run, Pallas kernels for 0% -> 0%
where the time goes in v4:
time: 56.2 us; the launch traced here: 55.8 us
  blocking collectives  20.6 us (37%)
  matrix products  13.7 us (24%)
  other arithmetic  7.92 us (14%)
  waiting for transfers between devices  6.35 us (11%)
  starting transfers between devices  4.88 us (9%)
  local copies, waits for them, and re-layouts  1.47 us (3%)
  between operations  0.88 us (2%)
    all_gather x1, blocking collectives, per_device(): gathered = lax.all_gather(packed, 'it')  20.6 us
    ppermute x5, waiting for transfers between devices, shifted(): return lax.ppermute(block, axis, route)  6.35 us
    dot_general x9, matrix products, residual_tile(): scores_t = jnp.dot(item_rows, user_rows.T, precision=MATMUL_PRECISION)  6.01 us
    dot_general x6, matrix products, per_device(): lax.dot_general(residual_t, block, (((0,), (0,)), ((), ())), precision=MA...  5.98 us
    ppermute x5, starting transfers between devices, shifted(): return lax.ppermute(block, axis, route)  4.88 us
    reduce_sum x3, other arithmetic, build_tiles(): jnp.sum(jnp.where(matches, jnp.abs(signed_rows)[:, :, None, :], 0.0), axi...  4.77 us
    dot_general x3, matrix products, per_device(): item_grad = jnp.dot(residual_t, user_rows, precision=MATMUL_PRECISION)  1.73 us
    unnamed x2, other arithmetic  1.5 us
  transfers between devices with their start and end apart: 5, of which 4 were waited for; matrix products, arithmetic and copies ran while one was open for 11% of the time, Pallas kernels for 0%

profile of v4, /device:TPU:0, one launch (start us, length us, event | category | flops | bytes accessed | tf_op | source)
XLA Modules:
  0.0 55.8 jit_solution(13350470161325718877)
XLA Ops:
  0.6 0.7 %convert_bitcast_fusion = f32[3,2,8,128]{3,2,1,0:T(8,128)S(1)} fusion(s32[3,256,8]{1,2,0:T(8,128)} %param.7), kind=kLoop, calls=%fused_computation.111 | loop fusion | flops 6144 | bytes 49152
  1.4 0.8 %fusion.63 = f32[3,2,8,128]{3,2,1,0:T(8,128)S(1)} fusion(f32[3,256,8]{1,2,0:T(8,128)} %param.9, s32[3,256,8]{1,2,0:T(8,128)} %param.8), kind=kLoop, calls=%fused_computation.110 | loop fusion | flops 18432 | bytes 73728
  2.2 0.9 %pad_maximum_fusion = f32[45056]{0:T(1024)S(1)} fusion(f32[6144]{0:T(1024)S(1)} %bitcast.128, f32[6144]{0:T(1024)S(1)} %bitcast.127, f32[32768]{0:T(1024)} %bitcast.126), kind=kLoop, calls=%fused_computation.87 | loop fusion | flops 90112 | bytes 360448 | tf_op jit(solution)/shard_map/concatenate | solution.py:39
  3.1 20.6 %all-gather = f32[180224]{0:T(1024)S(1)} all-gather(f32[45056]{0:T(1024)S(1)} %pad_maximum_fusion), channel_id=2, replica_groups=mesh['grp'=2,'ub'=4,'it'=4] {'it'}, dimensions={0}, use_global_device_ids=true | all-gather | bytes 901120 | tf_op jit(solution)/shard_map/all_gather | solution.py:46
  24.5 1.6 %select_reduce_fusion.5 = (f32[4,256,256]{2,1,0:T(8,128)S(1)}, f32[4,256,256]{2,1,0:T(8,128)S(1)}) fusion(f32[4,8,256]{2,1,0:T(8,128)S(1)} %get-tuple-element.16, f32[4,8,256]{2,1,0:T(8,128)S(1)} %get-tuple-element.23, f32[4,8,256]{2,1,0:T(8,128)S(1)} %get-tuple-element.15), kind=kLoop, calls=%fused_computation.7 | loop fusion | flops 9961472 | bytes 2195456 | tf_op jit(solution)/shard_map/reduce_sum | solution.py:30
  26.1 0.7 %fusion.44 = f32[1024,256]{1,0:T(8,128)S(1)} fusion(f32[1024,256]{1,0:T(8,128)S(1)} %bitcast.118, f32[1024,256]{1,0:T(8,128)S(1)} %bitcast.115, f32[1024,128]{1,0:T(8,128)S(1)} %reshape.88, f32[256,128]{1,0:T(8,128)S(1)} %copy-done), kind=kOutput, calls=%fused_computation.62 | convolution fusion | flops 202637312 | bytes 3801088 | tf_op jit(solution)/shard_map/dot_general | solution.py:22
  26.8 1.0 %fusion.60 = f32[256,128]{1,0:T(8,128)S(1)} fusion(f32[256,128]{1,0:T(8,128)S(1)} %copy-done, f32[1024,256]{1,0:T(8,128)S(1)} %fusion.44, f32[1024,128]{1,0:T(8,128)S(1)} %reshape.88), kind=kOutput, calls=%fused_computation.86 | convolution fusion | flops 201424896 | bytes 1835008 | tf_op jit(solution)/shard_map/dot_general | solution.py:68
  28.5 1.0 %fusion.58 = f32[256,128]{1,0:T(8,128)S(1)} fusion(f32[256,128]{1,0:T(8,128)S(1)} %fusion.60, f32[1024,256]{1,0:T(8,128)S(1)} %fusion.39, f32[1024,128]{1,0:T(8,128)S(1)} %reshape.88), kind=kOutput, calls=%fused_computation.83 | convolution fusion | flops 201424896 | bytes 1835008 | tf_op jit(solution)/shard_map/dot_general | solution.py:68
  29.6 1.6 %collective-permute-start.1 = (f32[2,4,8,256]{3,2,1,0:T(8,128)S(1)}, f32[2,4,8,256]{3,2,1,0:T(8,128)S(1)}, u32[]{:S(2)}, u32[]{:S(2)}) collective-permute-start(f32[2,4,8,256]{3,2,1,0:T(8,128)S(1)} %pad_maximum_fusion.1), channel_id=1, source_target_pairs={{4,0},{8,4},{12,8},{0,12},{5,1},{9,5},{13,9},{1,13},{6,2},{10,6},{... | collective-permute-start | bytes 196616 | tf_op jit(solution)/shard_map/ppermute | solution.py:18
  33.4 1.6 %select_reduce_fusion.3 = (f32[4,256,256]{2,1,0:T(8,128)S(1)}, f32[4,256,256]{2,1,0:T(8,128)S(1)}) fusion(f32[4,8,256]{2,1,0:T(8,128)S(1)} %get-tuple-element.21, f32[4,8,256]{2,1,0:T(8,128)S(1)} %get-tuple-element.22, f32[4,8,256]{2,1,0:T(8,128)S(1)} %get-tuple-element.20), kind=kLoop, calls=%fused_computation.4 | loop fusion | flops 9961472 | bytes 2195456 | tf_op jit(solution)/shard_map/reduce_sum | solution.py:30
  35.0 1.0 %collective-permute-done.3 = f32[2,4,8,256]{3,2,1,0:T(8,128)S(1)} collective-permute-done((f32[2,4,8,256]{3,2,1,0:T(8,128)S(1)}, f32[2,4,8,256]{3,2,1,0:T(8,128)S(1)}, u32[]{:S(2)}, u32[]{:S(2)}) %collective-permute-start.3) | collective-permute-done | bytes 65568 | tf_op jit(solution)/shard_map/ppermute | solution.py:18
  36.1 1.6 %select_reduce_fusion.1 = (f32[4,256,256]{2,1,0:T(8,128)S(1)}, f32[4,256,256]{2,1,0:T(8,128)S(1)}) fusion(f32[4,8,256]{2,1,0:T(8,128)S(1)} %get-tuple-element.18, f32[4,8,256]{2,1,0:T(8,128)S(1)} %get-tuple-element.19, f32[4,8,256]{2,1,0:T(8,128)S(1)} %get-tuple-element.17), kind=kLoop, calls=%fused_computation.1 | loop fusion | flops 9961472 | bytes 2195456 | tf_op jit(solution)/shard_map/reduce_sum | solution.py:30
  38.4 1.0 %fusion.56 = f32[256,128]{1,0:T(8,128)S(1)} fusion(f32[256,128]{1,0:T(8,128)S(1)} %collective-permute-done, f32[1024,256]{1,0:T(8,128)S(1)} %fusion.29, f32[1024,128]{1,0:T(8,128)S(1)} %fusion.46), kind=kOutput, calls=%fused_computation.80 | convolution fusion | flops 201424896 | bytes 1835008 | tf_op jit(solution)/shard_map/dot_general | solution.py:68
  39.4 0.7 %fusion.24 = f32[1024,256]{1,0:T(8,128)S(1)} fusion(f32[1024,256]{1,0:T(8,128)S(1)} %bitcast.113, f32[1024,256]{1,0:T(8,128)S(1)} %bitcast.110, f32[1024,128]{1,0:T(8,128)S(1)} %fusion.46, f32[256,128]{1,0:T(8,128)S(1)} %fusion.56), kind=kOutput, calls=%fused_computation.38 | convolution fusion | flops 202637312 | bytes 3801088 | tf_op jit(solution)/shard_map/dot_general | solution.py:22
  40.1 1.0 %fusion.54 = f32[256,128]{1,0:T(8,128)S(1)} fusion(f32[256,128]{1,0:T(8,128)S(1)} %fusion.56, f32[1024,256]{1,0:T(8,128)S(1)} %fusion.24, f32[1024,128]{1,0:T(8,128)S(1)} %fusion.46), kind=kOutput, calls=%fused_computation.77 | convolution fusion | flops 201424896 | bytes 1835008 | tf_op jit(solution)/shard_map/dot_general | solution.py:68
  41.1 0.7 %fusion.19 = f32[1024,256]{1,0:T(8,128)S(1)} fusion(f32[1024,256]{1,0:T(8,128)S(1)} %bitcast.114, f32[1024,256]{1,0:T(8,128)S(1)} %bitcast.111, f32[1024,128]{1,0:T(8,128)S(1)} %fusion.46, f32[256,128]{1,0:T(8,128)S(1)} %fusion.54), kind=kOutput, calls=%fused_computation.32 | convolution fusion | flops 202637312 | bytes 3801088 | tf_op jit(solution)/shard_map/dot_general | solution.py:22
  41.7 1.1 %collective-permute-start.2 = (f32[256,128]{1,0:T(8,128)S(1)}, f32[256,128]{1,0:T(8,128)S(1)}, u32[]{:S(2)}, u32[]{:S(2)}) collective-permute-start(f32[256,128]{1,0:T(8,128)S(1)} %fusion.54), channel_id=1, source_target_pairs={{4,0},{8,4},{12,8},{0,12},{5,1},{9,5},{13,9},{1,13},{6,2},{10,6},{... | collective-permute-start | bytes 393224 | tf_op jit(solution)/shard_map/ppermute | solution.py:18
  43.5 1.9 %collective-permute-done.2 = f32[256,128]{1,0:T(8,128)S(1)} collective-permute-done((f32[256,128]{1,0:T(8,128)S(1)}, f32[256,128]{1,0:T(8,128)S(1)}, u32[]{:S(2)}, u32[]{:S(2)}) %collective-permute-start.2) | collective-permute-done | bytes 131104 | tf_op jit(solution)/shard_map/ppermute | solution.py:18
  46.1 1.0 %fusion.52 = f32[256,128]{1,0:T(8,128)S(1)} fusion(f32[256,128]{1,0:T(8,128)S(1)} %collective-permute-done.2, f32[1024,256]{1,0:T(8,128)S(1)} %fusion.14, f32[1024,128]{1,0:T(8,128)S(1)} %fusion.48), kind=kOutput, calls=%fused_computation.74 | convolution fusion | flops 201424896 | bytes 1835008 | tf_op jit(solution)/shard_map/dot_general | solution.py:68
  47.8 1.0 %fusion.50 = f32[256,128]{1,0:T(8,128)S(1)} fusion(f32[256,128]{1,0:T(8,128)S(1)} %fusion.52, f32[1024,256]{1,0:T(8,128)S(1)} %fusion.9, f32[1024,128]{1,0:T(8,128)S(1)} %fusion.48), kind=kOutput, calls=%fused_computation.71 | convolution fusion | flops 201424896 | bytes 1835008 | tf_op jit(solution)/shard_map/dot_general | solution.py:68
  48.8 0.7 %fusion.4 = f32[1024,256]{1,0:T(8,128)S(1)} fusion(f32[1024,256]{1,0:T(8,128)S(1)} %bitcast.108, f32[1024,256]{1,0:T(8,128)S(1)} %bitcast.105, f32[1024,128]{1,0:T(8,128)S(1)} %fusion.48, f32[256,128]{1,0:T(8,128)S(1)} %fusion.50), kind=kOutput, calls=%fused_computation.14 | convolution fusion | flops 202637312 | bytes 3801088 | tf_op jit(solution)/shard_map/dot_general | solution.py:22
  49.4 1.6 %collective-permute-start.4 = (f32[256,128]{1,0:T(8,128)S(1)}, f32[256,128]{1,0:T(8,128)S(1)}, u32[]{:S(2)}, u32[]{:S(2)}) collective-permute-start(f32[256,128]{1,0:T(8,128)S(1)} %fusion.50), channel_id=1, source_target_pairs={{8,0},{12,4},{0,8},{4,12},{9,1},{13,5},{1,9},{5,13},{10,2},{14,6},... | collective-permute-start | bytes 393224 | tf_op jit(solution)/shard_map/ppermute | solution.py:18
  51.6 0.7 %fusion.62 = f32[256,128]{1,0:T(8,128)} fusion(f32[1024,128]{1,0:T(8,128)S(1)} %fusion.65, s32[]{:T(128)S(6)} %select_n.33, f32[1024,128]{1,0:T(8,128)S(1)} %fusion.48), kind=kLoop, calls=%fused_computation.90 | loop fusion | flops 98304 | bytes 393220 | tf_op jit(solution)/shard_map/sub | solution.py:74
  52.2 2.9 %collective-permute-done.4 = f32[256,128]{1,0:T(8,128)S(1)} collective-permute-done((f32[256,128]{1,0:T(8,128)S(1)}, f32[256,128]{1,0:T(8,128)S(1)}, u32[]{:S(2)}, u32[]{:S(2)}) %collective-permute-start.4) | collective-permute-done | bytes 131104 | tf_op jit(solution)/shard_map/ppermute | solution.py:18
  (29 shorter events, 7.6 us)
Async XLA Ops:
  24.5 1.6 %copy-start = (f32[256,128]{1,0:T(8,128)S(1)}, f32[256,128]{1,0:T(8,128)}, u32[]{:S(2)}) copy-start(f32[256,128]{1,0:T(8,128)} %param.5) | copy-start | bytes 393220
  29.5 8.2 %collective-permute-start = (f32[256,128]{1,0:T(8,128)S(1)}, f32[256,128]{1,0:T(8,128)S(1)}, u32[]{:S(2)}, u32[]{:S(2)}) collective-permute-start(f32[256,128]{1,0:T(8,128)S(1)} %fusion.58), channel_id=1, source_target_pairs={{4,0},{8,4},{12,8},{0,12},{5,1},{9,5},{13,9},{1,13},{6,2},{10,6},{... | collective-permute-start | bytes 393224 | tf_op jit(solution)/shard_map/ppermute | solution.py:18
  29.6 3.9 %collective-permute-start.1 = (f32[2,4,8,256]{3,2,1,0:T(8,128)S(1)}, f32[2,4,8,256]{3,2,1,0:T(8,128)S(1)}, u32[]{:S(2)}, u32[]{:S(2)}) collective-permute-start(f32[2,4,8,256]{3,2,1,0:T(8,128)S(1)} %pad_maximum_fusion.1), channel_id=1, source_target_pairs={{4,0},{8,4},{12,8},{0,12},{5,1},{9,5},{13,9},{1,13},{6,2},{10,6},{... | collective-permute-start | bytes 196616 | tf_op jit(solution)/shard_map/ppermute | solution.py:18
  31.2 4.9 %collective-permute-start.3 = (f32[2,4,8,256]{3,2,1,0:T(8,128)S(1)}, f32[2,4,8,256]{3,2,1,0:T(8,128)S(1)}, u32[]{:S(2)}, u32[]{:S(2)}) collective-permute-start(f32[2,4,8,256]{3,2,1,0:T(8,128)S(1)} %pad_maximum_fusion.2), channel_id=1, source_target_pairs={{8,0},{12,4},{0,8},{4,12},{9,1},{13,5},{1,9},{5,13},{10,2},{14,6},... | collective-permute-start | bytes 196616 | tf_op jit(solution)/shard_map/ppermute | solution.py:18
  41.7 3.7 %collective-permute-start.2 = (f32[256,128]{1,0:T(8,128)S(1)}, f32[256,128]{1,0:T(8,128)S(1)}, u32[]{:S(2)}, u32[]{:S(2)}) collective-permute-start(f32[256,128]{1,0:T(8,128)S(1)} %fusion.54), channel_id=1, source_target_pairs={{4,0},{8,4},{12,8},{0,12},{5,1},{9,5},{13,9},{1,13},{6,2},{10,6},{... | collective-permute-start | bytes 393224 | tf_op jit(solution)/shard_map/ppermute | solution.py:18
  49.4 5.7 %collective-permute-start.4 = (f32[256,128]{1,0:T(8,128)S(1)}, f32[256,128]{1,0:T(8,128)S(1)}, u32[]{:S(2)}, u32[]{:S(2)}) collective-permute-start(f32[256,128]{1,0:T(8,128)S(1)} %fusion.50), channel_id=1, source_target_pairs={{8,0},{12,4},{0,8},{4,12},{9,1},{13,5},{1,9},{5,13},{10,2},{14,6},... | collective-permute-start | bytes 393224 | tf_op jit(solution)/shard_map/ppermute | solution.py:18

commit v5 on v4

--- a/solution.py
+++ b/solution.py
@@ -18,6 +18,16 @@
     return lax.ppermute(block, axis, route)
 
 
+def gather_over(block, axis):
+    count = lax.axis_size(axis)
+    me = lax.axis_index(axis)
+    received = [block] + [
+        lax.ppermute(block, axis, [(i, i ^ k) for i in range(count)]) for k in range(1, count)
+    ]
+    order = jnp.arange(count, dtype=jnp.int32) ^ me
+    return jnp.take(jnp.stack(received), order, axis=0)
+
+
 def residual_tile(user_rows, item_rows, weight_t, target_t):
     scores_t = jnp.dot(item_rows, user_rows.T, precision=MATMUL_PRECISION)
     return weight_t * jax.nn.sigmoid(scores_t) - target_t
@@ -36,20 +46,14 @@
     strata, user_count, slot_count = item_index.shape
     slab_rows, width = item_factors.shape
     signed = jnp.where(labels > 0, confidence, -confidence)
-    packed = jnp.concatenate(
-        [
-            item_factors.reshape(-1),
-            jnp.transpose(item_index.astype(jnp.float32), (0, 2, 1)).reshape(-1),
-            jnp.transpose(signed, (0, 2, 1)).reshape(-1),
-        ]
+    slots_local = jnp.stack(
+        [jnp.transpose(item_index.astype(jnp.float32), (0, 2, 1)), jnp.transpose(signed, (0, 2, 1))], 1
     )
-    gathered = lax.all_gather(packed, "it")
-    slabs = gathered.shape[0]
-    cut = slab_rows * width
-    slot_size = strata * user_count * slot_count
-    block = gathered[:, :cut].reshape(slabs * slab_rows, width)
-    index_all = gathered[:, cut : cut + slot_size].reshape(slabs, strata, slot_count, user_count)
-    signed_all = gathered[:, cut + slot_size :].reshape(slabs, strata, slot_count, user_count)
+    slots_all = gather_over(slots_local, "it")
+    slabs = slots_all.shape[0]
+    block = gather_over(item_factors, "it").reshape(slabs * slab_rows, width)
+    index_all = slots_all[:, :, 0]
+    signed_all = slots_all[:, :, 1]
 
     slot_data = []
     for stratum in range(strata):

time: 56.2 us -> 53.8 us (0.957)
  blocking collectives: 20.6 us -> 0 us
  starting transfers between devices: 4.88 us -> 15.7 us
  waiting for transfers between devices: 6.35 us -> 8.79 us
  other arithmetic: 7.92 us -> 9.95 us
  local copies, waits for them, and re-layouts: 1.47 us -> 3.18 us
  matrix products: 13.7 us -> 14.8 us
    all_gather x1 -> x0, blocking collectives: 20.6 us -> none  [per_device(): gathered = lax.all_gather(packed, 'it')]
    ppermute x0 -> x6, starting transfers between devices: none -> 10.1 us  [gather_over(): lax.ppermute(block, axis, [(i, i ^ k) for i in range(count)])]
    reduce_sum x3, other arithmetic: 4.77 us -> 7.36 us  [build_tiles(): jnp.sum(jnp.where(matches, jnp.abs(signed_rows)[:, :, None, :], 0.0), axi...]
    ppermute x0 -> x6, waiting for transfers between devices: none -> 2.01 us  [gather_over(): lax.ppermute(block, axis, [(i, i ^ k) for i in range(count)])]
    another operation x0 -> x5, other arithmetic: none -> 1.56 us  [the longest x2 1.5 us: per_device(): jnp.stack([jnp.transpose(item_index.astype(jnp.float32), (0, 2, 1)), jnp....]
    unnamed x2 -> x0, other arithmetic: 1.5 us -> none
    unnamed x7 -> x14, local copies, waits for them, and re-layouts: 0.74 us -> 1.92 us
    gather x0 -> x2, local copies, waits for them, and re-layouts: none -> 1.14 us  [gather_over(): return jnp.take(jnp.stack(received), order, axis=0)]
  transfers between devices with their start and end apart: 5 -> 11, of which waited for: 4 -> 4; matrix products, arithmetic and copies ran while one was open for 11% -> 20% of each run, Pallas kernels for 0% -> 0%
where the time goes in v5:
time: 53.8 us; the launch traced here: 53.4 us
  starting transfers between devices  15.7 us (29%)
  matrix products  14.8 us (28%)
  other arithmetic  9.95 us (18%)
  waiting for transfers between devices  8.79 us (16%)
  local copies, waits for them, and re-layouts  3.18 us (6%)
  between operations  0.96 us (2%)
    ppermute x6, starting transfers between devices, gather_over(): lax.ppermute(block, axis, [(i, i ^ k) for i in range(count)])  10.1 us
    reduce_sum x3, other arithmetic, build_tiles(): jnp.sum(jnp.where(matches, jnp.abs(signed_rows)[:, :, None, :], 0.0), axi...  7.36 us
    dot_general x9, matrix products, residual_tile(): scores_t = jnp.dot(item_rows, user_rows.T, precision=MATMUL_PRECISION)  7.06 us
    ppermute x5, waiting for transfers between devices, shifted(): return lax.ppermute(block, axis, route)  6.78 us
    dot_general x6, matrix products, per_device(): lax.dot_general(residual_t, block, (((0,), (0,)), ((), ())), precision=MA...  5.98 us
    ppermute x5, starting transfers between devices, shifted(): return lax.ppermute(block, axis, route)  5.62 us
    ppermute x6, waiting for transfers between devices, gather_over(): lax.ppermute(block, axis, [(i, i ^ k) for i in range(count)])  2.01 us
    unnamed x14, local copies, waits for them, and re-layouts  1.92 us
  transfers between devices with their start and end apart: 11, of which 4 were waited for; matrix products, arithmetic and copies ran while one was open for 20% of the time, Pallas kernels for 0%

profile of v5, /device:TPU:0, one launch (start us, length us, event | category | flops | bytes accessed | tf_op | source)
XLA Modules:
  0.0 53.4 jit_solution(6900650803380655637)
XLA Ops:
  0.6 0.7 %convert_bitcast_fusion = f32[3,1,8,256]{3,2,0,1:T(8,128)S(1)} fusion(s32[3,256,8]{1,2,0:T(8,128)} %param.7), kind=kLoop, calls=%fused_computation.116 | loop fusion | flops 6144 | bytes 49152 | tf_op jit(solution)/shard_map/stack | solution.py:49
  1.4 0.8 %fusion.63 = f32[3,1,8,256]{3,2,0,1:T(8,128)S(1)} fusion(f32[3,256,8]{1,2,0:T(8,128)} %param.9, s32[3,256,8]{1,2,0:T(8,128)} %param.8), kind=kLoop, calls=%fused_computation.115 | loop fusion | flops 18432 | bytes 73728 | tf_op jit(solution)/shard_map/stack | solution.py:49
  2.1 3.1 %collective-permute-start = (f32[3,2,8,256]{3,2,0,1:T(8,128)S(1)}, f32[3,2,8,256]{3,2,0,1:T(8,128)S(1)}, u32[]{:S(2)}, u32[]{:S(2)}) collective-permute-start(f32[3,2,8,256]{3,2,0,1:T(8,128)S(1)} %get-tuple-element.24), channel_id=1, source_target_pairs={{0,1},{1,0},{2,3},{3,2},{4,5},{5,4},{6,7},{7,6},{8,9},{9,8},{10,11... | collective-permute-start | bytes 147464 | tf_op jit(solution)/shard_map/ppermute | solution.py:25
  5.2 2.6 %collective-permute-start.1 = (f32[3,2,8,256]{3,2,0,1:T(8,128)S(1)}, f32[3,2,8,256]{3,2,0,1:T(8,128)S(1)}, u32[]{:S(2)}, u32[]{:S(2)}) collective-permute-start(f32[3,2,8,256]{3,2,0,1:T(8,128)S(1)} %get-tuple-element.24), channel_id=1, source_target_pairs={{0,2},{1,3},{2,0},{3,1},{4,6},{5,7},{6,4},{7,5},{8,10},{9,11},{10,... | collective-permute-start | bytes 147464 | tf_op jit(solution)/shard_map/ppermute | solution.py:25
  7.8 0.9 %collective-permute-start.3 = (f32[256,128]{1,0:T(8,128)}, f32[256,128]{1,0:T(8,128)S(1)}, u32[]{:S(2)}, u32[]{:S(2)}) collective-permute-start(f32[256,128]{1,0:T(8,128)} %param.6), channel_id=1, source_target_pairs={{0,1},{1,0},{2,3},{3,2},{4,5},{5,4},{6,7},{7,6},{8,9},{9,8},{10,11... | collective-permute-start | bytes 393224 | tf_op jit(solution)/shard_map/ppermute | solution.py:25
  8.7 3.5 %collective-permute-start.4 = (f32[256,128]{1,0:T(8,128)}, f32[256,128]{1,0:T(8,128)S(1)}, u32[]{:S(2)}, u32[]{:S(2)}) collective-permute-start(f32[256,128]{1,0:T(8,128)} %param.6), channel_id=1, source_target_pairs={{0,2},{1,3},{2,0},{3,1},{4,6},{5,7},{6,4},{7,5},{8,10},{9,11},{10,... | collective-permute-start | bytes 393224 | tf_op jit(solution)/shard_map/ppermute | solution.py:25
  12.4 2.0 %collective-permute-done.2 = f32[3,2,8,256]{3,2,0,1:T(8,128)S(1)} collective-permute-done((f32[3,2,8,256]{3,2,0,1:T(8,128)S(1)}, f32[3,2,8,256]{3,2,0,1:T(8,128)S(1)}, u32[]{:S(2)}, u32[]{:S(2)}) %collective-permute-start.2) | collective-permute-done | bytes 49184 | tf_op jit(solution)/shard_map/ppermute | solution.py:25
  15.3 1.6 %collective-permute-start.9 = (f32[2,4,8,256]{3,2,1,0:T(8,128)S(1)}, f32[2,4,8,256]{3,2,1,0:T(8,128)S(1)}, u32[]{:S(2)}, u32[]{:S(2)}) collective-permute-start(f32[2,4,8,256]{3,2,1,0:T(8,128)S(1)} %pad_maximum_fusion.3), channel_id=1, source_target_pairs={{8,0},{12,4},{0,8},{4,12},{9,1},{13,5},{1,9},{5,13},{10,2},{14,6},... | collective-permute-start | bytes 196616 | tf_op jit(solution)/shard_map/ppermute | solution.py:18
  16.8 2.9 %select_reduce_fusion.5 = (f32[4,256,256]{2,1,0:T(8,128)}, f32[4,256,256]{2,1,0:T(8,128)}) fusion(f32[4,8,256]{2,1,0:T(8,128)S(1)} %get-tuple-element.16, f32[4,8,256]{2,1,0:T(8,128)S(1)} %get-tuple-element.12, f32[4,8,256]{2,1,0:T(8,128)S(1)} %get-tuple-element.14), kind=kLoop, calls=%fused_computation.9 | loop fusion | flops 9961472 | bytes 2195456 | tf_op jit(solution)/shard_map/reduce_sum | solution.py:40
  19.7 2.9 %select_reduce_fusion.3 = (f32[4,256,256]{2,1,0:T(8,128)}, f32[4,256,256]{2,1,0:T(8,128)}) fusion(f32[4,8,256]{2,1,0:T(8,128)S(1)} %get-tuple-element.21, f32[4,8,256]{2,1,0:T(8,128)S(1)} %get-tuple-element.22, f32[4,8,256]{2,1,0:T(8,128)S(1)} %get-tuple-element.20), kind=kLoop, calls=%fused_computation.6 | loop fusion | flops 9961472 | bytes 2195456 | tf_op jit(solution)/shard_map/reduce_sum | solution.py:40
  22.6 1.6 %select_reduce_fusion.1 = (f32[4,256,256]{2,1,0:T(8,128)S(1)}, f32[4,256,256]{2,1,0:T(8,128)S(1)}) fusion(f32[4,8,256]{2,1,0:T(8,128)S(1)} %get-tuple-element.18, f32[4,8,256]{2,1,0:T(8,128)S(1)} %get-tuple-element.19, f32[4,8,256]{2,1,0:T(8,128)S(1)} %get-tuple-element.17), kind=kLoop, calls=%fused_computation.3 | loop fusion | flops 9961472 | bytes 2195456 | tf_op jit(solution)/shard_map/reduce_sum | solution.py:40
  25.2 0.9 %copy-done.2 = f32[4,256,256]{2,1,0:T(8,128)S(1)} copy-done((f32[4,256,256]{2,1,0:T(8,128)S(1)}, f32[4,256,256]{2,1,0:T(8,128)}, u32[]{:S(2)}) %copy-start.2) | copy-done | bytes 1048600
  26.1 1.9 %fusion.44 = f32[1024,256]{1,0:T(8,128)S(1)} fusion(f32[1024,256]{1,0:T(8,128)} %bitcast.111, f32[1024,256]{1,0:T(8,128)S(1)} %bitcast.108, f32[1024,128]{1,0:T(8,128)S(1)} %bitcast_select_fusion, f32[256,128]{1,0:T(8,128)S(1)} %copy-done.4), kind=kOutput, calls=%fused_computation.64 | convolution fusion | flops 202637312 | bytes 3801088 | tf_op jit(solution)/shard_map/dot_general | solution.py:32
  28.0 1.0 %fusion.60 = f32[256,128]{1,0:T(8,128)S(1)} fusion(f32[256,128]{1,0:T(8,128)S(1)} %copy-done.4, f32[1024,256]{1,0:T(8,128)S(1)} %fusion.44, f32[1024,128]{1,0:T(8,128)S(1)} %bitcast_select_fusion), kind=kOutput, calls=%fused_computation.88 | convolution fusion | flops 201424896 | bytes 1835008 | tf_op jit(solution)/shard_map/dot_general | solution.py:72
  29.9 1.0 %fusion.58 = f32[256,128]{1,0:T(8,128)S(1)} fusion(f32[256,128]{1,0:T(8,128)S(1)} %fusion.60, f32[1024,256]{1,0:T(8,128)S(1)} %fusion.39, f32[1024,128]{1,0:T(8,128)S(1)} %bitcast_select_fusion), kind=kOutput, calls=%fused_computation.85 | convolution fusion | flops 201424896 | bytes 1835008 | tf_op jit(solution)/shard_map/dot_general | solution.py:72
  32.7 1.9 %collective-permute-done.6 = f32[256,128]{1,0:T(8,128)S(1)} collective-permute-done((f32[256,128]{1,0:T(8,128)S(1)}, f32[256,128]{1,0:T(8,128)S(1)}, u32[]{:S(2)}, u32[]{:S(2)}) %collective-permute-start.6) | collective-permute-done | bytes 131104 | tf_op jit(solution)/shard_map/ppermute | solution.py:18
  35.3 1.0 %fusion.56 = f32[256,128]{1,0:T(8,128)S(1)} fusion(f32[256,128]{1,0:T(8,128)S(1)} %collective-permute-done.6, f32[1024,256]{1,0:T(8,128)S(1)} %fusion.29, f32[1024,128]{1,0:T(8,128)S(1)} %fusion.46), kind=kOutput, calls=%fused_computation.82 | convolution fusion | flops 201424896 | bytes 1835008 | tf_op jit(solution)/shard_map/dot_general | solution.py:72
  36.9 1.0 %fusion.54 = f32[256,128]{1,0:T(8,128)S(1)} fusion(f32[256,128]{1,0:T(8,128)S(1)} %fusion.56, f32[1024,256]{1,0:T(8,128)S(1)} %fusion.24, f32[1024,128]{1,0:T(8,128)S(1)} %fusion.46), kind=kOutput, calls=%fused_computation.79 | convolution fusion | flops 201424896 | bytes 1835008 | tf_op jit(solution)/shard_map/dot_general | solution.py:72
  38.6 1.9 %collective-permute-start.8 = (f32[256,128]{1,0:T(8,128)S(1)}, f32[256,128]{1,0:T(8,128)S(1)}, u32[]{:S(2)}, u32[]{:S(2)}) collective-permute-start(f32[256,128]{1,0:T(8,128)S(1)} %fusion.54), channel_id=1, source_target_pairs={{4,0},{8,4},{12,8},{0,12},{5,1},{9,5},{13,9},{1,13},{6,2},{10,6},{... | collective-permute-start | bytes 393224 | tf_op jit(solution)/shard_map/ppermute | solution.py:18
  41.1 1.9 %collective-permute-done.8 = f32[256,128]{1,0:T(8,128)S(1)} collective-permute-done((f32[256,128]{1,0:T(8,128)S(1)}, f32[256,128]{1,0:T(8,128)S(1)}, u32[]{:S(2)}, u32[]{:S(2)}) %collective-permute-start.8) | collective-permute-done | bytes 131104 | tf_op jit(solution)/shard_map/ppermute | solution.py:18
  43.7 1.0 %fusion.52 = f32[256,128]{1,0:T(8,128)S(1)} fusion(f32[256,128]{1,0:T(8,128)S(1)} %collective-permute-done.8, f32[1024,256]{1,0:T(8,128)S(1)} %fusion.14, f32[1024,128]{1,0:T(8,128)S(1)} %fusion.48), kind=kOutput, calls=%fused_computation.76 | convolution fusion | flops 201424896 | bytes 1835008 | tf_op jit(solution)/shard_map/dot_general | solution.py:72
  45.4 1.0 %fusion.50 = f32[256,128]{1,0:T(8,128)S(1)} fusion(f32[256,128]{1,0:T(8,128)S(1)} %fusion.52, f32[1024,256]{1,0:T(8,128)S(1)} %fusion.9, f32[1024,128]{1,0:T(8,128)S(1)} %fusion.48), kind=kOutput, calls=%fused_computation.73 | convolution fusion | flops 201424896 | bytes 1835008 | tf_op jit(solution)/shard_map/dot_general | solution.py:72
  47.0 1.6 %collective-permute-start.10 = (f32[256,128]{1,0:T(8,128)S(1)}, f32[256,128]{1,0:T(8,128)S(1)}, u32[]{:S(2)}, u32[]{:S(2)}) collective-permute-start(f32[256,128]{1,0:T(8,128)S(1)} %fusion.50), channel_id=1, source_target_pairs={{8,0},{12,4},{0,8},{4,12},{9,1},{13,5},{1,9},{5,13},{10,2},{14,6},... | collective-permute-start | bytes 393224 | tf_op jit(solution)/shard_map/ppermute | solution.py:18
  49.8 2.9 %collective-permute-done.10 = f32[256,128]{1,0:T(8,128)S(1)} collective-permute-done((f32[256,128]{1,0:T(8,128)S(1)}, f32[256,128]{1,0:T(8,128)S(1)}, u32[]{:S(2)}, u32[]{:S(2)}) %collective-permute-start.10) | collective-permute-done | bytes 131104 | tf_op jit(solution)/shard_map/ppermute | solution.py:18
  (55 shorter events, 10.9 us)
Async XLA Ops:
  2.1 10.2 %collective-permute-start = (f32[3,2,8,256]{3,2,0,1:T(8,128)S(1)}, f32[3,2,8,256]{3,2,0,1:T(8,128)S(1)}, u32[]{:S(2)}, u32[]{:S(2)}) collective-permute-start(f32[3,2,8,256]{3,2,0,1:T(8,128)S(1)} %get-tuple-element.24), channel_id=1, source_target_pairs={{0,1},{1,0},{2,3},{3,2},{4,5},{5,4},{6,7},{7,6},{8,9},{9,8},{10,11... | collective-permute-start | bytes 147464 | tf_op jit(solution)/shard_map/ppermute | solution.py:25
  5.2 7.2 %collective-permute-start.1 = (f32[3,2,8,256]{3,2,0,1:T(8,128)S(1)}, f32[3,2,8,256]{3,2,0,1:T(8,128)S(1)}, u32[]{:S(2)}, u32[]{:S(2)}) collective-permute-start(f32[3,2,8,256]{3,2,0,1:T(8,128)S(1)} %get-tuple-element.24), channel_id=1, source_target_pairs={{0,2},{1,3},{2,0},{3,1},{4,6},{5,7},{6,4},{7,5},{8,10},{9,11},{10,... | collective-permute-start | bytes 147464 | tf_op jit(solution)/shard_map/ppermute | solution.py:25
  7.8 6.6 %collective-permute-start.2 = (f32[3,2,8,256]{3,2,0,1:T(8,128)S(1)}, f32[3,2,8,256]{3,2,0,1:T(8,128)S(1)}, u32[]{:S(2)}, u32[]{:S(2)}) collective-permute-start(f32[3,2,8,256]{3,2,0,1:T(8,128)S(1)} %get-tuple-element.24), channel_id=1, source_target_pairs={{0,3},{1,2},{2,1},{3,0},{4,7},{5,6},{6,5},{7,4},{8,11},{9,10},{10,... | collective-permute-start | bytes 147464 | tf_op jit(solution)/shard_map/ppermute | solution.py:25
  7.8 16.4 %collective-permute-start.3 = (f32[256,128]{1,0:T(8,128)}, f32[256,128]{1,0:T(8,128)S(1)}, u32[]{:S(2)}, u32[]{:S(2)}) collective-permute-start(f32[256,128]{1,0:T(8,128)} %param.6), channel_id=1, source_target_pairs={{0,1},{1,0},{2,3},{3,2},{4,5},{5,4},{6,7},{7,6},{8,9},{9,8},{10,11... | collective-permute-start | bytes 393224 | tf_op jit(solution)/shard_map/ppermute | solution.py:25
  8.7 15.5 %collective-permute-start.4 = (f32[256,128]{1,0:T(8,128)}, f32[256,128]{1,0:T(8,128)S(1)}, u32[]{:S(2)}, u32[]{:S(2)}) collective-permute-start(f32[256,128]{1,0:T(8,128)} %param.6), channel_id=1, source_target_pairs={{0,2},{1,3},{2,0},{3,1},{4,6},{5,7},{6,4},{7,5},{8,10},{9,11},{10,... | collective-permute-start | bytes 393224 | tf_op jit(solution)/shard_map/ppermute | solution.py:25
  12.3 11.9 %collective-permute-start.5 = (f32[256,128]{1,0:T(8,128)}, f32[256,128]{1,0:T(8,128)S(1)}, u32[]{:S(2)}, u32[]{:S(2)}) collective-permute-start(f32[256,128]{1,0:T(8,128)} %param.6), channel_id=1, source_target_pairs={{0,3},{1,2},{2,1},{3,0},{4,7},{5,6},{6,5},{7,4},{8,11},{9,10},{10,... | collective-permute-start | bytes 393224 | tf_op jit(solution)/shard_map/ppermute | solution.py:25
  15.2 4.5 %collective-permute-start.7 = (f32[2,4,8,256]{3,2,1,0:T(8,128)S(1)}, f32[2,4,8,256]{3,2,1,0:T(8,128)S(1)}, u32[]{:S(2)}, u32[]{:S(2)}) collective-permute-start(f32[2,4,8,256]{3,2,1,0:T(8,128)S(1)} %pad_maximum_fusion.2), channel_id=1, source_target_pairs={{4,0},{8,4},{12,8},{0,12},{5,1},{9,5},{13,9},{1,13},{6,2},{10,6},{... | collective-permute-start | bytes 196616 | tf_op jit(solution)/shard_map/ppermute | solution.py:18
  15.3 7.3 %collective-permute-start.9 = (f32[2,4,8,256]{3,2,1,0:T(8,128)S(1)}, f32[2,4,8,256]{3,2,1,0:T(8,128)S(1)}, u32[]{:S(2)}, u32[]{:S(2)}) collective-permute-start(f32[2,4,8,256]{3,2,1,0:T(8,128)S(1)} %pad_maximum_fusion.3), channel_id=1, source_target_pairs={{8,0},{12,4},{0,8},{4,12},{9,1},{13,5},{1,9},{5,13},{10,2},{14,6},... | collective-permute-start | bytes 196616 | tf_op jit(solution)/shard_map/ppermute | solution.py:18
  22.6 1.7 %copy-start.5 = (f32[256,128]{1,0:T(8,128)S(1)}, f32[256,128]{1,0:T(8,128)}, u32[]{:S(2)}) copy-start(f32[256,128]{1,0:T(8,128)} %param.6) | copy-start | bytes 393220
  24.3 0.9 %copy-start.4 = (f32[256,128]{1,0:T(8,128)S(1)}, f32[256,128]{1,0:T(8,128)}, u32[]{:S(2)}) copy-start(f32[256,128]{1,0:T(8,128)} %param.5) | copy-start | bytes 393220
  24.9 1.2 %copy-start.2 = (f32[4,256,256]{2,1,0:T(8,128)S(1)}, f32[4,256,256]{2,1,0:T(8,128)}, u32[]{:S(2)}) copy-start(f32[4,256,256]{2,1,0:T(8,128)} %get-tuple-element.6) | copy-start | bytes 3145732
  28.0 1.2 %copy-start.3 = (f32[4,256,256]{2,1,0:T(8,128)S(1)}, f32[4,256,256]{2,1,0:T(8,128)}, u32[]{:S(2)}) copy-start(f32[4,256,256]{2,1,0:T(8,128)} %get-tuple-element.7) | copy-start | bytes 3145732
  31.6 3.1 %copy-start = (f32[4,256,256]{2,1,0:T(8,128)S(1)}, f32[4,256,256]{2,1,0:T(8,128)}, u32[]{:S(2)}) copy-start(f32[4,256,256]{2,1,0:T(8,128)} %get-tuple-element.4) | copy-start | bytes 3145732
  31.6 3.1 %copy-start.1 = (f32[4,256,256]{2,1,0:T(8,128)S(1)}, f32[4,256,256]{2,1,0:T(8,128)}, u32[]{:S(2)}) copy-start(f32[4,256,256]{2,1,0:T(8,128)} %get-tuple-element.5) | copy-start | bytes 3145732
  31.6 3.1 %collective-permute-start.6 = (f32[256,128]{1,0:T(8,128)S(1)}, f32[256,128]{1,0:T(8,128)S(1)}, u32[]{:S(2)}, u32[]{:S(2)}) collective-permute-start(f32[256,128]{1,0:T(8,128)S(1)} %fusion.58), channel_id=1, source_target_pairs={{4,0},{8,4},{12,8},{0,12},{5,1},{9,5},{13,9},{1,13},{6,2},{10,6},{... | collective-permute-start | bytes 393224 | tf_op jit(solution)/shard_map/ppermute | solution.py:18
  38.6 4.4 %collective-permute-start.8 = (f32[256,128]{1,0:T(8,128)S(1)}, f32[256,128]{1,0:T(8,128)S(1)}, u32[]{:S(2)}, u32[]{:S(2)}) collective-permute-start(f32[256,128]{1,0:T(8,128)S(1)} %fusion.54), channel_id=1, source_target_pairs={{4,0},{8,4},{12,8},{0,12},{5,1},{9,5},{13,9},{1,13},{6,2},{10,6},{... | collective-permute-start | bytes 393224 | tf_op jit(solution)/shard_map/ppermute | solution.py:18
  47.0 5.7 %collective-permute-start.10 = (f32[256,128]{1,0:T(8,128)S(1)}, f32[256,128]{1,0:T(8,128)S(1)}, u32[]{:S(2)}, u32[]{:S(2)}) collective-permute-start(f32[256,128]{1,0:T(8,128)S(1)} %fusion.50), channel_id=1, source_target_pairs={{8,0},{12,4},{0,8},{4,12},{9,1},{13,5},{1,9},{5,13},{10,2},{14,6},... | collective-permute-start | bytes 393224 | tf_op jit(solution)/shard_map/ppermute | solution.py:18

commit v6 on v5

--- a/solution.py
+++ b/solution.py
@@ -62,21 +62,31 @@
             here = shifted(here, "ub", stratum)
         slot_data.append(here)
 
-    user_rows = user_factors
+    pieces = 2 if user_count % 256 == 0 else 1
+    rows = user_count // pieces
+    chunks = [user_factors[k * rows : (k + 1) * rows] for k in range(pieces)]
     for stratum in range(strata):
         if stratum > 0:
-            user_rows = shifted(user_rows, "ub", 1)
+            chunks = [shifted(chunk, "ub", 1) for chunk in chunks]
         weight, target = build_tiles(slot_data[stratum][0], slot_data[stratum][1], slab_rows)
-        for inner_step in range(INNER):
-            residual_t = residual_tile(user_rows, block, weight, target)
-            gradient = lax.dot_general(
-                residual_t, block, (((0,), (0,)), ((), ())), precision=MATMUL_PRECISION
-            )
-            user_rows = user_rows - LR_USER * (gradient + LAMBDA_REG * user_rows)
-        residual_t = residual_tile(user_rows, block, weight, target)
-        item_grad = jnp.dot(residual_t, user_rows, precision=MATMUL_PRECISION)
+        finished = []
+        residuals = []
+        for k, chunk in enumerate(chunks):
+            weight_k = weight[:, k * rows : (k + 1) * rows]
+            target_k = target[:, k * rows : (k + 1) * rows]
+            for inner_step in range(INNER):
+                residual_t = residual_tile(chunk, block, weight_k, target_k)
+                gradient = lax.dot_general(
+                    residual_t, block, (((0,), (0,)), ((), ())), precision=MATMUL_PRECISION
+                )
+                chunk = chunk - LR_USER * (gradient + LAMBDA_REG * chunk)
+            finished.append(chunk)
+            residuals.append(residual_tile(chunk, block, weight_k, target_k))
+        chunks = finished
+        residual_t = jnp.concatenate(residuals, 1)
+        item_grad = jnp.dot(residual_t, jnp.concatenate(chunks, 0), precision=MATMUL_PRECISION)
         block = block - LR_ITEM * (item_grad + LAMBDA_REG * block)
-    user_rows = shifted(user_rows, "ub", 1 - strata)
+    user_rows = jnp.concatenate([shifted(chunk, "ub", 1 - strata) for chunk in chunks], 0)
     me = lax.axis_index("it")
     slab = lax.dynamic_slice_in_dim(block, me * slab_rows, slab_rows, 0)
     return (user_rows, slab)

time: 53.8 us -> 52.5 us (0.976)
  waiting for transfers between devices: 8.79 us -> 3.53 us
  matrix products: 14.8 us -> 17.8 us
  starting transfers between devices: 15.7 us -> 16.5 us
  other arithmetic: 9.95 us -> 10.6 us
    ppermute x5 -> x8, waiting for transfers between devices: 6.78 us -> 1.52 us  [shifted(): return lax.ppermute(block, axis, route)]
    dot_general x9 -> x18, matrix products: 7.06 us -> 8.78 us  [residual_tile(): scores_t = jnp.dot(item_rows, user_rows.T, precision=MATMUL_PRECISION)]
    dot_general x6 -> x12, matrix products: 5.98 us -> 7.32 us  [per_device(): lax.dot_general(residual_t, block, (((0,), (0,)), ((), ())), precision=MA...]
    ppermute x5 -> x8, starting transfers between devices: 5.62 us -> 6.41 us  [shifted(): return lax.ppermute(block, axis, route)]
    concatenate x0 -> x1, other arithmetic: none -> 0.66 us  [per_device(): jnp.concatenate([shifted(chunk, 'ub', 1 - strata) for chunk in chunks], 0)]
    unnamed x14 -> x13, local copies, waits for them, and re-layouts: 1.92 us -> 1.4 us
  transfers between devices with their start and end apart: 11 -> 14, of which waited for: 4 -> 2; matrix products, arithmetic and copies ran while one was open for 20% -> 43% of each run, Pallas kernels for 0% -> 0%
where the time goes in v6:
time: 52.5 us; the launch traced here: 52.2 us
  matrix products  17.8 us (34%)
  starting transfers between devices  16.5 us (31%)
  other arithmetic  10.6 us (20%)
  waiting for transfers between devices  3.53 us (7%)
  local copies, waits for them, and re-layouts  2.65 us (5%)
  between operations  1.05 us (2%)
    ppermute x6, starting transfers between devices, gather_over(): lax.ppermute(block, axis, [(i, i ^ k) for i in range(count)])  10.1 us
    dot_general x18, matrix products, residual_tile(): scores_t = jnp.dot(item_rows, user_rows.T, precision=MATMUL_PRECISION)  8.78 us
    reduce_sum x3, other arithmetic, build_tiles(): jnp.sum(jnp.where(matches, jnp.abs(signed_rows)[:, :, None, :], 0.0), axi...  7.36 us
    dot_general x12, matrix products, per_device(): lax.dot_general(residual_t, block, (((0,), (0,)), ((), ())), precision=MA...  7.32 us
    ppermute x8, starting transfers between devices, shifted(): return lax.ppermute(block, axis, route)  6.41 us
    ppermute x6, waiting for transfers between devices, gather_over(): lax.ppermute(block, axis, [(i, i ^ k) for i in range(count)])  2.01 us
    dot_general x3, matrix products, per_device(): jnp.dot(residual_t, jnp.concatenate(chunks, 0), precision=MATMUL_PRECISION)  1.72 us
    ppermute x8, waiting for transfers between devices, shifted(): return lax.ppermute(block, axis, route)  1.52 us
  transfers between devices with their start and end apart: 14, of which 2 were waited for; matrix products, arithmetic and copies ran while one was open for 43% of the time, Pallas kernels for 0%

profile of v6, /device:TPU:0, one launch (start us, length us, event | category | flops | bytes accessed | tf_op | source)
XLA Modules:
  0.0 52.2 jit_solution(6749766254669326057)
XLA Ops:
  0.6 0.7 %convert_bitcast_fusion = f32[3,1,8,256]{3,2,0,1:T(8,128)S(1)} fusion(s32[3,256,8]{1,2,0:T(8,128)} %param.7), kind=kLoop, calls=%fused_computation.210 | loop fusion | flops 6144 | bytes 49152 | tf_op jit(solution)/shard_map/stack | solution.py:49
  1.4 0.8 %fusion.141 = f32[3,1,8,256]{3,2,0,1:T(8,128)S(1)} fusion(f32[3,256,8]{1,2,0:T(8,128)} %param.9, s32[3,256,8]{1,2,0:T(8,128)} %param.8), kind=kLoop, calls=%fused_computation.209 | loop fusion | flops 18432 | bytes 73728 | tf_op jit(solution)/shard_map/stack | solution.py:49
  2.1 3.1 %collective-permute-start = (f32[3,2,8,256]{3,2,0,1:T(8,128)S(1)}, f32[3,2,8,256]{3,2,0,1:T(8,128)S(1)}, u32[]{:S(2)}, u32[]{:S(2)}) collective-permute-start(f32[3,2,8,256]{3,2,0,1:T(8,128)S(1)} %get-tuple-element.24), channel_id=1, source_target_pairs={{0,1},{1,0},{2,3},{3,2},{4,5},{5,4},{6,7},{7,6},{8,9},{9,8},{10,11... | collective-permute-start | bytes 147464 | tf_op jit(solution)/shard_map/ppermute | solution.py:25
  5.2 2.6 %collective-permute-start.1 = (f32[3,2,8,256]{3,2,0,1:T(8,128)S(1)}, f32[3,2,8,256]{3,2,0,1:T(8,128)S(1)}, u32[]{:S(2)}, u32[]{:S(2)}) collective-permute-start(f32[3,2,8,256]{3,2,0,1:T(8,128)S(1)} %get-tuple-element.24), channel_id=1, source_target_pairs={{0,2},{1,3},{2,0},{3,1},{4,6},{5,7},{6,4},{7,5},{8,10},{9,11},{10,... | collective-permute-start | bytes 147464 | tf_op jit(solution)/shard_map/ppermute | solution.py:25
  7.8 0.9 %collective-permute-start.3 = (f32[256,128]{1,0:T(8,128)}, f32[256,128]{1,0:T(8,128)S(1)}, u32[]{:S(2)}, u32[]{:S(2)}) collective-permute-start(f32[256,128]{1,0:T(8,128)} %param.6), channel_id=1, source_target_pairs={{0,1},{1,0},{2,3},{3,2},{4,5},{5,4},{6,7},{7,6},{8,9},{9,8},{10,11... | collective-permute-start | bytes 393224 | tf_op jit(solution)/shard_map/ppermute | solution.py:25
  8.7 3.5 %collective-permute-start.4 = (f32[256,128]{1,0:T(8,128)}, f32[256,128]{1,0:T(8,128)S(1)}, u32[]{:S(2)}, u32[]{:S(2)}) collective-permute-start(f32[256,128]{1,0:T(8,128)} %param.6), channel_id=1, source_target_pairs={{0,2},{1,3},{2,0},{3,1},{4,6},{5,7},{6,4},{7,5},{8,10},{9,11},{10,... | collective-permute-start | bytes 393224 | tf_op jit(solution)/shard_map/ppermute | solution.py:25
  12.4 2.0 %collective-permute-done.2 = f32[3,2,8,256]{3,2,0,1:T(8,128)S(1)} collective-permute-done((f32[3,2,8,256]{3,2,0,1:T(8,128)S(1)}, f32[3,2,8,256]{3,2,0,1:T(8,128)S(1)}, u32[]{:S(2)}, u32[]{:S(2)}) %collective-permute-start.2) | collective-permute-done | bytes 49184 | tf_op jit(solution)/shard_map/ppermute | solution.py:25
  15.3 1.6 %collective-permute-start.9 = (f32[2,4,8,256]{3,2,1,0:T(8,128)S(1)}, f32[2,4,8,256]{3,2,1,0:T(8,128)S(1)}, u32[]{:S(2)}, u32[]{:S(2)}) collective-permute-start(f32[2,4,8,256]{3,2,1,0:T(8,128)S(1)} %pad_maximum_fusion.4), channel_id=1, source_target_pairs={{8,0},{12,4},{0,8},{4,12},{9,1},{13,5},{1,9},{5,13},{10,2},{14,6},... | collective-permute-start | bytes 196616 | tf_op jit(solution)/shard_map/ppermute | solution.py:18
  16.8 2.9 %select_reduce_fusion.5 = (f32[4,256,256]{2,1,0:T(8,128)}, f32[4,256,256]{2,1,0:T(8,128)}) fusion(f32[4,8,256]{2,1,0:T(8,128)S(1)} %get-tuple-element.16, f32[4,8,256]{2,1,0:T(8,128)S(1)} %get-tuple-element.12, f32[4,8,256]{2,1,0:T(8,128)S(1)} %get-tuple-element.14), kind=kLoop, calls=%fused_computation.9 | loop fusion | flops 9961472 | bytes 2195456 | tf_op jit(solution)/shard_map/reduce_sum | solution.py:40
  19.7 2.9 %select_reduce_fusion.3 = (f32[4,256,256]{2,1,0:T(8,128)}, f32[4,256,256]{2,1,0:T(8,128)}) fusion(f32[4,8,256]{2,1,0:T(8,128)S(1)} %get-tuple-element.21, f32[4,8,256]{2,1,0:T(8,128)S(1)} %get-tuple-element.22, f32[4,8,256]{2,1,0:T(8,128)S(1)} %get-tuple-element.20), kind=kLoop, calls=%fused_computation.6 | loop fusion | flops 9961472 | bytes 2195456 | tf_op jit(solution)/shard_map/reduce_sum | solution.py:40
  22.6 1.6 %select_reduce_fusion.1 = (f32[4,256,256]{2,1,0:T(8,128)S(1)}, f32[4,256,256]{2,1,0:T(8,128)S(1)}) fusion(f32[4,8,256]{2,1,0:T(8,128)S(1)} %get-tuple-element.18, f32[4,8,256]{2,1,0:T(8,128)S(1)} %get-tuple-element.19, f32[4,8,256]{2,1,0:T(8,128)S(1)} %get-tuple-element.17), kind=kLoop, calls=%fused_computation.3 | loop fusion | flops 9961472 | bytes 2195456 | tf_op jit(solution)/shard_map/reduce_sum | solution.py:40
  25.2 0.9 %copy-done.2 = f32[4,256,256]{2,1,0:T(8,128)S(1)} copy-done((f32[4,256,256]{2,1,0:T(8,128)S(1)}, f32[4,256,256]{2,1,0:T(8,128)}, u32[]{:S(2)}) %copy-start.2) | copy-done | bytes 1048600
  26.1 1.6 %fusion.25 = f32[1024,128]{1,0:T(8,128)S(1)} fusion(f32[1024,128]{1,0:T(8,128)S(1)} %bitcast_select_fusion, f32[1024,256]{1,0:T(8,128)} %bitcast.148, f32[1024,256]{1,0:T(8,128)S(1)} %bitcast.142, f32[256,128]{1,0:T(8,128)S(1)} %copy-done.4), kind=kOutput, calls=%fused_computation.56 | convolution fusion | flops 101318656 | bytes 2162688 | tf_op jit(solution)/shard_map/dot_general | solution.py:32
  31.6 0.6 %fusion.111 = f32[128,128]{1,0:T(8,128)S(1)} fusion(f32[128,128]{1,0:T(8,128)S(1)} %fusion.113, f32[1024,128]{1,0:T(8,128)S(1)} %fusion.41, f32[1024,128]{1,0:T(8,128)S(1)} %bitcast_select_fusion), kind=kOutput, calls=%fused_computation.151 | convolution fusion | flops 100712448 | bytes 1179648 | tf_op jit(solution)/shard_map/dot_general | solution.py:79
  35.7 0.6 %fusion.107 = f32[128,128]{1,0:T(8,128)S(1)} fusion(f32[128,128]{1,0:T(8,128)S(1)} %fusion.109, f32[1024,128]{1,0:T(8,128)S(1)} %fusion.53, f32[1024,128]{1,0:T(8,128)S(1)} %fusion.1), kind=kOutput, calls=%fused_computation.145 | convolution fusion | flops 100712448 | bytes 1179648 | tf_op jit(solution)/shard_map/dot_general | solution.py:79
  36.7 1.0 %collective-permute-start.8 = (f32[128,128]{1,0:T(8,128)S(1)}, f32[128,128]{1,0:T(8,128)S(1)}, u32[]{:S(2)}, u32[]{:S(2)}) collective-permute-start(f32[128,128]{1,0:T(8,128)S(1)} %fusion.107), channel_id=1, source_target_pairs={{4,0},{8,4},{12,8},{0,12},{5,1},{9,5},{13,9},{1,13},{6,2},{10,6},{... | collective-permute-start | bytes 196616 | tf_op jit(solution)/shard_map/ppermute | solution.py:18
  38.1 0.6 %fusion.105 = f32[128,128]{1,0:T(8,128)S(1)} fusion(f32[128,128]{1,0:T(8,128)S(1)} %collective-permute-done.10, f32[1024,128]{1,0:T(8,128)S(1)} %fusion.61, f32[1024,128]{1,0:T(8,128)S(1)} %fusion.1), kind=kOutput, calls=%fused_computation.142 | convolution fusion | flops 100712448 | bytes 1179648 | tf_op jit(solution)/shard_map/dot_general | solution.py:79
  39.2 0.6 %fusion.103 = f32[128,128]{1,0:T(8,128)S(1)} fusion(f32[128,128]{1,0:T(8,128)S(1)} %fusion.105, f32[1024,128]{1,0:T(8,128)S(1)} %fusion.65, f32[1024,128]{1,0:T(8,128)S(1)} %fusion.1), kind=kOutput, calls=%fused_computation.139 | convolution fusion | flops 100712448 | bytes 1179648 | tf_op jit(solution)/shard_map/dot_general | solution.py:79
  40.2 0.7 %collective-permute-start.12 = (f32[128,128]{1,0:T(8,128)S(1)}, f32[128,128]{1,0:T(8,128)S(1)}, u32[]{:S(2)}, u32[]{:S(2)}) collective-permute-start(f32[128,128]{1,0:T(8,128)S(1)} %fusion.103), channel_id=1, source_target_pairs={{4,0},{8,4},{12,8},{0,12},{5,1},{9,5},{13,9},{1,13},{6,2},{10,6},{... | collective-permute-start | bytes 196616 | tf_op jit(solution)/shard_map/ppermute | solution.py:18
  42.0 0.6 %fusion.101 = f32[128,128]{1,0:T(8,128)S(1)} fusion(f32[128,128]{1,0:T(8,128)S(1)} %collective-permute-done.8, f32[1024,128]{1,0:T(8,128)S(1)} %fusion.73, f32[1024,128]{1,0:T(8,128)S(1)} %fusion.3), kind=kOutput, calls=%fused_computation.136 | convolution fusion | flops 100712448 | bytes 1179648 | tf_op jit(solution)/shard_map/dot_general | solution.py:79
  47.2 1.6 %collective-permute-start.13 = (f32[128,128]{1,0:T(8,128)S(1)}, f32[128,128]{1,0:T(8,128)S(1)}, u32[]{:S(2)}, u32[]{:S(2)}) collective-permute-start(f32[128,128]{1,0:T(8,128)S(1)} %fusion.95), channel_id=1, source_target_pairs={{8,0},{12,4},{0,8},{4,12},{9,1},{13,5},{1,9},{5,13},{10,2},{14,6},... | collective-permute-start | bytes 196616 | tf_op jit(solution)/shard_map/ppermute | solution.py:18
  49.4 0.7 %fusion.129 = f32[256,128]{1,0:T(8,128)} fusion(f32[1024,128]{1,0:T(8,128)S(1)} %fusion.124, s32[]{:T(128)S(6)} %select_n.64, f32[1024,128]{1,0:T(8,128)S(1)} %fusion.3), kind=kLoop, calls=%fused_computation.176 | loop fusion | flops 98304 | bytes 393220 | tf_op jit(solution)/shard_map/sub | solution.py:88
  50.0 1.5 %collective-permute-done.13 = f32[128,128]{1,0:T(8,128)S(1)} collective-permute-done((f32[128,128]{1,0:T(8,128)S(1)}, f32[128,128]{1,0:T(8,128)S(1)}, u32[]{:S(2)}, u32[]{:S(2)}) %collective-permute-start.13) | collective-permute-done | bytes 65568 | tf_op jit(solution)/shard_map/ppermute | solution.py:18
  51.5 0.7 %pad_maximum_fusion.2 = f32[256,128]{1,0:T(8,128)} fusion(f32[128,128]{1,0:T(8,128)S(1)} %collective-permute-done.13, f32[128,128]{1,0:T(8,128)S(1)} %collective-permute-done.11), kind=kLoop, calls=%fused_computation.183 | loop fusion | flops 32768 | bytes 262144 | tf_op jit(solution)/shard_map/concatenate | solution.py:89
  (76 shorter events, 17.0 us)
Async XLA Ops:
  2.1 10.2 %collective-permute-start = (f32[3,2,8,256]{3,2,0,1:T(8,128)S(1)}, f32[3,2,8,256]{3,2,0,1:T(8,128)S(1)}, u32[]{:S(2)}, u32[]{:S(2)}) collective-permute-start(f32[3,2,8,256]{3,2,0,1:T(8,128)S(1)} %get-tuple-element.24), channel_id=1, source_target_pairs={{0,1},{1,0},{2,3},{3,2},{4,5},{5,4},{6,7},{7,6},{8,9},{9,8},{10,11... | collective-permute-start | bytes 147464 | tf_op jit(solution)/shard_map/ppermute | solution.py:25
  5.2 7.2 %collective-permute-start.1 = (f32[3,2,8,256]{3,2,0,1:T(8,128)S(1)}, f32[3,2,8,256]{3,2,0,1:T(8,128)S(1)}, u32[]{:S(2)}, u32[]{:S(2)}) collective-permute-start(f32[3,2,8,256]{3,2,0,1:T(8,128)S(1)} %get-tuple-element.24), channel_id=1, source_target_pairs={{0,2},{1,3},{2,0},{3,1},{4,6},{5,7},{6,4},{7,5},{8,10},{9,11},{10,... | collective-permute-start | bytes 147464 | tf_op jit(solution)/shard_map/ppermute | solution.py:25
  7.8 6.6 %collective-permute-start.2 = (f32[3,2,8,256]{3,2,0,1:T(8,128)S(1)}, f32[3,2,8,256]{3,2,0,1:T(8,128)S(1)}, u32[]{:S(2)}, u32[]{:S(2)}) collective-permute-start(f32[3,2,8,256]{3,2,0,1:T(8,128)S(1)} %get-tuple-element.24), channel_id=1, source_target_pairs={{0,3},{1,2},{2,1},{3,0},{4,7},{5,6},{6,5},{7,4},{8,11},{9,10},{10,... | collective-permute-start | bytes 147464 | tf_op jit(solution)/shard_map/ppermute | solution.py:25
  7.8 16.4 %collective-permute-start.3 = (f32[256,128]{1,0:T(8,128)}, f32[256,128]{1,0:T(8,128)S(1)}, u32[]{:S(2)}, u32[]{:S(2)}) collective-permute-start(f32[256,128]{1,0:T(8,128)} %param.6), channel_id=1, source_target_pairs={{0,1},{1,0},{2,3},{3,2},{4,5},{5,4},{6,7},{7,6},{8,9},{9,8},{10,11... | collective-permute-start | bytes 393224 | tf_op jit(solution)/shard_map/ppermute | solution.py:25
  8.7 15.5 %collective-permute-start.4 = (f32[256,128]{1,0:T(8,128)}, f32[256,128]{1,0:T(8,128)S(1)}, u32[]{:S(2)}, u32[]{:S(2)}) collective-permute-start(f32[256,128]{1,0:T(8,128)} %param.6), channel_id=1, source_target_pairs={{0,2},{1,3},{2,0},{3,1},{4,6},{5,7},{6,4},{7,5},{8,10},{9,11},{10,... | collective-permute-start | bytes 393224 | tf_op jit(solution)/shard_map/ppermute | solution.py:25
  12.3 11.9 %collective-permute-start.5 = (f32[256,128]{1,0:T(8,128)}, f32[256,128]{1,0:T(8,128)S(1)}, u32[]{:S(2)}, u32[]{:S(2)}) collective-permute-start(f32[256,128]{1,0:T(8,128)} %param.6), channel_id=1, source_target_pairs={{0,3},{1,2},{2,1},{3,0},{4,7},{5,6},{6,5},{7,4},{8,11},{9,10},{10,... | collective-permute-start | bytes 393224 | tf_op jit(solution)/shard_map/ppermute | solution.py:25
  15.2 4.5 %collective-permute-start.7 = (f32[2,4,8,256]{3,2,1,0:T(8,128)S(1)}, f32[2,4,8,256]{3,2,1,0:T(8,128)S(1)}, u32[]{:S(2)}, u32[]{:S(2)}) collective-permute-start(f32[2,4,8,256]{3,2,1,0:T(8,128)S(1)} %pad_maximum_fusion.3), channel_id=1, source_target_pairs={{4,0},{8,4},{12,8},{0,12},{5,1},{9,5},{13,9},{1,13},{6,2},{10,6},{... | collective-permute-start | bytes 196616 | tf_op jit(solution)/shard_map/ppermute | solution.py:18
  15.3 7.3 %collective-permute-start.9 = (f32[2,4,8,256]{3,2,1,0:T(8,128)S(1)}, f32[2,4,8,256]{3,2,1,0:T(8,128)S(1)}, u32[]{:S(2)}, u32[]{:S(2)}) collective-permute-start(f32[2,4,8,256]{3,2,1,0:T(8,128)S(1)} %pad_maximum_fusion.4), channel_id=1, source_target_pairs={{8,0},{12,4},{0,8},{4,12},{9,1},{13,5},{1,9},{5,13},{10,2},{14,6},... | collective-permute-start | bytes 196616 | tf_op jit(solution)/shard_map/ppermute | solution.py:18
  22.6 1.7 %copy-start.5 = (f32[256,128]{1,0:T(8,128)S(1)}, f32[256,128]{1,0:T(8,128)}, u32[]{:S(2)}) copy-start(f32[256,128]{1,0:T(8,128)} %param.6) | copy-start | bytes 393220
  24.3 0.9 %copy-start.4 = (f32[256,128]{1,0:T(8,128)S(1)}, f32[256,128]{1,0:T(8,128)}, u32[]{:S(2)}) copy-start(f32[256,128]{1,0:T(8,128)} %param.5) | copy-start | bytes 393220
  24.9 1.2 %copy-start.2 = (f32[4,256,256]{2,1,0:T(8,128)S(1)}, f32[4,256,256]{2,1,0:T(8,128)}, u32[]{:S(2)}) copy-start(f32[4,256,256]{2,1,0:T(8,128)} %get-tuple-element.6) | copy-start | bytes 3145732
  26.1 1.6 %copy-start.3 = (f32[4,256,256]{2,1,0:T(8,128)S(1)}, f32[4,256,256]{2,1,0:T(8,128)}, u32[]{:S(2)}) copy-start(f32[4,256,256]{2,1,0:T(8,128)} %get-tuple-element.7) | copy-start | bytes 3145732
  30.2 3.6 %collective-permute-start.6 = (f32[128,128]{1,0:T(8,128)S(1)}, f32[128,128]{1,0:T(8,128)S(1)}, u32[]{:S(2)}, u32[]{:S(2)}) collective-permute-start(f32[128,128]{1,0:T(8,128)S(1)} %fusion.115), channel_id=1, source_target_pairs={{4,0},{8,4},{12,8},{0,12},{5,1},{9,5},{13,9},{1,13},{6,2},{10,6},{... | collective-permute-start | bytes 196616 | tf_op jit(solution)/shard_map/ppermute | solution.py:18
  32.6 1.2 %copy-start = (f32[4,256,256]{2,1,0:T(8,128)S(1)}, f32[4,256,256]{2,1,0:T(8,128)}, u32[]{:S(2)}) copy-start(f32[4,256,256]{2,1,0:T(8,128)} %get-tuple-element.4) | copy-start | bytes 3145732
  32.7 1.5 %copy-start.1 = (f32[4,256,256]{2,1,0:T(8,128)S(1)}, f32[4,256,256]{2,1,0:T(8,128)}, u32[]{:S(2)}) copy-start(f32[4,256,256]{2,1,0:T(8,128)} %get-tuple-element.5) | copy-start | bytes 3145732
  32.7 5.0 %collective-permute-start.10 = (f32[128,128]{1,0:T(8,128)S(1)}, f32[128,128]{1,0:T(8,128)S(1)}, u32[]{:S(2)}, u32[]{:S(2)}) collective-permute-start(f32[128,128]{1,0:T(8,128)S(1)} %fusion.111), channel_id=1, source_target_pairs={{4,0},{8,4},{12,8},{0,12},{5,1},{9,5},{13,9},{1,13},{6,2},{10,6},{... | collective-permute-start | bytes 196616 | tf_op jit(solution)/shard_map/ppermute | solution.py:18
  36.7 4.8 %collective-permute-start.8 = (f32[128,128]{1,0:T(8,128)S(1)}, f32[128,128]{1,0:T(8,128)S(1)}, u32[]{:S(2)}, u32[]{:S(2)}) collective-permute-start(f32[128,128]{1,0:T(8,128)S(1)} %fusion.107), channel_id=1, source_target_pairs={{4,0},{8,4},{12,8},{0,12},{5,1},{9,5},{13,9},{1,13},{6,2},{10,6},{... | collective-permute-start | bytes 196616 | tf_op jit(solution)/shard_map/ppermute | solution.py:18
  40.2 4.4 %collective-permute-start.12 = (f32[128,128]{1,0:T(8,128)S(1)}, f32[128,128]{1,0:T(8,128)S(1)}, u32[]{:S(2)}, u32[]{:S(2)}) collective-permute-start(f32[128,128]{1,0:T(8,128)S(1)} %fusion.103), channel_id=1, source_target_pairs={{4,0},{8,4},{12,8},{0,12},{5,1},{9,5},{13,9},{1,13},{6,2},{10,6},{... | collective-permute-start | bytes 196616 | tf_op jit(solution)/shard_map/ppermute | solution.py:18
  44.1 6.0 %collective-permute-start.11 = (f32[128,128]{1,0:T(8,128)S(1)}, f32[128,128]{1,0:T(8,128)S(1)}, u32[]{:S(2)}, u32[]{:S(2)}) collective-permute-start(f32[128,128]{1,0:T(8,128)S(1)} %fusion.99), channel_id=1, source_target_pairs={{8,0},{12,4},{0,8},{4,12},{9,1},{13,5},{1,9},{5,13},{10,2},{14,6},... | collective-permute-start | bytes 196616 | tf_op jit(solution)/shard_map/ppermute | solution.py:18
  47.2 4.3 %collective-permute-start.13 = (f32[128,128]{1,0:T(8,128)S(1)}, f32[128,128]{1,0:T(8,128)S(1)}, u32[]{:S(2)}, u32[]{:S(2)}) collective-permute-start(f32[128,128]{1,0:T(8,128)S(1)} %fusion.95), channel_id=1, source_target_pairs={{8,0},{12,4},{0,8},{4,12},{9,1},{13,5},{1,9},{5,13},{10,2},{14,6},... | collective-permute-start | bytes 196616 | tf_op jit(solution)/shard_map/ppermute | solution.py:18

commit v7 on v6

--- a/solution.py
+++ b/solution.py
@@ -1,6 +1,8 @@
 import jax
 import jax.numpy as jnp
 from jax import lax
+from jax.experimental import pallas as pl
+from jax.experimental.pallas import tpu as pltpu
 from jax.sharding import PartitionSpec as P
 
 INNER = 2
@@ -33,13 +35,59 @@
     return weight_t * jax.nn.sigmoid(scores_t) - target_t
 
 
-def build_tiles(index_rows, signed_rows, slab_width):
+def build_tiles(index_rows, signed_rows, slab_width, pieces):
     slabs, slot_count, user_count = index_rows.shape
-    columns = jnp.arange(slab_width, dtype=jnp.float32)[None, None, :, None]
-    matches = index_rows[:, :, None, :] == columns
-    weight = jnp.sum(jnp.where(matches, jnp.abs(signed_rows)[:, :, None, :], 0.0), axis=1)
-    target = jnp.sum(jnp.where(matches, jnp.maximum(signed_rows, 0.0)[:, :, None, :], 0.0), axis=1)
-    return weight.reshape(slabs * slab_width, user_count), target.reshape(slabs * slab_width, user_count)
+    rows = user_count // pieces
+    index_rows = jnp.transpose(index_rows.reshape(slabs, slot_count, pieces, rows), (2, 0, 1, 3))
+    signed_rows = jnp.transpose(signed_rows.reshape(slabs, slot_count, pieces, rows), (2, 0, 1, 3))
+    columns = jnp.arange(slab_width, dtype=jnp.float32)[None, None, None, :, None]
+    matches = index_rows[:, :, :, None, :] == columns
+    weight = jnp.sum(jnp.where(matches, jnp.abs(signed_rows)[:, :, :, None, :], 0.0), axis=2)
+    target = jnp.sum(jnp.where(matches, jnp.maximum(signed_rows, 0.0)[:, :, :, None, :], 0.0), axis=2)
+    return weight.reshape(pieces, slabs * slab_width, rows), target.reshape(pieces, slabs * slab_width, rows)
+
+
+def user_steps_kernel(p_ref, q_ref, w_ref, t_ref, p_out, r_out):
+    q = q_ref[...]
+    w = w_ref[...]
+    t = t_ref[...]
+
+    def residual(p):
+        scores_t = lax.dot_general(
+            q, p, (((1,), (1,)), ((), ())), precision=lax.Precision.HIGHEST, preferred_element_type=jnp.float32
+        )
+        return w * jax.nn.sigmoid(scores_t) - t
+
+    p = p_ref[...]
+    for inner_step in range(INNER):
+        gradient = lax.dot_general(
+            residual(p), q, (((0,), (0,)), ((), ())), precision=lax.Precision.HIGHEST,
+            preferred_element_type=jnp.float32,
+        )
+        p = p - LR_USER * (gradient + LAMBDA_REG * p)
+    p_out[...] = p
+    r_out[...] = residual(p)
+
+
+def user_steps(chunk, block, weight, target):
+    rows, width = chunk.shape
+    items = block.shape[0]
+    vmem = pl.BlockSpec(memory_space=pltpu.VMEM)
+    flops = (2 * INNER + 1) * 2 * items * rows * width
+    return pl.pallas_call(
+        user_steps_kernel,
+        out_shape=(
+            jax.ShapeDtypeStruct((rows, width), jnp.float32),
+            jax.ShapeDtypeStruct((items, rows), jnp.float32),
+        ),
+        in_specs=[vmem, vmem, vmem, vmem],
+        out_specs=(vmem, vmem),
+        cost_estimate=pl.CostEstimate(
+            flops=6 * flops,
+            transcendentals=(INNER + 1) * items * rows,
+            bytes_accessed=4 * (2 * rows * width + items * width + 3 * items * rows),
+        ),
+    )(chunk, block, weight, target)
 
 
 def per_device(user_factors, item_factors, item_index, labels, confidence):
@@ -68,20 +116,13 @@
     for stratum in range(strata):
         if stratum > 0:
             chunks = [shifted(chunk, "ub", 1) for chunk in chunks]
-        weight, target = build_tiles(slot_data[stratum][0], slot_data[stratum][1], slab_rows)
+        weight, target = build_tiles(slot_data[stratum][0], slot_data[stratum][1], slab_rows, pieces)
         finished = []
         residuals = []
         for k, chunk in enumerate(chunks):
-            weight_k = weight[:, k * rows : (k + 1) * rows]
-            target_k = target[:, k * rows : (k + 1) * rows]
-            for inner_step in range(INNER):
-                residual_t = residual_tile(chunk, block, weight_k, target_k)
-                gradient = lax.dot_general(
-                    residual_t, block, (((0,), (0,)), ((), ())), precision=MATMUL_PRECISION
-                )
-                chunk = chunk - LR_USER * (gradient + LAMBDA_REG * chunk)
+            chunk, residual_k = user_steps(chunk, block, weight[k], target[k])
             finished.append(chunk)
-            residuals.append(residual_tile(chunk, block, weight_k, target_k))
+            residuals.append(residual_k)
         chunks = finished
         residual_t = jnp.concatenate(residuals, 1)
         item_grad = jnp.dot(residual_t, jnp.concatenate(chunks, 0), precision=MATMUL_PRECISION)

time: 52.5 us -> 91.5 us (1.74)
  Pallas kernels: 0 us -> 38.9 us
  matrix products: 17.8 us -> 6.52 us
  local copies, waits for them, and re-layouts: 2.65 us -> 9.41 us
  starting transfers between devices: 16.5 us -> 22.7 us
  waiting for transfers between devices: 3.53 us -> 0.79 us
  other arithmetic: 10.6 us -> 11.8 us
    pallas_call x0 -> x6, Pallas kernels: none -> 38.9 us  [user_steps(): pl.pallas_call(user_steps_kernel, out_shape=(jax.ShapeDtypeStruct((rows,...]
    dot_general x30 -> x0, matrix products: 16.1 us -> none  [the longest x18 8.78 us: residual_tile(): scores_t = jnp.dot(item_rows, user_rows.T, precision=MATMUL_PRECISION)]
    ppermute x6, starting transfers between devices: 10.1 us -> 16.8 us  [gather_over(): lax.ppermute(block, axis, [(i, i ^ k) for i in range(count)])]
    slice x0 -> x4, local copies, waits for them, and re-layouts: none -> 5.59 us  [the longest x3 4.07 us: per_device(): chunk, residual_k = user_steps(chunk, block, weight[k], target[k])]
    dot_general x3, matrix products: 1.72 us -> 6.52 us  [per_device(): jnp.dot(residual_t, jnp.concatenate(chunks, 0), precision=MATMUL_PRECISION)]
    ppermute x8, waiting for transfers between devices: 1.52 us -> 0.02 us  [shifted(): return lax.ppermute(block, axis, route)]
    ppermute x6, waiting for transfers between devices: 2.01 us -> 0.77 us  [gather_over(): lax.ppermute(block, axis, [(i, i ^ k) for i in range(count)])]
    unnamed x13 -> x27, local copies, waits for them, and re-layouts: 1.4 us -> 2.56 us
  transfers between devices with their start and end apart: 14 -> 14, of which waited for: 2 -> 2; matrix products, arithmetic and copies ran while one was open for 43% -> 25% of each run, Pallas kernels for 0% -> 36%
where the time goes in v7:
time: 91.5 us; the launch traced here: 91 us
  Pallas kernels  38.9 us (43%)
  starting transfers between devices  22.7 us (25%)
  other arithmetic  11.8 us (13%)
  local copies, waits for them, and re-layouts  9.41 us (10%)
  matrix products  6.52 us (7%)
    pallas_call x6, Pallas kernels, user_steps(): pl.pallas_call(user_steps_kernel, out_shape=(jax.ShapeDtypeStruct((rows,...  38.9 us
    ppermute x6, starting transfers between devices, gather_over(): lax.ppermute(block, axis, [(i, i ^ k) for i in range(count)])  16.8 us
    reduce_sum x3, other arithmetic, build_tiles(): jnp.sum(jnp.where(matches, jnp.maximum(signed_rows, 0.0)[:, :, :, None, :...  6.85 us
    dot_general x3, matrix products, per_device(): jnp.dot(residual_t, jnp.concatenate(chunks, 0), precision=MATMUL_PRECISION)  6.52 us
    ppermute x8, starting transfers between devices, shifted(): return lax.ppermute(block, axis, route)  5.89 us
    slice x3, local copies, waits for them, and re-layouts, per_device(): chunk, residual_k = user_steps(chunk, block, weight[k], target[k])  4.07 us
    unnamed x27, local copies, waits for them, and re-layouts  2.56 us
  transfers between devices with their start and end apart: 14, of which 2 were waited for; matrix products, arithmetic and copies ran while one was open for 25% of the time, Pallas kernels for 36%

profile of v7, /device:TPU:0, one launch (start us, length us, event | category | flops | bytes accessed | tf_op | source)
XLA Modules:
  0.0 91.0 jit_solution(16966771012305440146)
XLA Ops:
  0.6 5.1 %collective-permute-start.2 = (f32[256,128]{1,0:T(8,128)}, f32[256,128]{1,0:T(8,128)S(1)}, u32[]{:S(2)}, u32[]{:S(2)}) collective-permute-start(f32[256,128]{1,0:T(8,128)} %param.6), channel_id=1, source_target_pairs={{0,3},{1,2},{2,1},{3,0},{4,7},{5,6},{6,5},{7,4},{8,11},{9,10},{10,... | collective-permute-start | bytes 393224 | tf_op jit(solution)/shard_map/ppermute | solution.py:27
  7.3 2.0 %collective-permute-start.5 = (f32[3,2,8,256]{3,2,0,1:T(8,128)S(1)}, f32[3,2,8,256]{3,2,0,1:T(8,128)S(1)}, u32[]{:S(2)}, u32[]{:S(2)}) collective-permute-start(f32[3,2,8,256]{3,2,0,1:T(8,128)S(1)} %get-tuple-element.62), channel_id=1, source_target_pairs={{0,3},{1,2},{2,1},{3,0},{4,7},{5,6},{6,5},{7,4},{8,11},{9,10},{10,... | collective-permute-start | bytes 147464 | tf_op jit(solution)/shard_map/ppermute | solution.py:27
  10.3 1.4 %collective-permute-start.3 = (f32[3,2,8,256]{3,2,0,1:T(8,128)S(1)}, f32[3,2,8,256]{3,2,0,1:T(8,128)S(1)}, u32[]{:S(2)}, u32[]{:S(2)}) collective-permute-start(f32[3,2,8,256]{3,2,0,1:T(8,128)S(1)} %get-tuple-element.62), channel_id=1, source_target_pairs={{0,1},{1,0},{2,3},{3,2},{4,5},{5,4},{6,7},{7,6},{8,9},{9,8},{10,11... | collective-permute-start | bytes 147464 | tf_op jit(solution)/shard_map/ppermute | solution.py:27
  11.7 1.5 %fusion.38 = (f32[128,128]{1,0:T(8,128)}, f32[128,128]{1,0:T(8,128)}) fusion(f32[256,128]{1,0:T(8,128)} %param.5), kind=kLoop, calls=%fused_computation.81 | loop fusion | bytes 262144 | tf_op jit(solution)/shard_map/slice | solution.py:115
  14.1 7.2 %collective-permute-start = (f32[256,128]{1,0:T(8,128)}, f32[256,128]{1,0:T(8,128)S(1)}, u32[]{:S(2)}, u32[]{:S(2)}) collective-permute-start(f32[256,128]{1,0:T(8,128)} %param.6), channel_id=1, source_target_pairs={{0,1},{1,0},{2,3},{3,2},{4,5},{5,4},{6,7},{7,6},{8,9},{9,8},{10,11... | collective-permute-start | bytes 393224 | tf_op jit(solution)/shard_map/ppermute | solution.py:27
  22.2 1.6 %collective-permute-start.10 = (f32[2,4,8,256]{3,2,1,0:T(8,128)S(1)}, f32[2,4,8,256]{3,2,1,0:T(8,128)S(1)}, u32[]{:S(2)}, u32[]{:S(2)}) collective-permute-start(f32[2,4,8,256]{3,2,1,0:T(8,128)S(1)} %pad_maximum_fusion.4), channel_id=1, source_target_pairs={{8,0},{12,4},{0,8},{4,12},{9,1},{13,5},{1,9},{5,13},{10,2},{14,6},... | collective-permute-start | bytes 196616 | tf_op jit(solution)/shard_map/ppermute | solution.py:20
  23.8 2.3 %select_reduce_fusion.4 = (f32[2,4,256,128]{3,2,1,0:T(8,128)S(1)}, f32[2,4,256,128]{3,2,1,0:T(8,128)S(1)}) fusion(f32[2,4,8,128]{3,2,0,1:T(8,128)S(1)} %get-tuple-element.54, f32[2,4,8,128]{3,2,0,1:T(8,128)S(1)} %get-tuple-element.50, f32[2,4,8,128]{3,2,0,1:T(8,128)S(1)} %get-tuple-element.52), kind=kLoop, calls=%fused_computation.8 | loop fusion | flops 9961472 | bytes 2195456 | tf_op jit(solution)/shard_map/reduce_sum | solution.py:46
  26.0 1.4 %fusion.35 = (f32[1,4,256,128]{3,2,1,0:T(8,128)}, f32[1,4,256,128]{3,2,1,0:T(8,128)}, f32[1,4,256,128]{3,2,1,0:T(8,128)}, f32[1,4,256,128]{3,2,1,0:T(8,128)}) fusion(f32[2,4,256,128]{3,2,1,0:T(8,128)S(1)} %get-tuple-element.30, f32[2,4,256,128]{3,2,1,0:T(8,128)S(1)} %get-tuple-element.31), kind=kLoop, calls=%fused_computation.78 | loop fusion | bytes 4194304 | tf_op jit(solution)/shard_map/slice | solution.py:123
  27.4 2.3 %select_reduce_fusion.2 = (f32[2,4,256,128]{3,2,1,0:T(8,128)S(1)}, f32[2,4,256,128]{3,2,1,0:T(8,128)S(1)}) fusion(f32[2,4,8,128]{3,2,0,1:T(8,128)S(1)} %get-tuple-element.58, f32[2,4,8,128]{3,2,0,1:T(8,128)S(1)} %get-tuple-element.60, f32[2,4,8,128]{3,2,0,1:T(8,128)S(1)} %get-tuple-element.59), kind=kLoop, calls=%fused_computation.5 | loop fusion | flops 9961472 | bytes 2195456 | tf_op jit(solution)/shard_map/reduce_sum | solution.py:46
  29.7 1.3 %fusion.33 = (f32[1,4,256,128]{3,2,1,0:T(8,128)}, f32[1,4,256,128]{3,2,1,0:T(8,128)}, f32[1,4,256,128]{3,2,1,0:T(8,128)}, f32[1,4,256,128]{3,2,1,0:T(8,128)}) fusion(f32[2,4,256,128]{3,2,1,0:T(8,128)S(1)} %get-tuple-element.28, f32[2,4,256,128]{3,2,1,0:T(8,128)S(1)} %get-tuple-element.29), kind=kLoop, calls=%fused_computation.76 | loop fusion | bytes 4194304 | tf_op jit(solution)/shard_map/slice | solution.py:123
  31.1 2.3 %select_reduce_fusion = (f32[2,4,256,128]{3,2,1,0:T(8,128)S(1)}, f32[2,4,256,128]{3,2,1,0:T(8,128)S(1)}) fusion(f32[2,4,8,128]{3,2,0,1:T(8,128)S(1)} %get-tuple-element.55, f32[2,4,8,128]{3,2,0,1:T(8,128)S(1)} %get-tuple-element.57, f32[2,4,8,128]{3,2,0,1:T(8,128)S(1)} %get-tuple-element.56), kind=kLoop, calls=%fused_computation.2 | loop fusion | flops 9961472 | bytes 2195456 | tf_op jit(solution)/shard_map/reduce_sum | solution.py:46
  33.4 1.4 %fusion.31 = (f32[1,4,256,128]{3,2,1,0:T(8,128)}, f32[1,4,256,128]{3,2,1,0:T(8,128)}, f32[1,4,256,128]{3,2,1,0:T(8,128)}, f32[1,4,256,128]{3,2,1,0:T(8,128)}) fusion(f32[2,4,256,128]{3,2,1,0:T(8,128)S(1)} %get-tuple-element.26, f32[2,4,256,128]{3,2,1,0:T(8,128)S(1)} %get-tuple-element.27), kind=kLoop, calls=%fused_computation.74 | loop fusion | bytes 4194304 | tf_op jit(solution)/shard_map/slice | solution.py:123
  36.4 6.4 %shard_map.69 = (f32[128,128]{1,0:T(8,128)}, f32[1024,128]{1,0:T(8,128)}) custom-call(f32[128,128]{1,0:T(8,128)} %get-tuple-element.47.p_ref, f32[1024,128]{1,0:T(8,128)} %bitcast_select_fusion.q_ref, f32[1024,128]{1,0:T(8,128)} %bitcast.95, f32[1024,128]{1,0:T(8,128)} %bitcast.94), custom_call_target="tpu_custom_call" | custom-call | flops 1006632960 | bytes 2228224 | tf_op jit(solution)/shard_map/pallas_call | solution.py:77
  43.2 6.6 %shard_map.68 = (f32[128,128]{1,0:T(8,128)}, f32[1024,128]{1,0:T(8,128)}) custom-call(f32[128,128]{1,0:T(8,128)} %get-tuple-element.46.p_ref, f32[1024,128]{1,0:T(8,128)} %bitcast_select_fusion.q_ref, f32[1024,128]{1,0:T(8,128)} %bitcast.91, f32[1024,128]{1,0:T(8,128)} %bitcast.90), custom_call_target="tpu_custom_call" | custom-call | flops 1006632960 | bytes 2228224 | tf_op jit(solution)/shard_map/pallas_call | solution.py:77
  50.1 2.5 %fusion.1.q_ref = f32[1024,128]{1,0:T(8,128)} fusion(f32[1024,128]{1,0:T(8,128)S(1)} %copy-done.1, f32[1024,128]{1,0:T(8,128)S(1)} %copy-done.3, f32[1024,128]{1,0:T(8,128)} %get-tuple-element.15, f32[128,128]{1,0:T(8,128)S(1)} %copy-done.7, f32[128,128]{1,0:T(8,128)} %get-tuple-element.14), kind=kOutput, calls=%fused_computation.14 | convolution fusion | flops 202014720 | bytes 2228224 | tf_op jit(solution)/shard_map/dot_general | solution.py:128
  53.2 6.4 %shard_map.71 = (f32[128,128]{1,0:T(8,128)}, f32[1024,128]{1,0:T(8,128)}) custom-call(f32[128,128]{1,0:T(8,128)} %copy-done.12, f32[1024,128]{1,0:T(8,128)} %fusion.1.q_ref, f32[1024,128]{1,0:T(8,128)} %bitcast.93, f32[1024,128]{1,0:T(8,128)} %bitcast.92), custom_call_target="tpu_custom_call" | custom-call | flops 1006632960 | bytes 2228224 | tf_op jit(solution)/shard_map/pallas_call | solution.py:77
  59.6 1.3 %collective-permute-start.12 = (f32[128,128]{1,0:T(8,128)}, f32[128,128]{1,0:T(8,128)S(1)}, u32[]{:S(2)}, u32[]{:S(2)}) collective-permute-start(f32[128,128]{1,0:T(8,128)} %get-tuple-element.21), channel_id=1, source_target_pairs={{4,0},{8,4},{12,8},{0,12},{5,1},{9,5},{13,9},{1,13},{6,2},{10,6},{... | collective-permute-start | bytes 196616 | tf_op jit(solution)/shard_map/ppermute | solution.py:20
  61.5 6.5 %shard_map.70 = (f32[128,128]{1,0:T(8,128)}, f32[1024,128]{1,0:T(8,128)}) custom-call(f32[128,128]{1,0:T(8,128)} %copy-done.9, f32[1024,128]{1,0:T(8,128)} %fusion.1.q_ref, f32[1024,128]{1,0:T(8,128)} %bitcast.87, f32[1024,128]{1,0:T(8,128)} %bitcast.86), custom_call_target="tpu_custom_call" | custom-call | flops 1006632960 | bytes 2228224 | tf_op jit(solution)/shard_map/pallas_call | solution.py:77
  68.4 2.4 %fusion.3.q_ref = f32[1024,128]{1,0:T(8,128)} fusion(f32[1024,128]{1,0:T(8,128)S(1)} %copy-done, f32[1024,128]{1,0:T(8,128)S(1)} %copy-done.2, f32[1024,128]{1,0:T(8,128)} %get-tuple-element.19, f32[128,128]{1,0:T(8,128)S(1)} %copy-done.6, f32[128,128]{1,0:T(8,128)} %get-tuple-element.18), kind=kOutput, calls=%fused_computation.16 | convolution fusion | flops 202014720 | bytes 2228224 | tf_op jit(solution)/shard_map/dot_general | solution.py:128
  71.5 6.5 %shard_map.73 = (f32[128,128]{1,0:T(8,128)}, f32[1024,128]{1,0:T(8,128)}) custom-call(f32[128,128]{1,0:T(8,128)} %copy-done.10, f32[1024,128]{1,0:T(8,128)} %fusion.3.q_ref, f32[1024,128]{1,0:T(8,128)} %bitcast.89, f32[1024,128]{1,0:T(8,128)} %bitcast.88), custom_call_target="tpu_custom_call" | custom-call | flops 1006632960 | bytes 2228224 | tf_op jit(solution)/shard_map/pallas_call | solution.py:77
  79.1 6.5 %shard_map.72 = (f32[128,128]{1,0:T(8,128)}, f32[1024,128]{1,0:T(8,128)}) custom-call(f32[128,128]{1,0:T(8,128)} %copy-done.11, f32[1024,128]{1,0:T(8,128)} %fusion.3.q_ref, f32[1024,128]{1,0:T(8,128)} %bitcast.85, f32[1024,128]{1,0:T(8,128)} %bitcast.84), custom_call_target="tpu_custom_call" | custom-call | flops 1006632960 | bytes 2228224 | tf_op jit(solution)/shard_map/pallas_call | solution.py:77
  85.6 1.5 %collective-permute-start.11 = (f32[128,128]{1,0:T(8,128)}, f32[128,128]{1,0:T(8,128)S(1)}, u32[]{:S(2)}, u32[]{:S(2)}) collective-permute-start(f32[128,128]{1,0:T(8,128)} %get-tuple-element.22), channel_id=1, source_target_pairs={{8,0},{12,4},{0,8},{4,12},{9,1},{13,5},{1,9},{5,13},{10,2},{14,6},... | collective-permute-start | bytes 196616 | tf_op jit(solution)/shard_map/ppermute | solution.py:20
  87.1 1.6 %fusion.10 = f32[1024,128]{1,0:T(8,128)S(1)} fusion(f32[1024,128]{1,0:T(8,128)S(1)} %copy-done.4, f32[1024,128]{1,0:T(8,128)} %get-tuple-element.24, f32[128,128]{1,0:T(8,128)S(1)} %copy-done.8, f32[128,128]{1,0:T(8,128)} %get-tuple-element.22), kind=kOutput, calls=%fused_computation.23 | convolution fusion | flops 201621504 | bytes 1703936 | tf_op jit(solution)/shard_map/dot_general | solution.py:128
  88.7 1.6 %fusion.15 = f32[256,128]{1,0:T(8,128)} fusion(f32[1024,128]{1,0:T(8,128)S(1)} %fusion.10, s32[]{:T(128)S(6)} %select_n.64, f32[1024,128]{1,0:T(8,128)} %fusion.3.q_ref), kind=kLoop, calls=%fused_computation.32 | loop fusion | flops 98304 | bytes 393220 | tf_op jit(solution)/shard_map/sub | solution.py:129
  (70 shorter events, 10.7 us)
Async XLA Ops:
  0.6 34.1 %collective-permute-start.2 = (f32[256,128]{1,0:T(8,128)}, f32[256,128]{1,0:T(8,128)S(1)}, u32[]{:S(2)}, u32[]{:S(2)}) collective-permute-start(f32[256,128]{1,0:T(8,128)} %param.6), channel_id=1, source_target_pairs={{0,3},{1,2},{2,1},{3,0},{4,7},{5,6},{6,5},{7,4},{8,11},{9,10},{10,... | collective-permute-start | bytes 393224 | tf_op jit(solution)/shard_map/ppermute | solution.py:27
  5.7 29.0 %collective-permute-start.1 = (f32[256,128]{1,0:T(8,128)}, f32[256,128]{1,0:T(8,128)S(1)}, u32[]{:S(2)}, u32[]{:S(2)}) collective-permute-start(f32[256,128]{1,0:T(8,128)} %param.6), channel_id=1, source_target_pairs={{0,2},{1,3},{2,0},{3,1},{4,6},{5,7},{6,4},{7,5},{8,10},{9,11},{10,... | collective-permute-start | bytes 393224 | tf_op jit(solution)/shard_map/ppermute | solution.py:27
  7.3 6.8 %collective-permute-start.5 = (f32[3,2,8,256]{3,2,0,1:T(8,128)S(1)}, f32[3,2,8,256]{3,2,0,1:T(8,128)S(1)}, u32[]{:S(2)}, u32[]{:S(2)}) collective-permute-start(f32[3,2,8,256]{3,2,0,1:T(8,128)S(1)} %get-tuple-element.62), channel_id=1, source_target_pairs={{0,3},{1,2},{2,1},{3,0},{4,7},{5,6},{6,5},{7,4},{8,11},{9,10},{10,... | collective-permute-start | bytes 147464 | tf_op jit(solution)/shard_map/ppermute | solution.py:27
  9.2 12.1 %collective-permute-start.4 = (f32[3,2,8,256]{3,2,0,1:T(8,128)S(1)}, f32[3,2,8,256]{3,2,0,1:T(8,128)S(1)}, u32[]{:S(2)}, u32[]{:S(2)}) collective-permute-start(f32[3,2,8,256]{3,2,0,1:T(8,128)S(1)} %get-tuple-element.62), channel_id=1, source_target_pairs={{0,2},{1,3},{2,0},{3,1},{4,6},{5,7},{6,4},{7,5},{8,10},{9,11},{10,... | collective-permute-start | bytes 147464 | tf_op jit(solution)/shard_map/ppermute | solution.py:27
  10.3 11.0 %collective-permute-start.3 = (f32[3,2,8,256]{3,2,0,1:T(8,128)S(1)}, f32[3,2,8,256]{3,2,0,1:T(8,128)S(1)}, u32[]{:S(2)}, u32[]{:S(2)}) collective-permute-start(f32[3,2,8,256]{3,2,0,1:T(8,128)S(1)} %get-tuple-element.62), channel_id=1, source_target_pairs={{0,1},{1,0},{2,3},{3,2},{4,5},{5,4},{6,7},{7,6},{8,9},{9,8},{10,11... | collective-permute-start | bytes 147464 | tf_op jit(solution)/shard_map/ppermute | solution.py:27
  14.1 20.7 %collective-permute-start = (f32[256,128]{1,0:T(8,128)}, f32[256,128]{1,0:T(8,128)S(1)}, u32[]{:S(2)}, u32[]{:S(2)}) collective-permute-start(f32[256,128]{1,0:T(8,128)} %param.6), channel_id=1, source_target_pairs={{0,1},{1,0},{2,3},{3,2},{4,5},{5,4},{6,7},{7,6},{8,9},{9,8},{10,11... | collective-permute-start | bytes 393224 | tf_op jit(solution)/shard_map/ppermute | solution.py:27
  22.1 5.3 %collective-permute-start.7 = (f32[2,4,8,256]{3,2,1,0:T(8,128)S(1)}, f32[2,4,8,256]{3,2,1,0:T(8,128)S(1)}, u32[]{:S(2)}, u32[]{:S(2)}) collective-permute-start(f32[2,4,8,256]{3,2,1,0:T(8,128)S(1)} %pad_maximum_fusion.3), channel_id=1, source_target_pairs={{4,0},{8,4},{12,8},{0,12},{5,1},{9,5},{13,9},{1,13},{6,2},{10,6},{... | collective-permute-start | bytes 196616 | tf_op jit(solution)/shard_map/ppermute | solution.py:20
  22.2 8.9 %collective-permute-start.10 = (f32[2,4,8,256]{3,2,1,0:T(8,128)S(1)}, f32[2,4,8,256]{3,2,1,0:T(8,128)S(1)}, u32[]{:S(2)}, u32[]{:S(2)}) collective-permute-start(f32[2,4,8,256]{3,2,1,0:T(8,128)S(1)} %pad_maximum_fusion.4), channel_id=1, source_target_pairs={{8,0},{12,4},{0,8},{4,12},{9,1},{13,5},{1,9},{5,13},{10,2},{14,6},... | collective-permute-start | bytes 196616 | tf_op jit(solution)/shard_map/ppermute | solution.py:20
  33.4 1.4 %copy-start.5 = (f32[256,128]{1,0:T(8,128)S(1)}, f32[256,128]{1,0:T(8,128)}, u32[]{:S(2)}) copy-start(f32[256,128]{1,0:T(8,128)} %param.6) | copy-start | bytes 393220
  42.9 9.7 %collective-permute-start.9 = (f32[128,128]{1,0:T(8,128)}, f32[128,128]{1,0:T(8,128)S(1)}, u32[]{:S(2)}, u32[]{:S(2)}) collective-permute-start(f32[128,128]{1,0:T(8,128)} %get-tuple-element.17), channel_id=1, source_target_pairs={{4,0},{8,4},{12,8},{0,12},{5,1},{9,5},{13,9},{1,13},{6,2},{10,6},{... | collective-permute-start | bytes 196616 | tf_op jit(solution)/shard_map/ppermute | solution.py:20
  43.2 6.9 %copy-start.1 = (f32[1024,128]{1,0:T(8,128)S(1)}, f32[1024,128]{1,0:T(8,128)}, u32[]{:S(2)}) copy-start(f32[1024,128]{1,0:T(8,128)} %bitcast_select_fusion.q_ref) | copy-start | bytes 1572868
  43.2 6.9 %copy-start.3 = (f32[1024,128]{1,0:T(8,128)S(1)}, f32[1024,128]{1,0:T(8,128)}, u32[]{:S(2)}) copy-start(f32[1024,128]{1,0:T(8,128)} %get-tuple-element.16) | copy-start | bytes 1572868
  43.2 6.9 %copy-start.7 = (f32[128,128]{1,0:T(8,128)S(1)}, f32[128,128]{1,0:T(8,128)}, u32[]{:S(2)}) copy-start(f32[128,128]{1,0:T(8,128)} %get-tuple-element.17) | copy-start | bytes 196612
  49.7 11.1 %collective-permute-start.6 = (f32[128,128]{1,0:T(8,128)}, f32[128,128]{1,0:T(8,128)S(1)}, u32[]{:S(2)}, u32[]{:S(2)}) collective-permute-start(f32[128,128]{1,0:T(8,128)} %get-tuple-element.14), channel_id=1, source_target_pairs={{4,0},{8,4},{12,8},{0,12},{5,1},{9,5},{13,9},{1,13},{6,2},{10,6},{... | collective-permute-start | bytes 196616 | tf_op jit(solution)/shard_map/ppermute | solution.py:20
  52.5 0.6 copy-start.12
  59.6 11.2 %collective-permute-start.12 = (f32[128,128]{1,0:T(8,128)}, f32[128,128]{1,0:T(8,128)S(1)}, u32[]{:S(2)}, u32[]{:S(2)}) collective-permute-start(f32[128,128]{1,0:T(8,128)} %get-tuple-element.21), channel_id=1, source_target_pairs={{4,0},{8,4},{12,8},{0,12},{5,1},{9,5},{13,9},{1,13},{6,2},{10,6},{... | collective-permute-start | bytes 196616 | tf_op jit(solution)/shard_map/ppermute | solution.py:20
  61.5 6.9 %copy-start = (f32[1024,128]{1,0:T(8,128)S(1)}, f32[1024,128]{1,0:T(8,128)}, u32[]{:S(2)}) copy-start(f32[1024,128]{1,0:T(8,128)} %fusion.1.q_ref) | copy-start | bytes 1572868
  61.5 6.9 %copy-start.2 = (f32[1024,128]{1,0:T(8,128)S(1)}, f32[1024,128]{1,0:T(8,128)}, u32[]{:S(2)}) copy-start(f32[1024,128]{1,0:T(8,128)} %get-tuple-element.20) | copy-start | bytes 1572868
  61.5 6.9 %copy-start.6 = (f32[128,128]{1,0:T(8,128)S(1)}, f32[128,128]{1,0:T(8,128)}, u32[]{:S(2)}) copy-start(f32[128,128]{1,0:T(8,128)} %get-tuple-element.21) | copy-start | bytes 196612
  68.1 10.4 %collective-permute-start.8 = (f32[128,128]{1,0:T(8,128)}, f32[128,128]{1,0:T(8,128)S(1)}, u32[]{:S(2)}, u32[]{:S(2)}) collective-permute-start(f32[128,128]{1,0:T(8,128)} %get-tuple-element.18), channel_id=1, source_target_pairs={{4,0},{8,4},{12,8},{0,12},{5,1},{9,5},{13,9},{1,13},{6,2},{10,6},{... | collective-permute-start | bytes 196616 | tf_op jit(solution)/shard_map/ppermute | solution.py:20
  77.9 12.4 %collective-permute-start.13 = (f32[128,128]{1,0:T(8,128)}, f32[128,128]{1,0:T(8,128)S(1)}, u32[]{:S(2)}, u32[]{:S(2)}) collective-permute-start(f32[128,128]{1,0:T(8,128)} %get-tuple-element.23), channel_id=1, source_target_pairs={{8,0},{12,4},{0,8},{4,12},{9,1},{13,5},{1,9},{5,13},{10,2},{14,6},... | collective-permute-start | bytes 196616 | tf_op jit(solution)/shard_map/ppermute | solution.py:20
  79.1 8.0 %copy-start.4 = (f32[1024,128]{1,0:T(8,128)S(1)}, f32[1024,128]{1,0:T(8,128)}, u32[]{:S(2)}) copy-start(f32[1024,128]{1,0:T(8,128)} %get-tuple-element.25) | copy-start | bytes 1572868
  79.1 8.0 %copy-start.8 = (f32[128,128]{1,0:T(8,128)S(1)}, f32[128,128]{1,0:T(8,128)}, u32[]{:S(2)}) copy-start(f32[128,128]{1,0:T(8,128)} %get-tuple-element.23) | copy-start | bytes 196612
  85.6 4.7 %collective-permute-start.11 = (f32[128,128]{1,0:T(8,128)}, f32[128,128]{1,0:T(8,128)S(1)}, u32[]{:S(2)}, u32[]{:S(2)}) collective-permute-start(f32[128,128]{1,0:T(8,128)} %get-tuple-element.22), channel_id=1, source_target_pairs={{8,0},{12,4},{0,8},{4,12},{9,1},{13,5},{1,9},{5,13},{10,2},{14,6},... | collective-permute-start | bytes 196616 | tf_op jit(solution)/shard_map/ppermute | solution.py:20
  (3 other events, 1.9 us)

commit v8 on v7

--- a/solution.py
+++ b/solution.py
@@ -35,55 +35,65 @@
     return weight_t * jax.nn.sigmoid(scores_t) - target_t
 
 
-def build_tiles(index_rows, signed_rows, slab_width, pieces):
+def build_tiles(index_rows, signed_rows, slab_width):
     slabs, slot_count, user_count = index_rows.shape
-    rows = user_count // pieces
-    index_rows = jnp.transpose(index_rows.reshape(slabs, slot_count, pieces, rows), (2, 0, 1, 3))
-    signed_rows = jnp.transpose(signed_rows.reshape(slabs, slot_count, pieces, rows), (2, 0, 1, 3))
-    columns = jnp.arange(slab_width, dtype=jnp.float32)[None, None, None, :, None]
-    matches = index_rows[:, :, :, None, :] == columns
-    weight = jnp.sum(jnp.where(matches, jnp.abs(signed_rows)[:, :, :, None, :], 0.0), axis=2)
-    target = jnp.sum(jnp.where(matches, jnp.maximum(signed_rows, 0.0)[:, :, :, None, :], 0.0), axis=2)
-    return weight.reshape(pieces, slabs * slab_width, rows), target.reshape(pieces, slabs * slab_width, rows)
+    columns = jnp.arange(slab_width, dtype=jnp.float32)[None, None, :, None]
+    matches = index_rows[:, :, None, :] == columns
+    weight = jnp.sum(jnp.where(matches, jnp.abs(signed_rows)[:, :, None, :], 0.0), axis=1)
+    target = jnp.sum(jnp.where(matches, jnp.maximum(signed_rows, 0.0)[:, :, None, :], 0.0), axis=1)
+    return weight.reshape(slabs * slab_width, user_count), target.reshape(slabs * slab_width, user_count)
+
+
+def split_bf16(x):
+    high = x.astype(jnp.bfloat16)
+    return high, (x - high.astype(jnp.float32)).astype(jnp.bfloat16)
+
+
+def dot_three(a_parts, b_parts, dims):
+    def one(a, b):
+        return lax.dot_general(a, b, dims, preferred_element_type=jnp.float32)
+
+    return one(a_parts[0], b_parts[0]) + (one(a_parts[0], b_parts[1]) + one(a_parts[1], b_parts[0]))
 
 
 def user_steps_kernel(p_ref, q_ref, w_ref, t_ref, p_out, r_out):
     q = q_ref[...]
+    q_parts = split_bf16(q)
     w = w_ref[...]
     t = t_ref[...]
+    rows_by_rows = (((1,), (1,)), ((), ()))
+    plain = (((1,), (0,)), ((), ()))
 
     def residual(p):
-        scores_t = lax.dot_general(
-            q, p, (((1,), (1,)), ((), ())), precision=lax.Precision.HIGHEST, preferred_element_type=jnp.float32
-        )
+        scores_t = dot_three(q_parts, split_bf16(p), rows_by_rows)
         return w * jax.nn.sigmoid(scores_t) - t
 
     p = p_ref[...]
     for inner_step in range(INNER):
-        gradient = lax.dot_general(
-            residual(p), q, (((0,), (0,)), ((), ())), precision=lax.Precision.HIGHEST,
-            preferred_element_type=jnp.float32,
-        )
+        residual_rows = residual(p).T
+        gradient = dot_three(split_bf16(residual_rows), q_parts, plain)
         p = p - LR_USER * (gradient + LAMBDA_REG * p)
     p_out[...] = p
     r_out[...] = residual(p)
 
 
-def user_steps(chunk, block, weight, target):
+def user_steps(chunk, block, weight, target, piece):
     rows, width = chunk.shape
     items = block.shape[0]
     vmem = pl.BlockSpec(memory_space=pltpu.VMEM)
+    columns = pl.BlockSpec((items, rows), lambda step: (0, piece))
     flops = (2 * INNER + 1) * 2 * items * rows * width
     return pl.pallas_call(
         user_steps_kernel,
+        grid=(1,),
         out_shape=(
             jax.ShapeDtypeStruct((rows, width), jnp.float32),
             jax.ShapeDtypeStruct((items, rows), jnp.float32),
         ),
-        in_specs=[vmem, vmem, vmem, vmem],
+        in_specs=[vmem, vmem, columns, columns],
         out_specs=(vmem, vmem),
         cost_estimate=pl.CostEstimate(
-            flops=6 * flops,
+            flops=3 * flops,
             transcendentals=(INNER + 1) * items * rows,
             bytes_accessed=4 * (2 * rows * width + items * width + 3 * items * rows),
         ),
@@ -116,11 +126,11 @@
     for stratum in range(strata):
         if stratum > 0:
             chunks = [shifted(chunk, "ub", 1) for chunk in chunks]
-        weight, target = build_tiles(slot_data[stratum][0], slot_data[stratum][1], slab_rows, pieces)
+        weight, target = build_tiles(slot_data[stratum][0], slot_data[stratum][1], slab_rows)
         finished = []
         residuals = []
         for k, chunk in enumerate(chunks):
-            chunk, residual_k = user_steps(chunk, block, weight[k], target[k])
+            chunk, residual_k = user_steps(chunk, block, weight, target, k)
             finished.append(chunk)
             residuals.append(residual_k)
         chunks = finished

time: 91.5 us -> 71.4 us (0.78)
  Pallas kernels: 38.9 us -> 28 us
  starting transfers between devices: 22.7 us -> 16.1 us
  local copies, waits for them, and re-layouts: 9.41 us -> 5.35 us
  other arithmetic: 11.8 us -> 13.6 us
    pallas_call x6, Pallas kernels: 38.9 us -> 28 us  [user_steps(): pl.pallas_call(user_steps_kernel, grid=(1,), out_shape=(jax.ShapeDtypeStr...]
    ppermute x6, starting transfers between devices: 16.8 us -> 10.1 us  [gather_over(): lax.ppermute(block, axis, [(i, i ^ k) for i in range(count)])]
    slice x3 -> x0, local copies, waits for them, and re-layouts: 4.07 us -> none  [per_device(): chunk, residual_k = user_steps(chunk, block, weight[k], target[k])]
    reduce_sum x3, other arithmetic: 6.85 us -> 8.63 us  [build_tiles(): jnp.sum(jnp.where(matches, jnp.maximum(signed_rows, 0.0)[:, :, None, :],...]
  transfers between devices with their start and end apart: 14 -> 14, of which waited for: 2 -> 1; matrix products, arithmetic and copies ran while one was open for 25% -> 27% of each run, Pallas kernels for 36% -> 26%
where the time goes in v8:
time: 71.4 us; the launch traced here: 70.9 us
  Pallas kernels  28 us (39%)
  starting transfers between devices  16.1 us (23%)
  other arithmetic  13.6 us (19%)
  matrix products  6.5 us (9%)
  local copies, waits for them, and re-layouts  5.35 us (7%)
  between operations  0.81 us (1%)
    pallas_call x6, Pallas kernels, user_steps(): pl.pallas_call(user_steps_kernel, grid=(1,), out_shape=(jax.ShapeDtypeStr...  28 us
    ppermute x6, starting transfers between devices, gather_over(): lax.ppermute(block, axis, [(i, i ^ k) for i in range(count)])  10.1 us
    reduce_sum x3, other arithmetic, build_tiles(): jnp.sum(jnp.where(matches, jnp.maximum(signed_rows, 0.0)[:, :, None, :],...  8.63 us
    dot_general x3, matrix products, per_device(): jnp.dot(residual_t, jnp.concatenate(chunks, 0), precision=MATMUL_PRECISION)  6.5 us
    ppermute x8, starting transfers between devices, shifted(): return lax.ppermute(block, axis, route)  5.95 us
    unnamed x27, local copies, waits for them, and re-layouts  2.56 us
    sub x1, other arithmetic, per_device(): block = block - LR_ITEM * (item_grad + LAMBDA_REG * block)  1.59 us
    slice x1, local copies, waits for them, and re-layouts, per_device(): chunks = [user_factors[k * rows:(k + 1) * rows] for k in range(pieces)]  1.53 us
  transfers between devices with their start and end apart: 14, of which 1 were waited for; matrix products, arithmetic and copies ran while one was open for 27% of the time, Pallas kernels for 26%

profile of v8, /device:TPU:0, one launch (start us, length us, event | category | flops | bytes accessed | tf_op | source)
XLA Modules:
  0.0 70.9 jit_solution(14126760894516610265)
XLA Ops:
  1.4 0.8 %fusion.25 = f32[3,1,8,256]{3,2,0,1:T(8,128)S(1)} fusion(f32[3,256,8]{1,2,0:T(8,128)} %param.9, s32[3,256,8]{1,2,0:T(8,128)} %param.8), kind=kLoop, calls=%fused_computation.63 | loop fusion | flops 18432 | bytes 73728 | tf_op jit(solution)/shard_map/stack | solution.py:107
  2.1 3.1 %collective-permute-start.3 = (f32[3,2,8,256]{3,2,0,1:T(8,128)S(1)}, f32[3,2,8,256]{3,2,0,1:T(8,128)S(1)}, u32[]{:S(2)}, u32[]{:S(2)}) collective-permute-start(f32[3,2,8,256]{3,2,0,1:T(8,128)S(1)} %get-tuple-element.50), channel_id=1, source_target_pairs={{0,1},{1,0},{2,3},{3,2},{4,5},{5,4},{6,7},{7,6},{8,9},{9,8},{10,11... | collective-permute-start | bytes 147464 | tf_op jit(solution)/shard_map/ppermute | solution.py:27
  5.2 2.6 %collective-permute-start.4 = (f32[3,2,8,256]{3,2,0,1:T(8,128)S(1)}, f32[3,2,8,256]{3,2,0,1:T(8,128)S(1)}, u32[]{:S(2)}, u32[]{:S(2)}) collective-permute-start(f32[3,2,8,256]{3,2,0,1:T(8,128)S(1)} %get-tuple-element.50), channel_id=1, source_target_pairs={{0,2},{1,3},{2,0},{3,1},{4,6},{5,7},{6,4},{7,5},{8,10},{9,11},{10,... | collective-permute-start | bytes 147464 | tf_op jit(solution)/shard_map/ppermute | solution.py:27
  7.8 0.9 %collective-permute-start = (f32[256,128]{1,0:T(8,128)}, f32[256,128]{1,0:T(8,128)S(1)}, u32[]{:S(2)}, u32[]{:S(2)}) collective-permute-start(f32[256,128]{1,0:T(8,128)} %param.6), channel_id=1, source_target_pairs={{0,1},{1,0},{2,3},{3,2},{4,5},{5,4},{6,7},{7,6},{8,9},{9,8},{10,11... | collective-permute-start | bytes 393224 | tf_op jit(solution)/shard_map/ppermute | solution.py:27
  8.7 3.5 %collective-permute-start.1 = (f32[256,128]{1,0:T(8,128)}, f32[256,128]{1,0:T(8,128)S(1)}, u32[]{:S(2)}, u32[]{:S(2)}) collective-permute-start(f32[256,128]{1,0:T(8,128)} %param.6), channel_id=1, source_target_pairs={{0,2},{1,3},{2,0},{3,1},{4,6},{5,7},{6,4},{7,5},{8,10},{9,11},{10,... | collective-permute-start | bytes 393224 | tf_op jit(solution)/shard_map/ppermute | solution.py:27
  12.2 1.5 %fusion.32 = (f32[128,128]{1,0:T(8,128)}, f32[128,128]{1,0:T(8,128)}) fusion(f32[256,128]{1,0:T(8,128)} %param.5), kind=kLoop, calls=%fused_computation.75 | loop fusion | bytes 262144 | tf_op jit(solution)/shard_map/slice | solution.py:125
  15.3 1.6 %collective-permute-start.10 = (f32[2,4,8,256]{3,2,1,0:T(8,128)S(1)}, f32[2,4,8,256]{3,2,1,0:T(8,128)S(1)}, u32[]{:S(2)}, u32[]{:S(2)}) collective-permute-start(f32[2,4,8,256]{3,2,1,0:T(8,128)S(1)} %pad_maximum_fusion.4), channel_id=1, source_target_pairs={{8,0},{12,4},{0,8},{4,12},{9,1},{13,5},{1,9},{5,13},{10,2},{14,6},... | collective-permute-start | bytes 196616 | tf_op jit(solution)/shard_map/ppermute | solution.py:20
  16.8 2.9 %select_reduce_fusion.4 = (f32[4,256,256]{2,1,0:T(8,128)}, f32[4,256,256]{2,1,0:T(8,128)}) fusion(f32[4,8,256]{2,1,0:T(8,128)S(1)} %get-tuple-element.40, f32[4,8,256]{2,1,0:T(8,128)S(1)} %get-tuple-element.38, f32[4,8,256]{2,1,0:T(8,128)S(1)} %get-tuple-element.42), kind=kLoop, calls=%fused_computation.8 | loop fusion | flops 9961472 | bytes 2195456 | tf_op jit(solution)/shard_map/reduce_sum | solution.py:43
  19.7 2.9 %select_reduce_fusion.2 = (f32[4,256,256]{2,1,0:T(8,128)}, f32[4,256,256]{2,1,0:T(8,128)}) fusion(f32[4,8,256]{2,1,0:T(8,128)S(1)} %get-tuple-element.47, f32[4,8,256]{2,1,0:T(8,128)S(1)} %get-tuple-element.48, f32[4,8,256]{2,1,0:T(8,128)S(1)} %get-tuple-element.46), kind=kLoop, calls=%fused_computation.5 | loop fusion | flops 9961472 | bytes 2195456 | tf_op jit(solution)/shard_map/reduce_sum | solution.py:43
  22.6 2.9 %select_reduce_fusion = (f32[4,256,256]{2,1,0:T(8,128)}, f32[4,256,256]{2,1,0:T(8,128)}) fusion(f32[4,8,256]{2,1,0:T(8,128)S(1)} %get-tuple-element.44, f32[4,8,256]{2,1,0:T(8,128)S(1)} %get-tuple-element.45, f32[4,8,256]{2,1,0:T(8,128)S(1)} %get-tuple-element.43), kind=kLoop, calls=%fused_computation.2 | loop fusion | flops 9961472 | bytes 2195456 | tf_op jit(solution)/shard_map/reduce_sum | solution.py:43
  26.1 1.0 %bitcast_select_fusion.q_ref = f32[1024,128]{1,0:T(8,128)} fusion(f32[4,256,128]{2,1,0:T(8,128)S(1)} %gather_fusion, pred[1024]{0:T(1024)(128)(4,1)S(1)} %broadcast_in_dim.76), kind=kLoop, calls=%fused_computation.28 | loop fusion | flops 131072 | bytes 1049600 | tf_op jit(solution)/shard_map/jit(_take)/select_n | solution.py:30
  27.1 4.7 %shard_map.68 = (f32[128,128]{1,0:T(8,128)}, f32[1024,128]{1,0:T(8,128)}) custom-call(f32[128,128]{1,0:T(8,128)} %get-tuple-element.34.p_ref, f32[1024,128]{1,0:T(8,128)} %bitcast_select_fusion.q_ref, f32[1024,256]{1,0:T(8,128)} %bitcast.70, f32[1024,256]{1,0:T(8,128)} %bitcast.68), custom_call_target="tpu_custom_call" | custom-call | flops 503316480 | bytes 2228224 | tf_op jit(solution)/shard_map/pallas_call | solution.py:86
  31.8 4.8 %shard_map.69 = (f32[128,128]{1,0:T(8,128)}, f32[1024,128]{1,0:T(8,128)}) custom-call(f32[128,128]{1,0:T(8,128)} %get-tuple-element.35.p_ref, f32[1024,128]{1,0:T(8,128)} %bitcast_select_fusion.q_ref, f32[1024,256]{1,0:T(8,128)} %bitcast.71, f32[1024,256]{1,0:T(8,128)} %bitcast.69), custom_call_target="tpu_custom_call" | custom-call | flops 503316480 | bytes 2228224 | tf_op jit(solution)/shard_map/pallas_call | solution.py:86
  37.2 2.4 %fusion.1.q_ref = f32[1024,128]{1,0:T(8,128)} fusion(f32[1024,128]{1,0:T(8,128)S(1)} %copy-done.1, f32[1024,128]{1,0:T(8,128)} %get-tuple-element.16, f32[1024,128]{1,0:T(8,128)S(1)} %copy-done.3, f32[128,128]{1,0:T(8,128)} %get-tuple-element.17, f32[128,128]{1,0:T(8,128)S(1)} %copy-done.7), kind=kOutput, calls=%fused_computation.14 | convolution fusion | flops 202014720 | bytes 2228224 | tf_op jit(solution)/shard_map/dot_general | solution.py:138
  40.3 4.7 %shard_map.70 = (f32[128,128]{1,0:T(8,128)}, f32[1024,128]{1,0:T(8,128)}) custom-call(f32[128,128]{1,0:T(8,128)} %copy-done.12, f32[1024,128]{1,0:T(8,128)} %fusion.1.q_ref, f32[1024,256]{1,0:T(8,128)} %bitcast.66, f32[1024,256]{1,0:T(8,128)} %bitcast.64), custom_call_target="tpu_custom_call" | custom-call | flops 503316480 | bytes 2228224 | tf_op jit(solution)/shard_map/pallas_call | solution.py:86
  45.0 1.3 %collective-permute-start.8 = (f32[128,128]{1,0:T(8,128)}, f32[128,128]{1,0:T(8,128)S(1)}, u32[]{:S(2)}, u32[]{:S(2)}) collective-permute-start(f32[128,128]{1,0:T(8,128)} %get-tuple-element.18), channel_id=1, source_target_pairs={{4,0},{8,4},{12,8},{0,12},{5,1},{9,5},{13,9},{1,13},{6,2},{10,6},{... | collective-permute-start | bytes 196616 | tf_op jit(solution)/shard_map/ppermute | solution.py:20
  46.9 4.7 %shard_map.71 = (f32[128,128]{1,0:T(8,128)}, f32[1024,128]{1,0:T(8,128)}) custom-call(f32[128,128]{1,0:T(8,128)} %copy-done.9, f32[1024,128]{1,0:T(8,128)} %fusion.1.q_ref, f32[1024,256]{1,0:T(8,128)} %bitcast.67, f32[1024,256]{1,0:T(8,128)} %bitcast.65), custom_call_target="tpu_custom_call" | custom-call | flops 503316480 | bytes 2228224 | tf_op jit(solution)/shard_map/pallas_call | solution.py:86
  51.9 2.4 %fusion.3.q_ref = f32[1024,128]{1,0:T(8,128)} fusion(f32[1024,128]{1,0:T(8,128)S(1)} %copy-done, f32[1024,128]{1,0:T(8,128)} %get-tuple-element.20, f32[1024,128]{1,0:T(8,128)S(1)} %copy-done.2, f32[128,128]{1,0:T(8,128)} %get-tuple-element.21, f32[128,128]{1,0:T(8,128)S(1)} %copy-done.6), kind=kOutput, calls=%fused_computation.16 | convolution fusion | flops 202014720 | bytes 2228224 | tf_op jit(solution)/shard_map/dot_general | solution.py:138
  55.0 4.7 %shard_map.72 = (f32[128,128]{1,0:T(8,128)}, f32[1024,128]{1,0:T(8,128)}) custom-call(f32[128,128]{1,0:T(8,128)} %copy-done.10, f32[1024,128]{1,0:T(8,128)} %fusion.3.q_ref, f32[1024,256]{1,0:T(8,128)} %bitcast.62, f32[1024,256]{1,0:T(8,128)} %bitcast.60), custom_call_target="tpu_custom_call" | custom-call | flops 503316480 | bytes 2228224 | tf_op jit(solution)/shard_map/pallas_call | solution.py:86
  59.7 0.8 %collective-permute-start.11 = (f32[128,128]{1,0:T(8,128)}, f32[128,128]{1,0:T(8,128)S(1)}, u32[]{:S(2)}, u32[]{:S(2)}) collective-permute-start(f32[128,128]{1,0:T(8,128)} %get-tuple-element.22), channel_id=1, source_target_pairs={{8,0},{12,4},{0,8},{4,12},{9,1},{13,5},{1,9},{5,13},{10,2},{14,6},... | collective-permute-start | bytes 196616 | tf_op jit(solution)/shard_map/ppermute | solution.py:20
  61.1 4.7 %shard_map.73 = (f32[128,128]{1,0:T(8,128)}, f32[1024,128]{1,0:T(8,128)}) custom-call(f32[128,128]{1,0:T(8,128)} %copy-done.11, f32[1024,128]{1,0:T(8,128)} %fusion.3.q_ref, f32[1024,256]{1,0:T(8,128)} %bitcast.63, f32[1024,256]{1,0:T(8,128)} %bitcast.61), custom_call_target="tpu_custom_call" | custom-call | flops 503316480 | bytes 2228224 | tf_op jit(solution)/shard_map/pallas_call | solution.py:86
  65.7 1.2 %collective-permute-start.13 = (f32[128,128]{1,0:T(8,128)}, f32[128,128]{1,0:T(8,128)S(1)}, u32[]{:S(2)}, u32[]{:S(2)}) collective-permute-start(f32[128,128]{1,0:T(8,128)} %get-tuple-element.23), channel_id=1, source_target_pairs={{8,0},{12,4},{0,8},{4,12},{9,1},{13,5},{1,9},{5,13},{10,2},{14,6},... | collective-permute-start | bytes 196616 | tf_op jit(solution)/shard_map/ppermute | solution.py:20
  67.0 1.6 %fusion.10 = f32[1024,128]{1,0:T(8,128)S(1)} fusion(f32[1024,128]{1,0:T(8,128)} %get-tuple-element.25, f32[1024,128]{1,0:T(8,128)S(1)} %copy-done.4, f32[128,128]{1,0:T(8,128)} %get-tuple-element.23, f32[128,128]{1,0:T(8,128)S(1)} %copy-done.8), kind=kOutput, calls=%fused_computation.23 | convolution fusion | flops 201621504 | bytes 1703936 | tf_op jit(solution)/shard_map/dot_general | solution.py:138
  68.6 1.6 %fusion.15 = f32[256,128]{1,0:T(8,128)} fusion(f32[1024,128]{1,0:T(8,128)S(1)} %fusion.10, s32[]{:T(128)S(6)} %select_n.64, f32[1024,128]{1,0:T(8,128)} %fusion.3.q_ref), kind=kLoop, calls=%fused_computation.32 | loop fusion | flops 98304 | bytes 393220 | tf_op jit(solution)/shard_map/sub | solution.py:139
  (67 shorter events, 7.1 us)
Async XLA Ops:
  2.1 11.7 %collective-permute-start.3 = (f32[3,2,8,256]{3,2,0,1:T(8,128)S(1)}, f32[3,2,8,256]{3,2,0,1:T(8,128)S(1)}, u32[]{:S(2)}, u32[]{:S(2)}) collective-permute-start(f32[3,2,8,256]{3,2,0,1:T(8,128)S(1)} %get-tuple-element.50), channel_id=1, source_target_pairs={{0,1},{1,0},{2,3},{3,2},{4,5},{5,4},{6,7},{7,6},{8,9},{9,8},{10,11... | collective-permute-start | bytes 147464 | tf_op jit(solution)/shard_map/ppermute | solution.py:27
  5.2 8.7 %collective-permute-start.4 = (f32[3,2,8,256]{3,2,0,1:T(8,128)S(1)}, f32[3,2,8,256]{3,2,0,1:T(8,128)S(1)}, u32[]{:S(2)}, u32[]{:S(2)}) collective-permute-start(f32[3,2,8,256]{3,2,0,1:T(8,128)S(1)} %get-tuple-element.50), channel_id=1, source_target_pairs={{0,2},{1,3},{2,0},{3,1},{4,6},{5,7},{6,4},{7,5},{8,10},{9,11},{10,... | collective-permute-start | bytes 147464 | tf_op jit(solution)/shard_map/ppermute | solution.py:27
  7.8 6.6 %collective-permute-start.5 = (f32[3,2,8,256]{3,2,0,1:T(8,128)S(1)}, f32[3,2,8,256]{3,2,0,1:T(8,128)S(1)}, u32[]{:S(2)}, u32[]{:S(2)}) collective-permute-start(f32[3,2,8,256]{3,2,0,1:T(8,128)S(1)} %get-tuple-element.50), channel_id=1, source_target_pairs={{0,3},{1,2},{2,1},{3,0},{4,7},{5,6},{6,5},{7,4},{8,11},{9,10},{10,... | collective-permute-start | bytes 147464 | tf_op jit(solution)/shard_map/ppermute | solution.py:27
  7.8 17.7 %collective-permute-start = (f32[256,128]{1,0:T(8,128)}, f32[256,128]{1,0:T(8,128)S(1)}, u32[]{:S(2)}, u32[]{:S(2)}) collective-permute-start(f32[256,128]{1,0:T(8,128)} %param.6), channel_id=1, source_target_pairs={{0,1},{1,0},{2,3},{3,2},{4,5},{5,4},{6,7},{7,6},{8,9},{9,8},{10,11... | collective-permute-start | bytes 393224 | tf_op jit(solution)/shard_map/ppermute | solution.py:27
  8.7 16.8 %collective-permute-start.1 = (f32[256,128]{1,0:T(8,128)}, f32[256,128]{1,0:T(8,128)S(1)}, u32[]{:S(2)}, u32[]{:S(2)}) collective-permute-start(f32[256,128]{1,0:T(8,128)} %param.6), channel_id=1, source_target_pairs={{0,2},{1,3},{2,0},{3,1},{4,6},{5,7},{6,4},{7,5},{8,10},{9,11},{10,... | collective-permute-start | bytes 393224 | tf_op jit(solution)/shard_map/ppermute | solution.py:27
  13.9 11.6 %collective-permute-start.2 = (f32[256,128]{1,0:T(8,128)}, f32[256,128]{1,0:T(8,128)S(1)}, u32[]{:S(2)}, u32[]{:S(2)}) collective-permute-start(f32[256,128]{1,0:T(8,128)} %param.6), channel_id=1, source_target_pairs={{0,3},{1,2},{2,1},{3,0},{4,7},{5,6},{6,5},{7,4},{8,11},{9,10},{10,... | collective-permute-start | bytes 393224 | tf_op jit(solution)/shard_map/ppermute | solution.py:27
  15.2 4.5 %collective-permute-start.7 = (f32[2,4,8,256]{3,2,1,0:T(8,128)S(1)}, f32[2,4,8,256]{3,2,1,0:T(8,128)S(1)}, u32[]{:S(2)}, u32[]{:S(2)}) collective-permute-start(f32[2,4,8,256]{3,2,1,0:T(8,128)S(1)} %pad_maximum_fusion.3), channel_id=1, source_target_pairs={{4,0},{8,4},{12,8},{0,12},{5,1},{9,5},{13,9},{1,13},{6,2},{10,6},{... | collective-permute-start | bytes 196616 | tf_op jit(solution)/shard_map/ppermute | solution.py:20
  15.3 7.3 %collective-permute-start.10 = (f32[2,4,8,256]{3,2,1,0:T(8,128)S(1)}, f32[2,4,8,256]{3,2,1,0:T(8,128)S(1)}, u32[]{:S(2)}, u32[]{:S(2)}) collective-permute-start(f32[2,4,8,256]{3,2,1,0:T(8,128)S(1)} %pad_maximum_fusion.4), channel_id=1, source_target_pairs={{8,0},{12,4},{0,8},{4,12},{9,1},{13,5},{1,9},{5,13},{10,2},{14,6},... | collective-permute-start | bytes 196616 | tf_op jit(solution)/shard_map/ppermute | solution.py:20
  22.6 2.9 %copy-start.5 = (f32[256,128]{1,0:T(8,128)S(1)}, f32[256,128]{1,0:T(8,128)}, u32[]{:S(2)}) copy-start(f32[256,128]{1,0:T(8,128)} %param.6) | copy-start | bytes 393220
  31.8 4.8 %copy-start.7 = (f32[128,128]{1,0:T(8,128)S(1)}, f32[128,128]{1,0:T(8,128)}, u32[]{:S(2)}) copy-start(f32[128,128]{1,0:T(8,128)} %get-tuple-element.14) | copy-start | bytes 196612
  31.8 5.4 %copy-start.1 = (f32[1024,128]{1,0:T(8,128)S(1)}, f32[1024,128]{1,0:T(8,128)}, u32[]{:S(2)}) copy-start(f32[1024,128]{1,0:T(8,128)} %bitcast_select_fusion.q_ref) | copy-start | bytes 1572868
  31.8 5.4 %copy-start.3 = (f32[1024,128]{1,0:T(8,128)S(1)}, f32[1024,128]{1,0:T(8,128)}, u32[]{:S(2)}) copy-start(f32[1024,128]{1,0:T(8,128)} %get-tuple-element.15) | copy-start | bytes 1572868
  36.6 3.1 %collective-permute-start.6 = (f32[128,128]{1,0:T(8,128)S(1)}, f32[128,128]{1,0:T(8,128)S(1)}, u32[]{:S(2)}, u32[]{:S(2)}) collective-permute-start(f32[128,128]{1,0:T(8,128)S(1)} %copy-done.7), channel_id=1, source_target_pairs={{4,0},{8,4},{12,8},{0,12},{5,1},{9,5},{13,9},{1,13},{6,2},{10,6},{... | collective-permute-start | bytes 196616 | tf_op jit(solution)/shard_map/ppermute | solution.py:20
  36.9 9.4 %collective-permute-start.9 = (f32[128,128]{1,0:T(8,128)}, f32[128,128]{1,0:T(8,128)S(1)}, u32[]{:S(2)}, u32[]{:S(2)}) collective-permute-start(f32[128,128]{1,0:T(8,128)} %get-tuple-element.17), channel_id=1, source_target_pairs={{4,0},{8,4},{12,8},{0,12},{5,1},{9,5},{13,9},{1,13},{6,2},{10,6},{... | collective-permute-start | bytes 196616 | tf_op jit(solution)/shard_map/ppermute | solution.py:20
  39.7 0.6 copy-start.12
  45.0 7.0 %copy-start = (f32[1024,128]{1,0:T(8,128)S(1)}, f32[1024,128]{1,0:T(8,128)}, u32[]{:S(2)}) copy-start(f32[1024,128]{1,0:T(8,128)} %fusion.1.q_ref) | copy-start | bytes 1572868
  45.0 7.0 %copy-start.2 = (f32[1024,128]{1,0:T(8,128)S(1)}, f32[1024,128]{1,0:T(8,128)}, u32[]{:S(2)}) copy-start(f32[1024,128]{1,0:T(8,128)} %get-tuple-element.19) | copy-start | bytes 1572868
  45.0 7.0 %copy-start.6 = (f32[128,128]{1,0:T(8,128)S(1)}, f32[128,128]{1,0:T(8,128)}, u32[]{:S(2)}) copy-start(f32[128,128]{1,0:T(8,128)} %get-tuple-element.18) | copy-start | bytes 196612
  45.0 9.4 %collective-permute-start.8 = (f32[128,128]{1,0:T(8,128)}, f32[128,128]{1,0:T(8,128)S(1)}, u32[]{:S(2)}, u32[]{:S(2)}) collective-permute-start(f32[128,128]{1,0:T(8,128)} %get-tuple-element.18), channel_id=1, source_target_pairs={{4,0},{8,4},{12,8},{0,12},{5,1},{9,5},{13,9},{1,13},{6,2},{10,6},{... | collective-permute-start | bytes 196616 | tf_op jit(solution)/shard_map/ppermute | solution.py:20
  51.6 8.9 %collective-permute-start.12 = (f32[128,128]{1,0:T(8,128)}, f32[128,128]{1,0:T(8,128)S(1)}, u32[]{:S(2)}, u32[]{:S(2)}) collective-permute-start(f32[128,128]{1,0:T(8,128)} %get-tuple-element.21), channel_id=1, source_target_pairs={{4,0},{8,4},{12,8},{0,12},{5,1},{9,5},{13,9},{1,13},{6,2},{10,6},{... | collective-permute-start | bytes 196616 | tf_op jit(solution)/shard_map/ppermute | solution.py:20
  59.7 7.3 %copy-start.4 = (f32[1024,128]{1,0:T(8,128)S(1)}, f32[1024,128]{1,0:T(8,128)}, u32[]{:S(2)}) copy-start(f32[1024,128]{1,0:T(8,128)} %get-tuple-element.24) | copy-start | bytes 1572868
  59.7 7.3 %copy-start.8 = (f32[128,128]{1,0:T(8,128)S(1)}, f32[128,128]{1,0:T(8,128)}, u32[]{:S(2)}) copy-start(f32[128,128]{1,0:T(8,128)} %get-tuple-element.22) | copy-start | bytes 196612
  59.7 10.6 %collective-permute-start.11 = (f32[128,128]{1,0:T(8,128)}, f32[128,128]{1,0:T(8,128)S(1)}, u32[]{:S(2)}, u32[]{:S(2)}) collective-permute-start(f32[128,128]{1,0:T(8,128)} %get-tuple-element.22), channel_id=1, source_target_pairs={{8,0},{12,4},{0,8},{4,12},{9,1},{13,5},{1,9},{5,13},{10,2},{14,6},... | collective-permute-start | bytes 196616 | tf_op jit(solution)/shard_map/ppermute | solution.py:20
  65.7 4.5 %collective-permute-start.13 = (f32[128,128]{1,0:T(8,128)}, f32[128,128]{1,0:T(8,128)S(1)}, u32[]{:S(2)}, u32[]{:S(2)}) collective-permute-start(f32[128,128]{1,0:T(8,128)} %get-tuple-element.23), channel_id=1, source_target_pairs={{8,0},{12,4},{0,8},{4,12},{9,1},{13,5},{1,9},{5,13},{10,2},{14,6},... | collective-permute-start | bytes 196616 | tf_op jit(solution)/shard_map/ppermute | solution.py:20
  (3 other events, 1.9 us)

commit v9 on v6

--- a/solution.py
+++ b/solution.py
@@ -80,6 +80,8 @@
                     residual_t, block, (((0,), (0,)), ((), ())), precision=MATMUL_PRECISION
                 )
                 chunk = chunk - LR_USER * (gradient + LAMBDA_REG * chunk)
+            if k == 0 and stratum + 1 < strata:
+                slot_data[stratum + 1], chunk = lax.optimization_barrier((slot_data[stratum + 1], chunk))
             finished.append(chunk)
             residuals.append(residual_tile(chunk, block, weight_k, target_k))
         chunks = finished

time: 52.5 us -> 54.1 us (1.030)
  waiting for transfers between devices: 3.53 us -> 10.1 us
  other arithmetic: 10.6 us -> 8.11 us
  local copies, waits for them, and re-layouts: 2.65 us -> 1.37 us
  matrix products: 17.8 us -> 16.7 us
    ppermute x6, waiting for transfers between devices: 2.01 us -> 7.66 us  [gather_over(): lax.ppermute(block, axis, [(i, i ^ k) for i in range(count)])]
    reduce_sum x3, other arithmetic: 7.36 us -> 4.85 us  [build_tiles(): jnp.sum(jnp.where(matches, jnp.abs(signed_rows)[:, :, None, :], 0.0), axi...]
    unnamed x13 -> x5, local copies, waits for them, and re-layouts: 1.4 us -> 0.11 us
    dot_general x18, matrix products: 8.78 us -> 7.61 us  [residual_tile(): scores_t = jnp.dot(item_rows, user_rows.T, precision=MATMUL_PRECISION)]
    ppermute x8, waiting for transfers between devices: 1.52 us -> 2.48 us  [shifted(): return lax.ppermute(block, axis, route)]
  transfers between devices with their start and end apart: 14 -> 14, of which waited for: 2 -> 4; matrix products, arithmetic and copies ran while one was open for 43% -> 44% of each run, Pallas kernels for 0% -> 0%
where the time goes in v9:
time: 54.1 us; the launch traced here: 53.8 us
  matrix products  16.7 us (31%)
  starting transfers between devices  16.5 us (30%)
  waiting for transfers between devices  10.1 us (19%)
  other arithmetic  8.11 us (15%)
  local copies, waits for them, and re-layouts  1.37 us (3%)
  between operations  1.01 us (2%)
    ppermute x6, starting transfers between devices, gather_over(): lax.ppermute(block, axis, [(i, i ^ k) for i in range(count)])  10.1 us
    ppermute x6, waiting for transfers between devices, gather_over(): lax.ppermute(block, axis, [(i, i ^ k) for i in range(count)])  7.66 us
    dot_general x18, matrix products, residual_tile(): scores_t = jnp.dot(item_rows, user_rows.T, precision=MATMUL_PRECISION)  7.61 us
    dot_general x12, matrix products, per_device(): lax.dot_general(residual_t, block, (((0,), (0,)), ((), ())), precision=MA...  7.3 us
    ppermute x8, starting transfers between devices, shifted(): return lax.ppermute(block, axis, route)  6.39 us
    reduce_sum x3, other arithmetic, build_tiles(): jnp.sum(jnp.where(matches, jnp.abs(signed_rows)[:, :, None, :], 0.0), axi...  4.85 us
    ppermute x8, waiting for transfers between devices, shifted(): return lax.ppermute(block, axis, route)  2.48 us
    dot_general x3, matrix products, per_device(): jnp.dot(residual_t, jnp.concatenate(chunks, 0), precision=MATMUL_PRECISION)  1.75 us
  transfers between devices with their start and end apart: 14, of which 4 were waited for; matrix products, arithmetic and copies ran while one was open for 44% of the time, Pallas kernels for 0%

profile of v9, /device:TPU:0, one launch (start us, length us, event | category | flops | bytes accessed | tf_op | source)
XLA Modules:
  0.0 53.8 jit_solution(645877131037244455)
XLA Ops:
  0.6 0.7 %convert_bitcast_fusion = f32[3,1,8,256]{3,2,0,1:T(8,128)S(1)} fusion(s32[3,256,8]{1,2,0:T(8,128)} %param.7), kind=kLoop, calls=%fused_computation.210 | loop fusion | flops 6144 | bytes 49152 | tf_op jit(solution)/shard_map/stack | solution.py:49
  1.4 0.8 %fusion.141 = f32[3,1,8,256]{3,2,0,1:T(8,128)S(1)} fusion(f32[3,256,8]{1,2,0:T(8,128)} %param.9, s32[3,256,8]{1,2,0:T(8,128)} %param.8), kind=kLoop, calls=%fused_computation.209 | loop fusion | flops 18432 | bytes 73728 | tf_op jit(solution)/shard_map/stack | solution.py:49
  2.1 4.1 %collective-permute-start.1 = (f32[3,2,8,256]{3,2,0,1:T(8,128)S(1)}, f32[3,2,8,256]{3,2,0,1:T(8,128)S(1)}, u32[]{:S(2)}, u32[]{:S(2)}) collective-permute-start(f32[3,2,8,256]{3,2,0,1:T(8,128)S(1)} %get-tuple-element.32), channel_id=1, source_target_pairs={{0,2},{1,3},{2,0},{3,1},{4,6},{5,7},{6,4},{7,5},{8,10},{9,11},{10,... | collective-permute-start | bytes 147464 | tf_op jit(solution)/shard_map/ppermute | solution.py:25
  6.2 1.6 %collective-permute-start = (f32[3,2,8,256]{3,2,0,1:T(8,128)S(1)}, f32[3,2,8,256]{3,2,0,1:T(8,128)S(1)}, u32[]{:S(2)}, u32[]{:S(2)}) collective-permute-start(f32[3,2,8,256]{3,2,0,1:T(8,128)S(1)} %get-tuple-element.32), channel_id=1, source_target_pairs={{0,1},{1,0},{2,3},{3,2},{4,5},{5,4},{6,7},{7,6},{8,9},{9,8},{10,11... | collective-permute-start | bytes 147464 | tf_op jit(solution)/shard_map/ppermute | solution.py:25
  7.8 0.9 %collective-permute-start.5 = (f32[256,128]{1,0:T(8,128)}, f32[256,128]{1,0:T(8,128)S(1)}, u32[]{:S(2)}, u32[]{:S(2)}) collective-permute-start(f32[256,128]{1,0:T(8,128)} %param.6), channel_id=1, source_target_pairs={{0,1},{1,0},{2,3},{3,2},{4,5},{5,4},{6,7},{7,6},{8,9},{9,8},{10,11... | collective-permute-start | bytes 393224 | tf_op jit(solution)/shard_map/ppermute | solution.py:25
  8.7 2.9 %collective-permute-start.7 = (f32[256,128]{1,0:T(8,128)}, f32[256,128]{1,0:T(8,128)S(1)}, u32[]{:S(2)}, u32[]{:S(2)}) collective-permute-start(f32[256,128]{1,0:T(8,128)} %param.6), channel_id=1, source_target_pairs={{0,3},{1,2},{2,1},{3,0},{4,7},{5,6},{6,5},{7,4},{8,11},{9,10},{10,... | collective-permute-start | bytes 393224 | tf_op jit(solution)/shard_map/ppermute | solution.py:25
  11.8 0.6 %collective-permute-start.6 = (f32[256,128]{1,0:T(8,128)}, f32[256,128]{1,0:T(8,128)S(1)}, u32[]{:S(2)}, u32[]{:S(2)}) collective-permute-start(f32[256,128]{1,0:T(8,128)} %param.6), channel_id=1, source_target_pairs={{0,2},{1,3},{2,0},{3,1},{4,6},{5,7},{6,4},{7,5},{8,10},{9,11},{10,... | collective-permute-start | bytes 393224 | tf_op jit(solution)/shard_map/ppermute | solution.py:25
  12.4 2.1 %collective-permute-done.2 = f32[3,2,8,256]{3,2,0,1:T(8,128)S(1)} collective-permute-done((f32[3,2,8,256]{3,2,0,1:T(8,128)S(1)}, f32[3,2,8,256]{3,2,0,1:T(8,128)S(1)}, u32[]{:S(2)}, u32[]{:S(2)}) %collective-permute-start.2) | collective-permute-done | bytes 49184 | tf_op jit(solution)/shard_map/ppermute | solution.py:25
  15.3 1.6 %collective-permute-start.3 = (f32[2,4,8,256]{3,2,1,0:T(8,128)S(1)}, f32[2,4,8,256]{3,2,1,0:T(8,128)S(1)}, u32[]{:S(2)}, u32[]{:S(2)}) collective-permute-start(f32[2,4,8,256]{3,2,1,0:T(8,128)S(1)} %pad_maximum_fusion.3), channel_id=1, source_target_pairs={{8,0},{12,4},{0,8},{4,12},{9,1},{13,5},{1,9},{5,13},{10,2},{14,6},... | collective-permute-start | bytes 196616 | tf_op jit(solution)/shard_map/ppermute | solution.py:18
  16.9 1.6 %select_reduce_fusion.5 = (f32[4,256,256]{2,1,0:T(8,128)S(1)}, f32[4,256,256]{2,1,0:T(8,128)S(1)}) fusion(f32[4,8,256]{2,1,0:T(8,128)S(1)} %get-tuple-element.23, f32[4,8,256]{2,1,0:T(8,128)S(1)} %get-tuple-element.19, f32[4,8,256]{2,1,0:T(8,128)S(1)} %get-tuple-element.22), kind=kLoop, calls=%fused_computation.9 | loop fusion | flops 9961472 | bytes 2195456 | tf_op jit(solution)/shard_map/reduce_sum | solution.py:40
  18.5 1.1 %collective-permute-done.7 = f32[256,128]{1,0:T(8,128)S(1)} collective-permute-done((f32[256,128]{1,0:T(8,128)}, f32[256,128]{1,0:T(8,128)S(1)}, u32[]{:S(2)}, u32[]{:S(2)}) %collective-permute-start.7) | collective-permute-done | bytes 131104 | tf_op jit(solution)/shard_map/ppermute | solution.py:25
  19.6 4.5 %collective-permute-done.6 = f32[256,128]{1,0:T(8,128)S(1)} collective-permute-done((f32[256,128]{1,0:T(8,128)}, f32[256,128]{1,0:T(8,128)S(1)}, u32[]{:S(2)}, u32[]{:S(2)}) %collective-permute-start.6) | collective-permute-done | bytes 131104 | tf_op jit(solution)/shard_map/ppermute | solution.py:25
  30.1 1.6 %collective-permute-start.8 = (f32[128,128]{1,0:T(8,128)S(1)}, f32[128,128]{1,0:T(8,128)S(1)}, u32[]{:S(2)}, u32[]{:S(2)}) collective-permute-start(f32[128,128]{1,0:T(8,128)S(1)} %fusion.115), channel_id=1, source_target_pairs={{4,0},{8,4},{12,8},{0,12},{5,1},{9,5},{13,9},{1,13},{6,2},{10,6},{... | collective-permute-start | bytes 196616 | tf_op jit(solution)/shard_map/ppermute | solution.py:18
  31.8 1.6 %select_reduce_fusion.3 = (f32[4,256,256]{2,1,0:T(8,128)S(1)}, f32[4,256,256]{2,1,0:T(8,128)S(1)}) fusion(f32[4,8,256]{2,1,0:T(8,128)S(1)} %get-tuple-element.29, f32[4,8,256]{2,1,0:T(8,128)S(1)} %get-tuple-element.30, f32[4,8,256]{2,1,0:T(8,128)S(1)} %get-tuple-element.28), kind=kLoop, calls=%fused_computation.6 | loop fusion | flops 9961472 | bytes 2195456 | tf_op jit(solution)/shard_map/reduce_sum | solution.py:40
  39.3 0.7 %collective-permute-start.9 = (f32[128,128]{1,0:T(8,128)S(1)}, f32[128,128]{1,0:T(8,128)S(1)}, u32[]{:S(2)}, u32[]{:S(2)}) collective-permute-start(f32[128,128]{1,0:T(8,128)S(1)} %fusion.107), channel_id=1, source_target_pairs={{4,0},{8,4},{12,8},{0,12},{5,1},{9,5},{13,9},{1,13},{6,2},{10,6},{... | collective-permute-start | bytes 196616 | tf_op jit(solution)/shard_map/ppermute | solution.py:18
  40.0 1.6 %select_reduce_fusion.1 = (f32[4,256,256]{2,1,0:T(8,128)S(1)}, f32[4,256,256]{2,1,0:T(8,128)S(1)}) fusion(f32[4,8,256]{2,1,0:T(8,128)S(1)} %get-tuple-element.26, f32[4,8,256]{2,1,0:T(8,128)S(1)} %get-tuple-element.27, f32[4,8,256]{2,1,0:T(8,128)S(1)} %get-tuple-element.25), kind=kLoop, calls=%fused_computation.3 | loop fusion | flops 9961472 | bytes 2195456 | tf_op jit(solution)/shard_map/reduce_sum | solution.py:40
  42.6 0.6 %fusion.97 = f32[128,128]{1,0:T(8,128)S(1)} fusion(f32[128,128]{1,0:T(8,128)S(1)} %collective-permute-done.12, f32[1024,128]{1,0:T(8,128)S(1)} %fusion.81, f32[1024,128]{1,0:T(8,128)S(1)} %fusion.3), kind=kOutput, calls=%fused_computation.130 | convolution fusion | flops 100712448 | bytes 1179648 | tf_op jit(solution)/shard_map/dot_general | solution.py:79
  43.7 0.6 %fusion.95 = f32[128,128]{1,0:T(8,128)S(1)} fusion(f32[128,128]{1,0:T(8,128)S(1)} %fusion.97, f32[1024,128]{1,0:T(8,128)S(1)} %fusion.85, f32[1024,128]{1,0:T(8,128)S(1)} %fusion.3), kind=kOutput, calls=%fused_computation.127 | convolution fusion | flops 100712448 | bytes 1179648 | tf_op jit(solution)/shard_map/dot_general | solution.py:79
  44.3 1.6 %collective-permute-start.13 = (f32[128,128]{1,0:T(8,128)S(1)}, f32[128,128]{1,0:T(8,128)S(1)}, u32[]{:S(2)}, u32[]{:S(2)}) collective-permute-start(f32[128,128]{1,0:T(8,128)S(1)} %fusion.95), channel_id=1, source_target_pairs={{8,0},{12,4},{0,8},{4,12},{9,1},{13,5},{1,9},{5,13},{10,2},{14,6},... | collective-permute-start | bytes 196616 | tf_op jit(solution)/shard_map/ppermute | solution.py:18
  46.7 0.6 %fusion.101 = f32[128,128]{1,0:T(8,128)S(1)} fusion(f32[128,128]{1,0:T(8,128)S(1)} %collective-permute-done.9, f32[1024,128]{1,0:T(8,128)S(1)} %fusion.73, f32[1024,128]{1,0:T(8,128)S(1)} %fusion.3), kind=kOutput, calls=%fused_computation.136 | convolution fusion | flops 100712448 | bytes 1179648 | tf_op jit(solution)/shard_map/dot_general | solution.py:79
  47.8 0.6 %fusion.99 = f32[128,128]{1,0:T(8,128)S(1)} fusion(f32[128,128]{1,0:T(8,128)S(1)} %fusion.101, f32[1024,128]{1,0:T(8,128)S(1)} %fusion.77, f32[1024,128]{1,0:T(8,128)S(1)} %fusion.3), kind=kOutput, calls=%fused_computation.133 | convolution fusion | flops 100712448 | bytes 1179648 | tf_op jit(solution)/shard_map/dot_general | solution.py:79
  50.0 0.7 %fusion.129 = f32[256,128]{1,0:T(8,128)} fusion(f32[1024,128]{1,0:T(8,128)S(1)} %fusion.124, s32[]{:T(128)S(6)} %select_n.64, f32[1024,128]{1,0:T(8,128)S(1)} %fusion.3), kind=kLoop, calls=%fused_computation.176 | loop fusion | flops 98304 | bytes 393220 | tf_op jit(solution)/shard_map/sub | solution.py:90
  50.7 2.5 %collective-permute-done.11 = f32[128,128]{1,0:T(8,128)S(1)} collective-permute-done((f32[128,128]{1,0:T(8,128)S(1)}, f32[128,128]{1,0:T(8,128)S(1)}, u32[]{:S(2)}, u32[]{:S(2)}) %collective-permute-start.11) | collective-permute-done | bytes 65568 | tf_op jit(solution)/shard_map/ppermute | solution.py:18
  53.1 0.7 %pad_maximum_fusion.2 = f32[256,128]{1,0:T(8,128)} fusion(f32[128,128]{1,0:T(8,128)S(1)} %collective-permute-done.13, f32[128,128]{1,0:T(8,128)S(1)} %collective-permute-done.11), kind=kLoop, calls=%fused_computation.183 | loop fusion | flops 32768 | bytes 262144 | tf_op jit(solution)/shard_map/concatenate | solution.py:91
  (68 shorter events, 17.0 us)
Async XLA Ops:
  2.1 9.6 %collective-permute-start.1 = (f32[3,2,8,256]{3,2,0,1:T(8,128)S(1)}, f32[3,2,8,256]{3,2,0,1:T(8,128)S(1)}, u32[]{:S(2)}, u32[]{:S(2)}) collective-permute-start(f32[3,2,8,256]{3,2,0,1:T(8,128)S(1)} %get-tuple-element.32), channel_id=1, source_target_pairs={{0,2},{1,3},{2,0},{3,1},{4,6},{5,7},{6,4},{7,5},{8,10},{9,11},{10,... | collective-permute-start | bytes 147464 | tf_op jit(solution)/shard_map/ppermute | solution.py:25
  6.2 6.1 %collective-permute-start = (f32[3,2,8,256]{3,2,0,1:T(8,128)S(1)}, f32[3,2,8,256]{3,2,0,1:T(8,128)S(1)}, u32[]{:S(2)}, u32[]{:S(2)}) collective-permute-start(f32[3,2,8,256]{3,2,0,1:T(8,128)S(1)} %get-tuple-element.32), channel_id=1, source_target_pairs={{0,1},{1,0},{2,3},{3,2},{4,5},{5,4},{6,7},{7,6},{8,9},{9,8},{10,11... | collective-permute-start | bytes 147464 | tf_op jit(solution)/shard_map/ppermute | solution.py:25
  7.8 6.6 %collective-permute-start.2 = (f32[3,2,8,256]{3,2,0,1:T(8,128)S(1)}, f32[3,2,8,256]{3,2,0,1:T(8,128)S(1)}, u32[]{:S(2)}, u32[]{:S(2)}) collective-permute-start(f32[3,2,8,256]{3,2,0,1:T(8,128)S(1)} %get-tuple-element.32), channel_id=1, source_target_pairs={{0,3},{1,2},{2,1},{3,0},{4,7},{5,6},{6,5},{7,4},{8,11},{9,10},{10,... | collective-permute-start | bytes 147464 | tf_op jit(solution)/shard_map/ppermute | solution.py:25
  7.8 10.7 %collective-permute-start.5 = (f32[256,128]{1,0:T(8,128)}, f32[256,128]{1,0:T(8,128)S(1)}, u32[]{:S(2)}, u32[]{:S(2)}) collective-permute-start(f32[256,128]{1,0:T(8,128)} %param.6), channel_id=1, source_target_pairs={{0,1},{1,0},{2,3},{3,2},{4,5},{5,4},{6,7},{7,6},{8,9},{9,8},{10,11... | collective-permute-start | bytes 393224 | tf_op jit(solution)/shard_map/ppermute | solution.py:25
  8.7 10.8 %collective-permute-start.7 = (f32[256,128]{1,0:T(8,128)}, f32[256,128]{1,0:T(8,128)S(1)}, u32[]{:S(2)}, u32[]{:S(2)}) collective-permute-start(f32[256,128]{1,0:T(8,128)} %param.6), channel_id=1, source_target_pairs={{0,3},{1,2},{2,1},{3,0},{4,7},{5,6},{6,5},{7,4},{8,11},{9,10},{10,... | collective-permute-start | bytes 393224 | tf_op jit(solution)/shard_map/ppermute | solution.py:25
  11.8 12.3 %collective-permute-start.6 = (f32[256,128]{1,0:T(8,128)}, f32[256,128]{1,0:T(8,128)S(1)}, u32[]{:S(2)}, u32[]{:S(2)}) collective-permute-start(f32[256,128]{1,0:T(8,128)} %param.6), channel_id=1, source_target_pairs={{0,2},{1,3},{2,0},{3,1},{4,6},{5,7},{6,4},{7,5},{8,10},{9,11},{10,... | collective-permute-start | bytes 393224 | tf_op jit(solution)/shard_map/ppermute | solution.py:25
  15.2 14.5 %collective-permute-start.4 = (f32[2,4,8,256]{3,2,1,0:T(8,128)S(1)}, f32[2,4,8,256]{3,2,1,0:T(8,128)S(1)}, u32[]{:S(2)}, u32[]{:S(2)}) collective-permute-start(f32[2,4,8,256]{3,2,1,0:T(8,128)S(1)} %pad_maximum_fusion.4), channel_id=1, source_target_pairs={{4,0},{8,4},{12,8},{0,12},{5,1},{9,5},{13,9},{1,13},{6,2},{10,6},{... | collective-permute-start | bytes 196616 | tf_op jit(solution)/shard_map/ppermute | solution.py:18
  15.3 23.6 %collective-permute-start.3 = (f32[2,4,8,256]{3,2,1,0:T(8,128)S(1)}, f32[2,4,8,256]{3,2,1,0:T(8,128)S(1)}, u32[]{:S(2)}, u32[]{:S(2)}) collective-permute-start(f32[2,4,8,256]{3,2,1,0:T(8,128)S(1)} %pad_maximum_fusion.3), channel_id=1, source_target_pairs={{8,0},{12,4},{0,8},{4,12},{9,1},{13,5},{1,9},{5,13},{10,2},{14,6},... | collective-permute-start | bytes 196616 | tf_op jit(solution)/shard_map/ppermute | solution.py:18
  16.9 7.2 %copy-start.1 = (f32[256,128]{1,0:T(8,128)S(1)}, f32[256,128]{1,0:T(8,128)}, u32[]{:S(2)}) copy-start(f32[256,128]{1,0:T(8,128)} %param.6) | copy-start | bytes 393220
  24.1 0.9 %copy-start = (f32[256,128]{1,0:T(8,128)S(1)}, f32[256,128]{1,0:T(8,128)}, u32[]{:S(2)}) copy-start(f32[256,128]{1,0:T(8,128)} %param.5) | copy-start | bytes 393220
  27.1 6.9 %collective-permute-start.10 = (f32[128,128]{1,0:T(8,128)S(1)}, f32[128,128]{1,0:T(8,128)S(1)}, u32[]{:S(2)}, u32[]{:S(2)}) collective-permute-start(f32[128,128]{1,0:T(8,128)S(1)} %fusion.111), channel_id=1, source_target_pairs={{4,0},{8,4},{12,8},{0,12},{5,1},{9,5},{13,9},{1,13},{6,2},{10,6},{... | collective-permute-start | bytes 196616 | tf_op jit(solution)/shard_map/ppermute | solution.py:18
  30.1 6.6 %collective-permute-start.8 = (f32[128,128]{1,0:T(8,128)S(1)}, f32[128,128]{1,0:T(8,128)S(1)}, u32[]{:S(2)}, u32[]{:S(2)}) collective-permute-start(f32[128,128]{1,0:T(8,128)S(1)} %fusion.115), channel_id=1, source_target_pairs={{4,0},{8,4},{12,8},{0,12},{5,1},{9,5},{13,9},{1,13},{6,2},{10,6},{... | collective-permute-start | bytes 196616 | tf_op jit(solution)/shard_map/ppermute | solution.py:18
  36.1 6.1 %collective-permute-start.12 = (f32[128,128]{1,0:T(8,128)S(1)}, f32[128,128]{1,0:T(8,128)S(1)}, u32[]{:S(2)}, u32[]{:S(2)}) collective-permute-start(f32[128,128]{1,0:T(8,128)S(1)} %fusion.103), channel_id=1, source_target_pairs={{4,0},{8,4},{12,8},{0,12},{5,1},{9,5},{13,9},{1,13},{6,2},{10,6},{... | collective-permute-start | bytes 196616 | tf_op jit(solution)/shard_map/ppermute | solution.py:18
  39.3 7.0 %collective-permute-start.9 = (f32[128,128]{1,0:T(8,128)S(1)}, f32[128,128]{1,0:T(8,128)S(1)}, u32[]{:S(2)}, u32[]{:S(2)}) collective-permute-start(f32[128,128]{1,0:T(8,128)S(1)} %fusion.107), channel_id=1, source_target_pairs={{4,0},{8,4},{12,8},{0,12},{5,1},{9,5},{13,9},{1,13},{6,2},{10,6},{... | collective-permute-start | bytes 196616 | tf_op jit(solution)/shard_map/ppermute | solution.py:18
  44.3 6.4 %collective-permute-start.13 = (f32[128,128]{1,0:T(8,128)S(1)}, f32[128,128]{1,0:T(8,128)S(1)}, u32[]{:S(2)}, u32[]{:S(2)}) collective-permute-start(f32[128,128]{1,0:T(8,128)S(1)} %fusion.95), channel_id=1, source_target_pairs={{8,0},{12,4},{0,8},{4,12},{9,1},{13,5},{1,9},{5,13},{10,2},{14,6},... | collective-permute-start | bytes 196616 | tf_op jit(solution)/shard_map/ppermute | solution.py:18
  48.8 4.3 %collective-permute-start.11 = (f32[128,128]{1,0:T(8,128)S(1)}, f32[128,128]{1,0:T(8,128)S(1)}, u32[]{:S(2)}, u32[]{:S(2)}) collective-permute-start(f32[128,128]{1,0:T(8,128)S(1)} %fusion.99), channel_id=1, source_target_pairs={{8,0},{12,4},{0,8},{4,12},{9,1},{13,5},{1,9},{5,13},{10,2},{14,6},... | collective-permute-start | bytes 196616 | tf_op jit(solution)/shard_map/ppermute | solution.py:18

commit v10 on v9

--- a/solution.py
+++ b/solution.py
@@ -49,9 +49,12 @@
     slots_local = jnp.stack(
         [jnp.transpose(item_index.astype(jnp.float32), (0, 2, 1)), jnp.transpose(signed, (0, 2, 1))], 1
     )
-    slots_all = gather_over(slots_local, "it")
-    slabs = slots_all.shape[0]
-    block = gather_over(item_factors, "it").reshape(slabs * slab_rows, width)
+    packed = jnp.concatenate([item_factors.reshape(-1), slots_local.reshape(-1)])
+    gathered = gather_over(packed, "it")
+    slabs = gathered.shape[0]
+    cut = slab_rows * width
+    block = gathered[:, :cut].reshape(slabs * slab_rows, width)
+    slots_all = gathered[:, cut:].reshape((slabs,) + slots_local.shape)
     index_all = slots_all[:, :, 0]
     signed_all = slots_all[:, :, 1]
 

time: 54.1 us -> 59.1 us (1.092)
  waiting for transfers between devices: 10.1 us -> 16.9 us
  starting transfers between devices: 16.5 us -> 13.2 us
  other arithmetic: 8.11 us -> 9.59 us
    ppermute x6 -> x3, waiting for transfers between devices: 7.66 us -> 14.6 us  [gather_over(): lax.ppermute(block, axis, [(i, i ^ k) for i in range(count)])]
    ppermute x6 -> x3, starting transfers between devices: 10.1 us -> 5.76 us  [gather_over(): lax.ppermute(block, axis, [(i, i ^ k) for i in range(count)])]
    ppermute x8, starting transfers between devices: 6.39 us -> 7.47 us  [shifted(): return lax.ppermute(block, axis, route)]
    concatenate x0 -> x1, other arithmetic: none -> 0.92 us  [per_device(): jnp.concatenate([item_factors.reshape(-1), slots_local.reshape(-1)])]
    another operation x3 -> x1, other arithmetic: 0.06 us -> 0.68 us  [gather_over(): return jnp.take(jnp.stack(received), order, axis=0)]
    another operation x2 -> x3, other arithmetic: 1.5 us -> 1.51 us  [per_device(): jnp.stack([jnp.transpose(item_index.astype(jnp.float32), (0, 2, 1)), jnp....]
  transfers between devices with their start and end apart: 14 -> 11, of which waited for: 4 -> 3; matrix products, arithmetic and copies ran while one was open for 44% -> 32% of each run, Pallas kernels for 0% -> 0%
where the time goes in v10:
time: 59.1 us; the launch traced here: 58.8 us
  waiting for transfers between devices  16.9 us (29%)
  matrix products  16.6 us (28%)
  starting transfers between devices  13.2 us (22%)
  other arithmetic  9.59 us (16%)
  local copies, waits for them, and re-layouts  1.44 us (2%)
  between operations  1.02 us (2%)
    ppermute x3, waiting for transfers between devices, gather_over(): lax.ppermute(block, axis, [(i, i ^ k) for i in range(count)])  14.6 us
    dot_general x18, matrix products, residual_tile(): scores_t = jnp.dot(item_rows, user_rows.T, precision=MATMUL_PRECISION)  7.57 us
    ppermute x8, starting transfers between devices, shifted(): return lax.ppermute(block, axis, route)  7.47 us
    dot_general x12, matrix products, per_device(): lax.dot_general(residual_t, block, (((0,), (0,)), ((), ())), precision=MA...  7.33 us
    ppermute x3, starting transfers between devices, gather_over(): lax.ppermute(block, axis, [(i, i ^ k) for i in range(count)])  5.76 us
    reduce_sum x3, other arithmetic, build_tiles(): jnp.sum(jnp.where(matches, jnp.abs(signed_rows)[:, :, None, :], 0.0), axi...  4.85 us
    ppermute x8, waiting for transfers between devices, shifted(): return lax.ppermute(block, axis, route)  2.31 us
    dot_general x3, matrix products, per_device(): jnp.dot(residual_t, jnp.concatenate(chunks, 0), precision=MATMUL_PRECISION)  1.75 us
  transfers between devices with their start and end apart: 11, of which 3 were waited for; matrix products, arithmetic and copies ran while one was open for 32% of the time, Pallas kernels for 0%

profile of v10, /device:TPU:0, one launch (start us, length us, event | category | flops | bytes accessed | tf_op | source)
XLA Modules:
  0.0 58.8 jit_solution(6986437637381785749)
XLA Ops:
  0.6 0.7 %convert_bitcast_fusion = f32[3,1,8,256]{3,2,0,1:T(8,128)S(1)} fusion(s32[3,256,8]{1,2,0:T(8,128)} %param.7), kind=kLoop, calls=%fused_computation.208 | loop fusion | flops 6144 | bytes 49152 | tf_op jit(solution)/shard_map/stack | solution.py:49
  1.4 0.8 %fusion.141 = f32[3,1,8,256]{3,2,0,1:T(8,128)S(1)} fusion(f32[3,256,8]{1,2,0:T(8,128)} %param.9, s32[3,256,8]{1,2,0:T(8,128)} %param.8), kind=kLoop, calls=%fused_computation.207 | loop fusion | flops 18432 | bytes 73728 | tf_op jit(solution)/shard_map/stack | solution.py:49
  2.2 0.9 %pad_maximum_fusion.1 = f32[45056]{0:T(1024)S(1)} fusion(f32[12288]{0:T(1024)S(1)} %bitcast.158, f32[32768]{0:T(1024)} %bitcast.162), kind=kLoop, calls=%fused_computation.172 | loop fusion | flops 45056 | bytes 360448 | tf_op jit(solution)/shard_map/concatenate | solution.py:52
  3.1 5.1 %collective-permute-start.2 = (f32[45056]{0:T(1024)S(1)}, f32[45056]{0:T(1024)S(1)}, u32[]{:S(2)}, u32[]{:S(2)}) collective-permute-start(f32[45056]{0:T(1024)S(1)} %pad_maximum_fusion.1), channel_id=1, source_target_pairs={{0,3},{1,2},{2,1},{3,0},{4,7},{5,6},{6,5},{7,4},{8,11},{9,10},{10,... | collective-permute-start | bytes 540680 | tf_op jit(solution)/shard_map/ppermute | solution.py:25
  8.2 0.6 %collective-permute-start = (f32[45056]{0:T(1024)S(1)}, f32[45056]{0:T(1024)S(1)}, u32[]{:S(2)}, u32[]{:S(2)}) collective-permute-start(f32[45056]{0:T(1024)S(1)} %pad_maximum_fusion.1), channel_id=1, source_target_pairs={{0,1},{1,0},{2,3},{3,2},{4,5},{5,4},{6,7},{7,6},{8,9},{9,8},{10,11... | collective-permute-start | bytes 540680 | tf_op jit(solution)/shard_map/ppermute | solution.py:25
  8.9 4.8 %collective-permute-done.2 = f32[45056]{0:T(1024)S(1)} collective-permute-done((f32[45056]{0:T(1024)S(1)}, f32[45056]{0:T(1024)S(1)}, u32[]{:S(2)}, u32[]{:S(2)}) %collective-permute-start.2) | collective-permute-done | bytes 180256 | tf_op jit(solution)/shard_map/ppermute | solution.py:25
  13.7 9.8 %collective-permute-done.1 = f32[45056]{0:T(1024)S(1)} collective-permute-done((f32[45056]{0:T(1024)S(1)}, f32[45056]{0:T(1024)S(1)}, u32[]{:S(2)}, u32[]{:S(2)}) %collective-permute-start.1) | collective-permute-done | bytes 180256 | tf_op jit(solution)/shard_map/ppermute | solution.py:25
  23.5 0.7 %pad_maximum_fusion = f32[4,45056]{1,0:T(4,128)S(1)} fusion(f32[1,45056]{1,0:T(1,128)S(1)} %bitcast.159, f32[1,45056]{1,0:T(1,128)S(1)} %bitcast.160, f32[1,45056]{1,0:T(1,128)S(1)} %bitcast.161, f32[1,45056]{1,0:T(1,128)S(1)} %bitcast.155), kind=kLoop, calls=%fused_computation.170 | loop fusion | flops 540672 | bytes 1441792 | tf_op jit(solution)/shard_map/stack | solution.py:28
  24.2 0.9 %gather_fusion = f32[4,45056]{1,0:T(4,128)S(1)} fusion(f32[4,45056]{1,0:T(4,128)S(1)} %pad_maximum_fusion, s32[1024]{0:T(1024)S(1)} %pad_clamp_fusion), kind=kCustom, calls=%fused_computation | custom fusion | bytes 1441808 | tf_op jit(solution)/shard_map/jit(_take)/gather | solution.py:28
  25.9 1.6 %select_reduce_fusion.5 = (f32[4,256,256]{2,1,0:T(8,128)S(1)}, f32[4,256,256]{2,1,0:T(8,128)S(1)}) fusion(f32[4,8,256]{2,1,0:T(8,128)S(1)} %get-tuple-element.23, f32[4,8,256]{2,1,0:T(8,128)S(1)} %get-tuple-element.19, f32[4,8,256]{2,1,0:T(8,128)S(1)} %get-tuple-element.22), kind=kLoop, calls=%fused_computation.8 | loop fusion | flops 9961472 | bytes 2195456 | tf_op jit(solution)/shard_map/reduce_sum | solution.py:40
  28.0 0.6 %fusion.113 = f32[128,128]{1,0:T(8,128)S(1)} fusion(f32[1024,128]{1,0:T(8,128)S(1)} %fusion.37, f32[1024,128]{1,0:T(8,128)S(1)} %reshape.101, f32[256,128]{1,0:T(8,128)S(1)} %copy-done), kind=kOutput, calls=%fused_computation.153 | convolution fusion | flops 100712448 | bytes 1179648 | tf_op jit(solution)/shard_map/dot_general | solution.py:82
  29.0 0.6 %fusion.111 = f32[128,128]{1,0:T(8,128)S(1)} fusion(f32[128,128]{1,0:T(8,128)S(1)} %fusion.113, f32[1024,128]{1,0:T(8,128)S(1)} %fusion.41, f32[1024,128]{1,0:T(8,128)S(1)} %reshape.101), kind=kOutput, calls=%fused_computation.150 | convolution fusion | flops 100712448 | bytes 1179648 | tf_op jit(solution)/shard_map/dot_general | solution.py:82
  30.8 1.4 %collective-permute-start.4 = (f32[2,4,8,256]{3,2,1,0:T(8,128)S(1)}, f32[2,4,8,256]{3,2,1,0:T(8,128)S(1)}, u32[]{:S(2)}, u32[]{:S(2)}) collective-permute-start(f32[2,4,8,256]{3,2,1,0:T(8,128)S(1)} %pad_maximum_fusion.4), channel_id=1, source_target_pairs={{4,0},{8,4},{12,8},{0,12},{5,1},{9,5},{13,9},{1,13},{6,2},{10,6},{... | collective-permute-start | bytes 196616 | tf_op jit(solution)/shard_map/ppermute | solution.py:18
  33.8 0.6 %fusion.115 = f32[128,128]{1,0:T(8,128)S(1)} fusion(f32[128,128]{1,0:T(8,128)S(1)} %fusion.117, f32[1024,128]{1,0:T(8,128)S(1)} %fusion.29, f32[1024,128]{1,0:T(8,128)S(1)} %reshape.101), kind=kOutput, calls=%fused_computation.156 | convolution fusion | flops 100712448 | bytes 1179648 | tf_op jit(solution)/shard_map/dot_general | solution.py:82
  34.9 1.9 %collective-permute-start.5 = (f32[128,128]{1,0:T(8,128)S(1)}, f32[128,128]{1,0:T(8,128)S(1)}, u32[]{:S(2)}, u32[]{:S(2)}) collective-permute-start(f32[128,128]{1,0:T(8,128)S(1)} %fusion.115), channel_id=1, source_target_pairs={{4,0},{8,4},{12,8},{0,12},{5,1},{9,5},{13,9},{1,13},{6,2},{10,6},{... | collective-permute-start | bytes 196616 | tf_op jit(solution)/shard_map/ppermute | solution.py:18
  36.8 1.6 %select_reduce_fusion.3 = (f32[4,256,256]{2,1,0:T(8,128)S(1)}, f32[4,256,256]{2,1,0:T(8,128)S(1)}) fusion(f32[4,8,256]{2,1,0:T(8,128)S(1)} %get-tuple-element.29, f32[4,8,256]{2,1,0:T(8,128)S(1)} %get-tuple-element.30, f32[4,8,256]{2,1,0:T(8,128)S(1)} %get-tuple-element.28), kind=kLoop, calls=%fused_computation.5 | loop fusion | flops 9961472 | bytes 2195456 | tf_op jit(solution)/shard_map/reduce_sum | solution.py:40
  44.1 1.1 %collective-permute-start.6 = (f32[128,128]{1,0:T(8,128)S(1)}, f32[128,128]{1,0:T(8,128)S(1)}, u32[]{:S(2)}, u32[]{:S(2)}) collective-permute-start(f32[128,128]{1,0:T(8,128)S(1)} %fusion.107), channel_id=1, source_target_pairs={{4,0},{8,4},{12,8},{0,12},{5,1},{9,5},{13,9},{1,13},{6,2},{10,6},{... | collective-permute-start | bytes 196616 | tf_op jit(solution)/shard_map/ppermute | solution.py:18
  45.2 1.6 %select_reduce_fusion.1 = (f32[4,256,256]{2,1,0:T(8,128)S(1)}, f32[4,256,256]{2,1,0:T(8,128)S(1)}) fusion(f32[4,8,256]{2,1,0:T(8,128)S(1)} %get-tuple-element.26, f32[4,8,256]{2,1,0:T(8,128)S(1)} %get-tuple-element.27, f32[4,8,256]{2,1,0:T(8,128)S(1)} %get-tuple-element.25), kind=kLoop, calls=%fused_computation.2 | loop fusion | flops 9961472 | bytes 2195456 | tf_op jit(solution)/shard_map/reduce_sum | solution.py:40
  49.5 1.4 %collective-permute-start.10 = (f32[128,128]{1,0:T(8,128)S(1)}, f32[128,128]{1,0:T(8,128)S(1)}, u32[]{:S(2)}, u32[]{:S(2)}) collective-permute-start(f32[128,128]{1,0:T(8,128)S(1)} %fusion.95), channel_id=1, source_target_pairs={{8,0},{12,4},{0,8},{4,12},{9,1},{13,5},{1,9},{5,13},{10,2},{14,6},... | collective-permute-start | bytes 196616 | tf_op jit(solution)/shard_map/ppermute | solution.py:18
  52.8 0.6 %fusion.99 = f32[128,128]{1,0:T(8,128)S(1)} fusion(f32[128,128]{1,0:T(8,128)S(1)} %fusion.101, f32[1024,128]{1,0:T(8,128)S(1)} %fusion.77, f32[1024,128]{1,0:T(8,128)S(1)} %fusion.3), kind=kOutput, calls=%fused_computation.132 | convolution fusion | flops 100712448 | bytes 1179648 | tf_op jit(solution)/shard_map/dot_general | solution.py:82
  53.8 0.8 %collective-permute-start.8 = (f32[128,128]{1,0:T(8,128)S(1)}, f32[128,128]{1,0:T(8,128)S(1)}, u32[]{:S(2)}, u32[]{:S(2)}) collective-permute-start(f32[128,128]{1,0:T(8,128)S(1)} %fusion.99), channel_id=1, source_target_pairs={{8,0},{12,4},{0,8},{4,12},{9,1},{13,5},{1,9},{5,13},{10,2},{14,6},... | collective-permute-start | bytes 196616 | tf_op jit(solution)/shard_map/ppermute | solution.py:18
  55.2 0.7 %fusion.129 = f32[256,128]{1,0:T(8,128)} fusion(f32[1024,128]{1,0:T(8,128)S(1)} %fusion.124, s32[]{:T(128)S(6)} %select_n.56, f32[1024,128]{1,0:T(8,128)S(1)} %fusion.3), kind=kLoop, calls=%fused_computation.175 | loop fusion | flops 98304 | bytes 393220 | tf_op jit(solution)/shard_map/sub | solution.py:93
  55.9 2.3 %collective-permute-done.8 = f32[128,128]{1,0:T(8,128)S(1)} collective-permute-done((f32[128,128]{1,0:T(8,128)S(1)}, f32[128,128]{1,0:T(8,128)S(1)}, u32[]{:S(2)}, u32[]{:S(2)}) %collective-permute-start.8) | collective-permute-done | bytes 65568 | tf_op jit(solution)/shard_map/ppermute | solution.py:18
  58.2 0.7 %pad_maximum_fusion.2 = f32[256,128]{1,0:T(8,128)} fusion(f32[128,128]{1,0:T(8,128)S(1)} %collective-permute-done.10, f32[128,128]{1,0:T(8,128)S(1)} %collective-permute-done.8), kind=kLoop, calls=%fused_computation.182 | loop fusion | flops 32768 | bytes 262144 | tf_op jit(solution)/shard_map/concatenate | solution.py:94
  (62 shorter events, 15.9 us)
Async XLA Ops:
  3.1 10.6 %collective-permute-start.2 = (f32[45056]{0:T(1024)S(1)}, f32[45056]{0:T(1024)S(1)}, u32[]{:S(2)}, u32[]{:S(2)}) collective-permute-start(f32[45056]{0:T(1024)S(1)} %pad_maximum_fusion.1), channel_id=1, source_target_pairs={{0,3},{1,2},{2,1},{3,0},{4,7},{5,6},{6,5},{7,4},{8,11},{9,10},{10,... | collective-permute-start | bytes 540680 | tf_op jit(solution)/shard_map/ppermute | solution.py:25
  8.2 15.3 %collective-permute-start.1 = (f32[45056]{0:T(1024)S(1)}, f32[45056]{0:T(1024)S(1)}, u32[]{:S(2)}, u32[]{:S(2)}) collective-permute-start(f32[45056]{0:T(1024)S(1)} %pad_maximum_fusion.1), channel_id=1, source_target_pairs={{0,2},{1,3},{2,0},{3,1},{4,6},{5,7},{6,4},{7,5},{8,10},{9,11},{10,... | collective-permute-start | bytes 540680 | tf_op jit(solution)/shard_map/ppermute | solution.py:25
  8.2 15.3 %collective-permute-start = (f32[45056]{0:T(1024)S(1)}, f32[45056]{0:T(1024)S(1)}, u32[]{:S(2)}, u32[]{:S(2)}) collective-permute-start(f32[45056]{0:T(1024)S(1)} %pad_maximum_fusion.1), channel_id=1, source_target_pairs={{0,1},{1,0},{2,3},{3,2},{4,5},{5,4},{6,7},{7,6},{8,9},{9,8},{10,11... | collective-permute-start | bytes 540680 | tf_op jit(solution)/shard_map/ppermute | solution.py:25
  25.9 1.6 %copy-start = (f32[256,128]{1,0:T(8,128)S(1)}, f32[256,128]{1,0:T(8,128)}, u32[]{:S(2)}) copy-start(f32[256,128]{1,0:T(8,128)} %param.5) | copy-start | bytes 393220
  29.6 9.4 %collective-permute-start.7 = (f32[128,128]{1,0:T(8,128)S(1)}, f32[128,128]{1,0:T(8,128)S(1)}, u32[]{:S(2)}, u32[]{:S(2)}) collective-permute-start(f32[128,128]{1,0:T(8,128)S(1)} %fusion.111), channel_id=1, source_target_pairs={{4,0},{8,4},{12,8},{0,12},{5,1},{9,5},{13,9},{1,13},{6,2},{10,6},{... | collective-permute-start | bytes 196616 | tf_op jit(solution)/shard_map/ppermute | solution.py:18
  30.8 3.6 %collective-permute-start.4 = (f32[2,4,8,256]{3,2,1,0:T(8,128)S(1)}, f32[2,4,8,256]{3,2,1,0:T(8,128)S(1)}, u32[]{:S(2)}, u32[]{:S(2)}) collective-permute-start(f32[2,4,8,256]{3,2,1,0:T(8,128)S(1)} %pad_maximum_fusion.4), channel_id=1, source_target_pairs={{4,0},{8,4},{12,8},{0,12},{5,1},{9,5},{13,9},{1,13},{6,2},{10,6},{... | collective-permute-start | bytes 196616 | tf_op jit(solution)/shard_map/ppermute | solution.py:18
  32.2 11.5 %collective-permute-start.3 = (f32[2,4,8,256]{3,2,1,0:T(8,128)S(1)}, f32[2,4,8,256]{3,2,1,0:T(8,128)S(1)}, u32[]{:S(2)}, u32[]{:S(2)}) collective-permute-start(f32[2,4,8,256]{3,2,1,0:T(8,128)S(1)} %pad_maximum_fusion.3), channel_id=1, source_target_pairs={{8,0},{12,4},{0,8},{4,12},{9,1},{13,5},{1,9},{5,13},{10,2},{14,6},... | collective-permute-start | bytes 196616 | tf_op jit(solution)/shard_map/ppermute | solution.py:18
  34.9 6.7 %collective-permute-start.5 = (f32[128,128]{1,0:T(8,128)S(1)}, f32[128,128]{1,0:T(8,128)S(1)}, u32[]{:S(2)}, u32[]{:S(2)}) collective-permute-start(f32[128,128]{1,0:T(8,128)S(1)} %fusion.115), channel_id=1, source_target_pairs={{4,0},{8,4},{12,8},{0,12},{5,1},{9,5},{13,9},{1,13},{6,2},{10,6},{... | collective-permute-start | bytes 196616 | tf_op jit(solution)/shard_map/ppermute | solution.py:18
  41.1 6.3 %collective-permute-start.9 = (f32[128,128]{1,0:T(8,128)S(1)}, f32[128,128]{1,0:T(8,128)S(1)}, u32[]{:S(2)}, u32[]{:S(2)}) collective-permute-start(f32[128,128]{1,0:T(8,128)S(1)} %fusion.103), channel_id=1, source_target_pairs={{4,0},{8,4},{12,8},{0,12},{5,1},{9,5},{13,9},{1,13},{6,2},{10,6},{... | collective-permute-start | bytes 196616 | tf_op jit(solution)/shard_map/ppermute | solution.py:18
  44.1 7.2 %collective-permute-start.6 = (f32[128,128]{1,0:T(8,128)S(1)}, f32[128,128]{1,0:T(8,128)S(1)}, u32[]{:S(2)}, u32[]{:S(2)}) collective-permute-start(f32[128,128]{1,0:T(8,128)S(1)} %fusion.107), channel_id=1, source_target_pairs={{4,0},{8,4},{12,8},{0,12},{5,1},{9,5},{13,9},{1,13},{6,2},{10,6},{... | collective-permute-start | bytes 196616 | tf_op jit(solution)/shard_map/ppermute | solution.py:18
  49.5 6.4 %collective-permute-start.10 = (f32[128,128]{1,0:T(8,128)S(1)}, f32[128,128]{1,0:T(8,128)S(1)}, u32[]{:S(2)}, u32[]{:S(2)}) collective-permute-start(f32[128,128]{1,0:T(8,128)S(1)} %fusion.95), channel_id=1, source_target_pairs={{8,0},{12,4},{0,8},{4,12},{9,1},{13,5},{1,9},{5,13},{10,2},{14,6},... | collective-permute-start | bytes 196616 | tf_op jit(solution)/shard_map/ppermute | solution.py:18
  53.8 4.3 %collective-permute-start.8 = (f32[128,128]{1,0:T(8,128)S(1)}, f32[128,128]{1,0:T(8,128)S(1)}, u32[]{:S(2)}, u32[]{:S(2)}) collective-permute-start(f32[128,128]{1,0:T(8,128)S(1)} %fusion.99), channel_id=1, source_target_pairs={{8,0},{12,4},{0,8},{4,12},{9,1},{13,5},{1,9},{5,13},{10,2},{14,6},... | collective-permute-start | bytes 196616 | tf_op jit(solution)/shard_map/ppermute | solution.py:18

commit v11 on v6

--- a/solution.py
+++ b/solution.py
@@ -28,6 +28,22 @@
     return jnp.take(jnp.stack(received), order, axis=0)
 
 
+def gather_line(block, axis):
+    count = lax.axis_size(axis)
+    if count != 4:
+        return gather_over(block, axis)
+    me = lax.axis_index(axis)
+    from_left = lax.ppermute(block, axis, [(i, i + 1) for i in range(count - 1)])
+    from_right = lax.ppermute(block, axis, [(i + 1, i) for i in range(count - 1)])
+    two_left = lax.ppermute(from_left, axis, [(1, 2), (2, 3)])
+    two_right = lax.ppermute(from_right, axis, [(2, 1), (1, 0)])
+    three_left = lax.ppermute(from_left, axis, [(1, 3)])
+    three_right = lax.ppermute(from_right, axis, [(2, 0)])
+    stacked = jnp.stack([three_left, two_left, from_left, block, from_right, two_right, three_right])
+    order = jnp.arange(count, dtype=jnp.int32) - me + (count - 1)
+    return jnp.take(stacked, order, axis=0)
+
+
 def residual_tile(user_rows, item_rows, weight_t, target_t):
     scores_t = jnp.dot(item_rows, user_rows.T, precision=MATMUL_PRECISION)
     return weight_t * jax.nn.sigmoid(scores_t) - target_t
@@ -49,9 +65,9 @@
     slots_local = jnp.stack(
         [jnp.transpose(item_index.astype(jnp.float32), (0, 2, 1)), jnp.transpose(signed, (0, 2, 1))], 1
     )
-    slots_all = gather_over(slots_local, "it")
+    slots_all = gather_line(slots_local, "it")
     slabs = slots_all.shape[0]
-    block = gather_over(item_factors, "it").reshape(slabs * slab_rows, width)
+    block = gather_line(item_factors, "it").reshape(slabs * slab_rows, width)
     index_all = slots_all[:, :, 0]
     signed_all = slots_all[:, :, 1]
 

time: 52.5 us -> 75.6 us (1.44)
  waiting for transfers between devices: 3.53 us -> 16 us
  starting transfers between devices: 16.5 us -> 26.2 us
    ppermute x6 -> x12, waiting for transfers between devices: 2.01 us -> 14.9 us  [the longest x2 6.42 us: gather_line(): two_right = lax.ppermute(from_right, axis, [(2, 1), (1, 0)])]
    ppermute x6 -> x12, starting transfers between devices: 10.1 us -> 19.9 us  [the longest x2 9.49 us: gather_line(): lax.ppermute(block, axis, [(i, i + 1) for i in range(count - 1)])]
    unnamed x13 -> x24, local copies, waits for them, and re-layouts: 1.4 us -> 1.78 us
  transfers between devices with their start and end apart: 14 -> 20, of which waited for: 2 -> 7; matrix products, arithmetic and copies ran while one was open for 43% -> 34% of each run, Pallas kernels for 0% -> 0%
where the time goes in v11:
time: 75.6 us; the launch traced here: 75 us
  starting transfers between devices  26.2 us (35%)
  matrix products  17.8 us (24%)
  waiting for transfers between devices  16 us (21%)
  other arithmetic  10.6 us (14%)
  local copies, waits for them, and re-layouts  3.05 us (4%)
  between operations  1.28 us (2%)
    ppermute x2, starting transfers between devices, gather_line(): lax.ppermute(block, axis, [(i, i + 1) for i in range(count - 1)])  9.49 us
    dot_general x18, matrix products, residual_tile(): scores_t = jnp.dot(item_rows, user_rows.T, precision=MATMUL_PRECISION)  8.75 us
    reduce_sum x3, other arithmetic, build_tiles(): jnp.sum(jnp.where(matches, jnp.abs(signed_rows)[:, :, None, :], 0.0), axi...  7.37 us
    dot_general x12, matrix products, per_device(): lax.dot_general(residual_t, block, (((0,), (0,)), ((), ())), precision=MA...  7.36 us
    ppermute x2, waiting for transfers between devices, gather_line(): two_right = lax.ppermute(from_right, axis, [(2, 1), (1, 0)])  6.42 us
    ppermute x8, starting transfers between devices, shifted(): return lax.ppermute(block, axis, route)  6.36 us
    ppermute x2, waiting for transfers between devices, gather_line(): three_right = lax.ppermute(from_right, axis, [(2, 0)])  5.22 us
    ppermute x2, waiting for transfers between devices, gather_line(): lax.ppermute(block, axis, [(i + 1, i) for i in range(count - 1)])  2.83 us
  transfers between devices with their start and end apart: 20, of which 7 were waited for; matrix products, arithmetic and copies ran while one was open for 34% of the time, Pallas kernels for 0%

profile of v11, /device:TPU:0, one launch (start us, length us, event | category | flops | bytes accessed | tf_op | source)
XLA Modules:
  0.0 75.0 jit_solution(16512944595554932585)
XLA Ops:
  0.6 4.9 %collective-permute-start.6 = (f32[256,128]{1,0:T(8,128)}, f32[256,128]{1,0:T(8,128)S(1)}, u32[]{:S(2)}, u32[]{:S(2)}) collective-permute-start(f32[256,128]{1,0:T(8,128)} %param.6), channel_id=1, source_target_pairs={{0,1},{1,2},{2,3},{4,5},{5,6},{6,7},{8,9},{9,10},{10,11},{12,13},{... | collective-permute-start | bytes 393224 | tf_op jit(solution)/shard_map/ppermute | solution.py:36
  5.6 1.3 %collective-permute-start.9 = (f32[256,128]{1,0:T(8,128)}, f32[256,128]{1,0:T(8,128)S(1)}, u32[]{:S(2)}, u32[]{:S(2)}) collective-permute-start(f32[256,128]{1,0:T(8,128)} %param.6), channel_id=1, source_target_pairs={{1,0},{2,1},{3,2},{5,4},{6,5},{7,6},{9,8},{10,9},{11,10},{13,12},{... | collective-permute-start | bytes 393224 | tf_op jit(solution)/shard_map/ppermute | solution.py:37
  6.9 0.7 convert_bitcast_fusion
  7.6 0.8 %fusion.141 = f32[3,1,8,256]{3,2,0,1:T(8,128)S(1)} fusion(f32[3,256,8]{1,2,0:T(8,128)} %param.9, s32[3,256,8]{1,2,0:T(8,128)} %param.8), kind=kLoop, calls=%fused_computation.221 | loop fusion | flops 18432 | bytes 73728 | tf_op jit(solution)/shard_map/stack | solution.py:65
  8.4 4.6 %collective-permute-start = (f32[3,2,8,256]{3,2,0,1:T(8,128)S(1)}, f32[3,2,8,256]{3,2,0,1:T(8,128)S(1)}, u32[]{:S(2)}, u32[]{:S(2)}) collective-permute-start(f32[3,2,8,256]{3,2,0,1:T(8,128)S(1)} %pad_maximum_fusion.3), channel_id=1, source_target_pairs={{0,1},{1,2},{2,3},{4,5},{5,6},{6,7},{8,9},{9,10},{10,11},{12,13},{... | collective-permute-start | bytes 147464 | tf_op jit(solution)/shard_map/ppermute | solution.py:36
  12.9 1.3 %collective-permute-start.3 = (f32[3,2,8,256]{3,2,0,1:T(8,128)S(1)}, f32[3,2,8,256]{3,2,0,1:T(8,128)S(1)}, u32[]{:S(2)}, u32[]{:S(2)}) collective-permute-start(f32[3,2,8,256]{3,2,0,1:T(8,128)S(1)} %pad_maximum_fusion.3), channel_id=1, source_target_pairs={{1,0},{2,1},{3,2},{5,4},{6,5},{7,6},{9,8},{10,9},{11,10},{13,12},{... | collective-permute-start | bytes 147464 | tf_op jit(solution)/shard_map/ppermute | solution.py:37
  16.1 2.8 %collective-permute-done.3 = f32[3,2,8,256]{3,2,0,1:T(8,128)S(1)} collective-permute-done((f32[3,2,8,256]{3,2,0,1:T(8,128)S(1)}, f32[3,2,8,256]{3,2,0,1:T(8,128)S(1)}, u32[]{:S(2)}, u32[]{:S(2)}) %collective-permute-start.3) | collective-permute-done | bytes 49184 | tf_op jit(solution)/shard_map/ppermute | solution.py:37
  18.9 1.3 %collective-permute-start.4 = (f32[3,2,8,256]{3,2,0,1:T(8,128)S(1)}, f32[3,2,8,256]{3,2,0,1:T(8,128)S(1)}, u32[]{:S(2)}, u32[]{:S(2)}) collective-permute-start(f32[3,2,8,256]{3,2,0,1:T(8,128)S(1)} %collective-permute-done.3), channel_id=1, source_target_pairs={{2,1},{1,0},{6,5},{5,4},{10,9},{9,8},{14,13},{13,12},{18,17},{17,1... | collective-permute-start | bytes 147464 | tf_op jit(solution)/shard_map/ppermute | solution.py:39
  20.2 1.3 %collective-permute-start.5 = (f32[3,2,8,256]{3,2,0,1:T(8,128)S(1)}, f32[3,2,8,256]{3,2,0,1:T(8,128)S(1)}, u32[]{:S(2)}, u32[]{:S(2)}) collective-permute-start(f32[3,2,8,256]{3,2,0,1:T(8,128)S(1)} %collective-permute-done.3), channel_id=1, source_target_pairs={{2,0},{6,4},{10,8},{14,12},{18,16},{22,20},{26,24},{30,28}} | collective-permute-start | bytes 147464 | tf_op jit(solution)/shard_map/ppermute | solution.py:41
  21.6 5.8 %collective-permute-done.4 = f32[3,2,8,256]{3,2,0,1:T(8,128)S(1)} collective-permute-done((f32[3,2,8,256]{3,2,0,1:T(8,128)S(1)}, f32[3,2,8,256]{3,2,0,1:T(8,128)S(1)}, u32[]{:S(2)}, u32[]{:S(2)}) %collective-permute-start.4) | collective-permute-done | bytes 49184 | tf_op jit(solution)/shard_map/ppermute | solution.py:39
  27.4 2.2 %collective-permute-done.5 = f32[3,2,8,256]{3,2,0,1:T(8,128)S(1)} collective-permute-done((f32[3,2,8,256]{3,2,0,1:T(8,128)S(1)}, f32[3,2,8,256]{3,2,0,1:T(8,128)S(1)}, u32[]{:S(2)}, u32[]{:S(2)}) %collective-permute-start.5) | collective-permute-done | bytes 49184 | tf_op jit(solution)/shard_map/ppermute | solution.py:41
  30.5 1.6 %collective-permute-start.15 = (f32[2,4,8,256]{3,2,1,0:T(8,128)S(1)}, f32[2,4,8,256]{3,2,1,0:T(8,128)S(1)}, u32[]{:S(2)}, u32[]{:S(2)}) collective-permute-start(f32[2,4,8,256]{3,2,1,0:T(8,128)S(1)} %pad_maximum_fusion.2), channel_id=1, source_target_pairs={{8,0},{12,4},{0,8},{4,12},{9,1},{13,5},{1,9},{5,13},{10,2},{14,6},... | collective-permute-start | bytes 196616 | tf_op jit(solution)/shard_map/ppermute | solution.py:18
  32.0 2.9 %select_reduce_fusion.5 = (f32[4,256,256]{2,1,0:T(8,128)}, f32[4,256,256]{2,1,0:T(8,128)}) fusion(f32[4,8,256]{2,1,0:T(8,128)S(1)} %get-tuple-element.16, f32[4,8,256]{2,1,0:T(8,128)S(1)} %get-tuple-element.12, f32[4,8,256]{2,1,0:T(8,128)S(1)} %get-tuple-element.14), kind=kLoop, calls=%fused_computation.9 | loop fusion | flops 9961472 | bytes 2195456 | tf_op jit(solution)/shard_map/reduce_sum | solution.py:56
  36.3 1.3 %collective-permute-start.10 = (f32[256,128]{1,0:T(8,128)S(1)}, f32[256,128]{1,0:T(8,128)S(1)}, u32[]{:S(2)}, u32[]{:S(2)}) collective-permute-start(f32[256,128]{1,0:T(8,128)S(1)} %collective-permute-done.9), channel_id=1, source_target_pairs={{2,1},{1,0},{6,5},{5,4},{10,9},{9,8},{14,13},{13,12},{18,17},{17,1... | collective-permute-start | bytes 393224 | tf_op jit(solution)/shard_map/ppermute | solution.py:39
  37.6 1.3 %collective-permute-start.11 = (f32[256,128]{1,0:T(8,128)S(1)}, f32[256,128]{1,0:T(8,128)S(1)}, u32[]{:S(2)}, u32[]{:S(2)}) collective-permute-start(f32[256,128]{1,0:T(8,128)S(1)} %collective-permute-done.9), channel_id=1, source_target_pairs={{2,0},{6,4},{10,8},{14,12},{18,16},{22,20},{26,24},{30,28}} | collective-permute-start | bytes 393224 | tf_op jit(solution)/shard_map/ppermute | solution.py:41
  38.9 2.9 %select_reduce_fusion.3 = (f32[4,256,256]{2,1,0:T(8,128)}, f32[4,256,256]{2,1,0:T(8,128)}) fusion(f32[4,8,256]{2,1,0:T(8,128)S(1)} %get-tuple-element.21, f32[4,8,256]{2,1,0:T(8,128)S(1)} %get-tuple-element.22, f32[4,8,256]{2,1,0:T(8,128)S(1)} %get-tuple-element.20), kind=kLoop, calls=%fused_computation.6 | loop fusion | flops 9961472 | bytes 2195456 | tf_op jit(solution)/shard_map/reduce_sum | solution.py:56
  41.8 1.6 %select_reduce_fusion.1 = (f32[4,256,256]{2,1,0:T(8,128)S(1)}, f32[4,256,256]{2,1,0:T(8,128)S(1)}) fusion(f32[4,8,256]{2,1,0:T(8,128)S(1)} %get-tuple-element.18, f32[4,8,256]{2,1,0:T(8,128)S(1)} %get-tuple-element.19, f32[4,8,256]{2,1,0:T(8,128)S(1)} %get-tuple-element.17), kind=kLoop, calls=%fused_computation.3 | loop fusion | flops 9961472 | bytes 2195456 | tf_op jit(solution)/shard_map/reduce_sum | solution.py:56
  44.2 3.0 %collective-permute-done.11 = f32[256,128]{1,0:T(8,128)S(1)} collective-permute-done((f32[256,128]{1,0:T(8,128)S(1)}, f32[256,128]{1,0:T(8,128)S(1)}, u32[]{:S(2)}, u32[]{:S(2)}) %collective-permute-start.11) | collective-permute-done | bytes 131104 | tf_op jit(solution)/shard_map/ppermute | solution.py:41
  48.0 1.0 %copy-done.2 = f32[4,256,256]{2,1,0:T(8,128)S(1)} copy-done((f32[4,256,256]{2,1,0:T(8,128)S(1)}, f32[4,256,256]{2,1,0:T(8,128)}, u32[]{:S(2)}) %copy-start.2) | copy-done | bytes 1048600
  49.0 1.5 %fusion.37 = f32[1024,128]{1,0:T(8,128)S(1)} fusion(f32[1024,128]{1,0:T(8,128)S(1)} %bitcast_select_fusion, f32[1024,256]{1,0:T(8,128)} %bitcast.167, f32[1024,256]{1,0:T(8,128)S(1)} %bitcast.161, f32[256,128]{1,0:T(8,128)} %param.5), kind=kOutput, calls=%fused_computation.68 | convolution fusion | flops 101318656 | bytes 2162688 | tf_op jit(solution)/shard_map/dot_general | solution.py:48
  55.9 0.9 %collective-permute-start.12 = (f32[128,128]{1,0:T(8,128)S(1)}, f32[128,128]{1,0:T(8,128)S(1)}, u32[]{:S(2)}, u32[]{:S(2)}) collective-permute-start(f32[128,128]{1,0:T(8,128)S(1)} %fusion.115), channel_id=1, source_target_pairs={{4,0},{8,4},{12,8},{0,12},{5,1},{9,5},{13,9},{1,13},{6,2},{10,6},{... | collective-permute-start | bytes 196616 | tf_op jit(solution)/shard_map/ppermute | solution.py:18
  63.1 1.0 %collective-permute-start.14 = (f32[128,128]{1,0:T(8,128)S(1)}, f32[128,128]{1,0:T(8,128)S(1)}, u32[]{:S(2)}, u32[]{:S(2)}) collective-permute-start(f32[128,128]{1,0:T(8,128)S(1)} %fusion.107), channel_id=1, source_target_pairs={{4,0},{8,4},{12,8},{0,12},{5,1},{9,5},{13,9},{1,13},{6,2},{10,6},{... | collective-permute-start | bytes 196616 | tf_op jit(solution)/shard_map/ppermute | solution.py:18
  70.0 1.5 %collective-permute-start.17 = (f32[128,128]{1,0:T(8,128)S(1)}, f32[128,128]{1,0:T(8,128)S(1)}, u32[]{:S(2)}, u32[]{:S(2)}) collective-permute-start(f32[128,128]{1,0:T(8,128)S(1)} %fusion.99), channel_id=1, source_target_pairs={{8,0},{12,4},{0,8},{4,12},{9,1},{13,5},{1,9},{5,13},{10,2},{14,6},... | collective-permute-start | bytes 196616 | tf_op jit(solution)/shard_map/ppermute | solution.py:18
  73.2 1.1 %collective-permute-done.17 = f32[128,128]{1,0:T(8,128)S(1)} collective-permute-done((f32[128,128]{1,0:T(8,128)S(1)}, f32[128,128]{1,0:T(8,128)S(1)}, u32[]{:S(2)}, u32[]{:S(2)}) %collective-permute-start.17) | collective-permute-done | bytes 65568 | tf_op jit(solution)/shard_map/ppermute | solution.py:18
  (100 shorter events, 25.2 us)
Async XLA Ops:
  0.6 34.3 %collective-permute-start.6 = (f32[256,128]{1,0:T(8,128)}, f32[256,128]{1,0:T(8,128)S(1)}, u32[]{:S(2)}, u32[]{:S(2)}) collective-permute-start(f32[256,128]{1,0:T(8,128)} %param.6), channel_id=1, source_target_pairs={{0,1},{1,2},{2,3},{4,5},{5,6},{6,7},{8,9},{9,10},{10,11},{12,13},{... | collective-permute-start | bytes 393224 | tf_op jit(solution)/shard_map/ppermute | solution.py:36
  5.6 30.7 %collective-permute-start.9 = (f32[256,128]{1,0:T(8,128)}, f32[256,128]{1,0:T(8,128)S(1)}, u32[]{:S(2)}, u32[]{:S(2)}) collective-permute-start(f32[256,128]{1,0:T(8,128)} %param.6), channel_id=1, source_target_pairs={{1,0},{2,1},{3,2},{5,4},{6,5},{7,6},{9,8},{10,9},{11,10},{13,12},{... | collective-permute-start | bytes 393224 | tf_op jit(solution)/shard_map/ppermute | solution.py:37
  8.4 6.3 %collective-permute-start = (f32[3,2,8,256]{3,2,0,1:T(8,128)S(1)}, f32[3,2,8,256]{3,2,0,1:T(8,128)S(1)}, u32[]{:S(2)}, u32[]{:S(2)}) collective-permute-start(f32[3,2,8,256]{3,2,0,1:T(8,128)S(1)} %pad_maximum_fusion.3), channel_id=1, source_target_pairs={{0,1},{1,2},{2,3},{4,5},{5,6},{6,7},{8,9},{9,10},{10,11},{12,13},{... | collective-permute-start | bytes 147464 | tf_op jit(solution)/shard_map/ppermute | solution.py:36
  12.9 6.0 %collective-permute-start.3 = (f32[3,2,8,256]{3,2,0,1:T(8,128)S(1)}, f32[3,2,8,256]{3,2,0,1:T(8,128)S(1)}, u32[]{:S(2)}, u32[]{:S(2)}) collective-permute-start(f32[3,2,8,256]{3,2,0,1:T(8,128)S(1)} %pad_maximum_fusion.3), channel_id=1, source_target_pairs={{1,0},{2,1},{3,2},{5,4},{6,5},{7,6},{9,8},{10,9},{11,10},{13,12},{... | collective-permute-start | bytes 147464 | tf_op jit(solution)/shard_map/ppermute | solution.py:37
  14.7 5.5 %collective-permute-start.1 = (f32[3,2,8,256]{3,2,0,1:T(8,128)S(1)}, f32[3,2,8,256]{3,2,0,1:T(8,128)S(1)}, u32[]{:S(2)}, u32[]{:S(2)}) collective-permute-start(f32[3,2,8,256]{3,2,0,1:T(8,128)S(1)} %collective-permute-done), channel_id=1, source_target_pairs={{1,3},{5,7},{9,11},{13,15},{17,19},{21,23},{25,27},{29,31}} | collective-permute-start | bytes 147464 | tf_op jit(solution)/shard_map/ppermute | solution.py:40
  15.4 6.1 %collective-permute-start.2 = (f32[3,2,8,256]{3,2,0,1:T(8,128)S(1)}, f32[3,2,8,256]{3,2,0,1:T(8,128)S(1)}, u32[]{:S(2)}, u32[]{:S(2)}) collective-permute-start(f32[3,2,8,256]{3,2,0,1:T(8,128)S(1)} %collective-permute-done), channel_id=1, source_target_pairs={{1,2},{2,3},{5,6},{6,7},{9,10},{10,11},{13,14},{14,15},{17,18},{18... | collective-permute-start | bytes 147464 | tf_op jit(solution)/shard_map/ppermute | solution.py:38
  18.9 8.5 %collective-permute-start.4 = (f32[3,2,8,256]{3,2,0,1:T(8,128)S(1)}, f32[3,2,8,256]{3,2,0,1:T(8,128)S(1)}, u32[]{:S(2)}, u32[]{:S(2)}) collective-permute-start(f32[3,2,8,256]{3,2,0,1:T(8,128)S(1)} %collective-permute-done.3), channel_id=1, source_target_pairs={{2,1},{1,0},{6,5},{5,4},{10,9},{9,8},{14,13},{13,12},{18,17},{17,1... | collective-permute-start | bytes 147464 | tf_op jit(solution)/shard_map/ppermute | solution.py:39
  20.2 9.4 %collective-permute-start.5 = (f32[3,2,8,256]{3,2,0,1:T(8,128)S(1)}, f32[3,2,8,256]{3,2,0,1:T(8,128)S(1)}, u32[]{:S(2)}, u32[]{:S(2)}) collective-permute-start(f32[3,2,8,256]{3,2,0,1:T(8,128)S(1)} %collective-permute-done.3), channel_id=1, source_target_pairs={{2,0},{6,4},{10,8},{14,12},{18,16},{22,20},{26,24},{30,28}} | collective-permute-start | bytes 147464 | tf_op jit(solution)/shard_map/ppermute | solution.py:41
  30.4 7.2 %collective-permute-start.13 = (f32[2,4,8,256]{3,2,1,0:T(8,128)S(1)}, f32[2,4,8,256]{3,2,1,0:T(8,128)S(1)}, u32[]{:S(2)}, u32[]{:S(2)}) collective-permute-start(f32[2,4,8,256]{3,2,1,0:T(8,128)S(1)} %pad_maximum_fusion.1), channel_id=1, source_target_pairs={{4,0},{8,4},{12,8},{0,12},{5,1},{9,5},{13,9},{1,13},{6,2},{10,6},{... | collective-permute-start | bytes 196616 | tf_op jit(solution)/shard_map/ppermute | solution.py:18
  30.5 11.3 %collective-permute-start.15 = (f32[2,4,8,256]{3,2,1,0:T(8,128)S(1)}, f32[2,4,8,256]{3,2,1,0:T(8,128)S(1)}, u32[]{:S(2)}, u32[]{:S(2)}) collective-permute-start(f32[2,4,8,256]{3,2,1,0:T(8,128)S(1)} %pad_maximum_fusion.2), channel_id=1, source_target_pairs={{8,0},{12,4},{0,8},{4,12},{9,1},{13,5},{1,9},{5,13},{10,2},{14,6},... | collective-permute-start | bytes 196616 | tf_op jit(solution)/shard_map/ppermute | solution.py:18
  34.9 8.5 %collective-permute-start.7 = (f32[256,128]{1,0:T(8,128)S(1)}, f32[256,128]{1,0:T(8,128)S(1)}, u32[]{:S(2)}, u32[]{:S(2)}) collective-permute-start(f32[256,128]{1,0:T(8,128)S(1)} %collective-permute-done.6), channel_id=1, source_target_pairs={{1,3},{5,7},{9,11},{13,15},{17,19},{21,23},{25,27},{29,31}} | collective-permute-start | bytes 393224 | tf_op jit(solution)/shard_map/ppermute | solution.py:40
  35.6 7.9 %collective-permute-start.8 = (f32[256,128]{1,0:T(8,128)S(1)}, f32[256,128]{1,0:T(8,128)S(1)}, u32[]{:S(2)}, u32[]{:S(2)}) collective-permute-start(f32[256,128]{1,0:T(8,128)S(1)} %collective-permute-done.6), channel_id=1, source_target_pairs={{1,2},{2,3},{5,6},{6,7},{9,10},{10,11},{13,14},{14,15},{17,18},{18... | collective-permute-start | bytes 393224 | tf_op jit(solution)/shard_map/ppermute | solution.py:38
  36.3 7.9 %collective-permute-start.10 = (f32[256,128]{1,0:T(8,128)S(1)}, f32[256,128]{1,0:T(8,128)S(1)}, u32[]{:S(2)}, u32[]{:S(2)}) collective-permute-start(f32[256,128]{1,0:T(8,128)S(1)} %collective-permute-done.9), channel_id=1, source_target_pairs={{2,1},{1,0},{6,5},{5,4},{10,9},{9,8},{14,13},{13,12},{18,17},{17,1... | collective-permute-start | bytes 393224 | tf_op jit(solution)/shard_map/ppermute | solution.py:39
  37.6 9.6 %collective-permute-start.11 = (f32[256,128]{1,0:T(8,128)S(1)}, f32[256,128]{1,0:T(8,128)S(1)}, u32[]{:S(2)}, u32[]{:S(2)}) collective-permute-start(f32[256,128]{1,0:T(8,128)S(1)} %collective-permute-done.9), channel_id=1, source_target_pairs={{2,0},{6,4},{10,8},{14,12},{18,16},{22,20},{26,24},{30,28}} | collective-permute-start | bytes 393224 | tf_op jit(solution)/shard_map/ppermute | solution.py:41
  41.8 1.7 %copy-start.5 = (f32[256,128]{1,0:T(8,128)S(1)}, f32[256,128]{1,0:T(8,128)}, u32[]{:S(2)}) copy-start(f32[256,128]{1,0:T(8,128)} %param.6) | copy-start | bytes 393220
  49.0 1.5 %copy-start.4 = (f32[256,128]{1,0:T(8,128)S(1)}, f32[256,128]{1,0:T(8,128)}, u32[]{:S(2)}) copy-start(f32[256,128]{1,0:T(8,128)} %param.5) | copy-start | bytes 393220
  52.8 4.5 %collective-permute-start.16 = (f32[128,128]{1,0:T(8,128)S(1)}, f32[128,128]{1,0:T(8,128)S(1)}, u32[]{:S(2)}, u32[]{:S(2)}) collective-permute-start(f32[128,128]{1,0:T(8,128)S(1)} %fusion.111), channel_id=1, source_target_pairs={{4,0},{8,4},{12,8},{0,12},{5,1},{9,5},{13,9},{1,13},{6,2},{10,6},{... | collective-permute-start | bytes 196616 | tf_op jit(solution)/shard_map/ppermute | solution.py:18
  55.8 1.5 %copy-start = (f32[4,256,256]{2,1,0:T(8,128)S(1)}, f32[4,256,256]{2,1,0:T(8,128)}, u32[]{:S(2)}) copy-start(f32[4,256,256]{2,1,0:T(8,128)} %get-tuple-element.4) | copy-start | bytes 3145732
  55.9 1.5 %copy-start.1 = (f32[4,256,256]{2,1,0:T(8,128)S(1)}, f32[4,256,256]{2,1,0:T(8,128)}, u32[]{:S(2)}) copy-start(f32[4,256,256]{2,1,0:T(8,128)} %get-tuple-element.5) | copy-start | bytes 3145732
  55.9 4.7 %collective-permute-start.12 = (f32[128,128]{1,0:T(8,128)S(1)}, f32[128,128]{1,0:T(8,128)S(1)}, u32[]{:S(2)}, u32[]{:S(2)}) collective-permute-start(f32[128,128]{1,0:T(8,128)S(1)} %fusion.115), channel_id=1, source_target_pairs={{4,0},{8,4},{12,8},{0,12},{5,1},{9,5},{13,9},{1,13},{6,2},{10,6},{... | collective-permute-start | bytes 196616 | tf_op jit(solution)/shard_map/ppermute | solution.py:18
  59.5 5.2 %collective-permute-start.18 = (f32[128,128]{1,0:T(8,128)S(1)}, f32[128,128]{1,0:T(8,128)S(1)}, u32[]{:S(2)}, u32[]{:S(2)}) collective-permute-start(f32[128,128]{1,0:T(8,128)S(1)} %fusion.103), channel_id=1, source_target_pairs={{4,0},{8,4},{12,8},{0,12},{5,1},{9,5},{13,9},{1,13},{6,2},{10,6},{... | collective-permute-start | bytes 196616 | tf_op jit(solution)/shard_map/ppermute | solution.py:18
  63.1 4.8 %collective-permute-start.14 = (f32[128,128]{1,0:T(8,128)S(1)}, f32[128,128]{1,0:T(8,128)S(1)}, u32[]{:S(2)}, u32[]{:S(2)}) collective-permute-start(f32[128,128]{1,0:T(8,128)S(1)} %fusion.107), channel_id=1, source_target_pairs={{4,0},{8,4},{12,8},{0,12},{5,1},{9,5},{13,9},{1,13},{6,2},{10,6},{... | collective-permute-start | bytes 196616 | tf_op jit(solution)/shard_map/ppermute | solution.py:18
  66.8 6.4 %collective-permute-start.19 = (f32[128,128]{1,0:T(8,128)S(1)}, f32[128,128]{1,0:T(8,128)S(1)}, u32[]{:S(2)}, u32[]{:S(2)}) collective-permute-start(f32[128,128]{1,0:T(8,128)S(1)} %fusion.95), channel_id=1, source_target_pairs={{8,0},{12,4},{0,8},{4,12},{9,1},{13,5},{1,9},{5,13},{10,2},{14,6},... | collective-permute-start | bytes 196616 | tf_op jit(solution)/shard_map/ppermute | solution.py:18
  70.0 4.3 %collective-permute-start.17 = (f32[128,128]{1,0:T(8,128)S(1)}, f32[128,128]{1,0:T(8,128)S(1)}, u32[]{:S(2)}, u32[]{:S(2)}) collective-permute-start(f32[128,128]{1,0:T(8,128)S(1)} %fusion.99), channel_id=1, source_target_pairs={{8,0},{12,4},{0,8},{4,12},{9,1},{13,5},{1,9},{5,13},{10,2},{14,6},... | collective-permute-start | bytes 196616 | tf_op jit(solution)/shard_map/ppermute | solution.py:18
  (2 other events, 2.5 us)

commit v12 on v6

--- a/solution.py
+++ b/solution.py
@@ -68,6 +68,9 @@
     for stratum in range(strata):
         if stratum > 0:
             chunks = [shifted(chunk, "ub", 1) for chunk in chunks]
+        if stratum == strata - 1 and len(chunks) > 1:
+            chunks = [jnp.concatenate(chunks, 0)]
+        rows = chunks[0].shape[0]
         weight, target = build_tiles(slot_data[stratum][0], slot_data[stratum][1], slab_rows)
         finished = []
         residuals = []

time: 52.5 us -> 54.8 us (1.044)
  waiting for transfers between devices: 3.53 us -> 7.66 us
  matrix products: 17.8 us -> 16.8 us
  other arithmetic: 10.6 us -> 9.96 us
    ppermute x8 -> x7, waiting for transfers between devices: 1.52 us -> 5.65 us  [shifted(): return lax.ppermute(block, axis, route)]
    concatenate x1 -> x0, other arithmetic: 0.66 us -> none  [per_device(): jnp.concatenate([shifted(chunk, 'ub', 1 - strata) for chunk in chunks], 0)]
    dot_general x18 -> x15, matrix products: 8.78 us -> 8.17 us  [residual_tile(): scores_t = jnp.dot(item_rows, user_rows.T, precision=MATMUL_PRECISION)]
    dot_general x12 -> x10, matrix products: 7.32 us -> 6.9 us  [per_device(): lax.dot_general(residual_t, block, (((0,), (0,)), ((), ())), precision=MA...]
    ppermute x8 -> x7, starting transfers between devices: 6.41 us -> 6.01 us  [shifted(): return lax.ppermute(block, axis, route)]
    unnamed x13 -> x15, local copies, waits for them, and re-layouts: 1.4 us -> 1.72 us
  transfers between devices with their start and end apart: 14 -> 13, of which waited for: 2 -> 4; matrix products, arithmetic and copies ran while one was open for 43% -> 32% of each run, Pallas kernels for 0% -> 0%
where the time goes in v12:
time: 54.8 us; the launch traced here: 54.5 us
  matrix products  16.8 us (31%)
  starting transfers between devices  16.1 us (29%)
  other arithmetic  9.96 us (18%)
  waiting for transfers between devices  7.66 us (14%)
  local copies, waits for them, and re-layouts  2.98 us (5%)
  between operations  1.02 us (2%)
    ppermute x6, starting transfers between devices, gather_over(): lax.ppermute(block, axis, [(i, i ^ k) for i in range(count)])  10.1 us
    dot_general x15, matrix products, residual_tile(): scores_t = jnp.dot(item_rows, user_rows.T, precision=MATMUL_PRECISION)  8.17 us
    reduce_sum x3, other arithmetic, build_tiles(): jnp.sum(jnp.where(matches, jnp.abs(signed_rows)[:, :, None, :], 0.0), axi...  7.37 us
    dot_general x10, matrix products, per_device(): lax.dot_general(residual_t, block, (((0,), (0,)), ((), ())), precision=MA...  6.9 us
    ppermute x7, starting transfers between devices, shifted(): return lax.ppermute(block, axis, route)  6.01 us
    ppermute x7, waiting for transfers between devices, shifted(): return lax.ppermute(block, axis, route)  5.65 us
    ppermute x6, waiting for transfers between devices, gather_over(): lax.ppermute(block, axis, [(i, i ^ k) for i in range(count)])  2.01 us
    dot_general x3, matrix products, per_device(): jnp.dot(residual_t, jnp.concatenate(chunks, 0), precision=MATMUL_PRECISION)  1.73 us
  transfers between devices with their start and end apart: 13, of which 4 were waited for; matrix products, arithmetic and copies ran while one was open for 32% of the time, Pallas kernels for 0%

profile of v12, /device:TPU:0, one launch (start us, length us, event | category | flops | bytes accessed | tf_op | source)
XLA Modules:
  0.0 54.5 jit_solution(6155042821650489474)
XLA Ops:
  0.6 0.7 %convert_bitcast_fusion = f32[3,1,8,256]{3,2,0,1:T(8,128)S(1)} fusion(s32[3,256,8]{1,2,0:T(8,128)} %param.7), kind=kLoop, calls=%fused_computation.178 | loop fusion | flops 6144 | bytes 49152 | tf_op jit(solution)/shard_map/stack | solution.py:49
  1.4 0.8 %fusion.115 = f32[3,1,8,256]{3,2,0,1:T(8,128)S(1)} fusion(f32[3,256,8]{1,2,0:T(8,128)} %param.9, s32[3,256,8]{1,2,0:T(8,128)} %param.8), kind=kLoop, calls=%fused_computation.177 | loop fusion | flops 18432 | bytes 73728 | tf_op jit(solution)/shard_map/stack | solution.py:49
  2.1 3.1 %collective-permute-start = (f32[3,2,8,256]{3,2,0,1:T(8,128)S(1)}, f32[3,2,8,256]{3,2,0,1:T(8,128)S(1)}, u32[]{:S(2)}, u32[]{:S(2)}) collective-permute-start(f32[3,2,8,256]{3,2,0,1:T(8,128)S(1)} %get-tuple-element.24), channel_id=1, source_target_pairs={{0,1},{1,0},{2,3},{3,2},{4,5},{5,4},{6,7},{7,6},{8,9},{9,8},{10,11... | collective-permute-start | bytes 147464 | tf_op jit(solution)/shard_map/ppermute | solution.py:25
  5.2 2.6 %collective-permute-start.1 = (f32[3,2,8,256]{3,2,0,1:T(8,128)S(1)}, f32[3,2,8,256]{3,2,0,1:T(8,128)S(1)}, u32[]{:S(2)}, u32[]{:S(2)}) collective-permute-start(f32[3,2,8,256]{3,2,0,1:T(8,128)S(1)} %get-tuple-element.24), channel_id=1, source_target_pairs={{0,2},{1,3},{2,0},{3,1},{4,6},{5,7},{6,4},{7,5},{8,10},{9,11},{10,... | collective-permute-start | bytes 147464 | tf_op jit(solution)/shard_map/ppermute | solution.py:25
  7.8 0.9 %collective-permute-start.3 = (f32[256,128]{1,0:T(8,128)}, f32[256,128]{1,0:T(8,128)S(1)}, u32[]{:S(2)}, u32[]{:S(2)}) collective-permute-start(f32[256,128]{1,0:T(8,128)} %param.6), channel_id=1, source_target_pairs={{0,1},{1,0},{2,3},{3,2},{4,5},{5,4},{6,7},{7,6},{8,9},{9,8},{10,11... | collective-permute-start | bytes 393224 | tf_op jit(solution)/shard_map/ppermute | solution.py:25
  8.7 3.5 %collective-permute-start.4 = (f32[256,128]{1,0:T(8,128)}, f32[256,128]{1,0:T(8,128)S(1)}, u32[]{:S(2)}, u32[]{:S(2)}) collective-permute-start(f32[256,128]{1,0:T(8,128)} %param.6), channel_id=1, source_target_pairs={{0,2},{1,3},{2,0},{3,1},{4,6},{5,7},{6,4},{7,5},{8,10},{9,11},{10,... | collective-permute-start | bytes 393224 | tf_op jit(solution)/shard_map/ppermute | solution.py:25
  12.4 2.0 %collective-permute-done.2 = f32[3,2,8,256]{3,2,0,1:T(8,128)S(1)} collective-permute-done((f32[3,2,8,256]{3,2,0,1:T(8,128)S(1)}, f32[3,2,8,256]{3,2,0,1:T(8,128)S(1)}, u32[]{:S(2)}, u32[]{:S(2)}) %collective-permute-start.2) | collective-permute-done | bytes 49184 | tf_op jit(solution)/shard_map/ppermute | solution.py:25
  15.3 1.6 %collective-permute-start.11 = (f32[2,4,8,256]{3,2,1,0:T(8,128)S(1)}, f32[2,4,8,256]{3,2,1,0:T(8,128)S(1)}, u32[]{:S(2)}, u32[]{:S(2)}) collective-permute-start(f32[2,4,8,256]{3,2,1,0:T(8,128)S(1)} %pad_maximum_fusion.3), channel_id=1, source_target_pairs={{8,0},{12,4},{0,8},{4,12},{9,1},{13,5},{1,9},{5,13},{10,2},{14,6},... | collective-permute-start | bytes 196616 | tf_op jit(solution)/shard_map/ppermute | solution.py:18
  16.8 2.9 %select_reduce_fusion.5 = (f32[4,256,256]{2,1,0:T(8,128)}, f32[4,256,256]{2,1,0:T(8,128)}) fusion(f32[4,8,256]{2,1,0:T(8,128)S(1)} %get-tuple-element.16, f32[4,8,256]{2,1,0:T(8,128)S(1)} %get-tuple-element.12, f32[4,8,256]{2,1,0:T(8,128)S(1)} %get-tuple-element.14), kind=kLoop, calls=%fused_computation.9 | loop fusion | flops 9961472 | bytes 2195456 | tf_op jit(solution)/shard_map/reduce_sum | solution.py:40
  19.7 2.9 %select_reduce_fusion.3 = (f32[4,256,256]{2,1,0:T(8,128)}, f32[4,256,256]{2,1,0:T(8,128)}) fusion(f32[4,8,256]{2,1,0:T(8,128)S(1)} %get-tuple-element.21, f32[4,8,256]{2,1,0:T(8,128)S(1)} %get-tuple-element.22, f32[4,8,256]{2,1,0:T(8,128)S(1)} %get-tuple-element.20), kind=kLoop, calls=%fused_computation.6 | loop fusion | flops 9961472 | bytes 2195456 | tf_op jit(solution)/shard_map/reduce_sum | solution.py:40
  22.6 1.6 %select_reduce_fusion.1 = (f32[4,256,256]{2,1,0:T(8,128)S(1)}, f32[4,256,256]{2,1,0:T(8,128)S(1)}) fusion(f32[4,8,256]{2,1,0:T(8,128)S(1)} %get-tuple-element.18, f32[4,8,256]{2,1,0:T(8,128)S(1)} %get-tuple-element.19, f32[4,8,256]{2,1,0:T(8,128)S(1)} %get-tuple-element.17), kind=kLoop, calls=%fused_computation.3 | loop fusion | flops 9961472 | bytes 2195456 | tf_op jit(solution)/shard_map/reduce_sum | solution.py:40
  25.2 0.9 %copy-done.2 = f32[4,256,256]{2,1,0:T(8,128)S(1)} copy-done((f32[4,256,256]{2,1,0:T(8,128)S(1)}, f32[4,256,256]{2,1,0:T(8,128)}, u32[]{:S(2)}) %copy-start.2) | copy-done | bytes 1048600
  26.2 1.6 %fusion.34 = f32[1024,128]{1,0:T(8,128)S(1)} fusion(f32[1024,128]{1,0:T(8,128)S(1)} %bitcast_select_fusion, f32[1024,256]{1,0:T(8,128)} %bitcast.134, f32[1024,256]{1,0:T(8,128)S(1)} %bitcast.128, f32[256,128]{1,0:T(8,128)S(1)} %copy-done.4), kind=kOutput, calls=%fused_computation.62 | convolution fusion | flops 101318656 | bytes 2162688 | tf_op jit(solution)/shard_map/dot_general | solution.py:32
  33.9 1.3 %collective-permute-done.9 = f32[128,128]{1,0:T(8,128)S(1)} collective-permute-done((f32[128,128]{1,0:T(8,128)S(1)}, f32[128,128]{1,0:T(8,128)S(1)}, u32[]{:S(2)}, u32[]{:S(2)}) %collective-permute-start.9) | collective-permute-done | bytes 65568 | tf_op jit(solution)/shard_map/ppermute | solution.py:18
  37.7 1.8 %collective-permute-start.10 = (f32[128,128]{1,0:T(8,128)S(1)}, f32[128,128]{1,0:T(8,128)S(1)}, u32[]{:S(2)}, u32[]{:S(2)}) collective-permute-start(f32[128,128]{1,0:T(8,128)S(1)} %fusion.84), channel_id=1, source_target_pairs={{4,0},{8,4},{12,8},{0,12},{5,1},{9,5},{13,9},{1,13},{6,2},{10,6},{... | collective-permute-start | bytes 196616 | tf_op jit(solution)/shard_map/ppermute | solution.py:18
  42.8 1.3 %collective-permute-done.8 = f32[128,128]{1,0:T(8,128)S(1)} collective-permute-done((f32[128,128]{1,0:T(8,128)S(1)}, f32[128,128]{1,0:T(8,128)S(1)}, u32[]{:S(2)}, u32[]{:S(2)}) %collective-permute-start.8) | collective-permute-done | bytes 65568 | tf_op jit(solution)/shard_map/ppermute | solution.py:18
  44.8 1.0 %fusion.82 = f32[256,128]{1,0:T(8,128)S(1)} fusion(f32[256,128]{1,0:T(8,128)S(1)} %constant_dynamic-update-slice_fusion, f32[1024,256]{1,0:T(8,128)S(1)} %fusion.14, f32[1024,128]{1,0:T(8,128)S(1)} %fusion.18), kind=kOutput, calls=%fused_computation.112 | convolution fusion | flops 201424896 | bytes 1835008 | tf_op jit(solution)/shard_map/dot_general | solution.py:82
  45.8 0.7 %fusion.9 = f32[1024,256]{1,0:T(8,128)S(1)} fusion(f32[1024,256]{1,0:T(8,128)S(1)} %bitcast.114, f32[1024,256]{1,0:T(8,128)S(1)} %bitcast.111, f32[1024,128]{1,0:T(8,128)S(1)} %fusion.18, f32[256,128]{1,0:T(8,128)S(1)} %fusion.82), kind=kOutput, calls=%fused_computation.22 | convolution fusion | flops 202637312 | bytes 3801088 | tf_op jit(solution)/shard_map/dot_general | solution.py:32
  46.4 1.0 %fusion.80 = f32[256,128]{1,0:T(8,128)S(1)} fusion(f32[256,128]{1,0:T(8,128)S(1)} %fusion.82, f32[1024,256]{1,0:T(8,128)S(1)} %fusion.9, f32[1024,128]{1,0:T(8,128)S(1)} %fusion.18), kind=kOutput, calls=%fused_computation.109 | convolution fusion | flops 201424896 | bytes 1835008 | tf_op jit(solution)/shard_map/dot_general | solution.py:82
  47.4 0.7 %fusion.4 = f32[1024,256]{1,0:T(8,128)S(1)} fusion(f32[1024,256]{1,0:T(8,128)S(1)} %bitcast.115, f32[1024,256]{1,0:T(8,128)S(1)} %bitcast.112, f32[1024,128]{1,0:T(8,128)S(1)} %fusion.18, f32[256,128]{1,0:T(8,128)S(1)} %fusion.80), kind=kOutput, calls=%fused_computation.16 | convolution fusion | flops 202637312 | bytes 3801088 | tf_op jit(solution)/shard_map/dot_general | solution.py:32
  48.1 1.6 %collective-permute-start.12 = (f32[256,128]{1,0:T(8,128)S(1)}, f32[256,128]{1,0:T(8,128)S(1)}, u32[]{:S(2)}, u32[]{:S(2)}) collective-permute-start(f32[256,128]{1,0:T(8,128)S(1)} %fusion.80), channel_id=1, source_target_pairs={{8,0},{12,4},{0,8},{4,12},{9,1},{13,5},{1,9},{5,13},{10,2},{14,6},... | collective-permute-start | bytes 393224 | tf_op jit(solution)/shard_map/ppermute | solution.py:18
  50.2 0.7 %fusion.106 = f32[256,128]{1,0:T(8,128)} fusion(f32[1024,128]{1,0:T(8,128)S(1)} %fusion.121, s32[]{:T(128)S(6)} %select_n.64, f32[1024,128]{1,0:T(8,128)S(1)} %fusion.18), kind=kLoop, calls=%fused_computation.148 | loop fusion | flops 98304 | bytes 393220 | tf_op jit(solution)/shard_map/sub | solution.py:91
  50.9 3.0 %collective-permute-done.12 = f32[256,128]{1,0:T(8,128)S(1)} collective-permute-done((f32[256,128]{1,0:T(8,128)S(1)}, f32[256,128]{1,0:T(8,128)S(1)}, u32[]{:S(2)}, u32[]{:S(2)}) %collective-permute-start.12) | collective-permute-done | bytes 131104 | tf_op jit(solution)/shard_map/ppermute | solution.py:18
  53.9 0.7 %copy.17 = f32[256,128]{1,0:T(8,128)} copy(f32[256,128]{1,0:T(8,128)S(1)} %collective-permute-done.12) | data formatting | bytes 262144
  (71 shorter events, 14.9 us)
Async XLA Ops:
  2.1 10.2 %collective-permute-start = (f32[3,2,8,256]{3,2,0,1:T(8,128)S(1)}, f32[3,2,8,256]{3,2,0,1:T(8,128)S(1)}, u32[]{:S(2)}, u32[]{:S(2)}) collective-permute-start(f32[3,2,8,256]{3,2,0,1:T(8,128)S(1)} %get-tuple-element.24), channel_id=1, source_target_pairs={{0,1},{1,0},{2,3},{3,2},{4,5},{5,4},{6,7},{7,6},{8,9},{9,8},{10,11... | collective-permute-start | bytes 147464 | tf_op jit(solution)/shard_map/ppermute | solution.py:25
  5.2 7.2 %collective-permute-start.1 = (f32[3,2,8,256]{3,2,0,1:T(8,128)S(1)}, f32[3,2,8,256]{3,2,0,1:T(8,128)S(1)}, u32[]{:S(2)}, u32[]{:S(2)}) collective-permute-start(f32[3,2,8,256]{3,2,0,1:T(8,128)S(1)} %get-tuple-element.24), channel_id=1, source_target_pairs={{0,2},{1,3},{2,0},{3,1},{4,6},{5,7},{6,4},{7,5},{8,10},{9,11},{10,... | collective-permute-start | bytes 147464 | tf_op jit(solution)/shard_map/ppermute | solution.py:25
  7.8 6.6 %collective-permute-start.2 = (f32[3,2,8,256]{3,2,0,1:T(8,128)S(1)}, f32[3,2,8,256]{3,2,0,1:T(8,128)S(1)}, u32[]{:S(2)}, u32[]{:S(2)}) collective-permute-start(f32[3,2,8,256]{3,2,0,1:T(8,128)S(1)} %get-tuple-element.24), channel_id=1, source_target_pairs={{0,3},{1,2},{2,1},{3,0},{4,7},{5,6},{6,5},{7,4},{8,11},{9,10},{10,... | collective-permute-start | bytes 147464 | tf_op jit(solution)/shard_map/ppermute | solution.py:25
  7.8 16.4 %collective-permute-start.3 = (f32[256,128]{1,0:T(8,128)}, f32[256,128]{1,0:T(8,128)S(1)}, u32[]{:S(2)}, u32[]{:S(2)}) collective-permute-start(f32[256,128]{1,0:T(8,128)} %param.6), channel_id=1, source_target_pairs={{0,1},{1,0},{2,3},{3,2},{4,5},{5,4},{6,7},{7,6},{8,9},{9,8},{10,11... | collective-permute-start | bytes 393224 | tf_op jit(solution)/shard_map/ppermute | solution.py:25
  8.7 15.5 %collective-permute-start.4 = (f32[256,128]{1,0:T(8,128)}, f32[256,128]{1,0:T(8,128)S(1)}, u32[]{:S(2)}, u32[]{:S(2)}) collective-permute-start(f32[256,128]{1,0:T(8,128)} %param.6), channel_id=1, source_target_pairs={{0,2},{1,3},{2,0},{3,1},{4,6},{5,7},{6,4},{7,5},{8,10},{9,11},{10,... | collective-permute-start | bytes 393224 | tf_op jit(solution)/shard_map/ppermute | solution.py:25
  12.3 11.9 %collective-permute-start.5 = (f32[256,128]{1,0:T(8,128)}, f32[256,128]{1,0:T(8,128)S(1)}, u32[]{:S(2)}, u32[]{:S(2)}) collective-permute-start(f32[256,128]{1,0:T(8,128)} %param.6), channel_id=1, source_target_pairs={{0,3},{1,2},{2,1},{3,0},{4,7},{5,6},{6,5},{7,4},{8,11},{9,10},{10,... | collective-permute-start | bytes 393224 | tf_op jit(solution)/shard_map/ppermute | solution.py:25
  15.2 4.5 %collective-permute-start.7 = (f32[2,4,8,256]{3,2,1,0:T(8,128)S(1)}, f32[2,4,8,256]{3,2,1,0:T(8,128)S(1)}, u32[]{:S(2)}, u32[]{:S(2)}) collective-permute-start(f32[2,4,8,256]{3,2,1,0:T(8,128)S(1)} %pad_maximum_fusion.2), channel_id=1, source_target_pairs={{4,0},{8,4},{12,8},{0,12},{5,1},{9,5},{13,9},{1,13},{6,2},{10,6},{... | collective-permute-start | bytes 196616 | tf_op jit(solution)/shard_map/ppermute | solution.py:18
  15.3 7.3 %collective-permute-start.11 = (f32[2,4,8,256]{3,2,1,0:T(8,128)S(1)}, f32[2,4,8,256]{3,2,1,0:T(8,128)S(1)}, u32[]{:S(2)}, u32[]{:S(2)}) collective-permute-start(f32[2,4,8,256]{3,2,1,0:T(8,128)S(1)} %pad_maximum_fusion.3), channel_id=1, source_target_pairs={{8,0},{12,4},{0,8},{4,12},{9,1},{13,5},{1,9},{5,13},{10,2},{14,6},... | collective-permute-start | bytes 196616 | tf_op jit(solution)/shard_map/ppermute | solution.py:18
  22.6 1.7 %copy-start.5 = (f32[256,128]{1,0:T(8,128)S(1)}, f32[256,128]{1,0:T(8,128)}, u32[]{:S(2)}) copy-start(f32[256,128]{1,0:T(8,128)} %param.6) | copy-start | bytes 393220
  24.3 0.9 %copy-start.4 = (f32[256,128]{1,0:T(8,128)S(1)}, f32[256,128]{1,0:T(8,128)}, u32[]{:S(2)}) copy-start(f32[256,128]{1,0:T(8,128)} %param.5) | copy-start | bytes 393220
  24.9 1.2 %copy-start.2 = (f32[4,256,256]{2,1,0:T(8,128)S(1)}, f32[4,256,256]{2,1,0:T(8,128)}, u32[]{:S(2)}) copy-start(f32[4,256,256]{2,1,0:T(8,128)} %get-tuple-element.6) | copy-start | bytes 3145732
  26.2 1.6 %copy-start.3 = (f32[4,256,256]{2,1,0:T(8,128)S(1)}, f32[4,256,256]{2,1,0:T(8,128)}, u32[]{:S(2)}) copy-start(f32[4,256,256]{2,1,0:T(8,128)} %get-tuple-element.7) | copy-start | bytes 3145732
  30.3 9.3 %collective-permute-start.6 = (f32[128,128]{1,0:T(8,128)S(1)}, f32[128,128]{1,0:T(8,128)S(1)}, u32[]{:S(2)}, u32[]{:S(2)}) collective-permute-start(f32[128,128]{1,0:T(8,128)S(1)} %fusion.96), channel_id=1, source_target_pairs={{4,0},{8,4},{12,8},{0,12},{5,1},{9,5},{13,9},{1,13},{6,2},{10,6},{... | collective-permute-start | bytes 196616 | tf_op jit(solution)/shard_map/ppermute | solution.py:18
  32.7 2.5 %copy-start = (f32[4,256,256]{2,1,0:T(8,128)S(1)}, f32[4,256,256]{2,1,0:T(8,128)}, u32[]{:S(2)}) copy-start(f32[4,256,256]{2,1,0:T(8,128)} %get-tuple-element.4) | copy-start | bytes 3145732
  32.7 2.5 %copy-start.1 = (f32[4,256,256]{2,1,0:T(8,128)S(1)}, f32[4,256,256]{2,1,0:T(8,128)}, u32[]{:S(2)}) copy-start(f32[4,256,256]{2,1,0:T(8,128)} %get-tuple-element.5) | copy-start | bytes 3145732
  32.7 2.5 %collective-permute-start.9 = (f32[128,128]{1,0:T(8,128)S(1)}, f32[128,128]{1,0:T(8,128)S(1)}, u32[]{:S(2)}, u32[]{:S(2)}) collective-permute-start(f32[128,128]{1,0:T(8,128)S(1)} %fusion.92), channel_id=1, source_target_pairs={{4,0},{8,4},{12,8},{0,12},{5,1},{9,5},{13,9},{1,13},{6,2},{10,6},{... | collective-permute-start | bytes 196616 | tf_op jit(solution)/shard_map/ppermute | solution.py:18
  37.7 6.4 %collective-permute-start.10 = (f32[128,128]{1,0:T(8,128)S(1)}, f32[128,128]{1,0:T(8,128)S(1)}, u32[]{:S(2)}, u32[]{:S(2)}) collective-permute-start(f32[128,128]{1,0:T(8,128)S(1)} %fusion.84), channel_id=1, source_target_pairs={{4,0},{8,4},{12,8},{0,12},{5,1},{9,5},{13,9},{1,13},{6,2},{10,6},{... | collective-permute-start | bytes 196616 | tf_op jit(solution)/shard_map/ppermute | solution.py:18
  42.1 2.0 %collective-permute-start.8 = (f32[128,128]{1,0:T(8,128)S(1)}, f32[128,128]{1,0:T(8,128)S(1)}, u32[]{:S(2)}, u32[]{:S(2)}) collective-permute-start(f32[128,128]{1,0:T(8,128)S(1)} %fusion.88), channel_id=1, source_target_pairs={{4,0},{8,4},{12,8},{0,12},{5,1},{9,5},{13,9},{1,13},{6,2},{10,6},{... | collective-permute-start | bytes 196616 | tf_op jit(solution)/shard_map/ppermute | solution.py:18
  48.1 5.8 %collective-permute-start.12 = (f32[256,128]{1,0:T(8,128)S(1)}, f32[256,128]{1,0:T(8,128)S(1)}, u32[]{:S(2)}, u32[]{:S(2)}) collective-permute-start(f32[256,128]{1,0:T(8,128)S(1)} %fusion.80), channel_id=1, source_target_pairs={{8,0},{12,4},{0,8},{4,12},{9,1},{13,5},{1,9},{5,13},{10,2},{14,6},... | collective-permute-start | bytes 393224 | tf_op jit(solution)/shard_map/ppermute | solution.py:18

commit v13 on v6

--- a/solution.py
+++ b/solution.py
@@ -46,14 +46,17 @@
     strata, user_count, slot_count = item_index.shape
     slab_rows, width = item_factors.shape
     signed = jnp.where(labels > 0, confidence, -confidence)
-    slots_local = jnp.stack(
-        [jnp.transpose(item_index.astype(jnp.float32), (0, 2, 1)), jnp.transpose(signed, (0, 2, 1))], 1
-    )
+    index_t = jnp.transpose(item_index.astype(jnp.float32), (0, 2, 1))
+    half = slot_count // 2
+    index_pairs = index_t[:, :half] + 256.0 * index_t[:, half:]
+    slots_local = jnp.concatenate([jnp.transpose(signed, (0, 2, 1)), index_pairs], 1)
     slots_all = gather_over(slots_local, "it")
     slabs = slots_all.shape[0]
     block = gather_over(item_factors, "it").reshape(slabs * slab_rows, width)
-    index_all = slots_all[:, :, 0]
-    signed_all = slots_all[:, :, 1]
+    high = jnp.floor(slots_all[:, :, slot_count:] * (1.0 / 256.0))
+    low = slots_all[:, :, slot_count:] - 256.0 * high
+    index_all = jnp.concatenate([low, high], 2)
+    signed_all = slots_all[:, :, :slot_count]
 
     slot_data = []
     for stratum in range(strata):

time: 52.5 us -> 59.7 us (1.14)
  starting transfers between devices: 16.5 us -> 23.2 us
    ppermute x6, starting transfers between devices: 10.1 us -> 16.8 us  [gather_over(): lax.ppermute(block, axis, [(i, i ^ k) for i in range(count)])]
    transpose x0 -> x2, other arithmetic: none -> 1.5 us  [the longest x1 0.76 us: per_device(): jnp.transpose(signed, (0, 2, 1))]
    another operation x2 -> x0, other arithmetic: 1.5 us -> none  [per_device(): jnp.stack([jnp.transpose(item_index.astype(jnp.float32), (0, 2, 1)), jnp....]
    unnamed x13 -> x12, local copies, waits for them, and re-layouts: 1.4 us -> 1.98 us
  transfers between devices with their start and end apart: 14 -> 14, of which waited for: 2 -> 3; matrix products, arithmetic and copies ran while one was open for 43% -> 42% of each run, Pallas kernels for 0% -> 0%
where the time goes in v13:
time: 59.7 us; the launch traced here: 59.3 us
  starting transfers between devices  23.2 us (39%)
  matrix products  17.8 us (30%)
  other arithmetic  10.7 us (18%)
  waiting for transfers between devices  3.38 us (6%)
  local copies, waits for them, and re-layouts  3.21 us (5%)
  between operations  1.04 us (2%)
    ppermute x6, starting transfers between devices, gather_over(): lax.ppermute(block, axis, [(i, i ^ k) for i in range(count)])  16.8 us
    dot_general x18, matrix products, residual_tile(): scores_t = jnp.dot(item_rows, user_rows.T, precision=MATMUL_PRECISION)  8.67 us
    dot_general x12, matrix products, per_device(): lax.dot_general(residual_t, block, (((0,), (0,)), ((), ())), precision=MA...  7.36 us
    reduce_sum x3, other arithmetic, build_tiles(): jnp.sum(jnp.where(matches, jnp.abs(signed_rows)[:, :, None, :], 0.0), axi...  7.36 us
    ppermute x8, starting transfers between devices, shifted(): return lax.ppermute(block, axis, route)  6.41 us
    ppermute x6, waiting for transfers between devices, gather_over(): lax.ppermute(block, axis, [(i, i ^ k) for i in range(count)])  2.29 us
    unnamed x12, local copies, waits for them, and re-layouts  1.98 us
    dot_general x3, matrix products, per_device(): jnp.dot(residual_t, jnp.concatenate(chunks, 0), precision=MATMUL_PRECISION)  1.73 us
  transfers between devices with their start and end apart: 14, of which 3 were waited for; matrix products, arithmetic and copies ran while one was open for 42% of the time, Pallas kernels for 0%

profile of v13, /device:TPU:0, one launch (start us, length us, event | category | flops | bytes accessed | tf_op | source)
XLA Modules:
  0.0 59.3 jit_solution(14542304874845258324)
XLA Ops:
  0.6 5.1 %collective-permute-start.5 = (f32[256,128]{1,0:T(8,128)}, f32[256,128]{1,0:T(8,128)S(1)}, u32[]{:S(2)}, u32[]{:S(2)}) collective-permute-start(f32[256,128]{1,0:T(8,128)} %param.6), channel_id=1, source_target_pairs={{0,3},{1,2},{2,1},{3,0},{4,7},{5,6},{6,5},{7,4},{8,11},{9,10},{10,... | collective-permute-start | bytes 393224 | tf_op jit(solution)/shard_map/ppermute | solution.py:25
  5.7 0.7 %convert_bitcast_fusion = f32[3,8,256]{2,1,0:T(8,128)S(1)} fusion(s32[3,256,8]{1,2,0:T(8,128)} %param.7), kind=kLoop, calls=%fused_computation.217 | loop fusion | flops 6144 | bytes 49152 | tf_op jit(solution)/shard_map/transpose | solution.py:49
  6.5 0.8 %fusion.146 = f32[3,8,256]{2,1,0:T(8,128)S(1)} fusion(f32[3,256,8]{1,2,0:T(8,128)} %param.9, s32[3,256,8]{1,2,0:T(8,128)} %param.8), kind=kLoop, calls=%fused_computation.216 | loop fusion | flops 18432 | bytes 73728 | tf_op jit(solution)/shard_map/transpose | solution.py:52
  7.3 2.0 %collective-permute-start.2 = (f32[3,12,256]{2,1,0:T(8,128)S(1)}, f32[3,12,256]{2,1,0:T(8,128)S(1)}, u32[]{:S(2)}, u32[]{:S(2)}) collective-permute-start(f32[3,12,256]{2,1,0:T(8,128)S(1)} %get-tuple-element.24), channel_id=1, source_target_pairs={{0,3},{1,2},{2,1},{3,0},{4,7},{5,6},{6,5},{7,4},{8,11},{9,10},{10,... | collective-permute-start | bytes 110600 | tf_op jit(solution)/shard_map/ppermute | solution.py:25
  9.2 1.1 %collective-permute-start.1 = (f32[3,12,256]{2,1,0:T(8,128)S(1)}, f32[3,12,256]{2,1,0:T(8,128)S(1)}, u32[]{:S(2)}, u32[]{:S(2)}) collective-permute-start(f32[3,12,256]{2,1,0:T(8,128)S(1)} %get-tuple-element.24), channel_id=1, source_target_pairs={{0,2},{1,3},{2,0},{3,1},{4,6},{5,7},{6,4},{7,5},{8,10},{9,11},{10,... | collective-permute-start | bytes 110600 | tf_op jit(solution)/shard_map/ppermute | solution.py:25
  10.3 1.4 %collective-permute-start = (f32[3,12,256]{2,1,0:T(8,128)S(1)}, f32[3,12,256]{2,1,0:T(8,128)S(1)}, u32[]{:S(2)}, u32[]{:S(2)}) collective-permute-start(f32[3,12,256]{2,1,0:T(8,128)S(1)} %get-tuple-element.24), channel_id=1, source_target_pairs={{0,1},{1,0},{2,3},{3,2},{4,5},{5,4},{6,7},{7,6},{8,9},{9,8},{10,11... | collective-permute-start | bytes 110600 | tf_op jit(solution)/shard_map/ppermute | solution.py:25
  11.8 2.2 %collective-permute-done.2 = f32[3,12,256]{2,1,0:T(8,128)S(1)} collective-permute-done((f32[3,12,256]{2,1,0:T(8,128)S(1)}, f32[3,12,256]{2,1,0:T(8,128)S(1)}, u32[]{:S(2)}, u32[]{:S(2)}) %collective-permute-start.2) | collective-permute-done | bytes 36896 | tf_op jit(solution)/shard_map/ppermute | solution.py:25
  14.1 7.2 %collective-permute-start.3 = (f32[256,128]{1,0:T(8,128)}, f32[256,128]{1,0:T(8,128)S(1)}, u32[]{:S(2)}, u32[]{:S(2)}) collective-permute-start(f32[256,128]{1,0:T(8,128)} %param.6), channel_id=1, source_target_pairs={{0,1},{1,0},{2,3},{3,2},{4,5},{5,4},{6,7},{7,6},{8,9},{9,8},{10,11... | collective-permute-start | bytes 393224 | tf_op jit(solution)/shard_map/ppermute | solution.py:25
  22.2 1.6 %collective-permute-start.9 = (f32[2,4,8,256]{3,2,1,0:T(8,128)S(1)}, f32[2,4,8,256]{3,2,1,0:T(8,128)S(1)}, u32[]{:S(2)}, u32[]{:S(2)}) collective-permute-start(f32[2,4,8,256]{3,2,1,0:T(8,128)S(1)} %pad_maximum_fusion.4), channel_id=1, source_target_pairs={{8,0},{12,4},{0,8},{4,12},{9,1},{13,5},{1,9},{5,13},{10,2},{14,6},... | collective-permute-start | bytes 196616 | tf_op jit(solution)/shard_map/ppermute | solution.py:18
  23.8 2.9 %select_reduce_fusion.5 = (f32[4,256,256]{2,1,0:T(8,128)}, f32[4,256,256]{2,1,0:T(8,128)}) fusion(f32[4,8,256]{2,1,0:T(8,128)S(1)} %get-tuple-element.10, f32[4,8,256]{2,1,0:T(8,128)S(1)} %get-tuple-element.14, f32[4,8,256]{2,1,0:T(8,128)S(1)} %get-tuple-element.9), kind=kLoop, calls=%fused_computation.9 | loop fusion | flops 9961472 | bytes 2195456 | tf_op jit(solution)/shard_map/reduce_sum | solution.py:40
  26.7 2.9 %select_reduce_fusion.3 = (f32[4,256,256]{2,1,0:T(8,128)}, f32[4,256,256]{2,1,0:T(8,128)}) fusion(f32[4,8,256]{2,1,0:T(8,128)S(1)} %get-tuple-element.19, f32[4,8,256]{2,1,0:T(8,128)S(1)} %get-tuple-element.20, f32[4,8,256]{2,1,0:T(8,128)S(1)} %get-tuple-element.18), kind=kLoop, calls=%fused_computation.6 | loop fusion | flops 9961472 | bytes 2195456 | tf_op jit(solution)/shard_map/reduce_sum | solution.py:40
  29.5 1.6 %select_reduce_fusion.1 = (f32[4,256,256]{2,1,0:T(8,128)S(1)}, f32[4,256,256]{2,1,0:T(8,128)S(1)}) fusion(f32[4,8,256]{2,1,0:T(8,128)S(1)} %get-tuple-element.16, f32[4,8,256]{2,1,0:T(8,128)S(1)} %get-tuple-element.17, f32[4,8,256]{2,1,0:T(8,128)S(1)} %get-tuple-element.15), kind=kLoop, calls=%fused_computation.3 | loop fusion | flops 9961472 | bytes 2195456 | tf_op jit(solution)/shard_map/reduce_sum | solution.py:40
  32.2 0.9 %copy-done.2 = f32[4,256,256]{2,1,0:T(8,128)S(1)} copy-done((f32[4,256,256]{2,1,0:T(8,128)S(1)}, f32[4,256,256]{2,1,0:T(8,128)}, u32[]{:S(2)}) %copy-start.2) | copy-done | bytes 1048600
  33.1 1.5 %fusion.37 = f32[1024,128]{1,0:T(8,128)S(1)} fusion(f32[1024,128]{1,0:T(8,128)S(1)} %bitcast_select_fusion, f32[1024,256]{1,0:T(8,128)} %bitcast.139, f32[1024,256]{1,0:T(8,128)S(1)} %bitcast.133, f32[256,128]{1,0:T(8,128)S(1)} %copy-done.4), kind=kOutput, calls=%fused_computation.68 | convolution fusion | flops 101318656 | bytes 2162688 | tf_op jit(solution)/shard_map/dot_general | solution.py:32
  34.6 0.6 %fusion.113 = f32[128,128]{1,0:T(8,128)S(1)} fusion(f32[1024,128]{1,0:T(8,128)S(1)} %fusion.37, f32[1024,128]{1,0:T(8,128)S(1)} %bitcast_select_fusion, f32[256,128]{1,0:T(8,128)S(1)} %copy-done.4), kind=kOutput, calls=%fused_computation.154 | convolution fusion | flops 100712448 | bytes 1179648 | tf_op jit(solution)/shard_map/dot_general | solution.py:82
  38.0 0.6 %fusion.117 = f32[128,128]{1,0:T(8,128)S(1)} fusion(f32[1024,128]{1,0:T(8,128)S(1)} %fusion.25, f32[1024,128]{1,0:T(8,128)S(1)} %bitcast_select_fusion, f32[256,128]{1,0:T(8,128)S(1)} %copy-done.4), kind=kOutput, calls=%fused_computation.160 | convolution fusion | flops 100712448 | bytes 1179648 | tf_op jit(solution)/shard_map/dot_general | solution.py:82
  43.8 1.0 %collective-permute-start.12 = (f32[128,128]{1,0:T(8,128)S(1)}, f32[128,128]{1,0:T(8,128)S(1)}, u32[]{:S(2)}, u32[]{:S(2)}) collective-permute-start(f32[128,128]{1,0:T(8,128)S(1)} %fusion.103), channel_id=1, source_target_pairs={{4,0},{8,4},{12,8},{0,12},{5,1},{9,5},{13,9},{1,13},{6,2},{10,6},{... | collective-permute-start | bytes 196616 | tf_op jit(solution)/shard_map/ppermute | solution.py:18
  46.7 0.6 %fusion.107 = f32[128,128]{1,0:T(8,128)S(1)} fusion(f32[128,128]{1,0:T(8,128)S(1)} %fusion.109, f32[1024,128]{1,0:T(8,128)S(1)} %fusion.53, f32[1024,128]{1,0:T(8,128)S(1)} %fusion.1), kind=kOutput, calls=%fused_computation.145 | convolution fusion | flops 100712448 | bytes 1179648 | tf_op jit(solution)/shard_map/dot_general | solution.py:82
  47.7 0.7 %collective-permute-start.8 = (f32[128,128]{1,0:T(8,128)S(1)}, f32[128,128]{1,0:T(8,128)S(1)}, u32[]{:S(2)}, u32[]{:S(2)}) collective-permute-start(f32[128,128]{1,0:T(8,128)S(1)} %fusion.107), channel_id=1, source_target_pairs={{4,0},{8,4},{12,8},{0,12},{5,1},{9,5},{13,9},{1,13},{6,2},{10,6},{... | collective-permute-start | bytes 196616 | tf_op jit(solution)/shard_map/ppermute | solution.py:18
  50.5 0.6 %fusion.95 = f32[128,128]{1,0:T(8,128)S(1)} fusion(f32[128,128]{1,0:T(8,128)S(1)} %fusion.97, f32[1024,128]{1,0:T(8,128)S(1)} %fusion.85, f32[1024,128]{1,0:T(8,128)S(1)} %fusion.3), kind=kOutput, calls=%fused_computation.127 | convolution fusion | flops 100712448 | bytes 1179648 | tf_op jit(solution)/shard_map/dot_general | solution.py:82
  54.3 1.6 %collective-permute-start.11 = (f32[128,128]{1,0:T(8,128)S(1)}, f32[128,128]{1,0:T(8,128)S(1)}, u32[]{:S(2)}, u32[]{:S(2)}) collective-permute-start(f32[128,128]{1,0:T(8,128)S(1)} %fusion.99), channel_id=1, source_target_pairs={{8,0},{12,4},{0,8},{4,12},{9,1},{13,5},{1,9},{5,13},{10,2},{14,6},... | collective-permute-start | bytes 196616 | tf_op jit(solution)/shard_map/ppermute | solution.py:18
  56.9 0.7 %fusion.129 = f32[256,128]{1,0:T(8,128)} fusion(f32[1024,128]{1,0:T(8,128)S(1)} %fusion.124, s32[]{:T(128)S(6)} %select_n.64, f32[1024,128]{1,0:T(8,128)S(1)} %fusion.3), kind=kLoop, calls=%fused_computation.176 | loop fusion | flops 98304 | bytes 393220 | tf_op jit(solution)/shard_map/sub | solution.py:91
  57.5 1.1 %collective-permute-done.11 = f32[128,128]{1,0:T(8,128)S(1)} collective-permute-done((f32[128,128]{1,0:T(8,128)S(1)}, f32[128,128]{1,0:T(8,128)S(1)}, u32[]{:S(2)}, u32[]{:S(2)}) %collective-permute-start.11) | collective-permute-done | bytes 65568 | tf_op jit(solution)/shard_map/ppermute | solution.py:18
  58.6 0.7 %pad_maximum_fusion.2 = f32[256,128]{1,0:T(8,128)} fusion(f32[128,128]{1,0:T(8,128)S(1)} %collective-permute-done.13, f32[128,128]{1,0:T(8,128)S(1)} %collective-permute-done.11), kind=kLoop, calls=%fused_computation.183 | loop fusion | flops 32768 | bytes 262144 | tf_op jit(solution)/shard_map/concatenate | solution.py:92
  (76 shorter events, 18.3 us)
Async XLA Ops:
  0.6 30.5 %collective-permute-start.5 = (f32[256,128]{1,0:T(8,128)}, f32[256,128]{1,0:T(8,128)S(1)}, u32[]{:S(2)}, u32[]{:S(2)}) collective-permute-start(f32[256,128]{1,0:T(8,128)} %param.6), channel_id=1, source_target_pairs={{0,3},{1,2},{2,1},{3,0},{4,7},{5,6},{6,5},{7,4},{8,11},{9,10},{10,... | collective-permute-start | bytes 393224 | tf_op jit(solution)/shard_map/ppermute | solution.py:25
  5.7 25.4 %collective-permute-start.4 = (f32[256,128]{1,0:T(8,128)}, f32[256,128]{1,0:T(8,128)S(1)}, u32[]{:S(2)}, u32[]{:S(2)}) collective-permute-start(f32[256,128]{1,0:T(8,128)} %param.6), channel_id=1, source_target_pairs={{0,2},{1,3},{2,0},{3,1},{4,6},{5,7},{6,4},{7,5},{8,10},{9,11},{10,... | collective-permute-start | bytes 393224 | tf_op jit(solution)/shard_map/ppermute | solution.py:25
  7.3 6.8 %collective-permute-start.2 = (f32[3,12,256]{2,1,0:T(8,128)S(1)}, f32[3,12,256]{2,1,0:T(8,128)S(1)}, u32[]{:S(2)}, u32[]{:S(2)}) collective-permute-start(f32[3,12,256]{2,1,0:T(8,128)S(1)} %get-tuple-element.24), channel_id=1, source_target_pairs={{0,3},{1,2},{2,1},{3,0},{4,7},{5,6},{6,5},{7,4},{8,11},{9,10},{10,... | collective-permute-start | bytes 110600 | tf_op jit(solution)/shard_map/ppermute | solution.py:25
  9.2 12.1 %collective-permute-start.1 = (f32[3,12,256]{2,1,0:T(8,128)S(1)}, f32[3,12,256]{2,1,0:T(8,128)S(1)}, u32[]{:S(2)}, u32[]{:S(2)}) collective-permute-start(f32[3,12,256]{2,1,0:T(8,128)S(1)} %get-tuple-element.24), channel_id=1, source_target_pairs={{0,2},{1,3},{2,0},{3,1},{4,6},{5,7},{6,4},{7,5},{8,10},{9,11},{10,... | collective-permute-start | bytes 110600 | tf_op jit(solution)/shard_map/ppermute | solution.py:25
  10.3 11.0 %collective-permute-start = (f32[3,12,256]{2,1,0:T(8,128)S(1)}, f32[3,12,256]{2,1,0:T(8,128)S(1)}, u32[]{:S(2)}, u32[]{:S(2)}) collective-permute-start(f32[3,12,256]{2,1,0:T(8,128)S(1)} %get-tuple-element.24), channel_id=1, source_target_pairs={{0,1},{1,0},{2,3},{3,2},{4,5},{5,4},{6,7},{7,6},{8,9},{9,8},{10,11... | collective-permute-start | bytes 110600 | tf_op jit(solution)/shard_map/ppermute | solution.py:25
  14.1 17.1 %collective-permute-start.3 = (f32[256,128]{1,0:T(8,128)}, f32[256,128]{1,0:T(8,128)S(1)}, u32[]{:S(2)}, u32[]{:S(2)}) collective-permute-start(f32[256,128]{1,0:T(8,128)} %param.6), channel_id=1, source_target_pairs={{0,1},{1,0},{2,3},{3,2},{4,5},{5,4},{6,7},{7,6},{8,9},{9,8},{10,11... | collective-permute-start | bytes 393224 | tf_op jit(solution)/shard_map/ppermute | solution.py:25
  22.1 4.5 %collective-permute-start.7 = (f32[2,4,8,256]{3,2,1,0:T(8,128)S(1)}, f32[2,4,8,256]{3,2,1,0:T(8,128)S(1)}, u32[]{:S(2)}, u32[]{:S(2)}) collective-permute-start(f32[2,4,8,256]{3,2,1,0:T(8,128)S(1)} %pad_maximum_fusion.3), channel_id=1, source_target_pairs={{4,0},{8,4},{12,8},{0,12},{5,1},{9,5},{13,9},{1,13},{6,2},{10,6},{... | collective-permute-start | bytes 196616 | tf_op jit(solution)/shard_map/ppermute | solution.py:18
  22.2 7.3 %collective-permute-start.9 = (f32[2,4,8,256]{3,2,1,0:T(8,128)S(1)}, f32[2,4,8,256]{3,2,1,0:T(8,128)S(1)}, u32[]{:S(2)}, u32[]{:S(2)}) collective-permute-start(f32[2,4,8,256]{3,2,1,0:T(8,128)S(1)} %pad_maximum_fusion.4), channel_id=1, source_target_pairs={{8,0},{12,4},{0,8},{4,12},{9,1},{13,5},{1,9},{5,13},{10,2},{14,6},... | collective-permute-start | bytes 196616 | tf_op jit(solution)/shard_map/ppermute | solution.py:18
  29.5 1.7 %copy-start.5 = (f32[256,128]{1,0:T(8,128)S(1)}, f32[256,128]{1,0:T(8,128)}, u32[]{:S(2)}) copy-start(f32[256,128]{1,0:T(8,128)} %param.6) | copy-start | bytes 393220
  31.3 0.9 %copy-start.4 = (f32[256,128]{1,0:T(8,128)S(1)}, f32[256,128]{1,0:T(8,128)}, u32[]{:S(2)}) copy-start(f32[256,128]{1,0:T(8,128)} %param.5) | copy-start | bytes 393220
  31.9 1.2 %copy-start.2 = (f32[4,256,256]{2,1,0:T(8,128)S(1)}, f32[4,256,256]{2,1,0:T(8,128)}, u32[]{:S(2)}) copy-start(f32[4,256,256]{2,1,0:T(8,128)} %get-tuple-element.6) | copy-start | bytes 3145732
  34.6 1.2 %copy-start.3 = (f32[4,256,256]{2,1,0:T(8,128)S(1)}, f32[4,256,256]{2,1,0:T(8,128)}, u32[]{:S(2)}) copy-start(f32[4,256,256]{2,1,0:T(8,128)} %get-tuple-element.7) | copy-start | bytes 3145732
  36.8 4.5 %collective-permute-start.10 = (f32[128,128]{1,0:T(8,128)S(1)}, f32[128,128]{1,0:T(8,128)S(1)}, u32[]{:S(2)}, u32[]{:S(2)}) collective-permute-start(f32[128,128]{1,0:T(8,128)S(1)} %fusion.111), channel_id=1, source_target_pairs={{4,0},{8,4},{12,8},{0,12},{5,1},{9,5},{13,9},{1,13},{6,2},{10,6},{... | collective-permute-start | bytes 196616 | tf_op jit(solution)/shard_map/ppermute | solution.py:18
  40.1 1.2 %copy-start = (f32[4,256,256]{2,1,0:T(8,128)S(1)}, f32[4,256,256]{2,1,0:T(8,128)}, u32[]{:S(2)}) copy-start(f32[4,256,256]{2,1,0:T(8,128)} %get-tuple-element.4) | copy-start | bytes 3145732
  40.1 1.5 %copy-start.1 = (f32[4,256,256]{2,1,0:T(8,128)S(1)}, f32[4,256,256]{2,1,0:T(8,128)}, u32[]{:S(2)}) copy-start(f32[4,256,256]{2,1,0:T(8,128)} %get-tuple-element.5) | copy-start | bytes 3145732
  40.2 5.0 %collective-permute-start.6 = (f32[128,128]{1,0:T(8,128)S(1)}, f32[128,128]{1,0:T(8,128)S(1)}, u32[]{:S(2)}, u32[]{:S(2)}) collective-permute-start(f32[128,128]{1,0:T(8,128)S(1)} %fusion.115), channel_id=1, source_target_pairs={{4,0},{8,4},{12,8},{0,12},{5,1},{9,5},{13,9},{1,13},{6,2},{10,6},{... | collective-permute-start | bytes 196616 | tf_op jit(solution)/shard_map/ppermute | solution.py:18
  43.8 5.2 %collective-permute-start.12 = (f32[128,128]{1,0:T(8,128)S(1)}, f32[128,128]{1,0:T(8,128)S(1)}, u32[]{:S(2)}, u32[]{:S(2)}) collective-permute-start(f32[128,128]{1,0:T(8,128)S(1)} %fusion.103), channel_id=1, source_target_pairs={{4,0},{8,4},{12,8},{0,12},{5,1},{9,5},{13,9},{1,13},{6,2},{10,6},{... | collective-permute-start | bytes 196616 | tf_op jit(solution)/shard_map/ppermute | solution.py:18
  47.7 4.5 %collective-permute-start.8 = (f32[128,128]{1,0:T(8,128)S(1)}, f32[128,128]{1,0:T(8,128)S(1)}, u32[]{:S(2)}, u32[]{:S(2)}) collective-permute-start(f32[128,128]{1,0:T(8,128)S(1)} %fusion.107), channel_id=1, source_target_pairs={{4,0},{8,4},{12,8},{0,12},{5,1},{9,5},{13,9},{1,13},{6,2},{10,6},{... | collective-permute-start | bytes 196616 | tf_op jit(solution)/shard_map/ppermute | solution.py:18
  51.1 6.4 %collective-permute-start.13 = (f32[128,128]{1,0:T(8,128)S(1)}, f32[128,128]{1,0:T(8,128)S(1)}, u32[]{:S(2)}, u32[]{:S(2)}) collective-permute-start(f32[128,128]{1,0:T(8,128)S(1)} %fusion.95), channel_id=1, source_target_pairs={{8,0},{12,4},{0,8},{4,12},{9,1},{13,5},{1,9},{5,13},{10,2},{14,6},... | collective-permute-start | bytes 196616 | tf_op jit(solution)/shard_map/ppermute | solution.py:18
  54.3 4.3 %collective-permute-start.11 = (f32[128,128]{1,0:T(8,128)S(1)}, f32[128,128]{1,0:T(8,128)S(1)}, u32[]{:S(2)}, u32[]{:S(2)}) collective-permute-start(f32[128,128]{1,0:T(8,128)S(1)} %fusion.99), channel_id=1, source_target_pairs={{8,0},{12,4},{0,8},{4,12},{9,1},{13,5},{1,9},{5,13},{10,2},{14,6},... | collective-permute-start | bytes 196616 | tf_op jit(solution)/shard_map/ppermute | solution.py:18

commit v14 on v13

--- a/solution.py
+++ b/solution.py
@@ -52,6 +52,7 @@
     slots_local = jnp.concatenate([jnp.transpose(signed, (0, 2, 1)), index_pairs], 1)
     slots_all = gather_over(slots_local, "it")
     slabs = slots_all.shape[0]
+    slots_all, item_factors = lax.optimization_barrier((slots_all, item_factors))
     block = gather_over(item_factors, "it").reshape(slabs * slab_rows, width)
     high = jnp.floor(slots_all[:, :, slot_count:] * (1.0 / 256.0))
     low = slots_all[:, :, slot_count:] - 256.0 * high

time: 59.7 us -> 55.3 us (0.926)
  starting transfers between devices: 23.2 us -> 16.9 us
  waiting for transfers between devices: 3.38 us -> 5.59 us
    ppermute x6, starting transfers between devices: 16.8 us -> 10.2 us  [gather_over(): lax.ppermute(block, axis, [(i, i ^ k) for i in range(count)])]
    ppermute x6, waiting for transfers between devices: 2.29 us -> 4.24 us  [gather_over(): lax.ppermute(block, axis, [(i, i ^ k) for i in range(count)])]
where the time goes in v14:
time: 55.3 us; the launch traced here: 55 us
  matrix products  17.8 us (32%)
  starting transfers between devices  16.9 us (31%)
  other arithmetic  10.7 us (19%)
  waiting for transfers between devices  5.59 us (10%)
  local copies, waits for them, and re-layouts  2.88 us (5%)
  between operations  1.06 us (2%)
    ppermute x6, starting transfers between devices, gather_over(): lax.ppermute(block, axis, [(i, i ^ k) for i in range(count)])  10.2 us
    dot_general x18, matrix products, residual_tile(): scores_t = jnp.dot(item_rows, user_rows.T, precision=MATMUL_PRECISION)  8.68 us
    dot_general x12, matrix products, per_device(): lax.dot_general(residual_t, block, (((0,), (0,)), ((), ())), precision=MA...  7.36 us
    reduce_sum x3, other arithmetic, build_tiles(): jnp.sum(jnp.where(matches, jnp.abs(signed_rows)[:, :, None, :], 0.0), axi...  7.36 us
    ppermute x8, starting transfers between devices, shifted(): return lax.ppermute(block, axis, route)  6.73 us
    ppermute x6, waiting for transfers between devices, gather_over(): lax.ppermute(block, axis, [(i, i ^ k) for i in range(count)])  4.24 us
    dot_general x3, matrix products, per_device(): jnp.dot(residual_t, jnp.concatenate(chunks, 0), precision=MATMUL_PRECISION)  1.74 us
    unnamed x12, local copies, waits for them, and re-layouts  1.64 us
  transfers between devices with their start and end apart: 14, of which 3 were waited for; matrix products, arithmetic and copies ran while one was open for 42% of the time, Pallas kernels for 0%

profile of v14, /device:TPU:0, one launch (start us, length us, event | category | flops | bytes accessed | tf_op | source)
XLA Modules:
  0.0 55.0 jit_solution(177555435772116518)
XLA Ops:
  0.6 0.8 %convert_bitcast_fusion = f32[3,8,256]{2,1,0:T(8,128)S(1)} fusion(s32[3,256,8]{1,2,0:T(8,128)} %param.7), kind=kLoop, calls=%fused_computation.217 | loop fusion | flops 6144 | bytes 49152 | tf_op jit(solution)/shard_map/transpose | solution.py:49
  1.4 0.8 %fusion.146 = f32[3,8,256]{2,1,0:T(8,128)S(1)} fusion(f32[3,256,8]{1,2,0:T(8,128)} %param.9, s32[3,256,8]{1,2,0:T(8,128)} %param.8), kind=kLoop, calls=%fused_computation.216 | loop fusion | flops 18432 | bytes 73728 | tf_op jit(solution)/shard_map/transpose | solution.py:52
  2.2 5.1 %collective-permute-start.2 = (f32[3,12,256]{2,1,0:T(8,128)S(1)}, f32[3,12,256]{2,1,0:T(8,128)S(1)}, u32[]{:S(2)}, u32[]{:S(2)}) collective-permute-start(f32[3,12,256]{2,1,0:T(8,128)S(1)} %get-tuple-element.27), channel_id=1, source_target_pairs={{0,3},{1,2},{2,1},{3,0},{4,7},{5,6},{6,5},{7,4},{8,11},{9,10},{10,... | collective-permute-start | bytes 110600 | tf_op jit(solution)/shard_map/ppermute | solution.py:25
  7.3 0.6 %collective-permute-start = (f32[3,12,256]{2,1,0:T(8,128)S(1)}, f32[3,12,256]{2,1,0:T(8,128)S(1)}, u32[]{:S(2)}, u32[]{:S(2)}) collective-permute-start(f32[3,12,256]{2,1,0:T(8,128)S(1)} %get-tuple-element.27), channel_id=1, source_target_pairs={{0,1},{1,0},{2,3},{3,2},{4,5},{5,4},{6,7},{7,6},{8,9},{9,8},{10,11... | collective-permute-start | bytes 110600 | tf_op jit(solution)/shard_map/ppermute | solution.py:25
  8.1 1.5 %collective-permute-done.2 = f32[3,12,256]{2,1,0:T(8,128)S(1)} collective-permute-done((f32[3,12,256]{2,1,0:T(8,128)S(1)}, f32[3,12,256]{2,1,0:T(8,128)S(1)}, u32[]{:S(2)}, u32[]{:S(2)}) %collective-permute-start.2) | collective-permute-done | bytes 36896 | tf_op jit(solution)/shard_map/ppermute | solution.py:25
  9.5 2.8 %collective-permute-done.1 = f32[3,12,256]{2,1,0:T(8,128)S(1)} collective-permute-done((f32[3,12,256]{2,1,0:T(8,128)S(1)}, f32[3,12,256]{2,1,0:T(8,128)S(1)}, u32[]{:S(2)}, u32[]{:S(2)}) %collective-permute-start.1) | collective-permute-done | bytes 36896 | tf_op jit(solution)/shard_map/ppermute | solution.py:25
  13.0 2.2 %collective-permute-start.5 = (f32[256,128]{1,0:T(8,128)S(1)}, f32[256,128]{1,0:T(8,128)S(1)}, u32[]{:S(2)}, u32[]{:S(2)}) collective-permute-start(f32[256,128]{1,0:T(8,128)S(1)} %copy-done.5), channel_id=1, source_target_pairs={{0,3},{1,2},{2,1},{3,0},{4,7},{5,6},{6,5},{7,4},{8,11},{9,10},{10,... | collective-permute-start | bytes 393224 | tf_op jit(solution)/shard_map/ppermute | solution.py:25
  15.2 2.3 %collective-permute-start.3 = (f32[256,128]{1,0:T(8,128)S(1)}, f32[256,128]{1,0:T(8,128)S(1)}, u32[]{:S(2)}, u32[]{:S(2)}) collective-permute-start(f32[256,128]{1,0:T(8,128)S(1)} %copy-done.5), channel_id=1, source_target_pairs={{0,1},{1,0},{2,3},{3,2},{4,5},{5,4},{6,7},{7,6},{8,9},{9,8},{10,11... | collective-permute-start | bytes 393224 | tf_op jit(solution)/shard_map/ppermute | solution.py:25
  17.6 1.6 %collective-permute-start.9 = (f32[2,4,8,256]{3,2,1,0:T(8,128)S(1)}, f32[2,4,8,256]{3,2,1,0:T(8,128)S(1)}, u32[]{:S(2)}, u32[]{:S(2)}) collective-permute-start(f32[2,4,8,256]{3,2,1,0:T(8,128)S(1)} %pad_maximum_fusion.4), channel_id=1, source_target_pairs={{8,0},{12,4},{0,8},{4,12},{9,1},{13,5},{1,9},{5,13},{10,2},{14,6},... | collective-permute-start | bytes 196616 | tf_op jit(solution)/shard_map/ppermute | solution.py:18
  19.2 2.9 %select_reduce_fusion.5 = (f32[4,256,256]{2,1,0:T(8,128)}, f32[4,256,256]{2,1,0:T(8,128)}) fusion(f32[4,8,256]{2,1,0:T(8,128)S(1)} %get-tuple-element.14, f32[4,8,256]{2,1,0:T(8,128)S(1)} %get-tuple-element.19, f32[4,8,256]{2,1,0:T(8,128)S(1)} %get-tuple-element.13), kind=kLoop, calls=%fused_computation.9 | loop fusion | flops 9961472 | bytes 2195456 | tf_op jit(solution)/shard_map/reduce_sum | solution.py:40
  22.1 2.9 %select_reduce_fusion.3 = (f32[4,256,256]{2,1,0:T(8,128)}, f32[4,256,256]{2,1,0:T(8,128)}) fusion(f32[4,8,256]{2,1,0:T(8,128)S(1)} %get-tuple-element.24, f32[4,8,256]{2,1,0:T(8,128)S(1)} %get-tuple-element.25, f32[4,8,256]{2,1,0:T(8,128)S(1)} %get-tuple-element.23), kind=kLoop, calls=%fused_computation.6 | loop fusion | flops 9961472 | bytes 2195456 | tf_op jit(solution)/shard_map/reduce_sum | solution.py:40
  25.0 1.6 %select_reduce_fusion.1 = (f32[4,256,256]{2,1,0:T(8,128)S(1)}, f32[4,256,256]{2,1,0:T(8,128)S(1)}) fusion(f32[4,8,256]{2,1,0:T(8,128)S(1)} %get-tuple-element.21, f32[4,8,256]{2,1,0:T(8,128)S(1)} %get-tuple-element.22, f32[4,8,256]{2,1,0:T(8,128)S(1)} %get-tuple-element.20), kind=kLoop, calls=%fused_computation.3 | loop fusion | flops 9961472 | bytes 2195456 | tf_op jit(solution)/shard_map/reduce_sum | solution.py:40
  27.6 0.9 %copy-done.2 = f32[4,256,256]{2,1,0:T(8,128)S(1)} copy-done((f32[4,256,256]{2,1,0:T(8,128)S(1)}, f32[4,256,256]{2,1,0:T(8,128)}, u32[]{:S(2)}) %copy-start.2) | copy-done | bytes 1048600
  28.5 1.5 %fusion.37 = f32[1024,128]{1,0:T(8,128)S(1)} fusion(f32[1024,128]{1,0:T(8,128)S(1)} %bitcast_select_fusion, f32[1024,256]{1,0:T(8,128)} %bitcast.137, f32[1024,256]{1,0:T(8,128)S(1)} %bitcast.131, f32[256,128]{1,0:T(8,128)S(1)} %copy-done.4), kind=kOutput, calls=%fused_computation.68 | convolution fusion | flops 101318656 | bytes 2162688 | tf_op jit(solution)/shard_map/dot_general | solution.py:32
  30.0 0.6 %fusion.113 = f32[128,128]{1,0:T(8,128)S(1)} fusion(f32[1024,128]{1,0:T(8,128)S(1)} %fusion.37, f32[1024,128]{1,0:T(8,128)S(1)} %bitcast_select_fusion, f32[256,128]{1,0:T(8,128)S(1)} %copy-done.4), kind=kOutput, calls=%fused_computation.154 | convolution fusion | flops 100712448 | bytes 1179648 | tf_op jit(solution)/shard_map/dot_general | solution.py:83
  33.5 0.6 %fusion.117 = f32[128,128]{1,0:T(8,128)S(1)} fusion(f32[1024,128]{1,0:T(8,128)S(1)} %fusion.25, f32[1024,128]{1,0:T(8,128)S(1)} %bitcast_select_fusion, f32[256,128]{1,0:T(8,128)S(1)} %copy-done.4), kind=kOutput, calls=%fused_computation.160 | convolution fusion | flops 100712448 | bytes 1179648 | tf_op jit(solution)/shard_map/dot_general | solution.py:83
  35.6 1.2 %collective-permute-start.6 = (f32[128,128]{1,0:T(8,128)S(1)}, f32[128,128]{1,0:T(8,128)S(1)}, u32[]{:S(2)}, u32[]{:S(2)}) collective-permute-start(f32[128,128]{1,0:T(8,128)S(1)} %fusion.115), channel_id=1, source_target_pairs={{4,0},{8,4},{12,8},{0,12},{5,1},{9,5},{13,9},{1,13},{6,2},{10,6},{... | collective-permute-start | bytes 196616 | tf_op jit(solution)/shard_map/ppermute | solution.py:18
  39.5 0.7 %collective-permute-start.12 = (f32[128,128]{1,0:T(8,128)S(1)}, f32[128,128]{1,0:T(8,128)S(1)}, u32[]{:S(2)}, u32[]{:S(2)}) collective-permute-start(f32[128,128]{1,0:T(8,128)S(1)} %fusion.103), channel_id=1, source_target_pairs={{4,0},{8,4},{12,8},{0,12},{5,1},{9,5},{13,9},{1,13},{6,2},{10,6},{... | collective-permute-start | bytes 196616 | tf_op jit(solution)/shard_map/ppermute | solution.py:18
  43.1 0.7 %collective-permute-start.8 = (f32[128,128]{1,0:T(8,128)S(1)}, f32[128,128]{1,0:T(8,128)S(1)}, u32[]{:S(2)}, u32[]{:S(2)}) collective-permute-start(f32[128,128]{1,0:T(8,128)S(1)} %fusion.107), channel_id=1, source_target_pairs={{4,0},{8,4},{12,8},{0,12},{5,1},{9,5},{13,9},{1,13},{6,2},{10,6},{... | collective-permute-start | bytes 196616 | tf_op jit(solution)/shard_map/ppermute | solution.py:18
  46.6 0.9 %collective-permute-start.13 = (f32[128,128]{1,0:T(8,128)S(1)}, f32[128,128]{1,0:T(8,128)S(1)}, u32[]{:S(2)}, u32[]{:S(2)}) collective-permute-start(f32[128,128]{1,0:T(8,128)S(1)} %fusion.95), channel_id=1, source_target_pairs={{8,0},{12,4},{0,8},{4,12},{9,1},{13,5},{1,9},{5,13},{10,2},{14,6},... | collective-permute-start | bytes 196616 | tf_op jit(solution)/shard_map/ppermute | solution.py:18
  50.0 1.3 %collective-permute-start.11 = (f32[128,128]{1,0:T(8,128)S(1)}, f32[128,128]{1,0:T(8,128)S(1)}, u32[]{:S(2)}, u32[]{:S(2)}) collective-permute-start(f32[128,128]{1,0:T(8,128)S(1)} %fusion.99), channel_id=1, source_target_pairs={{8,0},{12,4},{0,8},{4,12},{9,1},{13,5},{1,9},{5,13},{10,2},{14,6},... | collective-permute-start | bytes 196616 | tf_op jit(solution)/shard_map/ppermute | solution.py:18
  52.3 0.7 %fusion.129 = f32[256,128]{1,0:T(8,128)} fusion(f32[1024,128]{1,0:T(8,128)S(1)} %fusion.124, s32[]{:T(128)S(6)} %select_n.64, f32[1024,128]{1,0:T(8,128)S(1)} %fusion.3), kind=kLoop, calls=%fused_computation.176 | loop fusion | flops 98304 | bytes 393220 | tf_op jit(solution)/shard_map/sub | solution.py:92
  53.0 1.3 %collective-permute-done.11 = f32[128,128]{1,0:T(8,128)S(1)} collective-permute-done((f32[128,128]{1,0:T(8,128)S(1)}, f32[128,128]{1,0:T(8,128)S(1)}, u32[]{:S(2)}, u32[]{:S(2)}) %collective-permute-start.11) | collective-permute-done | bytes 65568 | tf_op jit(solution)/shard_map/ppermute | solution.py:18
  54.3 0.7 %pad_maximum_fusion.2 = f32[256,128]{1,0:T(8,128)} fusion(f32[128,128]{1,0:T(8,128)S(1)} %collective-permute-done.13, f32[128,128]{1,0:T(8,128)S(1)} %collective-permute-done.11), kind=kLoop, calls=%fused_computation.183 | loop fusion | flops 32768 | bytes 262144 | tf_op jit(solution)/shard_map/concatenate | solution.py:93
  (77 shorter events, 17.9 us)
Async XLA Ops:
  0.6 12.4 %copy-start.5 = (f32[256,128]{1,0:T(8,128)S(1)}, f32[256,128]{1,0:T(8,128)}, u32[]{:S(2)}) copy-start(f32[256,128]{1,0:T(8,128)} %param.6) | copy-start | bytes 393220
  2.2 7.3 %collective-permute-start.2 = (f32[3,12,256]{2,1,0:T(8,128)S(1)}, f32[3,12,256]{2,1,0:T(8,128)S(1)}, u32[]{:S(2)}, u32[]{:S(2)}) collective-permute-start(f32[3,12,256]{2,1,0:T(8,128)S(1)} %get-tuple-element.27), channel_id=1, source_target_pairs={{0,3},{1,2},{2,1},{3,0},{4,7},{5,6},{6,5},{7,4},{8,11},{9,10},{10,... | collective-permute-start | bytes 110600 | tf_op jit(solution)/shard_map/ppermute | solution.py:25
  7.3 5.0 %collective-permute-start.1 = (f32[3,12,256]{2,1,0:T(8,128)S(1)}, f32[3,12,256]{2,1,0:T(8,128)S(1)}, u32[]{:S(2)}, u32[]{:S(2)}) collective-permute-start(f32[3,12,256]{2,1,0:T(8,128)S(1)} %get-tuple-element.27), channel_id=1, source_target_pairs={{0,2},{1,3},{2,0},{3,1},{4,6},{5,7},{6,4},{7,5},{8,10},{9,11},{10,... | collective-permute-start | bytes 110600 | tf_op jit(solution)/shard_map/ppermute | solution.py:25
  7.3 5.0 %collective-permute-start = (f32[3,12,256]{2,1,0:T(8,128)S(1)}, f32[3,12,256]{2,1,0:T(8,128)S(1)}, u32[]{:S(2)}, u32[]{:S(2)}) collective-permute-start(f32[3,12,256]{2,1,0:T(8,128)S(1)} %get-tuple-element.27), channel_id=1, source_target_pairs={{0,1},{1,0},{2,3},{3,2},{4,5},{5,4},{6,7},{7,6},{8,9},{9,8},{10,11... | collective-permute-start | bytes 110600 | tf_op jit(solution)/shard_map/ppermute | solution.py:25
  13.0 13.6 %collective-permute-start.5 = (f32[256,128]{1,0:T(8,128)S(1)}, f32[256,128]{1,0:T(8,128)S(1)}, u32[]{:S(2)}, u32[]{:S(2)}) collective-permute-start(f32[256,128]{1,0:T(8,128)S(1)} %copy-done.5), channel_id=1, source_target_pairs={{0,3},{1,2},{2,1},{3,0},{4,7},{5,6},{6,5},{7,4},{8,11},{9,10},{10,... | collective-permute-start | bytes 393224 | tf_op jit(solution)/shard_map/ppermute | solution.py:25
  15.2 11.4 %collective-permute-start.4 = (f32[256,128]{1,0:T(8,128)S(1)}, f32[256,128]{1,0:T(8,128)S(1)}, u32[]{:S(2)}, u32[]{:S(2)}) collective-permute-start(f32[256,128]{1,0:T(8,128)S(1)} %copy-done.5), channel_id=1, source_target_pairs={{0,2},{1,3},{2,0},{3,1},{4,6},{5,7},{6,4},{7,5},{8,10},{9,11},{10,... | collective-permute-start | bytes 393224 | tf_op jit(solution)/shard_map/ppermute | solution.py:25
  15.2 11.4 %collective-permute-start.3 = (f32[256,128]{1,0:T(8,128)S(1)}, f32[256,128]{1,0:T(8,128)S(1)}, u32[]{:S(2)}, u32[]{:S(2)}) collective-permute-start(f32[256,128]{1,0:T(8,128)S(1)} %copy-done.5), channel_id=1, source_target_pairs={{0,1},{1,0},{2,3},{3,2},{4,5},{5,4},{6,7},{7,6},{8,9},{9,8},{10,11... | collective-permute-start | bytes 393224 | tf_op jit(solution)/shard_map/ppermute | solution.py:25
  17.5 4.5 %collective-permute-start.7 = (f32[2,4,8,256]{3,2,1,0:T(8,128)S(1)}, f32[2,4,8,256]{3,2,1,0:T(8,128)S(1)}, u32[]{:S(2)}, u32[]{:S(2)}) collective-permute-start(f32[2,4,8,256]{3,2,1,0:T(8,128)S(1)} %pad_maximum_fusion.3), channel_id=1, source_target_pairs={{4,0},{8,4},{12,8},{0,12},{5,1},{9,5},{13,9},{1,13},{6,2},{10,6},{... | collective-permute-start | bytes 196616 | tf_op jit(solution)/shard_map/ppermute | solution.py:18
  17.6 7.3 %collective-permute-start.9 = (f32[2,4,8,256]{3,2,1,0:T(8,128)S(1)}, f32[2,4,8,256]{3,2,1,0:T(8,128)S(1)}, u32[]{:S(2)}, u32[]{:S(2)}) collective-permute-start(f32[2,4,8,256]{3,2,1,0:T(8,128)S(1)} %pad_maximum_fusion.4), channel_id=1, source_target_pairs={{8,0},{12,4},{0,8},{4,12},{9,1},{13,5},{1,9},{5,13},{10,2},{14,6},... | collective-permute-start | bytes 196616 | tf_op jit(solution)/shard_map/ppermute | solution.py:18
  26.7 0.9 %copy-start.4 = (f32[256,128]{1,0:T(8,128)S(1)}, f32[256,128]{1,0:T(8,128)}, u32[]{:S(2)}) copy-start(f32[256,128]{1,0:T(8,128)} %param.5) | copy-start | bytes 393220
  27.3 1.2 %copy-start.2 = (f32[4,256,256]{2,1,0:T(8,128)S(1)}, f32[4,256,256]{2,1,0:T(8,128)}, u32[]{:S(2)}) copy-start(f32[4,256,256]{2,1,0:T(8,128)} %get-tuple-element.10) | copy-start | bytes 3145732
  30.0 1.2 %copy-start.3 = (f32[4,256,256]{2,1,0:T(8,128)S(1)}, f32[4,256,256]{2,1,0:T(8,128)}, u32[]{:S(2)}) copy-start(f32[4,256,256]{2,1,0:T(8,128)} %get-tuple-element.11) | copy-start | bytes 3145732
  32.3 5.1 %collective-permute-start.10 = (f32[128,128]{1,0:T(8,128)S(1)}, f32[128,128]{1,0:T(8,128)S(1)}, u32[]{:S(2)}, u32[]{:S(2)}) collective-permute-start(f32[128,128]{1,0:T(8,128)S(1)} %fusion.111), channel_id=1, source_target_pairs={{4,0},{8,4},{12,8},{0,12},{5,1},{9,5},{13,9},{1,13},{6,2},{10,6},{... | collective-permute-start | bytes 196616 | tf_op jit(solution)/shard_map/ppermute | solution.py:18
  35.5 1.8 %copy-start = (f32[4,256,256]{2,1,0:T(8,128)S(1)}, f32[4,256,256]{2,1,0:T(8,128)}, u32[]{:S(2)}) copy-start(f32[4,256,256]{2,1,0:T(8,128)} %get-tuple-element.8) | copy-start | bytes 3145732
  35.6 1.8 %copy-start.1 = (f32[4,256,256]{2,1,0:T(8,128)S(1)}, f32[4,256,256]{2,1,0:T(8,128)}, u32[]{:S(2)}) copy-start(f32[4,256,256]{2,1,0:T(8,128)} %get-tuple-element.9) | copy-start | bytes 3145732
  35.6 5.0 %collective-permute-start.6 = (f32[128,128]{1,0:T(8,128)S(1)}, f32[128,128]{1,0:T(8,128)S(1)}, u32[]{:S(2)}, u32[]{:S(2)}) collective-permute-start(f32[128,128]{1,0:T(8,128)S(1)} %fusion.115), channel_id=1, source_target_pairs={{4,0},{8,4},{12,8},{0,12},{5,1},{9,5},{13,9},{1,13},{6,2},{10,6},{... | collective-permute-start | bytes 196616 | tf_op jit(solution)/shard_map/ppermute | solution.py:18
  39.5 5.0 %collective-permute-start.12 = (f32[128,128]{1,0:T(8,128)S(1)}, f32[128,128]{1,0:T(8,128)S(1)}, u32[]{:S(2)}, u32[]{:S(2)}) collective-permute-start(f32[128,128]{1,0:T(8,128)S(1)} %fusion.103), channel_id=1, source_target_pairs={{4,0},{8,4},{12,8},{0,12},{5,1},{9,5},{13,9},{1,13},{6,2},{10,6},{... | collective-permute-start | bytes 196616 | tf_op jit(solution)/shard_map/ppermute | solution.py:18
  43.1 4.7 %collective-permute-start.8 = (f32[128,128]{1,0:T(8,128)S(1)}, f32[128,128]{1,0:T(8,128)S(1)}, u32[]{:S(2)}, u32[]{:S(2)}) collective-permute-start(f32[128,128]{1,0:T(8,128)S(1)} %fusion.107), channel_id=1, source_target_pairs={{4,0},{8,4},{12,8},{0,12},{5,1},{9,5},{13,9},{1,13},{6,2},{10,6},{... | collective-permute-start | bytes 196616 | tf_op jit(solution)/shard_map/ppermute | solution.py:18
  46.6 6.4 %collective-permute-start.13 = (f32[128,128]{1,0:T(8,128)S(1)}, f32[128,128]{1,0:T(8,128)S(1)}, u32[]{:S(2)}, u32[]{:S(2)}) collective-permute-start(f32[128,128]{1,0:T(8,128)S(1)} %fusion.95), channel_id=1, source_target_pairs={{8,0},{12,4},{0,8},{4,12},{9,1},{13,5},{1,9},{5,13},{10,2},{14,6},... | collective-permute-start | bytes 196616 | tf_op jit(solution)/shard_map/ppermute | solution.py:18
  50.0 4.3 %collective-permute-start.11 = (f32[128,128]{1,0:T(8,128)S(1)}, f32[128,128]{1,0:T(8,128)S(1)}, u32[]{:S(2)}, u32[]{:S(2)}) collective-permute-start(f32[128,128]{1,0:T(8,128)S(1)} %fusion.99), channel_id=1, source_target_pairs={{8,0},{12,4},{0,8},{4,12},{9,1},{13,5},{1,9},{5,13},{10,2},{14,6},... | collective-permute-start | bytes 196616 | tf_op jit(solution)/shard_map/ppermute | solution.py:18

commit v15 on v6

--- a/solution.py
+++ b/solution.py
@@ -30,7 +30,7 @@
 
 def residual_tile(user_rows, item_rows, weight_t, target_t):
     scores_t = jnp.dot(item_rows, user_rows.T, precision=MATMUL_PRECISION)
-    return weight_t * jax.nn.sigmoid(scores_t) - target_t
+    return weight_t * (0.5 * jnp.tanh(0.5 * scores_t) + 0.5) - target_t
 
 
 def build_tiles(index_rows, signed_rows, slab_width):

time: 52.5 us -> 54.7 us (1.042)
  other arithmetic: 10.6 us -> 12.3 us
  local copies, waits for them, and re-layouts: 2.65 us -> 3.21 us
    gather x2, local copies, waits for them, and re-layouts: 1.14 us -> 3 us  [gather_over(): return jnp.take(jnp.stack(received), order, axis=0)]
    unnamed x13 -> x11, local copies, waits for them, and re-layouts: 1.4 us -> 0.1 us
    select_n x3, other arithmetic: 0.29 us -> 1.42 us  [gather_over(): return jnp.take(jnp.stack(received), order, axis=0)]
    another operation x3, other arithmetic: 0.06 us -> 0.87 us  [gather_over(): return jnp.take(jnp.stack(received), order, axis=0)]
  transfers between devices with their start and end apart: 14 -> 14, of which waited for: 2 -> 2; matrix products, arithmetic and copies ran while one was open for 43% -> 41% of each run, Pallas kernels for 0% -> 0%
where the time goes in v15:
time: 54.7 us; the launch traced here: 54.3 us
  matrix products  17.7 us (32%)
  starting transfers between devices  16.5 us (30%)
  other arithmetic  12.3 us (22%)
  waiting for transfers between devices  3.53 us (6%)
  local copies, waits for them, and re-layouts  3.21 us (6%)
  between operations  1.03 us (2%)
    ppermute x6, starting transfers between devices, gather_over(): lax.ppermute(block, axis, [(i, i ^ k) for i in range(count)])  10.1 us
    dot_general x18, matrix products, residual_tile(): scores_t = jnp.dot(item_rows, user_rows.T, precision=MATMUL_PRECISION)  8.68 us
    dot_general x12, matrix products, per_device(): lax.dot_general(residual_t, block, (((0,), (0,)), ((), ())), precision=MA...  7.32 us
    reduce_sum x3, other arithmetic, build_tiles(): jnp.sum(jnp.where(matches, jnp.abs(signed_rows)[:, :, None, :], 0.0), axi...  7.1 us
    ppermute x8, starting transfers between devices, shifted(): return lax.ppermute(block, axis, route)  6.41 us
    gather x2, local copies, waits for them, and re-layouts, gather_over(): return jnp.take(jnp.stack(received), order, axis=0)  3 us
    ppermute x6, waiting for transfers between devices, gather_over(): lax.ppermute(block, axis, [(i, i ^ k) for i in range(count)])  2.01 us
    dot_general x3, matrix products, per_device(): jnp.dot(residual_t, jnp.concatenate(chunks, 0), precision=MATMUL_PRECISION)  1.73 us
  transfers between devices with their start and end apart: 14, of which 2 were waited for; matrix products, arithmetic and copies ran while one was open for 41% of the time, Pallas kernels for 0%

profile of v15, /device:TPU:0, one launch (start us, length us, event | category | flops | bytes accessed | tf_op | source)
XLA Modules:
  0.0 54.3 jit_solution(13019732806413473162)
XLA Ops:
  0.6 0.7 %convert_bitcast_fusion = f32[3,1,8,256]{3,2,0,1:T(8,128)S(1)} fusion(s32[3,256,8]{1,2,0:T(8,128)} %param.7), kind=kLoop, calls=%fused_computation.210 | loop fusion | flops 6144 | bytes 49152 | tf_op jit(solution)/shard_map/stack | solution.py:49
  1.4 0.8 %fusion.141 = f32[3,1,8,256]{3,2,0,1:T(8,128)S(1)} fusion(f32[3,256,8]{1,2,0:T(8,128)} %param.9, s32[3,256,8]{1,2,0:T(8,128)} %param.8), kind=kLoop, calls=%fused_computation.209 | loop fusion | flops 18432 | bytes 73728 | tf_op jit(solution)/shard_map/stack | solution.py:49
  2.1 3.1 %collective-permute-start = (f32[3,2,8,256]{3,2,0,1:T(8,128)S(1)}, f32[3,2,8,256]{3,2,0,1:T(8,128)S(1)}, u32[]{:S(2)}, u32[]{:S(2)}) collective-permute-start(f32[3,2,8,256]{3,2,0,1:T(8,128)S(1)} %get-tuple-element.24), channel_id=1, source_target_pairs={{0,1},{1,0},{2,3},{3,2},{4,5},{5,4},{6,7},{7,6},{8,9},{9,8},{10,11... | collective-permute-start | bytes 147464 | tf_op jit(solution)/shard_map/ppermute | solution.py:25
  5.2 2.6 %collective-permute-start.1 = (f32[3,2,8,256]{3,2,0,1:T(8,128)S(1)}, f32[3,2,8,256]{3,2,0,1:T(8,128)S(1)}, u32[]{:S(2)}, u32[]{:S(2)}) collective-permute-start(f32[3,2,8,256]{3,2,0,1:T(8,128)S(1)} %get-tuple-element.24), channel_id=1, source_target_pairs={{0,2},{1,3},{2,0},{3,1},{4,6},{5,7},{6,4},{7,5},{8,10},{9,11},{10,... | collective-permute-start | bytes 147464 | tf_op jit(solution)/shard_map/ppermute | solution.py:25
  7.8 0.9 %collective-permute-start.3 = (f32[256,128]{1,0:T(8,128)}, f32[256,128]{1,0:T(8,128)S(1)}, u32[]{:S(2)}, u32[]{:S(2)}) collective-permute-start(f32[256,128]{1,0:T(8,128)} %param.6), channel_id=1, source_target_pairs={{0,1},{1,0},{2,3},{3,2},{4,5},{5,4},{6,7},{7,6},{8,9},{9,8},{10,11... | collective-permute-start | bytes 393224 | tf_op jit(solution)/shard_map/ppermute | solution.py:25
  8.7 3.5 %collective-permute-start.4 = (f32[256,128]{1,0:T(8,128)}, f32[256,128]{1,0:T(8,128)S(1)}, u32[]{:S(2)}, u32[]{:S(2)}) collective-permute-start(f32[256,128]{1,0:T(8,128)} %param.6), channel_id=1, source_target_pairs={{0,2},{1,3},{2,0},{3,1},{4,6},{5,7},{6,4},{7,5},{8,10},{9,11},{10,... | collective-permute-start | bytes 393224 | tf_op jit(solution)/shard_map/ppermute | solution.py:25
  12.4 2.0 %collective-permute-done.2 = f32[3,2,8,256]{3,2,0,1:T(8,128)S(1)} collective-permute-done((f32[3,2,8,256]{3,2,0,1:T(8,128)S(1)}, f32[3,2,8,256]{3,2,0,1:T(8,128)S(1)}, u32[]{:S(2)}, u32[]{:S(2)}) %collective-permute-start.2) | collective-permute-done | bytes 49184 | tf_op jit(solution)/shard_map/ppermute | solution.py:25
  15.3 1.6 %collective-permute-start.9 = (f32[2,4,8,256]{3,2,1,0:T(8,128)S(1)}, f32[2,4,8,256]{3,2,1,0:T(8,128)S(1)}, u32[]{:S(2)}, u32[]{:S(2)}) collective-permute-start(f32[2,4,8,256]{3,2,1,0:T(8,128)S(1)} %pad_maximum_fusion.4), channel_id=1, source_target_pairs={{8,0},{12,4},{0,8},{4,12},{9,1},{13,5},{1,9},{5,13},{10,2},{14,6},... | collective-permute-start | bytes 196616 | tf_op jit(solution)/shard_map/ppermute | solution.py:18
  16.8 2.9 %select_reduce_fusion.5 = (f32[4,256,256]{2,1,0:T(8,128)}, f32[4,256,256]{2,1,0:T(8,128)}) fusion(f32[4,8,256]{2,1,0:T(8,128)S(1)} %get-tuple-element.16, f32[4,8,256]{2,1,0:T(8,128)S(1)} %get-tuple-element.12, f32[4,8,256]{2,1,0:T(8,128)S(1)} %get-tuple-element.14), kind=kLoop, calls=%fused_computation.9 | loop fusion | flops 9961472 | bytes 2195456 | tf_op jit(solution)/shard_map/reduce_sum | solution.py:40
  19.7 2.6 %select_reduce_fusion.3 = (f32[4,256,256]{2,1,0:T(8,128)S(1)}, f32[4,256,256]{2,1,0:T(8,128)}) fusion(f32[4,8,256]{2,1,0:T(8,128)S(1)} %get-tuple-element.21, f32[4,8,256]{2,1,0:T(8,128)S(1)} %get-tuple-element.22, f32[4,8,256]{2,1,0:T(8,128)S(1)} %get-tuple-element.20), kind=kLoop, calls=%fused_computation.6 | loop fusion | flops 9961472 | bytes 2195456 | tf_op jit(solution)/shard_map/reduce_sum | solution.py:40
  22.3 1.6 %select_reduce_fusion.1 = (f32[4,256,256]{2,1,0:T(8,128)S(1)}, f32[4,256,256]{2,1,0:T(8,128)S(1)}) fusion(f32[4,8,256]{2,1,0:T(8,128)S(1)} %get-tuple-element.18, f32[4,8,256]{2,1,0:T(8,128)S(1)} %get-tuple-element.19, f32[4,8,256]{2,1,0:T(8,128)S(1)} %get-tuple-element.17), kind=kLoop, calls=%fused_computation.3 | loop fusion | flops 9961472 | bytes 2195456 | tf_op jit(solution)/shard_map/reduce_sum | solution.py:40
  24.0 0.8 %pad_maximum_fusion = f32[4,256,128]{2,1,0:T(8,128)} fusion(f32[1,256,128]{2,1,0:T(8,128)S(1)} %bitcast.158, f32[1,256,128]{2,1,0:T(8,128)S(1)} %bitcast.157, f32[1,256,128]{2,1,0:T(8,128)S(1)} %bitcast.156, f32[1,256,128]{2,1,0:T(8,128)S(1)} %bitcast.155), kind=kLoop, calls=%fused_computation.171 | loop fusion | flops 393216 | bytes 1048576 | tf_op jit(solution)/shard_map/stack | solution.py:28
  24.8 2.4 %gather_fusion.1 = f32[4,256,128]{2,1,0:T(8,128)} fusion(f32[4,256,128]{2,1,0:T(8,128)} %pad_maximum_fusion, s32[1024]{0:T(1024)S(1)} %pad_clamp_fusion), kind=kCustom, calls=%fused_computation.1 | custom fusion | bytes 1048592 | tf_op jit(solution)/shard_map/jit(_take)/gather | solution.py:28
  27.3 1.3 %bitcast_select_fusion = f32[1024,128]{1,0:T(8,128)S(1)} fusion(f32[4,256,128]{2,1,0:T(8,128)} %gather_fusion.1, pred[1024]{0:T(1024)(128)(4,1)S(1)} %broadcast_in_dim.80), kind=kLoop, calls=%fused_computation.172 | loop fusion | flops 131072 | bytes 1049600 | tf_op jit(solution)/shard_map/jit(_take)/select_n | solution.py:28
  28.7 1.5 %fusion.93 = f32[1024,128]{1,0:T(8,128)S(1)} fusion(f32[1024,128]{1,0:T(8,128)S(1)} %bitcast_select_fusion, f32[1024,256]{1,0:T(8,128)} %bitcast.148, f32[1024,256]{1,0:T(8,128)S(1)} %bitcast.142, f32[256,128]{1,0:T(8,128)S(1)} %copy-done.3), kind=kOutput, calls=%fused_computation.124 | convolution fusion | flops 101318656 | bytes 2162688 | tf_op jit(solution)/shard_map/dot_general | solution.py:32
  30.7 0.6 %fusion.117 = f32[128,128]{1,0:T(8,128)S(1)} fusion(f32[1024,128]{1,0:T(8,128)S(1)} %fusion.93, f32[1024,128]{1,0:T(8,128)S(1)} %bitcast_select_fusion, f32[256,128]{1,0:T(8,128)S(1)} %copy-done.3), kind=kOutput, calls=%fused_computation.160 | convolution fusion | flops 100712448 | bytes 1179648 | tf_op jit(solution)/shard_map/dot_general | solution.py:79
  36.8 0.6 %fusion.109 = f32[128,128]{1,0:T(8,128)S(1)} fusion(f32[128,128]{1,0:T(8,128)S(1)} %collective-permute-done.6, f32[1024,128]{1,0:T(8,128)S(1)} %fusion.63, f32[1024,128]{1,0:T(8,128)S(1)} %fusion.1), kind=kOutput, calls=%fused_computation.148 | convolution fusion | flops 100712448 | bytes 1179648 | tf_op jit(solution)/shard_map/dot_general | solution.py:79
  38.9 1.3 %collective-permute-start.8 = (f32[128,128]{1,0:T(8,128)S(1)}, f32[128,128]{1,0:T(8,128)S(1)}, u32[]{:S(2)}, u32[]{:S(2)}) collective-permute-start(f32[128,128]{1,0:T(8,128)S(1)} %fusion.107), channel_id=1, source_target_pairs={{4,0},{8,4},{12,8},{0,12},{5,1},{9,5},{13,9},{1,13},{6,2},{10,6},{... | collective-permute-start | bytes 196616 | tf_op jit(solution)/shard_map/ppermute | solution.py:18
  40.6 0.6 %fusion.105 = f32[128,128]{1,0:T(8,128)S(1)} fusion(f32[128,128]{1,0:T(8,128)S(1)} %collective-permute-done.10, f32[1024,128]{1,0:T(8,128)S(1)} %fusion.48, f32[1024,128]{1,0:T(8,128)S(1)} %fusion.1), kind=kOutput, calls=%fused_computation.142 | convolution fusion | flops 100712448 | bytes 1179648 | tf_op jit(solution)/shard_map/dot_general | solution.py:79
  44.1 0.6 %fusion.101 = f32[128,128]{1,0:T(8,128)S(1)} fusion(f32[128,128]{1,0:T(8,128)S(1)} %collective-permute-done.8, f32[1024,128]{1,0:T(8,128)S(1)} %fusion.33, f32[1024,128]{1,0:T(8,128)S(1)} %fusion.3), kind=kOutput, calls=%fused_computation.136 | convolution fusion | flops 100712448 | bytes 1179648 | tf_op jit(solution)/shard_map/dot_general | solution.py:79
  49.3 1.6 %collective-permute-start.13 = (f32[128,128]{1,0:T(8,128)S(1)}, f32[128,128]{1,0:T(8,128)S(1)}, u32[]{:S(2)}, u32[]{:S(2)}) collective-permute-start(f32[128,128]{1,0:T(8,128)S(1)} %fusion.95), channel_id=1, source_target_pairs={{8,0},{12,4},{0,8},{4,12},{9,1},{13,5},{1,9},{5,13},{10,2},{14,6},... | collective-permute-start | bytes 196616 | tf_op jit(solution)/shard_map/ppermute | solution.py:18
  51.5 0.7 %fusion.129 = f32[256,128]{1,0:T(8,128)} fusion(f32[1024,128]{1,0:T(8,128)S(1)} %fusion.124, s32[]{:T(128)S(6)} %select_n.64, f32[1024,128]{1,0:T(8,128)S(1)} %fusion.3), kind=kLoop, calls=%fused_computation.176 | loop fusion | flops 98304 | bytes 393220 | tf_op jit(solution)/shard_map/sub | solution.py:88
  52.2 1.5 %collective-permute-done.13 = f32[128,128]{1,0:T(8,128)S(1)} collective-permute-done((f32[128,128]{1,0:T(8,128)S(1)}, f32[128,128]{1,0:T(8,128)S(1)}, u32[]{:S(2)}, u32[]{:S(2)}) %collective-permute-start.13) | collective-permute-done | bytes 65568 | tf_op jit(solution)/shard_map/ppermute | solution.py:18
  53.7 0.7 %pad_maximum_fusion.2 = f32[256,128]{1,0:T(8,128)} fusion(f32[128,128]{1,0:T(8,128)S(1)} %collective-permute-done.13, f32[128,128]{1,0:T(8,128)S(1)} %collective-permute-done.11), kind=kLoop, calls=%fused_computation.183 | loop fusion | flops 32768 | bytes 262144 | tf_op jit(solution)/shard_map/concatenate | solution.py:89
  (74 shorter events, 16.8 us)
Async XLA Ops:
  2.1 10.2 %collective-permute-start = (f32[3,2,8,256]{3,2,0,1:T(8,128)S(1)}, f32[3,2,8,256]{3,2,0,1:T(8,128)S(1)}, u32[]{:S(2)}, u32[]{:S(2)}) collective-permute-start(f32[3,2,8,256]{3,2,0,1:T(8,128)S(1)} %get-tuple-element.24), channel_id=1, source_target_pairs={{0,1},{1,0},{2,3},{3,2},{4,5},{5,4},{6,7},{7,6},{8,9},{9,8},{10,11... | collective-permute-start | bytes 147464 | tf_op jit(solution)/shard_map/ppermute | solution.py:25
  5.2 7.2 %collective-permute-start.1 = (f32[3,2,8,256]{3,2,0,1:T(8,128)S(1)}, f32[3,2,8,256]{3,2,0,1:T(8,128)S(1)}, u32[]{:S(2)}, u32[]{:S(2)}) collective-permute-start(f32[3,2,8,256]{3,2,0,1:T(8,128)S(1)} %get-tuple-element.24), channel_id=1, source_target_pairs={{0,2},{1,3},{2,0},{3,1},{4,6},{5,7},{6,4},{7,5},{8,10},{9,11},{10,... | collective-permute-start | bytes 147464 | tf_op jit(solution)/shard_map/ppermute | solution.py:25
  7.8 6.6 %collective-permute-start.2 = (f32[3,2,8,256]{3,2,0,1:T(8,128)S(1)}, f32[3,2,8,256]{3,2,0,1:T(8,128)S(1)}, u32[]{:S(2)}, u32[]{:S(2)}) collective-permute-start(f32[3,2,8,256]{3,2,0,1:T(8,128)S(1)} %get-tuple-element.24), channel_id=1, source_target_pairs={{0,3},{1,2},{2,1},{3,0},{4,7},{5,6},{6,5},{7,4},{8,11},{9,10},{10,... | collective-permute-start | bytes 147464 | tf_op jit(solution)/shard_map/ppermute | solution.py:25
  7.8 16.1 %collective-permute-start.3 = (f32[256,128]{1,0:T(8,128)}, f32[256,128]{1,0:T(8,128)S(1)}, u32[]{:S(2)}, u32[]{:S(2)}) collective-permute-start(f32[256,128]{1,0:T(8,128)} %param.6), channel_id=1, source_target_pairs={{0,1},{1,0},{2,3},{3,2},{4,5},{5,4},{6,7},{7,6},{8,9},{9,8},{10,11... | collective-permute-start | bytes 393224 | tf_op jit(solution)/shard_map/ppermute | solution.py:25
  8.7 15.3 %collective-permute-start.4 = (f32[256,128]{1,0:T(8,128)}, f32[256,128]{1,0:T(8,128)S(1)}, u32[]{:S(2)}, u32[]{:S(2)}) collective-permute-start(f32[256,128]{1,0:T(8,128)} %param.6), channel_id=1, source_target_pairs={{0,2},{1,3},{2,0},{3,1},{4,6},{5,7},{6,4},{7,5},{8,10},{9,11},{10,... | collective-permute-start | bytes 393224 | tf_op jit(solution)/shard_map/ppermute | solution.py:25
  12.3 11.7 %collective-permute-start.5 = (f32[256,128]{1,0:T(8,128)}, f32[256,128]{1,0:T(8,128)S(1)}, u32[]{:S(2)}, u32[]{:S(2)}) collective-permute-start(f32[256,128]{1,0:T(8,128)} %param.6), channel_id=1, source_target_pairs={{0,3},{1,2},{2,1},{3,0},{4,7},{5,6},{6,5},{7,4},{8,11},{9,10},{10,... | collective-permute-start | bytes 393224 | tf_op jit(solution)/shard_map/ppermute | solution.py:25
  15.2 4.5 %collective-permute-start.7 = (f32[2,4,8,256]{3,2,1,0:T(8,128)S(1)}, f32[2,4,8,256]{3,2,1,0:T(8,128)S(1)}, u32[]{:S(2)}, u32[]{:S(2)}) collective-permute-start(f32[2,4,8,256]{3,2,1,0:T(8,128)S(1)} %pad_maximum_fusion.3), channel_id=1, source_target_pairs={{4,0},{8,4},{12,8},{0,12},{5,1},{9,5},{13,9},{1,13},{6,2},{10,6},{... | collective-permute-start | bytes 196616 | tf_op jit(solution)/shard_map/ppermute | solution.py:18
  15.3 7.1 %collective-permute-start.9 = (f32[2,4,8,256]{3,2,1,0:T(8,128)S(1)}, f32[2,4,8,256]{3,2,1,0:T(8,128)S(1)}, u32[]{:S(2)}, u32[]{:S(2)}) collective-permute-start(f32[2,4,8,256]{3,2,1,0:T(8,128)S(1)} %pad_maximum_fusion.4), channel_id=1, source_target_pairs={{8,0},{12,4},{0,8},{4,12},{9,1},{13,5},{1,9},{5,13},{10,2},{14,6},... | collective-permute-start | bytes 196616 | tf_op jit(solution)/shard_map/ppermute | solution.py:18
  22.3 1.7 %copy-start.4 = (f32[256,128]{1,0:T(8,128)S(1)}, f32[256,128]{1,0:T(8,128)}, u32[]{:S(2)}) copy-start(f32[256,128]{1,0:T(8,128)} %param.6) | copy-start | bytes 393220
  24.8 3.8 %copy-start.3 = (f32[256,128]{1,0:T(8,128)S(1)}, f32[256,128]{1,0:T(8,128)}, u32[]{:S(2)}) copy-start(f32[256,128]{1,0:T(8,128)} %param.5) | copy-start | bytes 393220
  27.3 1.4 %copy-start.1 = (f32[4,256,256]{2,1,0:T(8,128)S(1)}, f32[4,256,256]{2,1,0:T(8,128)}, u32[]{:S(2)}) copy-start(f32[4,256,256]{2,1,0:T(8,128)} %get-tuple-element.6) | copy-start | bytes 3145732
  28.7 1.6 %copy-start.2 = (f32[4,256,256]{2,1,0:T(8,128)S(1)}, f32[4,256,256]{2,1,0:T(8,128)}, u32[]{:S(2)}) copy-start(f32[4,256,256]{2,1,0:T(8,128)} %get-tuple-element.7) | copy-start | bytes 3145732
  32.8 3.6 %collective-permute-start.6 = (f32[128,128]{1,0:T(8,128)S(1)}, f32[128,128]{1,0:T(8,128)S(1)}, u32[]{:S(2)}, u32[]{:S(2)}) collective-permute-start(f32[128,128]{1,0:T(8,128)S(1)} %fusion.115), channel_id=1, source_target_pairs={{4,0},{8,4},{12,8},{0,12},{5,1},{9,5},{13,9},{1,13},{6,2},{10,6},{... | collective-permute-start | bytes 196616 | tf_op jit(solution)/shard_map/ppermute | solution.py:18
  35.1 1.2 %copy-start = (f32[4,256,256]{2,1,0:T(8,128)S(1)}, f32[4,256,256]{2,1,0:T(8,128)}, u32[]{:S(2)}) copy-start(f32[4,256,256]{2,1,0:T(8,128)} %get-tuple-element.5) | copy-start | bytes 3145732
  35.1 5.0 %collective-permute-start.10 = (f32[128,128]{1,0:T(8,128)S(1)}, f32[128,128]{1,0:T(8,128)S(1)}, u32[]{:S(2)}, u32[]{:S(2)}) collective-permute-start(f32[128,128]{1,0:T(8,128)S(1)} %fusion.111), channel_id=1, source_target_pairs={{4,0},{8,4},{12,8},{0,12},{5,1},{9,5},{13,9},{1,13},{6,2},{10,6},{... | collective-permute-start | bytes 196616 | tf_op jit(solution)/shard_map/ppermute | solution.py:18
  38.9 4.8 %collective-permute-start.8 = (f32[128,128]{1,0:T(8,128)S(1)}, f32[128,128]{1,0:T(8,128)S(1)}, u32[]{:S(2)}, u32[]{:S(2)}) collective-permute-start(f32[128,128]{1,0:T(8,128)S(1)} %fusion.107), channel_id=1, source_target_pairs={{4,0},{8,4},{12,8},{0,12},{5,1},{9,5},{13,9},{1,13},{6,2},{10,6},{... | collective-permute-start | bytes 196616 | tf_op jit(solution)/shard_map/ppermute | solution.py:18
  42.7 4.1 %collective-permute-start.12 = (f32[128,128]{1,0:T(8,128)S(1)}, f32[128,128]{1,0:T(8,128)S(1)}, u32[]{:S(2)}, u32[]{:S(2)}) collective-permute-start(f32[128,128]{1,0:T(8,128)S(1)} %fusion.103), channel_id=1, source_target_pairs={{4,0},{8,4},{12,8},{0,12},{5,1},{9,5},{13,9},{1,13},{6,2},{10,6},{... | collective-permute-start | bytes 196616 | tf_op jit(solution)/shard_map/ppermute | solution.py:18
  46.2 5.9 %collective-permute-start.11 = (f32[128,128]{1,0:T(8,128)S(1)}, f32[128,128]{1,0:T(8,128)S(1)}, u32[]{:S(2)}, u32[]{:S(2)}) collective-permute-start(f32[128,128]{1,0:T(8,128)S(1)} %fusion.99), channel_id=1, source_target_pairs={{8,0},{12,4},{0,8},{4,12},{9,1},{13,5},{1,9},{5,13},{10,2},{14,6},... | collective-permute-start | bytes 196616 | tf_op jit(solution)/shard_map/ppermute | solution.py:18
  49.3 4.3 %collective-permute-start.13 = (f32[128,128]{1,0:T(8,128)S(1)}, f32[128,128]{1,0:T(8,128)S(1)}, u32[]{:S(2)}, u32[]{:S(2)}) collective-permute-start(f32[128,128]{1,0:T(8,128)S(1)} %fusion.95), channel_id=1, source_target_pairs={{8,0},{12,4},{0,8},{4,12},{9,1},{13,5},{1,9},{5,13},{10,2},{14,6},... | collective-permute-start | bytes 196616 | tf_op jit(solution)/shard_map/ppermute | solution.py:18

commit v16 on v6

--- a/solution.py
+++ b/solution.py
@@ -49,7 +49,7 @@
     slots_local = jnp.stack(
         [jnp.transpose(item_index.astype(jnp.float32), (0, 2, 1)), jnp.transpose(signed, (0, 2, 1))], 1
     )
-    slots_all = gather_over(slots_local, "it")
+    slots_all = lax.all_gather(slots_local, "it")
     slabs = slots_all.shape[0]
     block = gather_over(item_factors, "it").reshape(slabs * slab_rows, width)
     index_all = slots_all[:, :, 0]

time: 52.5 us -> 64.1 us (1.22)
  blocking collectives: 0 us -> 18.7 us
  starting transfers between devices: 16.5 us -> 12.1 us
  waiting for transfers between devices: 3.53 us -> 1.53 us
    all_gather x0 -> x1, blocking collectives: none -> 18.7 us  [per_device(): slots_all = lax.all_gather(slots_local, 'it')]
    ppermute x6 -> x3, starting transfers between devices: 10.1 us -> 5.68 us  [gather_over(): lax.ppermute(block, axis, [(i, i ^ k) for i in range(count)])]
    ppermute x6 -> x3, waiting for transfers between devices: 2.01 us -> 0.01 us  [gather_over(): lax.ppermute(block, axis, [(i, i ^ k) for i in range(count)])]
    another operation x2 -> x3, other arithmetic: 1.5 us -> 1.51 us  [per_device(): jnp.stack([jnp.transpose(item_index.astype(jnp.float32), (0, 2, 1)), jnp....]
  transfers between devices with their start and end apart: 14 -> 11, of which waited for: 2 -> 1; matrix products, arithmetic and copies ran while one was open for 43% -> 37% of each run, Pallas kernels for 0% -> 0%
where the time goes in v16:
time: 64.1 us; the launch traced here: 63.8 us
  blocking collectives  18.7 us (29%)
  matrix products  17.8 us (28%)
  starting transfers between devices  12.1 us (19%)
  other arithmetic  10.5 us (16%)
  local copies, waits for them, and re-layouts  2.09 us (3%)
  waiting for transfers between devices  1.53 us (2%)
  between operations  1.02 us (2%)
    all_gather x1, blocking collectives, per_device(): slots_all = lax.all_gather(slots_local, 'it')  18.7 us
    dot_general x18, matrix products, residual_tile(): scores_t = jnp.dot(item_rows, user_rows.T, precision=MATMUL_PRECISION)  8.78 us
    dot_general x12, matrix products, per_device(): lax.dot_general(residual_t, block, (((0,), (0,)), ((), ())), precision=MA...  7.32 us
    reduce_sum x3, other arithmetic, build_tiles(): jnp.sum(jnp.where(matches, jnp.abs(signed_rows)[:, :, None, :], 0.0), axi...  7.32 us
    ppermute x8, starting transfers between devices, shifted(): return lax.ppermute(block, axis, route)  6.41 us
    ppermute x3, starting transfers between devices, gather_over(): lax.ppermute(block, axis, [(i, i ^ k) for i in range(count)])  5.68 us
    dot_general x3, matrix products, per_device(): jnp.dot(residual_t, jnp.concatenate(chunks, 0), precision=MATMUL_PRECISION)  1.72 us
    ppermute x8, waiting for transfers between devices, shifted(): return lax.ppermute(block, axis, route)  1.52 us
  transfers between devices with their start and end apart: 11, of which 1 were waited for; matrix products, arithmetic and copies ran while one was open for 37% of the time, Pallas kernels for 0%

profile of v16, /device:TPU:0, one launch (start us, length us, event | category | flops | bytes accessed | tf_op | source)
XLA Modules:
  0.0 63.8 jit_solution(3085257172148378080)
XLA Ops:
  0.6 3.1 %collective-permute-start = (f32[256,128]{1,0:T(8,128)}, f32[256,128]{1,0:T(8,128)S(1)}, u32[]{:S(2)}, u32[]{:S(2)}) collective-permute-start(f32[256,128]{1,0:T(8,128)} %param.6), channel_id=1, source_target_pairs={{0,1},{1,0},{2,3},{3,2},{4,5},{5,4},{6,7},{7,6},{8,9},{9,8},{10,11... | collective-permute-start | bytes 393224 | tf_op jit(solution)/shard_map/ppermute | solution.py:25
  3.7 2.6 %collective-permute-start.1 = (f32[256,128]{1,0:T(8,128)}, f32[256,128]{1,0:T(8,128)S(1)}, u32[]{:S(2)}, u32[]{:S(2)}) collective-permute-start(f32[256,128]{1,0:T(8,128)} %param.6), channel_id=1, source_target_pairs={{0,2},{1,3},{2,0},{3,1},{4,6},{5,7},{6,4},{7,5},{8,10},{9,11},{10,... | collective-permute-start | bytes 393224 | tf_op jit(solution)/shard_map/ppermute | solution.py:25
  6.3 0.7 %convert_bitcast_fusion = f32[3,1,8,256]{3,2,0,1:T(8,128)S(1)} fusion(s32[3,256,8]{1,2,0:T(8,128)} %param.7), kind=kLoop, calls=%fused_computation.207 | loop fusion | flops 6144 | bytes 49152 | tf_op jit(solution)/shard_map/stack | solution.py:49
  7.1 0.8 %fusion.141 = f32[3,1,8,256]{3,2,0,1:T(8,128)S(1)} fusion(f32[3,256,8]{1,2,0:T(8,128)} %param.9, s32[3,256,8]{1,2,0:T(8,128)} %param.8), kind=kLoop, calls=%fused_computation.206 | loop fusion | flops 18432 | bytes 73728 | tf_op jit(solution)/shard_map/stack | solution.py:49
  7.8 18.7 %all-gather = f32[12,2,8,256]{3,2,0,1:T(8,128)S(1)} all-gather(f32[3,2,8,256]{3,2,0,1:T(8,128)S(1)} %pad_maximum_fusion.4), channel_id=2, replica_groups=mesh['grp'=2,'ub'=4,'it'=4] {'it'}, dimensions={0}, use_global_device_ids=true | all-gather | bytes 245760 | tf_op jit(solution)/shard_map/all_gather | solution.py:52
  26.7 1.6 %collective-permute-start.6 = (f32[2,4,8,256]{3,2,1,0:T(8,128)S(1)}, f32[2,4,8,256]{3,2,1,0:T(8,128)S(1)}, u32[]{:S(2)}, u32[]{:S(2)}) collective-permute-start(f32[2,4,8,256]{3,2,1,0:T(8,128)S(1)} %pad_maximum_fusion.3), channel_id=1, source_target_pairs={{8,0},{12,4},{0,8},{4,12},{9,1},{13,5},{1,9},{5,13},{10,2},{14,6},... | collective-permute-start | bytes 196616 | tf_op jit(solution)/shard_map/ppermute | solution.py:18
  28.4 2.9 %select_reduce_fusion.5 = (f32[4,256,256]{2,1,0:T(8,128)}, f32[4,256,256]{2,1,0:T(8,128)}) fusion(f32[4,8,256]{2,1,0:T(8,128)S(1)} %get-tuple-element.16, f32[4,8,256]{2,1,0:T(8,128)S(1)} %get-tuple-element.12, f32[4,8,256]{2,1,0:T(8,128)S(1)} %get-tuple-element.14), kind=kLoop, calls=%fused_computation.8 | loop fusion | flops 9961472 | bytes 2195456 | tf_op jit(solution)/shard_map/reduce_sum | solution.py:40
  31.3 2.8 %select_reduce_fusion.3 = (f32[4,256,256]{2,1,0:T(8,128)}, f32[4,256,256]{2,1,0:T(8,128)}) fusion(f32[4,8,256]{2,1,0:T(8,128)S(1)} %get-tuple-element.21, f32[4,8,256]{2,1,0:T(8,128)S(1)} %get-tuple-element.22, f32[4,8,256]{2,1,0:T(8,128)S(1)} %get-tuple-element.20), kind=kLoop, calls=%fused_computation.5 | loop fusion | flops 9961472 | bytes 2195456 | tf_op jit(solution)/shard_map/reduce_sum | solution.py:40
  34.1 1.6 %select_reduce_fusion.1 = (f32[4,256,256]{2,1,0:T(8,128)S(1)}, f32[4,256,256]{2,1,0:T(8,128)S(1)}) fusion(f32[4,8,256]{2,1,0:T(8,128)S(1)} %get-tuple-element.18, f32[4,8,256]{2,1,0:T(8,128)S(1)} %get-tuple-element.19, f32[4,8,256]{2,1,0:T(8,128)S(1)} %get-tuple-element.17), kind=kLoop, calls=%fused_computation.2 | loop fusion | flops 9961472 | bytes 2195456 | tf_op jit(solution)/shard_map/reduce_sum | solution.py:40
  36.8 0.9 %copy-done.2 = f32[4,256,256]{2,1,0:T(8,128)S(1)} copy-done((f32[4,256,256]{2,1,0:T(8,128)S(1)}, f32[4,256,256]{2,1,0:T(8,128)}, u32[]{:S(2)}) %copy-start.2) | copy-done | bytes 1048600
  37.7 1.6 %fusion.25 = f32[1024,128]{1,0:T(8,128)S(1)} fusion(f32[1024,128]{1,0:T(8,128)S(1)} %bitcast_select_fusion, f32[1024,256]{1,0:T(8,128)} %bitcast.144, f32[1024,256]{1,0:T(8,128)S(1)} %bitcast.138, f32[256,128]{1,0:T(8,128)S(1)} %copy-done.4), kind=kOutput, calls=%fused_computation.55 | convolution fusion | flops 101318656 | bytes 2162688 | tf_op jit(solution)/shard_map/dot_general | solution.py:32
  43.1 0.6 fusion.111
  47.2 0.6 fusion.107
  48.3 1.0 %collective-permute-start.5 = (f32[128,128]{1,0:T(8,128)S(1)}, f32[128,128]{1,0:T(8,128)S(1)}, u32[]{:S(2)}, u32[]{:S(2)}) collective-permute-start(f32[128,128]{1,0:T(8,128)S(1)} %fusion.107), channel_id=1, source_target_pairs={{4,0},{8,4},{12,8},{0,12},{5,1},{9,5},{13,9},{1,13},{6,2},{10,6},{... | collective-permute-start | bytes 196616 | tf_op jit(solution)/shard_map/ppermute | solution.py:18
  49.7 0.6 fusion.105
  50.7 0.6 fusion.103
  51.8 0.7 %collective-permute-start.9 = (f32[128,128]{1,0:T(8,128)S(1)}, f32[128,128]{1,0:T(8,128)S(1)}, u32[]{:S(2)}, u32[]{:S(2)}) collective-permute-start(f32[128,128]{1,0:T(8,128)S(1)} %fusion.103), channel_id=1, source_target_pairs={{4,0},{8,4},{12,8},{0,12},{5,1},{9,5},{13,9},{1,13},{6,2},{10,6},{... | collective-permute-start | bytes 196616 | tf_op jit(solution)/shard_map/ppermute | solution.py:18
  53.5 0.6 fusion.101
  56.7 0.6 fusion.97
  57.7 0.6 fusion.95
  58.8 1.6 %collective-permute-start.10 = (f32[128,128]{1,0:T(8,128)S(1)}, f32[128,128]{1,0:T(8,128)S(1)}, u32[]{:S(2)}, u32[]{:S(2)}) collective-permute-start(f32[128,128]{1,0:T(8,128)S(1)} %fusion.95), channel_id=1, source_target_pairs={{8,0},{12,4},{0,8},{4,12},{9,1},{13,5},{1,9},{5,13},{10,2},{14,6},... | collective-permute-start | bytes 196616 | tf_op jit(solution)/shard_map/ppermute | solution.py:18
  60.9 0.7 %fusion.129 = f32[256,128]{1,0:T(8,128)} fusion(f32[1024,128]{1,0:T(8,128)S(1)} %fusion.124, s32[]{:T(128)S(6)} %select_n.57, f32[1024,128]{1,0:T(8,128)S(1)} %fusion.3), kind=kLoop, calls=%fused_computation.174 | loop fusion | flops 98304 | bytes 393220 | tf_op jit(solution)/shard_map/sub | solution.py:88
  61.6 1.5 %collective-permute-done.10 = f32[128,128]{1,0:T(8,128)S(1)} collective-permute-done((f32[128,128]{1,0:T(8,128)S(1)}, f32[128,128]{1,0:T(8,128)S(1)}, u32[]{:S(2)}, u32[]{:S(2)}) %collective-permute-start.10) | collective-permute-done | bytes 65568 | tf_op jit(solution)/shard_map/ppermute | solution.py:18
  63.1 0.7 %pad_maximum_fusion.1 = f32[256,128]{1,0:T(8,128)} fusion(f32[128,128]{1,0:T(8,128)S(1)} %collective-permute-done.10, f32[128,128]{1,0:T(8,128)S(1)} %collective-permute-done.8), kind=kLoop, calls=%fused_computation.181 | loop fusion | flops 32768 | bytes 262144 | tf_op jit(solution)/shard_map/concatenate | solution.py:89
  (68 shorter events, 15.0 us)
Async XLA Ops:
  0.6 35.1 %collective-permute-start = (f32[256,128]{1,0:T(8,128)}, f32[256,128]{1,0:T(8,128)S(1)}, u32[]{:S(2)}, u32[]{:S(2)}) collective-permute-start(f32[256,128]{1,0:T(8,128)} %param.6), channel_id=1, source_target_pairs={{0,1},{1,0},{2,3},{3,2},{4,5},{5,4},{6,7},{7,6},{8,9},{9,8},{10,11... | collective-permute-start | bytes 393224 | tf_op jit(solution)/shard_map/ppermute | solution.py:25
  3.7 32.1 %collective-permute-start.1 = (f32[256,128]{1,0:T(8,128)}, f32[256,128]{1,0:T(8,128)S(1)}, u32[]{:S(2)}, u32[]{:S(2)}) collective-permute-start(f32[256,128]{1,0:T(8,128)} %param.6), channel_id=1, source_target_pairs={{0,2},{1,3},{2,0},{3,1},{4,6},{5,7},{6,4},{7,5},{8,10},{9,11},{10,... | collective-permute-start | bytes 393224 | tf_op jit(solution)/shard_map/ppermute | solution.py:25
  6.3 29.5 %collective-permute-start.2 = (f32[256,128]{1,0:T(8,128)}, f32[256,128]{1,0:T(8,128)S(1)}, u32[]{:S(2)}, u32[]{:S(2)}) collective-permute-start(f32[256,128]{1,0:T(8,128)} %param.6), channel_id=1, source_target_pairs={{0,3},{1,2},{2,1},{3,0},{4,7},{5,6},{6,5},{7,4},{8,11},{9,10},{10,... | collective-permute-start | bytes 393224 | tf_op jit(solution)/shard_map/ppermute | solution.py:25
  26.6 4.6 %collective-permute-start.4 = (f32[2,4,8,256]{3,2,1,0:T(8,128)S(1)}, f32[2,4,8,256]{3,2,1,0:T(8,128)S(1)}, u32[]{:S(2)}, u32[]{:S(2)}) collective-permute-start(f32[2,4,8,256]{3,2,1,0:T(8,128)S(1)} %pad_maximum_fusion.2), channel_id=1, source_target_pairs={{4,0},{8,4},{12,8},{0,12},{5,1},{9,5},{13,9},{1,13},{6,2},{10,6},{... | collective-permute-start | bytes 196616 | tf_op jit(solution)/shard_map/ppermute | solution.py:18
  26.7 7.4 %collective-permute-start.6 = (f32[2,4,8,256]{3,2,1,0:T(8,128)S(1)}, f32[2,4,8,256]{3,2,1,0:T(8,128)S(1)}, u32[]{:S(2)}, u32[]{:S(2)}) collective-permute-start(f32[2,4,8,256]{3,2,1,0:T(8,128)S(1)} %pad_maximum_fusion.3), channel_id=1, source_target_pairs={{8,0},{12,4},{0,8},{4,12},{9,1},{13,5},{1,9},{5,13},{10,2},{14,6},... | collective-permute-start | bytes 196616 | tf_op jit(solution)/shard_map/ppermute | solution.py:18
  34.1 1.7 %copy-start.5 = (f32[256,128]{1,0:T(8,128)S(1)}, f32[256,128]{1,0:T(8,128)}, u32[]{:S(2)}) copy-start(f32[256,128]{1,0:T(8,128)} %param.6) | copy-start | bytes 393220
  35.8 0.9 %copy-start.4 = (f32[256,128]{1,0:T(8,128)S(1)}, f32[256,128]{1,0:T(8,128)}, u32[]{:S(2)}) copy-start(f32[256,128]{1,0:T(8,128)} %param.5) | copy-start | bytes 393220
  36.4 1.2 %copy-start.2 = (f32[4,256,256]{2,1,0:T(8,128)S(1)}, f32[4,256,256]{2,1,0:T(8,128)}, u32[]{:S(2)}) copy-start(f32[4,256,256]{2,1,0:T(8,128)} %get-tuple-element.6) | copy-start | bytes 3145732
  37.7 1.6 %copy-start.3 = (f32[4,256,256]{2,1,0:T(8,128)S(1)}, f32[4,256,256]{2,1,0:T(8,128)}, u32[]{:S(2)}) copy-start(f32[4,256,256]{2,1,0:T(8,128)} %get-tuple-element.7) | copy-start | bytes 3145732
  41.8 3.6 %collective-permute-start.3 = (f32[128,128]{1,0:T(8,128)S(1)}, f32[128,128]{1,0:T(8,128)S(1)}, u32[]{:S(2)}, u32[]{:S(2)}) collective-permute-start(f32[128,128]{1,0:T(8,128)S(1)} %fusion.115), channel_id=1, source_target_pairs={{4,0},{8,4},{12,8},{0,12},{5,1},{9,5},{13,9},{1,13},{6,2},{10,6},{... | collective-permute-start | bytes 196616 | tf_op jit(solution)/shard_map/ppermute | solution.py:18
  44.2 1.2 %copy-start = (f32[4,256,256]{2,1,0:T(8,128)S(1)}, f32[4,256,256]{2,1,0:T(8,128)}, u32[]{:S(2)}) copy-start(f32[4,256,256]{2,1,0:T(8,128)} %get-tuple-element.4) | copy-start | bytes 3145732
  44.2 1.5 %copy-start.1 = (f32[4,256,256]{2,1,0:T(8,128)S(1)}, f32[4,256,256]{2,1,0:T(8,128)}, u32[]{:S(2)}) copy-start(f32[4,256,256]{2,1,0:T(8,128)} %get-tuple-element.5) | copy-start | bytes 3145732
  44.2 5.0 %collective-permute-start.7 = (f32[128,128]{1,0:T(8,128)S(1)}, f32[128,128]{1,0:T(8,128)S(1)}, u32[]{:S(2)}, u32[]{:S(2)}) collective-permute-start(f32[128,128]{1,0:T(8,128)S(1)} %fusion.111), channel_id=1, source_target_pairs={{4,0},{8,4},{12,8},{0,12},{5,1},{9,5},{13,9},{1,13},{6,2},{10,6},{... | collective-permute-start | bytes 196616 | tf_op jit(solution)/shard_map/ppermute | solution.py:18
  48.3 4.8 %collective-permute-start.5 = (f32[128,128]{1,0:T(8,128)S(1)}, f32[128,128]{1,0:T(8,128)S(1)}, u32[]{:S(2)}, u32[]{:S(2)}) collective-permute-start(f32[128,128]{1,0:T(8,128)S(1)} %fusion.107), channel_id=1, source_target_pairs={{4,0},{8,4},{12,8},{0,12},{5,1},{9,5},{13,9},{1,13},{6,2},{10,6},{... | collective-permute-start | bytes 196616 | tf_op jit(solution)/shard_map/ppermute | solution.py:18
  51.8 4.4 %collective-permute-start.9 = (f32[128,128]{1,0:T(8,128)S(1)}, f32[128,128]{1,0:T(8,128)S(1)}, u32[]{:S(2)}, u32[]{:S(2)}) collective-permute-start(f32[128,128]{1,0:T(8,128)S(1)} %fusion.103), channel_id=1, source_target_pairs={{4,0},{8,4},{12,8},{0,12},{5,1},{9,5},{13,9},{1,13},{6,2},{10,6},{... | collective-permute-start | bytes 196616 | tf_op jit(solution)/shard_map/ppermute | solution.py:18
  55.6 6.0 %collective-permute-start.8 = (f32[128,128]{1,0:T(8,128)S(1)}, f32[128,128]{1,0:T(8,128)S(1)}, u32[]{:S(2)}, u32[]{:S(2)}) collective-permute-start(f32[128,128]{1,0:T(8,128)S(1)} %fusion.99), channel_id=1, source_target_pairs={{8,0},{12,4},{0,8},{4,12},{9,1},{13,5},{1,9},{5,13},{10,2},{14,6},... | collective-permute-start | bytes 196616 | tf_op jit(solution)/shard_map/ppermute | solution.py:18
  58.8 4.3 %collective-permute-start.10 = (f32[128,128]{1,0:T(8,128)S(1)}, f32[128,128]{1,0:T(8,128)S(1)}, u32[]{:S(2)}, u32[]{:S(2)}) collective-permute-start(f32[128,128]{1,0:T(8,128)S(1)} %fusion.95), channel_id=1, source_target_pairs={{8,0},{12,4},{0,8},{4,12},{9,1},{13,5},{1,9},{5,13},{10,2},{14,6},... | collective-permute-start | bytes 196616 | tf_op jit(solution)/shard_map/ppermute | solution.py:18

commit v17 on v16

--- a/solution.py
+++ b/solution.py
@@ -28,6 +28,25 @@
     return jnp.take(jnp.stack(received), order, axis=0)
 
 
+def gather_both(slab, slots, axis):
+    count = lax.axis_size(axis)
+    me = lax.axis_index(axis)
+    flat_slab, flat_slots = slab.reshape(-1), slots.reshape(-1)
+    slab_from, slots_from = [flat_slab], [flat_slots]
+    for k in range(1, count):
+        pairs = [(i, i ^ k) for i in range(count)]
+        if k == 1:
+            both = lax.ppermute(jnp.concatenate([flat_slots, flat_slab]), axis, pairs)
+            slots_from.append(both[: flat_slots.size])
+            slab_from.append(both[flat_slots.size :])
+        else:
+            slots_from.append(lax.ppermute(flat_slots, axis, pairs))
+            slab_from.append(lax.ppermute(flat_slab, axis, pairs))
+    order = jnp.arange(count, dtype=jnp.int32) ^ me
+    slots_all = jnp.take(jnp.stack(slots_from), order, axis=0)
+    return jnp.stack(slab_from), order, slots_all.reshape((count,) + slots.shape)
+
+
 def residual_tile(user_rows, item_rows, weight_t, target_t):
     scores_t = jnp.dot(item_rows, user_rows.T, precision=MATMUL_PRECISION)
     return weight_t * jax.nn.sigmoid(scores_t) - target_t
@@ -49,9 +68,8 @@
     slots_local = jnp.stack(
         [jnp.transpose(item_index.astype(jnp.float32), (0, 2, 1)), jnp.transpose(signed, (0, 2, 1))], 1
     )
-    slots_all = lax.all_gather(slots_local, "it")
+    slab_stack, order, slots_all = gather_both(item_factors, slots_local, "it")
     slabs = slots_all.shape[0]
-    block = gather_over(item_factors, "it").reshape(slabs * slab_rows, width)
     index_all = slots_all[:, :, 0]
     signed_all = slots_all[:, :, 1]
 
@@ -69,6 +87,9 @@
         if stratum > 0:
             chunks = [shifted(chunk, "ub", 1) for chunk in chunks]
         weight, target = build_tiles(slot_data[stratum][0], slot_data[stratum][1], slab_rows)
+        if stratum == 0:
+            slab_stack, weight, target = lax.optimization_barrier((slab_stack, weight, target))
+            block = jnp.take(slab_stack, order, axis=0).reshape(slabs * slab_rows, width)
         finished = []
         residuals = []
         for k, chunk in enumerate(chunks):

time: 64.1 us -> 59.9 us (0.934)
  blocking collectives: 18.7 us -> 0 us
  waiting for transfers between devices: 1.53 us -> 13 us
  starting transfers between devices: 12.1 us -> 15.9 us
  other arithmetic: 10.5 us -> 9.47 us
    all_gather x1 -> x0, blocking collectives: 18.7 us -> none  [per_device(): slots_all = lax.all_gather(slots_local, 'it')]
    ppermute x3 -> x5, waiting for transfers between devices: 0.01 us -> 9.95 us  [the longest x1 9.94 us: gather_both(): both = lax.ppermute(jnp.concatenate([flat_slots, flat_slab]), axis, pairs)]
    reduce_sum x3 -> x2, other arithmetic: 7.32 us -> 3.23 us  [build_tiles(): jnp.sum(jnp.where(matches, jnp.abs(signed_rows)[:, :, None, :], 0.0), axi...]
    ppermute x3 -> x5, starting transfers between devices: 5.68 us -> 9 us  [the longest x2 5.45 us: gather_both(): slots_from.append(lax.ppermute(flat_slots, axis, pairs))]
    reduce_sum x0 -> x1, other arithmetic: none -> 1.6 us  [build_tiles(): jnp.sum(jnp.where(matches, jnp.maximum(signed_rows, 0.0)[:, :, None, :],...]
    ppermute x8, waiting for transfers between devices: 1.52 us -> 3.03 us  [shifted(): return lax.ppermute(block, axis, route)]
    gather x1 -> x3, local copies, waits for them, and re-layouts: 0.58 us -> 1.82 us  [the longest x2 1.17 us: per_device(): jnp.take(slab_stack, order, axis=0).reshape(slabs * slab_rows, width)]
    concatenate x0 -> x1, other arithmetic: none -> 0.95 us  [gather_both(): both = lax.ppermute(jnp.concatenate([flat_slots, flat_slab]), axis, pairs)]
  transfers between devices with their start and end apart: 11 -> 13, of which waited for: 1 -> 3; matrix products, arithmetic and copies ran while one was open for 37% -> 37% of each run, Pallas kernels for 0% -> 0%
where the time goes in v17:
time: 59.9 us; the launch traced here: 59.7 us
  matrix products  17.7 us (30%)
  starting transfers between devices  15.9 us (27%)
  waiting for transfers between devices  13 us (22%)
  other arithmetic  9.47 us (16%)
  local copies, waits for them, and re-layouts  2.61 us (4%)
  between operations  1.03 us (2%)
    ppermute x1, waiting for transfers between devices, gather_both(): both = lax.ppermute(jnp.concatenate([flat_slots, flat_slab]), axis, pairs)  9.94 us
    dot_general x18, matrix products, residual_tile(): scores_t = jnp.dot(item_rows, user_rows.T, precision=MATMUL_PRECISION)  8.03 us
    dot_general x12, matrix products, per_device(): lax.dot_general(residual_t, block, (((0,), (0,)), ((), ())), precision=MA...  7.89 us
    ppermute x8, starting transfers between devices, shifted(): return lax.ppermute(block, axis, route)  6.91 us
    ppermute x2, starting transfers between devices, gather_both(): slots_from.append(lax.ppermute(flat_slots, axis, pairs))  5.45 us
    reduce_sum x2, other arithmetic, build_tiles(): jnp.sum(jnp.where(matches, jnp.abs(signed_rows)[:, :, None, :], 0.0), axi...  3.23 us
    ppermute x8, waiting for transfers between devices, shifted(): return lax.ppermute(block, axis, route)  3.03 us
    ppermute x2, starting transfers between devices, gather_both(): slab_from.append(lax.ppermute(flat_slab, axis, pairs))  2.59 us
  transfers between devices with their start and end apart: 13, of which 3 were waited for; matrix products, arithmetic and copies ran while one was open for 37% of the time, Pallas kernels for 0%

profile of v17, /device:TPU:0, one launch (start us, length us, event | category | flops | bytes accessed | tf_op | source)
XLA Modules:
  0.0 59.7 jit_solution(4199051732546018047)
XLA Ops:
  0.6 0.7 %convert_bitcast_fusion = f32[3,1,8,256]{3,2,0,1:T(8,128)S(1)} fusion(s32[3,256,8]{1,2,0:T(8,128)} %param.7), kind=kLoop, calls=%fused_computation.211 | loop fusion | flops 6144 | bytes 49152 | tf_op jit(solution)/shard_map/stack | solution.py:68
  1.4 0.8 %fusion.141 = f32[3,1,8,256]{3,2,0,1:T(8,128)S(1)} fusion(f32[3,256,8]{1,2,0:T(8,128)} %param.9, s32[3,256,8]{1,2,0:T(8,128)} %param.8), kind=kLoop, calls=%fused_computation.210 | loop fusion | flops 18432 | bytes 73728 | tf_op jit(solution)/shard_map/stack | solution.py:68
  2.2 4.1 %collective-permute-start.3 = (f32[12288]{0:T(1024)S(1)}, f32[12288]{0:T(1024)S(1)}, u32[]{:S(2)}, u32[]{:S(2)}) collective-permute-start(f32[12288]{0:T(1024)S(1)} %bitcast.158), channel_id=1, source_target_pairs={{0,2},{1,3},{2,0},{3,1},{4,6},{5,7},{6,4},{7,5},{8,10},{9,11},{10,... | collective-permute-start | bytes 147464 | tf_op jit(solution)/shard_map/ppermute | solution.py:43
  6.3 1.3 %collective-permute-start.4 = (f32[12288]{0:T(1024)S(1)}, f32[12288]{0:T(1024)S(1)}, u32[]{:S(2)}, u32[]{:S(2)}) collective-permute-start(f32[12288]{0:T(1024)S(1)} %bitcast.159), channel_id=1, source_target_pairs={{0,3},{1,2},{2,1},{3,0},{4,7},{5,6},{6,5},{7,4},{8,11},{9,10},{10,... | collective-permute-start | bytes 147464 | tf_op jit(solution)/shard_map/ppermute | solution.py:43
  7.6 1.7 %collective-permute-start.1 = (f32[32768]{0:T(1024)}, f32[32768]{0:T(1024)S(1)}, u32[]{:S(2)}, u32[]{:S(2)}) collective-permute-start(f32[32768]{0:T(1024)} %bitcast.151), channel_id=1, source_target_pairs={{0,2},{1,3},{2,0},{3,1},{4,6},{5,7},{6,4},{7,5},{8,10},{9,11},{10,... | collective-permute-start | bytes 393224 | tf_op jit(solution)/shard_map/ppermute | solution.py:44
  9.3 0.9 %collective-permute-start.2 = (f32[32768]{0:T(1024)}, f32[32768]{0:T(1024)S(1)}, u32[]{:S(2)}, u32[]{:S(2)}) collective-permute-start(f32[32768]{0:T(1024)} %bitcast.152), channel_id=1, source_target_pairs={{0,3},{1,2},{2,1},{3,0},{4,7},{5,6},{6,5},{7,4},{8,11},{9,10},{10,... | collective-permute-start | bytes 393224 | tf_op jit(solution)/shard_map/ppermute | solution.py:44
  10.2 0.9 %pad_maximum_fusion.2 = f32[45056]{0:T(1024)S(1)} fusion(f32[32768]{0:T(1024)} %bitcast.153, f32[12288]{0:T(1024)S(1)} %bitcast.160), kind=kLoop, calls=%fused_computation.174 | loop fusion | flops 45056 | bytes 360448 | tf_op jit(solution)/shard_map/concatenate | solution.py:39
  11.2 1.0 %collective-permute-start = (f32[45056]{0:T(1024)S(1)}, f32[45056]{0:T(1024)S(1)}, u32[]{:S(2)}, u32[]{:S(2)}) collective-permute-start(f32[45056]{0:T(1024)S(1)} %pad_maximum_fusion.2), channel_id=1, source_target_pairs={{0,1},{1,0},{2,3},{3,2},{4,5},{5,4},{6,7},{7,6},{8,9},{9,8},{10,11... | collective-permute-start | bytes 540680 | tf_op jit(solution)/shard_map/ppermute | solution.py:39
  12.3 9.9 %collective-permute-done = f32[45056]{0:T(1024)S(1)} collective-permute-done((f32[45056]{0:T(1024)S(1)}, f32[45056]{0:T(1024)S(1)}, u32[]{:S(2)}, u32[]{:S(2)}) %collective-permute-start) | collective-permute-done | bytes 180256 | tf_op jit(solution)/shard_map/ppermute | solution.py:39
  23.4 1.6 %select_reduce_fusion.4 = (f32[4,256,256]{2,1,0:T(8,128)S(1)}, f32[4,256,256]{2,1,0:T(8,128)S(1)}) fusion(f32[4,8,256]{2,1,0:T(8,128)S(1)} %get-tuple-element.20, f32[4,8,256]{2,1,0:T(8,128)S(1)} %get-tuple-element.18, f32[4,8,256]{2,1,0:T(8,128)S(1)} %get-tuple-element.22), kind=kLoop, calls=%fused_computation.8 | loop fusion | flops 9961472 | bytes 2195456 | tf_op jit(solution)/shard_map/reduce_sum | solution.py:60
  25.5 0.8 %gather_fusion.1 = f32[4,32768]{1,0:T(4,128)S(1)} fusion(f32[4,32768]{1,0:T(4,128)S(1)} %pad_maximum_fusion, s32[1024]{0:T(1024)S(1)} %pad_clamp_fusion), kind=kCustom, calls=%fused_computation.1 | custom fusion | bytes 1048592 | tf_op jit(solution)/shard_map/jit(_take)/gather | solution.py:92
  28.2 0.8 %fusion.117 = f32[128,128]{1,0:T(8,128)S(1)} fusion(f32[1024,128]{1,0:T(8,128)S(1)} %fusion.25, f32[256,128]{1,0:T(8,128)S(1)} %copy-done.1, f32[1024,128]{1,0:T(8,128)S(1)} %gather.15, pred[1024]{0:T(1024)(128)(4,1)S(1)} %broadcast_in_dim.81), kind=kOutput, calls=%fused_computation.160 | convolution fusion | flops 100843520 | bytes 1180672 | tf_op jit(solution)/shard_map/dot_general | solution.py:100
  29.5 0.8 %fusion.115 = f32[128,128]{1,0:T(8,128)S(1)} fusion(f32[128,128]{1,0:T(8,128)S(1)} %fusion.117, f32[1024,128]{1,0:T(8,128)S(1)} %fusion.29, f32[1024,128]{1,0:T(8,128)S(1)} %gather.15, pred[1024]{0:T(1024)(128)(4,1)S(1)} %broadcast_in_dim.81), kind=kOutput, calls=%fused_computation.157 | convolution fusion | flops 100843520 | bytes 1180672 | tf_op jit(solution)/shard_map/dot_general | solution.py:100
  30.9 0.8 %fusion.113 = f32[128,128]{1,0:T(8,128)S(1)} fusion(f32[1024,128]{1,0:T(8,128)S(1)} %fusion.37, f32[256,128]{1,0:T(8,128)S(1)} %copy-done.1, f32[1024,128]{1,0:T(8,128)S(1)} %gather.15, pred[1024]{0:T(1024)(128)(4,1)S(1)} %broadcast_in_dim.81), kind=kOutput, calls=%fused_computation.154 | convolution fusion | flops 100843520 | bytes 1180672 | tf_op jit(solution)/shard_map/dot_general | solution.py:100
  32.1 0.8 %fusion.111 = f32[128,128]{1,0:T(8,128)S(1)} fusion(f32[128,128]{1,0:T(8,128)S(1)} %fusion.113, f32[1024,128]{1,0:T(8,128)S(1)} %fusion.41, f32[1024,128]{1,0:T(8,128)S(1)} %gather.15, pred[1024]{0:T(1024)(128)(4,1)S(1)} %broadcast_in_dim.81), kind=kOutput, calls=%fused_computation.151 | convolution fusion | flops 100843520 | bytes 1180672 | tf_op jit(solution)/shard_map/dot_general | solution.py:100
  33.4 1.6 %collective-permute-start.9 = (f32[128,128]{1,0:T(8,128)S(1)}, f32[128,128]{1,0:T(8,128)S(1)}, u32[]{:S(2)}, u32[]{:S(2)}) collective-permute-start(f32[128,128]{1,0:T(8,128)S(1)} %fusion.111), channel_id=1, source_target_pairs={{4,0},{8,4},{12,8},{0,12},{5,1},{9,5},{13,9},{1,13},{6,2},{10,6},{... | collective-permute-start | bytes 196616 | tf_op jit(solution)/shard_map/ppermute | solution.py:18
  36.4 1.8 %collective-permute-done.6 = f32[2,4,8,256]{3,2,1,0:T(8,128)S(1)} collective-permute-done((f32[2,4,8,256]{3,2,1,0:T(8,128)S(1)}, f32[2,4,8,256]{3,2,1,0:T(8,128)S(1)}, u32[]{:S(2)}, u32[]{:S(2)}) %collective-permute-start.6) | collective-permute-done | bytes 65568 | tf_op jit(solution)/shard_map/ppermute | solution.py:18
  38.2 1.6 %select_reduce_fusion.3 = (f32[4,256,256]{2,1,0:T(8,128)S(1)}, f32[4,256,256]{2,1,0:T(8,128)S(1)}) fusion(f32[4,8,256]{2,1,0:T(8,128)S(1)} %get-tuple-element.27, f32[4,8,256]{2,1,0:T(8,128)S(1)} %get-tuple-element.28, f32[4,8,256]{2,1,0:T(8,128)S(1)} %get-tuple-element.26), kind=kLoop, calls=%fused_computation.6 | loop fusion | flops 9961472 | bytes 2195456 | tf_op jit(solution)/shard_map/reduce_sum | solution.py:59
  42.3 2.0 %collective-permute-start.7 = (f32[128,128]{1,0:T(8,128)S(1)}, f32[128,128]{1,0:T(8,128)S(1)}, u32[]{:S(2)}, u32[]{:S(2)}) collective-permute-start(f32[128,128]{1,0:T(8,128)S(1)} %fusion.107), channel_id=1, source_target_pairs={{4,0},{8,4},{12,8},{0,12},{5,1},{9,5},{13,9},{1,13},{6,2},{10,6},{... | collective-permute-start | bytes 196616 | tf_op jit(solution)/shard_map/ppermute | solution.py:18
  47.1 1.6 %select_reduce_fusion.1 = (f32[4,256,256]{2,1,0:T(8,128)S(1)}, f32[4,256,256]{2,1,0:T(8,128)S(1)}) fusion(f32[4,8,256]{2,1,0:T(8,128)S(1)} %get-tuple-element.24, f32[4,8,256]{2,1,0:T(8,128)S(1)} %get-tuple-element.25, f32[4,8,256]{2,1,0:T(8,128)S(1)} %get-tuple-element.23), kind=kLoop, calls=%fused_computation.3 | loop fusion | flops 9961472 | bytes 2195456 | tf_op jit(solution)/shard_map/reduce_sum | solution.py:59
  54.6 1.9 %collective-permute-start.12 = (f32[128,128]{1,0:T(8,128)S(1)}, f32[128,128]{1,0:T(8,128)S(1)}, u32[]{:S(2)}, u32[]{:S(2)}) collective-permute-start(f32[128,128]{1,0:T(8,128)S(1)} %fusion.95), channel_id=1, source_target_pairs={{8,0},{12,4},{0,8},{4,12},{9,1},{13,5},{1,9},{5,13},{10,2},{14,6},... | collective-permute-start | bytes 196616 | tf_op jit(solution)/shard_map/ppermute | solution.py:18
  57.1 0.7 %fusion.129 = f32[256,128]{1,0:T(8,128)} fusion(f32[1024,128]{1,0:T(8,128)S(1)} %fusion.124, s32[]{:T(128)S(6)} %select_n.65, f32[1024,128]{1,0:T(8,128)S(1)} %fusion.3), kind=kLoop, calls=%fused_computation.177 | loop fusion | flops 98304 | bytes 393220 | tf_op jit(solution)/shard_map/sub | solution.py:109
  57.8 1.2 %collective-permute-done.12 = f32[128,128]{1,0:T(8,128)S(1)} collective-permute-done((f32[128,128]{1,0:T(8,128)S(1)}, f32[128,128]{1,0:T(8,128)S(1)}, u32[]{:S(2)}, u32[]{:S(2)}) %collective-permute-start.12) | collective-permute-done | bytes 65568 | tf_op jit(solution)/shard_map/ppermute | solution.py:18
  59.0 0.7 %pad_maximum_fusion.3 = f32[256,128]{1,0:T(8,128)} fusion(f32[128,128]{1,0:T(8,128)S(1)} %collective-permute-done.12, f32[128,128]{1,0:T(8,128)S(1)} %collective-permute-done.10), kind=kLoop, calls=%fused_computation.184 | loop fusion | flops 32768 | bytes 262144 | tf_op jit(solution)/shard_map/concatenate | solution.py:110
  (73 shorter events, 18.8 us)
Async XLA Ops:
  2.2 20.1 %collective-permute-start.3 = (f32[12288]{0:T(1024)S(1)}, f32[12288]{0:T(1024)S(1)}, u32[]{:S(2)}, u32[]{:S(2)}) collective-permute-start(f32[12288]{0:T(1024)S(1)} %bitcast.158), channel_id=1, source_target_pairs={{0,2},{1,3},{2,0},{3,1},{4,6},{5,7},{6,4},{7,5},{8,10},{9,11},{10,... | collective-permute-start | bytes 147464 | tf_op jit(solution)/shard_map/ppermute | solution.py:43
  6.3 16.0 %collective-permute-start.4 = (f32[12288]{0:T(1024)S(1)}, f32[12288]{0:T(1024)S(1)}, u32[]{:S(2)}, u32[]{:S(2)}) collective-permute-start(f32[12288]{0:T(1024)S(1)} %bitcast.159), channel_id=1, source_target_pairs={{0,3},{1,2},{2,1},{3,0},{4,7},{5,6},{6,5},{7,4},{8,11},{9,10},{10,... | collective-permute-start | bytes 147464 | tf_op jit(solution)/shard_map/ppermute | solution.py:43
  7.6 17.3 %collective-permute-start.1 = (f32[32768]{0:T(1024)}, f32[32768]{0:T(1024)S(1)}, u32[]{:S(2)}, u32[]{:S(2)}) collective-permute-start(f32[32768]{0:T(1024)} %bitcast.151), channel_id=1, source_target_pairs={{0,2},{1,3},{2,0},{3,1},{4,6},{5,7},{6,4},{7,5},{8,10},{9,11},{10,... | collective-permute-start | bytes 393224 | tf_op jit(solution)/shard_map/ppermute | solution.py:44
  9.3 15.7 %collective-permute-start.2 = (f32[32768]{0:T(1024)}, f32[32768]{0:T(1024)S(1)}, u32[]{:S(2)}, u32[]{:S(2)}) collective-permute-start(f32[32768]{0:T(1024)} %bitcast.152), channel_id=1, source_target_pairs={{0,3},{1,2},{2,1},{3,0},{4,7},{5,6},{6,5},{7,4},{8,11},{9,10},{10,... | collective-permute-start | bytes 393224 | tf_op jit(solution)/shard_map/ppermute | solution.py:44
  11.2 11.1 %collective-permute-start = (f32[45056]{0:T(1024)S(1)}, f32[45056]{0:T(1024)S(1)}, u32[]{:S(2)}, u32[]{:S(2)}) collective-permute-start(f32[45056]{0:T(1024)S(1)} %pad_maximum_fusion.2), channel_id=1, source_target_pairs={{0,1},{1,0},{2,3},{3,2},{4,5},{5,4},{6,7},{7,6},{8,9},{9,8},{10,11... | collective-permute-start | bytes 540680 | tf_op jit(solution)/shard_map/ppermute | solution.py:39
  23.3 1.7 %copy-start = (f32[256,128]{1,0:T(8,128)S(1)}, f32[256,128]{1,0:T(8,128)}, u32[]{:S(2)}) copy-start(f32[256,128]{1,0:T(8,128)} %param.6) | copy-start | bytes 393220
  26.3 0.9 %copy-start.1 = (f32[256,128]{1,0:T(8,128)S(1)}, f32[256,128]{1,0:T(8,128)}, u32[]{:S(2)}) copy-start(f32[256,128]{1,0:T(8,128)} %param.5) | copy-start | bytes 393220
  30.8 9.0 %collective-permute-start.5 = (f32[128,128]{1,0:T(8,128)S(1)}, f32[128,128]{1,0:T(8,128)S(1)}, u32[]{:S(2)}, u32[]{:S(2)}) collective-permute-start(f32[128,128]{1,0:T(8,128)S(1)} %fusion.115), channel_id=1, source_target_pairs={{4,0},{8,4},{12,8},{0,12},{5,1},{9,5},{13,9},{1,13},{6,2},{10,6},{... | collective-permute-start | bytes 196616 | tf_op jit(solution)/shard_map/ppermute | solution.py:18
  33.4 10.9 %collective-permute-start.9 = (f32[128,128]{1,0:T(8,128)S(1)}, f32[128,128]{1,0:T(8,128)S(1)}, u32[]{:S(2)}, u32[]{:S(2)}) collective-permute-start(f32[128,128]{1,0:T(8,128)S(1)} %fusion.111), channel_id=1, source_target_pairs={{4,0},{8,4},{12,8},{0,12},{5,1},{9,5},{13,9},{1,13},{6,2},{10,6},{... | collective-permute-start | bytes 196616 | tf_op jit(solution)/shard_map/ppermute | solution.py:18
  35.0 3.2 %collective-permute-start.6 = (f32[2,4,8,256]{3,2,1,0:T(8,128)S(1)}, f32[2,4,8,256]{3,2,1,0:T(8,128)S(1)}, u32[]{:S(2)}, u32[]{:S(2)}) collective-permute-start(f32[2,4,8,256]{3,2,1,0:T(8,128)S(1)} %pad_maximum_fusion.4), channel_id=1, source_target_pairs={{4,0},{8,4},{12,8},{0,12},{5,1},{9,5},{13,9},{1,13},{6,2},{10,6},{... | collective-permute-start | bytes 196616 | tf_op jit(solution)/shard_map/ppermute | solution.py:18
  35.3 11.8 %collective-permute-start.8 = (f32[2,4,8,256]{3,2,1,0:T(8,128)S(1)}, f32[2,4,8,256]{3,2,1,0:T(8,128)S(1)}, u32[]{:S(2)}, u32[]{:S(2)}) collective-permute-start(f32[2,4,8,256]{3,2,1,0:T(8,128)S(1)} %pad_maximum_fusion.5), channel_id=1, source_target_pairs={{8,0},{12,4},{0,8},{4,12},{9,1},{13,5},{1,9},{5,13},{10,2},{14,6},... | collective-permute-start | bytes 196616 | tf_op jit(solution)/shard_map/ppermute | solution.py:18
  42.3 7.0 %collective-permute-start.7 = (f32[128,128]{1,0:T(8,128)S(1)}, f32[128,128]{1,0:T(8,128)S(1)}, u32[]{:S(2)}, u32[]{:S(2)}) collective-permute-start(f32[128,128]{1,0:T(8,128)S(1)} %fusion.107), channel_id=1, source_target_pairs={{4,0},{8,4},{12,8},{0,12},{5,1},{9,5},{13,9},{1,13},{6,2},{10,6},{... | collective-permute-start | bytes 196616 | tf_op jit(solution)/shard_map/ppermute | solution.py:18
  46.8 5.3 %collective-permute-start.11 = (f32[128,128]{1,0:T(8,128)S(1)}, f32[128,128]{1,0:T(8,128)S(1)}, u32[]{:S(2)}, u32[]{:S(2)}) collective-permute-start(f32[128,128]{1,0:T(8,128)S(1)} %fusion.103), channel_id=1, source_target_pairs={{4,0},{8,4},{12,8},{0,12},{5,1},{9,5},{13,9},{1,13},{6,2},{10,6},{... | collective-permute-start | bytes 196616 | tf_op jit(solution)/shard_map/ppermute | solution.py:18
  51.8 6.0 %collective-permute-start.10 = (f32[128,128]{1,0:T(8,128)S(1)}, f32[128,128]{1,0:T(8,128)S(1)}, u32[]{:S(2)}, u32[]{:S(2)}) collective-permute-start(f32[128,128]{1,0:T(8,128)S(1)} %fusion.99), channel_id=1, source_target_pairs={{8,0},{12,4},{0,8},{4,12},{9,1},{13,5},{1,9},{5,13},{10,2},{14,6},... | collective-permute-start | bytes 196616 | tf_op jit(solution)/shard_map/ppermute | solution.py:18
  54.6 4.4 %collective-permute-start.12 = (f32[128,128]{1,0:T(8,128)S(1)}, f32[128,128]{1,0:T(8,128)S(1)}, u32[]{:S(2)}, u32[]{:S(2)}) collective-permute-start(f32[128,128]{1,0:T(8,128)S(1)} %fusion.95), channel_id=1, source_target_pairs={{8,0},{12,4},{0,8},{4,12},{9,1},{13,5},{1,9},{5,13},{10,2},{14,6},... | collective-permute-start | bytes 196616 | tf_op jit(solution)/shard_map/ppermute | solution.py:18

commit v18 on v6

--- a/solution.py
+++ b/solution.py
@@ -33,6 +33,11 @@
     return weight_t * jax.nn.sigmoid(scores_t) - target_t
 
 
+def residual_tile_t(user_cols, item_rows, weight_t, target_t):
+    scores_t = jnp.dot(item_rows, user_cols, precision=MATMUL_PRECISION)
+    return weight_t * jax.nn.sigmoid(scores_t) - target_t
+
+
 def build_tiles(index_rows, signed_rows, slab_width):
     slabs, slot_count, user_count = index_rows.shape
     columns = jnp.arange(slab_width, dtype=jnp.float32)[None, None, :, None]
@@ -64,29 +69,30 @@
 
     pieces = 2 if user_count % 256 == 0 else 1
     rows = user_count // pieces
-    chunks = [user_factors[k * rows : (k + 1) * rows] for k in range(pieces)]
+    chunks = [user_factors[k * rows : (k + 1) * rows].T for k in range(pieces)]
     for stratum in range(strata):
         if stratum > 0:
             chunks = [shifted(chunk, "ub", 1) for chunk in chunks]
         weight, target = build_tiles(slot_data[stratum][0], slot_data[stratum][1], slab_rows)
+        block_t = block.T
         finished = []
         residuals = []
         for k, chunk in enumerate(chunks):
             weight_k = weight[:, k * rows : (k + 1) * rows]
             target_k = target[:, k * rows : (k + 1) * rows]
             for inner_step in range(INNER):
-                residual_t = residual_tile(chunk, block, weight_k, target_k)
-                gradient = lax.dot_general(
-                    residual_t, block, (((0,), (0,)), ((), ())), precision=MATMUL_PRECISION
-                )
-                chunk = chunk - LR_USER * (gradient + LAMBDA_REG * chunk)
+                residual_t = residual_tile_t(chunk, block, weight_k, target_k)
+                gradient_t = jnp.dot(block_t, residual_t, precision=MATMUL_PRECISION)
+                chunk = chunk - LR_USER * (gradient_t + LAMBDA_REG * chunk)
             finished.append(chunk)
-            residuals.append(residual_tile(chunk, block, weight_k, target_k))
+            residuals.append(residual_tile_t(chunk, block, weight_k, target_k))
         chunks = finished
         residual_t = jnp.concatenate(residuals, 1)
-        item_grad = jnp.dot(residual_t, jnp.concatenate(chunks, 0), precision=MATMUL_PRECISION)
+        item_grad = lax.dot_general(
+            residual_t, jnp.concatenate(chunks, 1), (((1,), (1,)), ((), ())), precision=MATMUL_PRECISION
+        )
         block = block - LR_ITEM * (item_grad + LAMBDA_REG * block)
-    user_rows = jnp.concatenate([shifted(chunk, "ub", 1 - strata) for chunk in chunks], 0)
+    user_rows = jnp.concatenate([shifted(chunk, "ub", 1 - strata) for chunk in chunks], 1).T
     me = lax.axis_index("it")
     slab = lax.dynamic_slice_in_dim(block, me * slab_rows, slab_rows, 0)
     return (user_rows, slab)

time: 52.5 us -> 52.5 us (level)
    concatenate x1 -> x0, other arithmetic: 0.66 us -> none  [per_device(): jnp.concatenate([shifted(chunk, 'ub', 1 - strata) for chunk in chunks], 0)]
    transpose x0 -> x1, other arithmetic: none -> 0.66 us  [per_device(): jnp.concatenate([shifted(chunk, 'ub', 1 - strata) for chunk in chunks], 1)]
where the time goes in v18:
time: 52.5 us; the launch traced here: 52.2 us
  matrix products  17.8 us (34%)
  starting transfers between devices  16.5 us (31%)
  other arithmetic  10.6 us (20%)
  waiting for transfers between devices  3.52 us (7%)
  local copies, waits for them, and re-layouts  2.65 us (5%)
  between operations  1.05 us (2%)
    ppermute x6, starting transfers between devices, gather_over(): lax.ppermute(block, axis, [(i, i ^ k) for i in range(count)])  10.1 us
    dot_general x18, matrix products, residual_tile_t(): scores_t = jnp.dot(item_rows, user_cols, precision=MATMUL_PRECISION)  8.79 us
    reduce_sum x3, other arithmetic, build_tiles(): jnp.sum(jnp.where(matches, jnp.abs(signed_rows)[:, :, None, :], 0.0), axi...  7.36 us
    dot_general x12, matrix products, per_device(): gradient_t = jnp.dot(block_t, residual_t, precision=MATMUL_PRECISION)  7.27 us
    ppermute x8, starting transfers between devices, shifted(): return lax.ppermute(block, axis, route)  6.41 us
    ppermute x6, waiting for transfers between devices, gather_over(): lax.ppermute(block, axis, [(i, i ^ k) for i in range(count)])  2.01 us
    dot_general x3, matrix products, per_device(): lax.dot_general(residual_t, jnp.concatenate(chunks, 1), (((1,), (1,)), ((...  1.72 us
    ppermute x8, waiting for transfers between devices, shifted(): return lax.ppermute(block, axis, route)  1.52 us
  transfers between devices with their start and end apart: 14, of which 2 were waited for; matrix products, arithmetic and copies ran while one was open for 43% of the time, Pallas kernels for 0%

profile of v18, /device:TPU:0, one launch (start us, length us, event | category | flops | bytes accessed | tf_op | source)
XLA Modules:
  0.0 52.2 jit_solution(7597609846071939260)
XLA Ops:
  0.6 0.7 %convert_bitcast_fusion = f32[3,1,8,256]{3,2,0,1:T(8,128)S(1)} fusion(s32[3,256,8]{1,2,0:T(8,128)} %param.7), kind=kLoop, calls=%fused_computation.210 | loop fusion | flops 6144 | bytes 49152 | tf_op jit(solution)/shard_map/stack | solution.py:54
  1.4 0.8 %fusion.141 = f32[3,1,8,256]{3,2,0,1:T(8,128)S(1)} fusion(f32[3,256,8]{1,2,0:T(8,128)} %param.9, s32[3,256,8]{1,2,0:T(8,128)} %param.8), kind=kLoop, calls=%fused_computation.209 | loop fusion | flops 18432 | bytes 73728 | tf_op jit(solution)/shard_map/stack | solution.py:54
  2.1 3.1 %collective-permute-start.3 = (f32[3,2,8,256]{3,2,0,1:T(8,128)S(1)}, f32[3,2,8,256]{3,2,0,1:T(8,128)S(1)}, u32[]{:S(2)}, u32[]{:S(2)}) collective-permute-start(f32[3,2,8,256]{3,2,0,1:T(8,128)S(1)} %get-tuple-element.24), channel_id=1, source_target_pairs={{0,1},{1,0},{2,3},{3,2},{4,5},{5,4},{6,7},{7,6},{8,9},{9,8},{10,11... | collective-permute-start | bytes 147464 | tf_op jit(solution)/shard_map/ppermute | solution.py:25
  5.2 2.6 %collective-permute-start.4 = (f32[3,2,8,256]{3,2,0,1:T(8,128)S(1)}, f32[3,2,8,256]{3,2,0,1:T(8,128)S(1)}, u32[]{:S(2)}, u32[]{:S(2)}) collective-permute-start(f32[3,2,8,256]{3,2,0,1:T(8,128)S(1)} %get-tuple-element.24), channel_id=1, source_target_pairs={{0,2},{1,3},{2,0},{3,1},{4,6},{5,7},{6,4},{7,5},{8,10},{9,11},{10,... | collective-permute-start | bytes 147464 | tf_op jit(solution)/shard_map/ppermute | solution.py:25
  7.8 0.9 %collective-permute-start = (f32[256,128]{1,0:T(8,128)}, f32[256,128]{1,0:T(8,128)S(1)}, u32[]{:S(2)}, u32[]{:S(2)}) collective-permute-start(f32[256,128]{1,0:T(8,128)} %param.6), channel_id=1, source_target_pairs={{0,1},{1,0},{2,3},{3,2},{4,5},{5,4},{6,7},{7,6},{8,9},{9,8},{10,11... | collective-permute-start | bytes 393224 | tf_op jit(solution)/shard_map/ppermute | solution.py:25
  8.7 3.5 %collective-permute-start.1 = (f32[256,128]{1,0:T(8,128)}, f32[256,128]{1,0:T(8,128)S(1)}, u32[]{:S(2)}, u32[]{:S(2)}) collective-permute-start(f32[256,128]{1,0:T(8,128)} %param.6), channel_id=1, source_target_pairs={{0,2},{1,3},{2,0},{3,1},{4,6},{5,7},{6,4},{7,5},{8,10},{9,11},{10,... | collective-permute-start | bytes 393224 | tf_op jit(solution)/shard_map/ppermute | solution.py:25
  12.4 2.0 %collective-permute-done.5 = f32[3,2,8,256]{3,2,0,1:T(8,128)S(1)} collective-permute-done((f32[3,2,8,256]{3,2,0,1:T(8,128)S(1)}, f32[3,2,8,256]{3,2,0,1:T(8,128)S(1)}, u32[]{:S(2)}, u32[]{:S(2)}) %collective-permute-start.5) | collective-permute-done | bytes 49184 | tf_op jit(solution)/shard_map/ppermute | solution.py:25
  15.3 1.6 %collective-permute-start.10 = (f32[2,4,8,256]{3,2,1,0:T(8,128)S(1)}, f32[2,4,8,256]{3,2,1,0:T(8,128)S(1)}, u32[]{:S(2)}, u32[]{:S(2)}) collective-permute-start(f32[2,4,8,256]{3,2,1,0:T(8,128)S(1)} %pad_maximum_fusion.3), channel_id=1, source_target_pairs={{8,0},{12,4},{0,8},{4,12},{9,1},{13,5},{1,9},{5,13},{10,2},{14,6},... | collective-permute-start | bytes 196616 | tf_op jit(solution)/shard_map/ppermute | solution.py:18
  16.8 2.9 %select_reduce_fusion.5 = (f32[4,256,256]{2,1,0:T(8,128)}, f32[4,256,256]{2,1,0:T(8,128)}) fusion(f32[4,8,256]{2,1,0:T(8,128)S(1)} %get-tuple-element.16, f32[4,8,256]{2,1,0:T(8,128)S(1)} %get-tuple-element.12, f32[4,8,256]{2,1,0:T(8,128)S(1)} %get-tuple-element.14), kind=kLoop, calls=%fused_computation.9 | loop fusion | flops 9961472 | bytes 2195456 | tf_op jit(solution)/shard_map/reduce_sum | solution.py:45
  19.7 2.9 %select_reduce_fusion.3 = (f32[4,256,256]{2,1,0:T(8,128)}, f32[4,256,256]{2,1,0:T(8,128)}) fusion(f32[4,8,256]{2,1,0:T(8,128)S(1)} %get-tuple-element.21, f32[4,8,256]{2,1,0:T(8,128)S(1)} %get-tuple-element.22, f32[4,8,256]{2,1,0:T(8,128)S(1)} %get-tuple-element.20), kind=kLoop, calls=%fused_computation.6 | loop fusion | flops 9961472 | bytes 2195456 | tf_op jit(solution)/shard_map/reduce_sum | solution.py:45
  22.6 1.6 %select_reduce_fusion.1 = (f32[4,256,256]{2,1,0:T(8,128)S(1)}, f32[4,256,256]{2,1,0:T(8,128)S(1)}) fusion(f32[4,8,256]{2,1,0:T(8,128)S(1)} %get-tuple-element.18, f32[4,8,256]{2,1,0:T(8,128)S(1)} %get-tuple-element.19, f32[4,8,256]{2,1,0:T(8,128)S(1)} %get-tuple-element.17), kind=kLoop, calls=%fused_computation.3 | loop fusion | flops 9961472 | bytes 2195456 | tf_op jit(solution)/shard_map/reduce_sum | solution.py:45
  25.2 0.9 %copy-done.2 = f32[4,256,256]{2,1,0:T(8,128)S(1)} copy-done((f32[4,256,256]{2,1,0:T(8,128)S(1)}, f32[4,256,256]{2,1,0:T(8,128)}, u32[]{:S(2)}) %copy-start.2) | copy-done | bytes 1048600
  26.1 1.6 %fusion.25 = f32[1024,128]{1,0:T(8,128)S(1)} fusion(f32[1024,128]{1,0:T(8,128)S(1)} %bitcast_select_fusion, f32[1024,256]{1,0:T(8,128)} %bitcast.154, f32[1024,256]{1,0:T(8,128)S(1)} %bitcast.148, f32[256,128]{1,0:T(8,128)S(1)} %copy-done.4), kind=kOutput, calls=%fused_computation.56 | convolution fusion | flops 101318656 | bytes 2162688 | tf_op jit(solution)/shard_map/dot_general | solution.py:37
  31.6 0.6 %fusion.111 = f32[128,128]{0,1:T(8,128)S(1)} fusion(f32[128,128]{0,1:T(8,128)S(1)} %fusion.113, f32[1024,128]{1,0:T(8,128)S(1)} %bitcast_select_fusion, f32[1024,128]{1,0:T(8,128)S(1)} %fusion.41), kind=kOutput, calls=%fused_computation.151 | convolution fusion | flops 100712448 | bytes 1179648 | tf_op jit(solution)/shard_map/dot_general | solution.py:85
  34.6 0.6 %fusion.109 = f32[128,128]{0,1:T(8,128)S(1)} fusion(f32[128,128]{0,1:T(8,128)S(1)} %collective-permute-done.6, f32[1024,128]{1,0:T(8,128)S(1)} %fusion.1, f32[1024,128]{1,0:T(8,128)S(1)} %fusion.49), kind=kOutput, calls=%fused_computation.148 | convolution fusion | flops 100712448 | bytes 1179648 | tf_op jit(solution)/shard_map/dot_general | solution.py:85
  35.6 0.6 %fusion.107 = f32[128,128]{0,1:T(8,128)S(1)} fusion(f32[128,128]{0,1:T(8,128)S(1)} %fusion.109, f32[1024,128]{1,0:T(8,128)S(1)} %fusion.1, f32[1024,128]{1,0:T(8,128)S(1)} %fusion.53), kind=kOutput, calls=%fused_computation.145 | convolution fusion | flops 100712448 | bytes 1179648 | tf_op jit(solution)/shard_map/dot_general | solution.py:85
  36.7 1.0 %collective-permute-start.8 = (f32[128,128]{0,1:T(8,128)S(1)}, f32[128,128]{0,1:T(8,128)S(1)}, u32[]{:S(2)}, u32[]{:S(2)}) collective-permute-start(f32[128,128]{0,1:T(8,128)S(1)} %fusion.107), channel_id=1, source_target_pairs={{4,0},{8,4},{12,8},{0,12},{5,1},{9,5},{13,9},{1,13},{6,2},{10,6},{... | collective-permute-start | bytes 196616 | tf_op jit(solution)/shard_map/ppermute | solution.py:18
  38.1 0.6 %fusion.105 = f32[128,128]{0,1:T(8,128)S(1)} fusion(f32[128,128]{0,1:T(8,128)S(1)} %collective-permute-done.9, f32[1024,128]{1,0:T(8,128)S(1)} %fusion.1, f32[1024,128]{1,0:T(8,128)S(1)} %fusion.61), kind=kOutput, calls=%fused_computation.142 | convolution fusion | flops 100712448 | bytes 1179648 | tf_op jit(solution)/shard_map/dot_general | solution.py:85
  40.2 0.7 %collective-permute-start.12 = (f32[128,128]{0,1:T(8,128)S(1)}, f32[128,128]{0,1:T(8,128)S(1)}, u32[]{:S(2)}, u32[]{:S(2)}) collective-permute-start(f32[128,128]{0,1:T(8,128)S(1)} %fusion.103), channel_id=1, source_target_pairs={{4,0},{8,4},{12,8},{0,12},{5,1},{9,5},{13,9},{1,13},{6,2},{10,6},{... | collective-permute-start | bytes 196616 | tf_op jit(solution)/shard_map/ppermute | solution.py:18
  43.0 0.6 %fusion.99 = f32[128,128]{0,1:T(8,128)S(1)} fusion(f32[128,128]{0,1:T(8,128)S(1)} %fusion.101, f32[1024,128]{1,0:T(8,128)S(1)} %fusion.3, f32[1024,128]{1,0:T(8,128)S(1)} %fusion.77), kind=kOutput, calls=%fused_computation.133 | convolution fusion | flops 100712448 | bytes 1179648 | tf_op jit(solution)/shard_map/dot_general | solution.py:85
  47.2 1.6 %collective-permute-start.13 = (f32[128,128]{0,1:T(8,128)S(1)}, f32[128,128]{0,1:T(8,128)S(1)}, u32[]{:S(2)}, u32[]{:S(2)}) collective-permute-start(f32[128,128]{0,1:T(8,128)S(1)} %fusion.95), channel_id=1, source_target_pairs={{8,0},{12,4},{0,8},{4,12},{9,1},{13,5},{1,9},{5,13},{10,2},{14,6},... | collective-permute-start | bytes 196616 | tf_op jit(solution)/shard_map/ppermute | solution.py:18
  49.3 0.7 %fusion.129 = f32[256,128]{1,0:T(8,128)} fusion(f32[1024,128]{1,0:T(8,128)S(1)} %fusion.124, s32[]{:T(128)S(6)} %select_n.64, f32[1024,128]{1,0:T(8,128)S(1)} %fusion.3), kind=kLoop, calls=%fused_computation.176 | loop fusion | flops 98304 | bytes 393220 | tf_op jit(solution)/shard_map/sub | solution.py:94
  50.0 1.5 %collective-permute-done.13 = f32[128,128]{0,1:T(8,128)S(1)} collective-permute-done((f32[128,128]{0,1:T(8,128)S(1)}, f32[128,128]{0,1:T(8,128)S(1)}, u32[]{:S(2)}, u32[]{:S(2)}) %collective-permute-start.13) | collective-permute-done | bytes 65568 | tf_op jit(solution)/shard_map/ppermute | solution.py:18
  51.5 0.7 %maximum_bitcast_fusion = f32[256,128]{1,0:T(8,128)} fusion(f32[128,128]{0,1:T(8,128)S(1)} %collective-permute-done.13, f32[128,128]{0,1:T(8,128)S(1)} %collective-permute-done.11), kind=kLoop, calls=%fused_computation.183 | loop fusion | flops 32768 | bytes 262144 | tf_op jit(solution)/shard_map/transpose | solution.py:95
  (76 shorter events, 17.0 us)
Async XLA Ops:
  2.1 10.2 %collective-permute-start.3 = (f32[3,2,8,256]{3,2,0,1:T(8,128)S(1)}, f32[3,2,8,256]{3,2,0,1:T(8,128)S(1)}, u32[]{:S(2)}, u32[]{:S(2)}) collective-permute-start(f32[3,2,8,256]{3,2,0,1:T(8,128)S(1)} %get-tuple-element.24), channel_id=1, source_target_pairs={{0,1},{1,0},{2,3},{3,2},{4,5},{5,4},{6,7},{7,6},{8,9},{9,8},{10,11... | collective-permute-start | bytes 147464 | tf_op jit(solution)/shard_map/ppermute | solution.py:25
  5.2 7.2 %collective-permute-start.4 = (f32[3,2,8,256]{3,2,0,1:T(8,128)S(1)}, f32[3,2,8,256]{3,2,0,1:T(8,128)S(1)}, u32[]{:S(2)}, u32[]{:S(2)}) collective-permute-start(f32[3,2,8,256]{3,2,0,1:T(8,128)S(1)} %get-tuple-element.24), channel_id=1, source_target_pairs={{0,2},{1,3},{2,0},{3,1},{4,6},{5,7},{6,4},{7,5},{8,10},{9,11},{10,... | collective-permute-start | bytes 147464 | tf_op jit(solution)/shard_map/ppermute | solution.py:25
  7.8 6.6 %collective-permute-start.5 = (f32[3,2,8,256]{3,2,0,1:T(8,128)S(1)}, f32[3,2,8,256]{3,2,0,1:T(8,128)S(1)}, u32[]{:S(2)}, u32[]{:S(2)}) collective-permute-start(f32[3,2,8,256]{3,2,0,1:T(8,128)S(1)} %get-tuple-element.24), channel_id=1, source_target_pairs={{0,3},{1,2},{2,1},{3,0},{4,7},{5,6},{6,5},{7,4},{8,11},{9,10},{10,... | collective-permute-start | bytes 147464 | tf_op jit(solution)/shard_map/ppermute | solution.py:25
  7.8 16.4 %collective-permute-start = (f32[256,128]{1,0:T(8,128)}, f32[256,128]{1,0:T(8,128)S(1)}, u32[]{:S(2)}, u32[]{:S(2)}) collective-permute-start(f32[256,128]{1,0:T(8,128)} %param.6), channel_id=1, source_target_pairs={{0,1},{1,0},{2,3},{3,2},{4,5},{5,4},{6,7},{7,6},{8,9},{9,8},{10,11... | collective-permute-start | bytes 393224 | tf_op jit(solution)/shard_map/ppermute | solution.py:25
  8.7 15.5 %collective-permute-start.1 = (f32[256,128]{1,0:T(8,128)}, f32[256,128]{1,0:T(8,128)S(1)}, u32[]{:S(2)}, u32[]{:S(2)}) collective-permute-start(f32[256,128]{1,0:T(8,128)} %param.6), channel_id=1, source_target_pairs={{0,2},{1,3},{2,0},{3,1},{4,6},{5,7},{6,4},{7,5},{8,10},{9,11},{10,... | collective-permute-start | bytes 393224 | tf_op jit(solution)/shard_map/ppermute | solution.py:25
  12.3 11.9 %collective-permute-start.2 = (f32[256,128]{1,0:T(8,128)}, f32[256,128]{1,0:T(8,128)S(1)}, u32[]{:S(2)}, u32[]{:S(2)}) collective-permute-start(f32[256,128]{1,0:T(8,128)} %param.6), channel_id=1, source_target_pairs={{0,3},{1,2},{2,1},{3,0},{4,7},{5,6},{6,5},{7,4},{8,11},{9,10},{10,... | collective-permute-start | bytes 393224 | tf_op jit(solution)/shard_map/ppermute | solution.py:25
  15.2 4.5 %collective-permute-start.7 = (f32[2,4,8,256]{3,2,1,0:T(8,128)S(1)}, f32[2,4,8,256]{3,2,1,0:T(8,128)S(1)}, u32[]{:S(2)}, u32[]{:S(2)}) collective-permute-start(f32[2,4,8,256]{3,2,1,0:T(8,128)S(1)} %pad_maximum_fusion.2), channel_id=1, source_target_pairs={{4,0},{8,4},{12,8},{0,12},{5,1},{9,5},{13,9},{1,13},{6,2},{10,6},{... | collective-permute-start | bytes 196616 | tf_op jit(solution)/shard_map/ppermute | solution.py:18
  15.3 7.3 %collective-permute-start.10 = (f32[2,4,8,256]{3,2,1,0:T(8,128)S(1)}, f32[2,4,8,256]{3,2,1,0:T(8,128)S(1)}, u32[]{:S(2)}, u32[]{:S(2)}) collective-permute-start(f32[2,4,8,256]{3,2,1,0:T(8,128)S(1)} %pad_maximum_fusion.3), channel_id=1, source_target_pairs={{8,0},{12,4},{0,8},{4,12},{9,1},{13,5},{1,9},{5,13},{10,2},{14,6},... | collective-permute-start | bytes 196616 | tf_op jit(solution)/shard_map/ppermute | solution.py:18
  22.6 1.7 %copy-start.5 = (f32[256,128]{1,0:T(8,128)S(1)}, f32[256,128]{1,0:T(8,128)}, u32[]{:S(2)}) copy-start(f32[256,128]{1,0:T(8,128)} %param.6) | copy-start | bytes 393220
  24.3 0.9 %copy-start.4 = (f32[256,128]{1,0:T(8,128)S(1)}, f32[256,128]{1,0:T(8,128)}, u32[]{:S(2)}) copy-start(f32[256,128]{1,0:T(8,128)} %param.5) | copy-start | bytes 393220
  24.9 1.2 %copy-start.2 = (f32[4,256,256]{2,1,0:T(8,128)S(1)}, f32[4,256,256]{2,1,0:T(8,128)}, u32[]{:S(2)}) copy-start(f32[4,256,256]{2,1,0:T(8,128)} %get-tuple-element.6) | copy-start | bytes 3145732
  26.1 1.6 %copy-start.3 = (f32[4,256,256]{2,1,0:T(8,128)S(1)}, f32[4,256,256]{2,1,0:T(8,128)}, u32[]{:S(2)}) copy-start(f32[4,256,256]{2,1,0:T(8,128)} %get-tuple-element.7) | copy-start | bytes 3145732
  30.2 3.6 %collective-permute-start.6 = (f32[128,128]{0,1:T(8,128)S(1)}, f32[128,128]{0,1:T(8,128)S(1)}, u32[]{:S(2)}, u32[]{:S(2)}) collective-permute-start(f32[128,128]{0,1:T(8,128)S(1)} %fusion.115), channel_id=1, source_target_pairs={{4,0},{8,4},{12,8},{0,12},{5,1},{9,5},{13,9},{1,13},{6,2},{10,6},{... | collective-permute-start | bytes 196616 | tf_op jit(solution)/shard_map/ppermute | solution.py:18
  32.6 1.2 %copy-start = (f32[4,256,256]{2,1,0:T(8,128)S(1)}, f32[4,256,256]{2,1,0:T(8,128)}, u32[]{:S(2)}) copy-start(f32[4,256,256]{2,1,0:T(8,128)} %get-tuple-element.4) | copy-start | bytes 3145732
  32.6 1.5 %copy-start.1 = (f32[4,256,256]{2,1,0:T(8,128)S(1)}, f32[4,256,256]{2,1,0:T(8,128)}, u32[]{:S(2)}) copy-start(f32[4,256,256]{2,1,0:T(8,128)} %get-tuple-element.5) | copy-start | bytes 3145732
  32.7 5.0 %collective-permute-start.9 = (f32[128,128]{0,1:T(8,128)S(1)}, f32[128,128]{0,1:T(8,128)S(1)}, u32[]{:S(2)}, u32[]{:S(2)}) collective-permute-start(f32[128,128]{0,1:T(8,128)S(1)} %fusion.111), channel_id=1, source_target_pairs={{4,0},{8,4},{12,8},{0,12},{5,1},{9,5},{13,9},{1,13},{6,2},{10,6},{... | collective-permute-start | bytes 196616 | tf_op jit(solution)/shard_map/ppermute | solution.py:18
  36.7 4.8 %collective-permute-start.8 = (f32[128,128]{0,1:T(8,128)S(1)}, f32[128,128]{0,1:T(8,128)S(1)}, u32[]{:S(2)}, u32[]{:S(2)}) collective-permute-start(f32[128,128]{0,1:T(8,128)S(1)} %fusion.107), channel_id=1, source_target_pairs={{4,0},{8,4},{12,8},{0,12},{5,1},{9,5},{13,9},{1,13},{6,2},{10,6},{... | collective-permute-start | bytes 196616 | tf_op jit(solution)/shard_map/ppermute | solution.py:18
  40.2 4.4 %collective-permute-start.12 = (f32[128,128]{0,1:T(8,128)S(1)}, f32[128,128]{0,1:T(8,128)S(1)}, u32[]{:S(2)}, u32[]{:S(2)}) collective-permute-start(f32[128,128]{0,1:T(8,128)S(1)} %fusion.103), channel_id=1, source_target_pairs={{4,0},{8,4},{12,8},{0,12},{5,1},{9,5},{13,9},{1,13},{6,2},{10,6},{... | collective-permute-start | bytes 196616 | tf_op jit(solution)/shard_map/ppermute | solution.py:18
  44.0 6.0 %collective-permute-start.11 = (f32[128,128]{0,1:T(8,128)S(1)}, f32[128,128]{0,1:T(8,128)S(1)}, u32[]{:S(2)}, u32[]{:S(2)}) collective-permute-start(f32[128,128]{0,1:T(8,128)S(1)} %fusion.99), channel_id=1, source_target_pairs={{8,0},{12,4},{0,8},{4,12},{9,1},{13,5},{1,9},{5,13},{10,2},{14,6},... | collective-permute-start | bytes 196616 | tf_op jit(solution)/shard_map/ppermute | solution.py:18
  47.2 4.3 %collective-permute-start.13 = (f32[128,128]{0,1:T(8,128)S(1)}, f32[128,128]{0,1:T(8,128)S(1)}, u32[]{:S(2)}, u32[]{:S(2)}) collective-permute-start(f32[128,128]{0,1:T(8,128)S(1)} %fusion.95), channel_id=1, source_target_pairs={{8,0},{12,4},{0,8},{4,12},{9,1},{13,5},{1,9},{5,13},{10,2},{14,6},... | collective-permute-start | bytes 196616 | tf_op jit(solution)/shard_map/ppermute | solution.py:18

commit v19 on v9

--- a/solution.py
+++ b/solution.py
@@ -80,7 +80,7 @@
                     residual_t, block, (((0,), (0,)), ((), ())), precision=MATMUL_PRECISION
                 )
                 chunk = chunk - LR_USER * (gradient + LAMBDA_REG * chunk)
-            if k == 0 and stratum + 1 < strata:
+            if k == 0 and stratum + 2 == strata:
                 slot_data[stratum + 1], chunk = lax.optimization_barrier((slot_data[stratum + 1], chunk))
             finished.append(chunk)
             residuals.append(residual_tile(chunk, block, weight_k, target_k))

time: 54.1 us -> 57.9 us (1.070)
  waiting for transfers between devices: 10.1 us -> 3.38 us
  starting transfers between devices: 16.5 us -> 23.2 us
  local copies, waits for them, and re-layouts: 1.37 us -> 2.9 us
  other arithmetic: 8.11 us -> 9.32 us
  matrix products: 16.7 us -> 17.7 us
    ppermute x6, starting transfers between devices: 10.1 us -> 16.8 us  [gather_over(): lax.ppermute(block, axis, [(i, i ^ k) for i in range(count)])]
    ppermute x6, waiting for transfers between devices: 7.66 us -> 2.3 us  [gather_over(): lax.ppermute(block, axis, [(i, i ^ k) for i in range(count)])]
    unnamed x5 -> x9, local copies, waits for them, and re-layouts: 0.11 us -> 1.64 us
    ppermute x8, waiting for transfers between devices: 2.48 us -> 1.08 us  [shifted(): return lax.ppermute(block, axis, route)]
    reduce_sum x3, other arithmetic: 4.85 us -> 6.07 us  [build_tiles(): jnp.sum(jnp.where(matches, jnp.abs(signed_rows)[:, :, None, :], 0.0), axi...]
    dot_general x18, matrix products: 7.61 us -> 8.67 us  [residual_tile(): scores_t = jnp.dot(item_rows, user_rows.T, precision=MATMUL_PRECISION)]
  transfers between devices with their start and end apart: 14 -> 14, of which waited for: 4 -> 3; matrix products, arithmetic and copies ran while one was open for 44% -> 48% of each run, Pallas kernels for 0% -> 0%
where the time goes in v19:
time: 57.9 us; the launch traced here: 57.6 us
  starting transfers between devices  23.2 us (40%)
  matrix products  17.7 us (31%)
  other arithmetic  9.32 us (16%)
  waiting for transfers between devices  3.38 us (6%)
  local copies, waits for them, and re-layouts  2.9 us (5%)
  between operations  1.05 us (2%)
    ppermute x6, starting transfers between devices, gather_over(): lax.ppermute(block, axis, [(i, i ^ k) for i in range(count)])  16.8 us
    dot_general x18, matrix products, residual_tile(): scores_t = jnp.dot(item_rows, user_rows.T, precision=MATMUL_PRECISION)  8.67 us
    dot_general x12, matrix products, per_device(): lax.dot_general(residual_t, block, (((0,), (0,)), ((), ())), precision=MA...  7.29 us
    ppermute x8, starting transfers between devices, shifted(): return lax.ppermute(block, axis, route)  6.41 us
    reduce_sum x3, other arithmetic, build_tiles(): jnp.sum(jnp.where(matches, jnp.abs(signed_rows)[:, :, None, :], 0.0), axi...  6.07 us
    ppermute x6, waiting for transfers between devices, gather_over(): lax.ppermute(block, axis, [(i, i ^ k) for i in range(count)])  2.3 us
    dot_general x3, matrix products, per_device(): jnp.dot(residual_t, jnp.concatenate(chunks, 0), precision=MATMUL_PRECISION)  1.74 us
    unnamed x9, local copies, waits for them, and re-layouts  1.64 us
  transfers between devices with their start and end apart: 14, of which 3 were waited for; matrix products, arithmetic and copies ran while one was open for 48% of the time, Pallas kernels for 0%

profile of v19, /device:TPU:0, one launch (start us, length us, event | category | flops | bytes accessed | tf_op | source)
XLA Modules:
  0.0 57.6 jit_solution(11121254216259407483)
XLA Ops:
  0.6 5.1 %collective-permute-start.6 = (f32[256,128]{1,0:T(8,128)}, f32[256,128]{1,0:T(8,128)S(1)}, u32[]{:S(2)}, u32[]{:S(2)}) collective-permute-start(f32[256,128]{1,0:T(8,128)} %param.6), channel_id=1, source_target_pairs={{0,3},{1,2},{2,1},{3,0},{4,7},{5,6},{6,5},{7,4},{8,11},{9,10},{10,... | collective-permute-start | bytes 393224 | tf_op jit(solution)/shard_map/ppermute | solution.py:25
  5.7 0.7 %convert_bitcast_fusion = f32[3,1,8,256]{3,2,0,1:T(8,128)S(1)} fusion(s32[3,256,8]{1,2,0:T(8,128)} %param.7), kind=kLoop, calls=%fused_computation.210 | loop fusion | flops 6144 | bytes 49152 | tf_op jit(solution)/shard_map/stack | solution.py:49
  6.5 0.8 %fusion.141 = f32[3,1,8,256]{3,2,0,1:T(8,128)S(1)} fusion(f32[3,256,8]{1,2,0:T(8,128)} %param.9, s32[3,256,8]{1,2,0:T(8,128)} %param.8), kind=kLoop, calls=%fused_computation.209 | loop fusion | flops 18432 | bytes 73728 | tf_op jit(solution)/shard_map/stack | solution.py:49
  7.3 2.0 %collective-permute-start.2 = (f32[3,2,8,256]{3,2,0,1:T(8,128)S(1)}, f32[3,2,8,256]{3,2,0,1:T(8,128)S(1)}, u32[]{:S(2)}, u32[]{:S(2)}) collective-permute-start(f32[3,2,8,256]{3,2,0,1:T(8,128)S(1)} %get-tuple-element.28), channel_id=1, source_target_pairs={{0,3},{1,2},{2,1},{3,0},{4,7},{5,6},{6,5},{7,4},{8,11},{9,10},{10,... | collective-permute-start | bytes 147464 | tf_op jit(solution)/shard_map/ppermute | solution.py:25
  9.2 1.1 %collective-permute-start.1 = (f32[3,2,8,256]{3,2,0,1:T(8,128)S(1)}, f32[3,2,8,256]{3,2,0,1:T(8,128)S(1)}, u32[]{:S(2)}, u32[]{:S(2)}) collective-permute-start(f32[3,2,8,256]{3,2,0,1:T(8,128)S(1)} %get-tuple-element.28), channel_id=1, source_target_pairs={{0,2},{1,3},{2,0},{3,1},{4,6},{5,7},{6,4},{7,5},{8,10},{9,11},{10,... | collective-permute-start | bytes 147464 | tf_op jit(solution)/shard_map/ppermute | solution.py:25
  10.3 1.4 %collective-permute-start = (f32[3,2,8,256]{3,2,0,1:T(8,128)S(1)}, f32[3,2,8,256]{3,2,0,1:T(8,128)S(1)}, u32[]{:S(2)}, u32[]{:S(2)}) collective-permute-start(f32[3,2,8,256]{3,2,0,1:T(8,128)S(1)} %get-tuple-element.28), channel_id=1, source_target_pairs={{0,1},{1,0},{2,3},{3,2},{4,5},{5,4},{6,7},{7,6},{8,9},{9,8},{10,11... | collective-permute-start | bytes 147464 | tf_op jit(solution)/shard_map/ppermute | solution.py:25
  11.8 2.2 %collective-permute-done.2 = f32[3,2,8,256]{3,2,0,1:T(8,128)S(1)} collective-permute-done((f32[3,2,8,256]{3,2,0,1:T(8,128)S(1)}, f32[3,2,8,256]{3,2,0,1:T(8,128)S(1)}, u32[]{:S(2)}, u32[]{:S(2)}) %collective-permute-start.2) | collective-permute-done | bytes 49184 | tf_op jit(solution)/shard_map/ppermute | solution.py:25
  14.1 7.2 %collective-permute-start.4 = (f32[256,128]{1,0:T(8,128)}, f32[256,128]{1,0:T(8,128)S(1)}, u32[]{:S(2)}, u32[]{:S(2)}) collective-permute-start(f32[256,128]{1,0:T(8,128)} %param.6), channel_id=1, source_target_pairs={{0,1},{1,0},{2,3},{3,2},{4,5},{5,4},{6,7},{7,6},{8,9},{9,8},{10,11... | collective-permute-start | bytes 393224 | tf_op jit(solution)/shard_map/ppermute | solution.py:25
  22.2 1.6 %collective-permute-start.3 = (f32[2,4,8,256]{3,2,1,0:T(8,128)S(1)}, f32[2,4,8,256]{3,2,1,0:T(8,128)S(1)}, u32[]{:S(2)}, u32[]{:S(2)}) collective-permute-start(f32[2,4,8,256]{3,2,1,0:T(8,128)S(1)} %pad_maximum_fusion.3), channel_id=1, source_target_pairs={{8,0},{12,4},{0,8},{4,12},{9,1},{13,5},{1,9},{5,13},{10,2},{14,6},... | collective-permute-start | bytes 196616 | tf_op jit(solution)/shard_map/ppermute | solution.py:18
  23.8 2.9 %select_reduce_fusion.5 = (f32[4,256,256]{2,1,0:T(8,128)}, f32[4,256,256]{2,1,0:T(8,128)}) fusion(f32[4,8,256]{2,1,0:T(8,128)S(1)} %get-tuple-element.20, f32[4,8,256]{2,1,0:T(8,128)S(1)} %get-tuple-element.16, f32[4,8,256]{2,1,0:T(8,128)S(1)} %get-tuple-element.18), kind=kLoop, calls=%fused_computation.9 | loop fusion | flops 9961472 | bytes 2195456 | tf_op jit(solution)/shard_map/reduce_sum | solution.py:40
  26.6 1.6 %select_reduce_fusion.3 = (f32[4,256,256]{2,1,0:T(8,128)S(1)}, f32[4,256,256]{2,1,0:T(8,128)S(1)}) fusion(f32[4,8,256]{2,1,0:T(8,128)S(1)} %get-tuple-element.25, f32[4,8,256]{2,1,0:T(8,128)S(1)} %get-tuple-element.26, f32[4,8,256]{2,1,0:T(8,128)S(1)} %get-tuple-element.24), kind=kLoop, calls=%fused_computation.6 | loop fusion | flops 9961472 | bytes 2195456 | tf_op jit(solution)/shard_map/reduce_sum | solution.py:40
  29.3 0.9 %copy-done = f32[4,256,256]{2,1,0:T(8,128)S(1)} copy-done((f32[4,256,256]{2,1,0:T(8,128)S(1)}, f32[4,256,256]{2,1,0:T(8,128)}, u32[]{:S(2)}) %copy-start) | copy-done | bytes 1048600
  30.2 1.5 %fusion.37 = f32[1024,128]{1,0:T(8,128)S(1)} fusion(f32[1024,128]{1,0:T(8,128)S(1)} %bitcast_select_fusion, f32[1024,256]{1,0:T(8,128)} %bitcast.136, f32[1024,256]{1,0:T(8,128)S(1)} %bitcast.130, f32[256,128]{1,0:T(8,128)S(1)} %copy-done.2), kind=kOutput, calls=%fused_computation.68 | convolution fusion | flops 101318656 | bytes 2162688 | tf_op jit(solution)/shard_map/dot_general | solution.py:32
  31.7 0.6 %fusion.113 = f32[128,128]{1,0:T(8,128)S(1)} fusion(f32[1024,128]{1,0:T(8,128)S(1)} %fusion.37, f32[1024,128]{1,0:T(8,128)S(1)} %bitcast_select_fusion, f32[256,128]{1,0:T(8,128)S(1)} %copy-done.2), kind=kOutput, calls=%fused_computation.154 | convolution fusion | flops 100712448 | bytes 1179648 | tf_op jit(solution)/shard_map/dot_general | solution.py:79
  33.3 0.6 %fusion.111 = f32[128,128]{1,0:T(8,128)S(1)} fusion(f32[128,128]{1,0:T(8,128)S(1)} %fusion.113, f32[1024,128]{1,0:T(8,128)S(1)} %fusion.41, f32[1024,128]{1,0:T(8,128)S(1)} %bitcast_select_fusion), kind=kOutput, calls=%fused_computation.151 | convolution fusion | flops 100712448 | bytes 1179648 | tf_op jit(solution)/shard_map/dot_general | solution.py:79
  35.1 0.6 %fusion.117 = f32[128,128]{1,0:T(8,128)S(1)} fusion(f32[1024,128]{1,0:T(8,128)S(1)} %fusion.25, f32[1024,128]{1,0:T(8,128)S(1)} %bitcast_select_fusion, f32[256,128]{1,0:T(8,128)S(1)} %copy-done.2), kind=kOutput, calls=%fused_computation.160 | convolution fusion | flops 100712448 | bytes 1179648 | tf_op jit(solution)/shard_map/dot_general | solution.py:79
  36.2 0.6 %fusion.115 = f32[128,128]{1,0:T(8,128)S(1)} fusion(f32[128,128]{1,0:T(8,128)S(1)} %fusion.117, f32[1024,128]{1,0:T(8,128)S(1)} %fusion.29, f32[1024,128]{1,0:T(8,128)S(1)} %bitcast_select_fusion), kind=kOutput, calls=%fused_computation.157 | convolution fusion | flops 100712448 | bytes 1179648 | tf_op jit(solution)/shard_map/dot_general | solution.py:79
  40.3 1.5 %collective-permute-start.12 = (f32[128,128]{1,0:T(8,128)S(1)}, f32[128,128]{1,0:T(8,128)S(1)}, u32[]{:S(2)}, u32[]{:S(2)}) collective-permute-start(f32[128,128]{1,0:T(8,128)S(1)} %fusion.103), channel_id=1, source_target_pairs={{4,0},{8,4},{12,8},{0,12},{5,1},{9,5},{13,9},{1,13},{6,2},{10,6},{... | collective-permute-start | bytes 196616 | tf_op jit(solution)/shard_map/ppermute | solution.py:18
  45.2 1.6 %select_reduce_fusion.1 = (f32[4,256,256]{2,1,0:T(8,128)S(1)}, f32[4,256,256]{2,1,0:T(8,128)S(1)}) fusion(f32[4,8,256]{2,1,0:T(8,128)S(1)} %get-tuple-element.22, f32[4,8,256]{2,1,0:T(8,128)S(1)} %get-tuple-element.23, f32[4,8,256]{2,1,0:T(8,128)S(1)} %get-tuple-element.21), kind=kLoop, calls=%fused_computation.3 | loop fusion | flops 9961472 | bytes 2195456 | tf_op jit(solution)/shard_map/reduce_sum | solution.py:40
  50.9 0.6 %fusion.101 = f32[128,128]{1,0:T(8,128)S(1)} fusion(f32[128,128]{1,0:T(8,128)S(1)} %collective-permute-done.9, f32[1024,128]{1,0:T(8,128)S(1)} %fusion.73, f32[1024,128]{1,0:T(8,128)S(1)} %fusion.3), kind=kOutput, calls=%fused_computation.136 | convolution fusion | flops 100712448 | bytes 1179648 | tf_op jit(solution)/shard_map/dot_general | solution.py:79
  52.6 1.6 %collective-permute-start.11 = (f32[128,128]{1,0:T(8,128)S(1)}, f32[128,128]{1,0:T(8,128)S(1)}, u32[]{:S(2)}, u32[]{:S(2)}) collective-permute-start(f32[128,128]{1,0:T(8,128)S(1)} %fusion.99), channel_id=1, source_target_pairs={{8,0},{12,4},{0,8},{4,12},{9,1},{13,5},{1,9},{5,13},{10,2},{14,6},... | collective-permute-start | bytes 196616 | tf_op jit(solution)/shard_map/ppermute | solution.py:18
  55.2 0.7 %fusion.129 = f32[256,128]{1,0:T(8,128)} fusion(f32[1024,128]{1,0:T(8,128)S(1)} %fusion.124, s32[]{:T(128)S(6)} %select_n.64, f32[1024,128]{1,0:T(8,128)S(1)} %fusion.3), kind=kLoop, calls=%fused_computation.176 | loop fusion | flops 98304 | bytes 393220 | tf_op jit(solution)/shard_map/sub | solution.py:90
  55.8 1.1 %collective-permute-done.11 = f32[128,128]{1,0:T(8,128)S(1)} collective-permute-done((f32[128,128]{1,0:T(8,128)S(1)}, f32[128,128]{1,0:T(8,128)S(1)}, u32[]{:S(2)}, u32[]{:S(2)}) %collective-permute-start.11) | collective-permute-done | bytes 65568 | tf_op jit(solution)/shard_map/ppermute | solution.py:18
  56.9 0.7 %pad_maximum_fusion.2 = f32[256,128]{1,0:T(8,128)} fusion(f32[128,128]{1,0:T(8,128)S(1)} %collective-permute-done.13, f32[128,128]{1,0:T(8,128)S(1)} %collective-permute-done.11), kind=kLoop, calls=%fused_computation.183 | loop fusion | flops 32768 | bytes 262144 | tf_op jit(solution)/shard_map/concatenate | solution.py:91
  (72 shorter events, 17.4 us)
Async XLA Ops:
  0.6 27.6 %collective-permute-start.6 = (f32[256,128]{1,0:T(8,128)}, f32[256,128]{1,0:T(8,128)S(1)}, u32[]{:S(2)}, u32[]{:S(2)}) collective-permute-start(f32[256,128]{1,0:T(8,128)} %param.6), channel_id=1, source_target_pairs={{0,3},{1,2},{2,1},{3,0},{4,7},{5,6},{6,5},{7,4},{8,11},{9,10},{10,... | collective-permute-start | bytes 393224 | tf_op jit(solution)/shard_map/ppermute | solution.py:25
  5.7 22.5 %collective-permute-start.5 = (f32[256,128]{1,0:T(8,128)}, f32[256,128]{1,0:T(8,128)S(1)}, u32[]{:S(2)}, u32[]{:S(2)}) collective-permute-start(f32[256,128]{1,0:T(8,128)} %param.6), channel_id=1, source_target_pairs={{0,2},{1,3},{2,0},{3,1},{4,6},{5,7},{6,4},{7,5},{8,10},{9,11},{10,... | collective-permute-start | bytes 393224 | tf_op jit(solution)/shard_map/ppermute | solution.py:25
  7.3 6.8 %collective-permute-start.2 = (f32[3,2,8,256]{3,2,0,1:T(8,128)S(1)}, f32[3,2,8,256]{3,2,0,1:T(8,128)S(1)}, u32[]{:S(2)}, u32[]{:S(2)}) collective-permute-start(f32[3,2,8,256]{3,2,0,1:T(8,128)S(1)} %get-tuple-element.28), channel_id=1, source_target_pairs={{0,3},{1,2},{2,1},{3,0},{4,7},{5,6},{6,5},{7,4},{8,11},{9,10},{10,... | collective-permute-start | bytes 147464 | tf_op jit(solution)/shard_map/ppermute | solution.py:25
  9.2 12.1 %collective-permute-start.1 = (f32[3,2,8,256]{3,2,0,1:T(8,128)S(1)}, f32[3,2,8,256]{3,2,0,1:T(8,128)S(1)}, u32[]{:S(2)}, u32[]{:S(2)}) collective-permute-start(f32[3,2,8,256]{3,2,0,1:T(8,128)S(1)} %get-tuple-element.28), channel_id=1, source_target_pairs={{0,2},{1,3},{2,0},{3,1},{4,6},{5,7},{6,4},{7,5},{8,10},{9,11},{10,... | collective-permute-start | bytes 147464 | tf_op jit(solution)/shard_map/ppermute | solution.py:25
  10.3 11.0 %collective-permute-start = (f32[3,2,8,256]{3,2,0,1:T(8,128)S(1)}, f32[3,2,8,256]{3,2,0,1:T(8,128)S(1)}, u32[]{:S(2)}, u32[]{:S(2)}) collective-permute-start(f32[3,2,8,256]{3,2,0,1:T(8,128)S(1)} %get-tuple-element.28), channel_id=1, source_target_pairs={{0,1},{1,0},{2,3},{3,2},{4,5},{5,4},{6,7},{7,6},{8,9},{9,8},{10,11... | collective-permute-start | bytes 147464 | tf_op jit(solution)/shard_map/ppermute | solution.py:25
  14.1 14.2 %collective-permute-start.4 = (f32[256,128]{1,0:T(8,128)}, f32[256,128]{1,0:T(8,128)S(1)}, u32[]{:S(2)}, u32[]{:S(2)}) collective-permute-start(f32[256,128]{1,0:T(8,128)} %param.6), channel_id=1, source_target_pairs={{0,1},{1,0},{2,3},{3,2},{4,5},{5,4},{6,7},{7,6},{8,9},{9,8},{10,11... | collective-permute-start | bytes 393224 | tf_op jit(solution)/shard_map/ppermute | solution.py:25
  22.1 4.5 %collective-permute-start.8 = (f32[2,4,8,256]{3,2,1,0:T(8,128)S(1)}, f32[2,4,8,256]{3,2,1,0:T(8,128)S(1)}, u32[]{:S(2)}, u32[]{:S(2)}) collective-permute-start(f32[2,4,8,256]{3,2,1,0:T(8,128)S(1)} %pad_maximum_fusion.4), channel_id=1, source_target_pairs={{4,0},{8,4},{12,8},{0,12},{5,1},{9,5},{13,9},{1,13},{6,2},{10,6},{... | collective-permute-start | bytes 196616 | tf_op jit(solution)/shard_map/ppermute | solution.py:18
  22.2 22.1 %collective-permute-start.3 = (f32[2,4,8,256]{3,2,1,0:T(8,128)S(1)}, f32[2,4,8,256]{3,2,1,0:T(8,128)S(1)}, u32[]{:S(2)}, u32[]{:S(2)}) collective-permute-start(f32[2,4,8,256]{3,2,1,0:T(8,128)S(1)} %pad_maximum_fusion.3), channel_id=1, source_target_pairs={{8,0},{12,4},{0,8},{4,12},{9,1},{13,5},{1,9},{5,13},{10,2},{14,6},... | collective-permute-start | bytes 196616 | tf_op jit(solution)/shard_map/ppermute | solution.py:18
  26.6 1.7 %copy-start.3 = (f32[256,128]{1,0:T(8,128)S(1)}, f32[256,128]{1,0:T(8,128)}, u32[]{:S(2)}) copy-start(f32[256,128]{1,0:T(8,128)} %param.6) | copy-start | bytes 393220
  28.4 0.9 %copy-start.2 = (f32[256,128]{1,0:T(8,128)S(1)}, f32[256,128]{1,0:T(8,128)}, u32[]{:S(2)}) copy-start(f32[256,128]{1,0:T(8,128)} %param.5) | copy-start | bytes 393220
  29.0 1.2 %copy-start = (f32[4,256,256]{2,1,0:T(8,128)S(1)}, f32[4,256,256]{2,1,0:T(8,128)}, u32[]{:S(2)}) copy-start(f32[4,256,256]{2,1,0:T(8,128)} %get-tuple-element.10) | copy-start | bytes 3145732
  31.7 1.2 %copy-start.1 = (f32[4,256,256]{2,1,0:T(8,128)S(1)}, f32[4,256,256]{2,1,0:T(8,128)}, u32[]{:S(2)}) copy-start(f32[4,256,256]{2,1,0:T(8,128)} %get-tuple-element.11) | copy-start | bytes 3145732
  33.9 4.3 %collective-permute-start.10 = (f32[128,128]{1,0:T(8,128)S(1)}, f32[128,128]{1,0:T(8,128)S(1)}, u32[]{:S(2)}, u32[]{:S(2)}) collective-permute-start(f32[128,128]{1,0:T(8,128)S(1)} %fusion.111), channel_id=1, source_target_pairs={{4,0},{8,4},{12,8},{0,12},{5,1},{9,5},{13,9},{1,13},{6,2},{10,6},{... | collective-permute-start | bytes 196616 | tf_op jit(solution)/shard_map/ppermute | solution.py:18
  37.2 5.0 %collective-permute-start.7 = (f32[128,128]{1,0:T(8,128)S(1)}, f32[128,128]{1,0:T(8,128)S(1)}, u32[]{:S(2)}, u32[]{:S(2)}) collective-permute-start(f32[128,128]{1,0:T(8,128)S(1)} %fusion.115), channel_id=1, source_target_pairs={{4,0},{8,4},{12,8},{0,12},{5,1},{9,5},{13,9},{1,13},{6,2},{10,6},{... | collective-permute-start | bytes 196616 | tf_op jit(solution)/shard_map/ppermute | solution.py:18
  40.3 7.1 %collective-permute-start.12 = (f32[128,128]{1,0:T(8,128)S(1)}, f32[128,128]{1,0:T(8,128)S(1)}, u32[]{:S(2)}, u32[]{:S(2)}) collective-permute-start(f32[128,128]{1,0:T(8,128)S(1)} %fusion.103), channel_id=1, source_target_pairs={{4,0},{8,4},{12,8},{0,12},{5,1},{9,5},{13,9},{1,13},{6,2},{10,6},{... | collective-permute-start | bytes 196616 | tf_op jit(solution)/shard_map/ppermute | solution.py:18
  44.8 5.7 %collective-permute-start.9 = (f32[128,128]{1,0:T(8,128)S(1)}, f32[128,128]{1,0:T(8,128)S(1)}, u32[]{:S(2)}, u32[]{:S(2)}) collective-permute-start(f32[128,128]{1,0:T(8,128)S(1)} %fusion.107), channel_id=1, source_target_pairs={{4,0},{8,4},{12,8},{0,12},{5,1},{9,5},{13,9},{1,13},{6,2},{10,6},{... | collective-permute-start | bytes 196616 | tf_op jit(solution)/shard_map/ppermute | solution.py:18
  49.4 6.4 %collective-permute-start.13 = (f32[128,128]{1,0:T(8,128)S(1)}, f32[128,128]{1,0:T(8,128)S(1)}, u32[]{:S(2)}, u32[]{:S(2)}) collective-permute-start(f32[128,128]{1,0:T(8,128)S(1)} %fusion.95), channel_id=1, source_target_pairs={{8,0},{12,4},{0,8},{4,12},{9,1},{13,5},{1,9},{5,13},{10,2},{14,6},... | collective-permute-start | bytes 196616 | tf_op jit(solution)/shard_map/ppermute | solution.py:18
  52.6 4.3 %collective-permute-start.11 = (f32[128,128]{1,0:T(8,128)S(1)}, f32[128,128]{1,0:T(8,128)S(1)}, u32[]{:S(2)}, u32[]{:S(2)}) collective-permute-start(f32[128,128]{1,0:T(8,128)S(1)} %fusion.99), channel_id=1, source_target_pairs={{8,0},{12,4},{0,8},{4,12},{9,1},{13,5},{1,9},{5,13},{10,2},{14,6},... | collective-permute-start | bytes 196616 | tf_op jit(solution)/shard_map/ppermute | solution.py:18

commit v20 on v6

--- a/solution.py
+++ b/solution.py
@@ -86,7 +86,7 @@
         residual_t = jnp.concatenate(residuals, 1)
         item_grad = jnp.dot(residual_t, jnp.concatenate(chunks, 0), precision=MATMUL_PRECISION)
         block = block - LR_ITEM * (item_grad + LAMBDA_REG * block)
-    user_rows = jnp.concatenate([shifted(chunk, "ub", 1 - strata) for chunk in chunks], 0)
+    user_rows = shifted(jnp.concatenate(chunks, 0), "ub", 1 - strata)
     me = lax.axis_index("it")
     slab = lax.dynamic_slice_in_dim(block, me * slab_rows, slab_rows, 0)
     return (user_rows, slab)

time: 52.5 us -> 52.9 us (level)
  waiting for transfers between devices: 3.53 us -> 5.45 us
  starting transfers between devices: 16.5 us -> 15 us
  other arithmetic: 10.6 us -> 9.92 us
  local copies, waits for them, and re-layouts: 2.65 us -> 3.31 us
    ppermute x8 -> x7, waiting for transfers between devices: 1.52 us -> 3.45 us  [shifted(): return lax.ppermute(block, axis, route)]
    ppermute x8 -> x7, starting transfers between devices: 6.41 us -> 4.85 us  [shifted(): return lax.ppermute(block, axis, route)]
    unnamed x13 -> x14, local copies, waits for them, and re-layouts: 1.4 us -> 2.05 us
    concatenate x1, other arithmetic: 0.66 us -> 0.01 us  [per_device(): user_rows = shifted(jnp.concatenate(chunks, 0), 'ub', 1 - strata)]
  transfers between devices with their start and end apart: 14 -> 13, of which waited for: 2 -> 2; matrix products, arithmetic and copies ran while one was open for 43% -> 38% of each run, Pallas kernels for 0% -> 0%
where the time goes in v20:
time: 52.9 us; the launch traced here: 52.6 us
  matrix products  17.8 us (34%)
  starting transfers between devices  15 us (28%)
  other arithmetic  9.92 us (19%)
  waiting for transfers between devices  5.45 us (10%)
  local copies, waits for them, and re-layouts  3.31 us (6%)
  between operations  1.06 us (2%)
    ppermute x6, starting transfers between devices, gather_over(): lax.ppermute(block, axis, [(i, i ^ k) for i in range(count)])  10.1 us
    dot_general x18, matrix products, residual_tile(): scores_t = jnp.dot(item_rows, user_rows.T, precision=MATMUL_PRECISION)  8.78 us
    dot_general x12, matrix products, per_device(): lax.dot_general(residual_t, block, (((0,), (0,)), ((), ())), precision=MA...  7.32 us
    reduce_sum x3, other arithmetic, build_tiles(): jnp.sum(jnp.where(matches, jnp.abs(signed_rows)[:, :, None, :], 0.0), axi...  7.32 us
    ppermute x7, starting transfers between devices, shifted(): return lax.ppermute(block, axis, route)  4.85 us
    ppermute x7, waiting for transfers between devices, shifted(): return lax.ppermute(block, axis, route)  3.45 us
    unnamed x14, local copies, waits for them, and re-layouts  2.05 us
    ppermute x6, waiting for transfers between devices, gather_over(): lax.ppermute(block, axis, [(i, i ^ k) for i in range(count)])  2.01 us
  transfers between devices with their start and end apart: 13, of which 2 were waited for; matrix products, arithmetic and copies ran while one was open for 38% of the time, Pallas kernels for 0%

profile of v20, /device:TPU:0, one launch (start us, length us, event | category | flops | bytes accessed | tf_op | source)
XLA Modules:
  0.0 52.6 jit_solution(7166298302779418962)
XLA Ops:
  0.6 0.7 %convert_bitcast_fusion = f32[3,1,8,256]{3,2,0,1:T(8,128)S(1)} fusion(s32[3,256,8]{1,2,0:T(8,128)} %param.7), kind=kLoop, calls=%fused_computation.207 | loop fusion | flops 6144 | bytes 49152 | tf_op jit(solution)/shard_map/stack | solution.py:49
  1.4 0.8 %fusion.138 = f32[3,1,8,256]{3,2,0,1:T(8,128)S(1)} fusion(f32[3,256,8]{1,2,0:T(8,128)} %param.9, s32[3,256,8]{1,2,0:T(8,128)} %param.8), kind=kLoop, calls=%fused_computation.206 | loop fusion | flops 18432 | bytes 73728 | tf_op jit(solution)/shard_map/stack | solution.py:49
  2.1 3.1 %collective-permute-start = (f32[3,2,8,256]{3,2,0,1:T(8,128)S(1)}, f32[3,2,8,256]{3,2,0,1:T(8,128)S(1)}, u32[]{:S(2)}, u32[]{:S(2)}) collective-permute-start(f32[3,2,8,256]{3,2,0,1:T(8,128)S(1)} %get-tuple-element.24), channel_id=1, source_target_pairs={{0,1},{1,0},{2,3},{3,2},{4,5},{5,4},{6,7},{7,6},{8,9},{9,8},{10,11... | collective-permute-start | bytes 147464 | tf_op jit(solution)/shard_map/ppermute | solution.py:25
  5.2 2.6 %collective-permute-start.1 = (f32[3,2,8,256]{3,2,0,1:T(8,128)S(1)}, f32[3,2,8,256]{3,2,0,1:T(8,128)S(1)}, u32[]{:S(2)}, u32[]{:S(2)}) collective-permute-start(f32[3,2,8,256]{3,2,0,1:T(8,128)S(1)} %get-tuple-element.24), channel_id=1, source_target_pairs={{0,2},{1,3},{2,0},{3,1},{4,6},{5,7},{6,4},{7,5},{8,10},{9,11},{10,... | collective-permute-start | bytes 147464 | tf_op jit(solution)/shard_map/ppermute | solution.py:25
  7.8 0.9 %collective-permute-start.3 = (f32[256,128]{1,0:T(8,128)}, f32[256,128]{1,0:T(8,128)S(1)}, u32[]{:S(2)}, u32[]{:S(2)}) collective-permute-start(f32[256,128]{1,0:T(8,128)} %param.6), channel_id=1, source_target_pairs={{0,1},{1,0},{2,3},{3,2},{4,5},{5,4},{6,7},{7,6},{8,9},{9,8},{10,11... | collective-permute-start | bytes 393224 | tf_op jit(solution)/shard_map/ppermute | solution.py:25
  8.7 3.5 %collective-permute-start.4 = (f32[256,128]{1,0:T(8,128)}, f32[256,128]{1,0:T(8,128)S(1)}, u32[]{:S(2)}, u32[]{:S(2)}) collective-permute-start(f32[256,128]{1,0:T(8,128)} %param.6), channel_id=1, source_target_pairs={{0,2},{1,3},{2,0},{3,1},{4,6},{5,7},{6,4},{7,5},{8,10},{9,11},{10,... | collective-permute-start | bytes 393224 | tf_op jit(solution)/shard_map/ppermute | solution.py:25
  12.4 2.0 %collective-permute-done.2 = f32[3,2,8,256]{3,2,0,1:T(8,128)S(1)} collective-permute-done((f32[3,2,8,256]{3,2,0,1:T(8,128)S(1)}, f32[3,2,8,256]{3,2,0,1:T(8,128)S(1)}, u32[]{:S(2)}, u32[]{:S(2)}) %collective-permute-start.2) | collective-permute-done | bytes 49184 | tf_op jit(solution)/shard_map/ppermute | solution.py:25
  15.3 1.6 %collective-permute-start.9 = (f32[2,4,8,256]{3,2,1,0:T(8,128)S(1)}, f32[2,4,8,256]{3,2,1,0:T(8,128)S(1)}, u32[]{:S(2)}, u32[]{:S(2)}) collective-permute-start(f32[2,4,8,256]{3,2,1,0:T(8,128)S(1)} %pad_maximum_fusion.4), channel_id=1, source_target_pairs={{8,0},{12,4},{0,8},{4,12},{9,1},{13,5},{1,9},{5,13},{10,2},{14,6},... | collective-permute-start | bytes 196616 | tf_op jit(solution)/shard_map/ppermute | solution.py:18
  16.8 2.9 %select_reduce_fusion.5 = (f32[4,256,256]{2,1,0:T(8,128)}, f32[4,256,256]{2,1,0:T(8,128)}) fusion(f32[4,8,256]{2,1,0:T(8,128)S(1)} %get-tuple-element.16, f32[4,8,256]{2,1,0:T(8,128)S(1)} %get-tuple-element.12, f32[4,8,256]{2,1,0:T(8,128)S(1)} %get-tuple-element.14), kind=kLoop, calls=%fused_computation.9 | loop fusion | flops 9961472 | bytes 2195456 | tf_op jit(solution)/shard_map/reduce_sum | solution.py:40
  19.7 2.8 %select_reduce_fusion.3 = (f32[4,256,256]{2,1,0:T(8,128)}, f32[4,256,256]{2,1,0:T(8,128)}) fusion(f32[4,8,256]{2,1,0:T(8,128)S(1)} %get-tuple-element.21, f32[4,8,256]{2,1,0:T(8,128)S(1)} %get-tuple-element.22, f32[4,8,256]{2,1,0:T(8,128)S(1)} %get-tuple-element.20), kind=kLoop, calls=%fused_computation.6 | loop fusion | flops 9961472 | bytes 2195456 | tf_op jit(solution)/shard_map/reduce_sum | solution.py:40
  22.6 1.6 %select_reduce_fusion.1 = (f32[4,256,256]{2,1,0:T(8,128)S(1)}, f32[4,256,256]{2,1,0:T(8,128)S(1)}) fusion(f32[4,8,256]{2,1,0:T(8,128)S(1)} %get-tuple-element.18, f32[4,8,256]{2,1,0:T(8,128)S(1)} %get-tuple-element.19, f32[4,8,256]{2,1,0:T(8,128)S(1)} %get-tuple-element.17), kind=kLoop, calls=%fused_computation.3 | loop fusion | flops 9961472 | bytes 2195456 | tf_op jit(solution)/shard_map/reduce_sum | solution.py:40
  25.2 0.9 %copy-done.2 = f32[4,256,256]{2,1,0:T(8,128)S(1)} copy-done((f32[4,256,256]{2,1,0:T(8,128)S(1)}, f32[4,256,256]{2,1,0:T(8,128)}, u32[]{:S(2)}) %copy-start.2) | copy-done | bytes 1048600
  26.1 1.6 %fusion.25 = f32[1024,128]{1,0:T(8,128)S(1)} fusion(f32[1024,128]{1,0:T(8,128)S(1)} %bitcast_select_fusion, f32[1024,256]{1,0:T(8,128)} %bitcast.148, f32[1024,256]{1,0:T(8,128)S(1)} %bitcast.142, f32[256,128]{1,0:T(8,128)S(1)} %copy-done.4), kind=kOutput, calls=%fused_computation.56 | convolution fusion | flops 101318656 | bytes 2162688 | tf_op jit(solution)/shard_map/dot_general | solution.py:32
  31.6 0.6 %fusion.111 = f32[128,128]{1,0:T(8,128)S(1)} fusion(f32[128,128]{1,0:T(8,128)S(1)} %fusion.113, f32[1024,128]{1,0:T(8,128)S(1)} %fusion.41, f32[1024,128]{1,0:T(8,128)S(1)} %bitcast_select_fusion), kind=kOutput, calls=%fused_computation.151 | convolution fusion | flops 100712448 | bytes 1179648 | tf_op jit(solution)/shard_map/dot_general | solution.py:79
  35.6 0.6 %fusion.107 = f32[128,128]{1,0:T(8,128)S(1)} fusion(f32[128,128]{1,0:T(8,128)S(1)} %fusion.109, f32[1024,128]{1,0:T(8,128)S(1)} %fusion.53, f32[1024,128]{1,0:T(8,128)S(1)} %fusion.1), kind=kOutput, calls=%fused_computation.145 | convolution fusion | flops 100712448 | bytes 1179648 | tf_op jit(solution)/shard_map/dot_general | solution.py:79
  36.7 1.0 %collective-permute-start.8 = (f32[128,128]{1,0:T(8,128)S(1)}, f32[128,128]{1,0:T(8,128)S(1)}, u32[]{:S(2)}, u32[]{:S(2)}) collective-permute-start(f32[128,128]{1,0:T(8,128)S(1)} %fusion.107), channel_id=1, source_target_pairs={{4,0},{8,4},{12,8},{0,12},{5,1},{9,5},{13,9},{1,13},{6,2},{10,6},{... | collective-permute-start | bytes 196616 | tf_op jit(solution)/shard_map/ppermute | solution.py:18
  38.1 0.6 %fusion.105 = f32[128,128]{1,0:T(8,128)S(1)} fusion(f32[128,128]{1,0:T(8,128)S(1)} %collective-permute-done.10, f32[1024,128]{1,0:T(8,128)S(1)} %fusion.61, f32[1024,128]{1,0:T(8,128)S(1)} %fusion.1), kind=kOutput, calls=%fused_computation.142 | convolution fusion | flops 100712448 | bytes 1179648 | tf_op jit(solution)/shard_map/dot_general | solution.py:79
  39.1 0.6 %fusion.103 = f32[128,128]{1,0:T(8,128)S(1)} fusion(f32[128,128]{1,0:T(8,128)S(1)} %fusion.105, f32[1024,128]{1,0:T(8,128)S(1)} %fusion.65, f32[1024,128]{1,0:T(8,128)S(1)} %fusion.1), kind=kOutput, calls=%fused_computation.139 | convolution fusion | flops 100712448 | bytes 1179648 | tf_op jit(solution)/shard_map/dot_general | solution.py:79
  40.2 0.7 %collective-permute-start.11 = (f32[128,128]{1,0:T(8,128)S(1)}, f32[128,128]{1,0:T(8,128)S(1)}, u32[]{:S(2)}, u32[]{:S(2)}) collective-permute-start(f32[128,128]{1,0:T(8,128)S(1)} %fusion.103), channel_id=1, source_target_pairs={{4,0},{8,4},{12,8},{0,12},{5,1},{9,5},{13,9},{1,13},{6,2},{10,6},{... | collective-permute-start | bytes 196616 | tf_op jit(solution)/shard_map/ppermute | solution.py:18
  41.9 0.6 %fusion.101 = f32[128,128]{1,0:T(8,128)S(1)} fusion(f32[128,128]{1,0:T(8,128)S(1)} %collective-permute-done.8, f32[1024,128]{1,0:T(8,128)S(1)} %fusion.73, f32[1024,128]{1,0:T(8,128)S(1)} %fusion.3), kind=kOutput, calls=%fused_computation.136 | convolution fusion | flops 100712448 | bytes 1179648 | tf_op jit(solution)/shard_map/dot_general | solution.py:79
  44.5 0.6 %fusion.97 = f32[128,128]{1,0:T(8,128)S(1)} fusion(f32[128,128]{1,0:T(8,128)S(1)} %collective-permute-done.11, f32[1024,128]{1,0:T(8,128)S(1)} %fusion.81, f32[1024,128]{1,0:T(8,128)S(1)} %fusion.3), kind=kOutput, calls=%fused_computation.130 | convolution fusion | flops 100712448 | bytes 1179648 | tf_op jit(solution)/shard_map/dot_general | solution.py:79
  47.8 0.7 %fusion.129 = f32[256,128]{1,0:T(8,128)} fusion(f32[1024,128]{1,0:T(8,128)S(1)} %fusion.124, s32[]{:T(128)S(6)} %select_n.64, f32[1024,128]{1,0:T(8,128)S(1)} %fusion.3), kind=kLoop, calls=%fused_computation.176 | loop fusion | flops 98304 | bytes 393220 | tf_op jit(solution)/shard_map/sub | solution.py:88
  48.5 3.4 %collective-permute-done.12 = f32[256,128]{1,0:T(8,128)S(1)} collective-permute-done((f32[256,128]{1,0:T(8,128)S(1)}, f32[256,128]{1,0:T(8,128)S(1)}, u32[]{:S(2)}, u32[]{:S(2)}) %collective-permute-start.12) | collective-permute-done | bytes 131104 | tf_op jit(solution)/shard_map/ppermute | solution.py:18
  51.9 0.7 %copy.16 = f32[256,128]{1,0:T(8,128)} copy(f32[256,128]{1,0:T(8,128)S(1)} %collective-permute-done.12) | data formatting | bytes 262144
  (75 shorter events, 16.4 us)
Async XLA Ops:
  2.1 10.2 %collective-permute-start = (f32[3,2,8,256]{3,2,0,1:T(8,128)S(1)}, f32[3,2,8,256]{3,2,0,1:T(8,128)S(1)}, u32[]{:S(2)}, u32[]{:S(2)}) collective-permute-start(f32[3,2,8,256]{3,2,0,1:T(8,128)S(1)} %get-tuple-element.24), channel_id=1, source_target_pairs={{0,1},{1,0},{2,3},{3,2},{4,5},{5,4},{6,7},{7,6},{8,9},{9,8},{10,11... | collective-permute-start | bytes 147464 | tf_op jit(solution)/shard_map/ppermute | solution.py:25
  5.2 7.2 %collective-permute-start.1 = (f32[3,2,8,256]{3,2,0,1:T(8,128)S(1)}, f32[3,2,8,256]{3,2,0,1:T(8,128)S(1)}, u32[]{:S(2)}, u32[]{:S(2)}) collective-permute-start(f32[3,2,8,256]{3,2,0,1:T(8,128)S(1)} %get-tuple-element.24), channel_id=1, source_target_pairs={{0,2},{1,3},{2,0},{3,1},{4,6},{5,7},{6,4},{7,5},{8,10},{9,11},{10,... | collective-permute-start | bytes 147464 | tf_op jit(solution)/shard_map/ppermute | solution.py:25
  7.8 6.6 %collective-permute-start.2 = (f32[3,2,8,256]{3,2,0,1:T(8,128)S(1)}, f32[3,2,8,256]{3,2,0,1:T(8,128)S(1)}, u32[]{:S(2)}, u32[]{:S(2)}) collective-permute-start(f32[3,2,8,256]{3,2,0,1:T(8,128)S(1)} %get-tuple-element.24), channel_id=1, source_target_pairs={{0,3},{1,2},{2,1},{3,0},{4,7},{5,6},{6,5},{7,4},{8,11},{9,10},{10,... | collective-permute-start | bytes 147464 | tf_op jit(solution)/shard_map/ppermute | solution.py:25
  7.8 16.4 %collective-permute-start.3 = (f32[256,128]{1,0:T(8,128)}, f32[256,128]{1,0:T(8,128)S(1)}, u32[]{:S(2)}, u32[]{:S(2)}) collective-permute-start(f32[256,128]{1,0:T(8,128)} %param.6), channel_id=1, source_target_pairs={{0,1},{1,0},{2,3},{3,2},{4,5},{5,4},{6,7},{7,6},{8,9},{9,8},{10,11... | collective-permute-start | bytes 393224 | tf_op jit(solution)/shard_map/ppermute | solution.py:25
  8.7 15.5 %collective-permute-start.4 = (f32[256,128]{1,0:T(8,128)}, f32[256,128]{1,0:T(8,128)S(1)}, u32[]{:S(2)}, u32[]{:S(2)}) collective-permute-start(f32[256,128]{1,0:T(8,128)} %param.6), channel_id=1, source_target_pairs={{0,2},{1,3},{2,0},{3,1},{4,6},{5,7},{6,4},{7,5},{8,10},{9,11},{10,... | collective-permute-start | bytes 393224 | tf_op jit(solution)/shard_map/ppermute | solution.py:25
  12.3 11.9 %collective-permute-start.5 = (f32[256,128]{1,0:T(8,128)}, f32[256,128]{1,0:T(8,128)S(1)}, u32[]{:S(2)}, u32[]{:S(2)}) collective-permute-start(f32[256,128]{1,0:T(8,128)} %param.6), channel_id=1, source_target_pairs={{0,3},{1,2},{2,1},{3,0},{4,7},{5,6},{6,5},{7,4},{8,11},{9,10},{10,... | collective-permute-start | bytes 393224 | tf_op jit(solution)/shard_map/ppermute | solution.py:25
  15.2 4.5 %collective-permute-start.7 = (f32[2,4,8,256]{3,2,1,0:T(8,128)S(1)}, f32[2,4,8,256]{3,2,1,0:T(8,128)S(1)}, u32[]{:S(2)}, u32[]{:S(2)}) collective-permute-start(f32[2,4,8,256]{3,2,1,0:T(8,128)S(1)} %pad_maximum_fusion.3), channel_id=1, source_target_pairs={{4,0},{8,4},{12,8},{0,12},{5,1},{9,5},{13,9},{1,13},{6,2},{10,6},{... | collective-permute-start | bytes 196616 | tf_op jit(solution)/shard_map/ppermute | solution.py:18
  15.3 7.3 %collective-permute-start.9 = (f32[2,4,8,256]{3,2,1,0:T(8,128)S(1)}, f32[2,4,8,256]{3,2,1,0:T(8,128)S(1)}, u32[]{:S(2)}, u32[]{:S(2)}) collective-permute-start(f32[2,4,8,256]{3,2,1,0:T(8,128)S(1)} %pad_maximum_fusion.4), channel_id=1, source_target_pairs={{8,0},{12,4},{0,8},{4,12},{9,1},{13,5},{1,9},{5,13},{10,2},{14,6},... | collective-permute-start | bytes 196616 | tf_op jit(solution)/shard_map/ppermute | solution.py:18
  22.5 1.7 %copy-start.5 = (f32[256,128]{1,0:T(8,128)S(1)}, f32[256,128]{1,0:T(8,128)}, u32[]{:S(2)}) copy-start(f32[256,128]{1,0:T(8,128)} %param.6) | copy-start | bytes 393220
  24.3 0.9 %copy-start.4 = (f32[256,128]{1,0:T(8,128)S(1)}, f32[256,128]{1,0:T(8,128)}, u32[]{:S(2)}) copy-start(f32[256,128]{1,0:T(8,128)} %param.5) | copy-start | bytes 393220
  24.9 1.2 %copy-start.2 = (f32[4,256,256]{2,1,0:T(8,128)S(1)}, f32[4,256,256]{2,1,0:T(8,128)}, u32[]{:S(2)}) copy-start(f32[4,256,256]{2,1,0:T(8,128)} %get-tuple-element.6) | copy-start | bytes 3145732
  26.1 1.6 %copy-start.3 = (f32[4,256,256]{2,1,0:T(8,128)S(1)}, f32[4,256,256]{2,1,0:T(8,128)}, u32[]{:S(2)}) copy-start(f32[4,256,256]{2,1,0:T(8,128)} %get-tuple-element.7) | copy-start | bytes 3145732
  30.2 3.6 %collective-permute-start.6 = (f32[128,128]{1,0:T(8,128)S(1)}, f32[128,128]{1,0:T(8,128)S(1)}, u32[]{:S(2)}, u32[]{:S(2)}) collective-permute-start(f32[128,128]{1,0:T(8,128)S(1)} %fusion.115), channel_id=1, source_target_pairs={{4,0},{8,4},{12,8},{0,12},{5,1},{9,5},{13,9},{1,13},{6,2},{10,6},{... | collective-permute-start | bytes 196616 | tf_op jit(solution)/shard_map/ppermute | solution.py:18
  32.6 1.2 %copy-start = (f32[4,256,256]{2,1,0:T(8,128)S(1)}, f32[4,256,256]{2,1,0:T(8,128)}, u32[]{:S(2)}) copy-start(f32[4,256,256]{2,1,0:T(8,128)} %get-tuple-element.4) | copy-start | bytes 3145732
  32.6 1.5 %copy-start.1 = (f32[4,256,256]{2,1,0:T(8,128)S(1)}, f32[4,256,256]{2,1,0:T(8,128)}, u32[]{:S(2)}) copy-start(f32[4,256,256]{2,1,0:T(8,128)} %get-tuple-element.5) | copy-start | bytes 3145732
  32.6 5.0 %collective-permute-start.10 = (f32[128,128]{1,0:T(8,128)S(1)}, f32[128,128]{1,0:T(8,128)S(1)}, u32[]{:S(2)}, u32[]{:S(2)}) collective-permute-start(f32[128,128]{1,0:T(8,128)S(1)} %fusion.111), channel_id=1, source_target_pairs={{4,0},{8,4},{12,8},{0,12},{5,1},{9,5},{13,9},{1,13},{6,2},{10,6},{... | collective-permute-start | bytes 196616 | tf_op jit(solution)/shard_map/ppermute | solution.py:18
  36.7 4.8 %collective-permute-start.8 = (f32[128,128]{1,0:T(8,128)S(1)}, f32[128,128]{1,0:T(8,128)S(1)}, u32[]{:S(2)}, u32[]{:S(2)}) collective-permute-start(f32[128,128]{1,0:T(8,128)S(1)} %fusion.107), channel_id=1, source_target_pairs={{4,0},{8,4},{12,8},{0,12},{5,1},{9,5},{13,9},{1,13},{6,2},{10,6},{... | collective-permute-start | bytes 196616 | tf_op jit(solution)/shard_map/ppermute | solution.py:18
  40.2 3.9 %collective-permute-start.11 = (f32[128,128]{1,0:T(8,128)S(1)}, f32[128,128]{1,0:T(8,128)S(1)}, u32[]{:S(2)}, u32[]{:S(2)}) collective-permute-start(f32[128,128]{1,0:T(8,128)S(1)} %fusion.103), channel_id=1, source_target_pairs={{4,0},{8,4},{12,8},{0,12},{5,1},{9,5},{13,9},{1,13},{6,2},{10,6},{... | collective-permute-start | bytes 196616 | tf_op jit(solution)/shard_map/ppermute | solution.py:18
  46.6 5.3 %collective-permute-start.12 = (f32[256,128]{1,0:T(8,128)S(1)}, f32[256,128]{1,0:T(8,128)S(1)}, u32[]{:S(2)}, u32[]{:S(2)}) collective-permute-start(f32[256,128]{1,0:T(8,128)S(1)} %pad_maximum_fusion.2), channel_id=1, source_target_pairs={{8,0},{12,4},{0,8},{4,12},{9,1},{13,5},{1,9},{5,13},{10,2},{14,6},... | collective-permute-start | bytes 393224 | tf_op jit(solution)/shard_map/ppermute | solution.py:18
